TPU v7x, 768 devices: a whole 4x8x12 slice. The times are simulated.
768 devices in a mesh: grp: 4 (over z_hi, core), lon: 48 (over z_lo, y), lat: 4 (over x).
Axes of the slice: x: 4, y: 8, z: 12 (z_hi: 2, z_lo: 6; z = z_hi * 6 + z_lo), core: 2. Of those that a mesh axis runs over, the one named last changes fastest.
Arguments:
- state: float32 [4, 40, 1152, 512], P('grp', None, 'lon', 'lat'), may hold values from -6 to 6
- depth: int32 [1152, 512], P('lon', 'lat'), may hold values from 0 to 6
- rates: float32 [20, 20], replicated, may hold values from -1.25 to 1.25
- grazing: float32 [20], replicated, may hold values from -3 to 3
Outputs:
- state_out: float32 [4, 40, 1152, 512], P('grp', None, 'lon', 'lat')
Inputs may be any that keep to these rules, and one draw needn't show every extreme that they name: `depth`: number of wet levels of a column; 0 is land.
All inputs are finite; a program needn't handle non-finite values.
Results may differ from a plain program's by a relative error of at most 0.0003.
Values sent between devices are 32-bit elements; how exact they have to be, the bound alone decides.
No kernel may reach another device: no remote copies, remote signals or barrier semaphores. Data moves between devices by JAX's collectives and lax.ppermute only.
A program may use at most 32 MiB of HBM per device.

v0:
```python
import jax
import jax.numpy as jnp
from jax import lax
from jax.sharding import PartitionSpec as P

LZ = 2
NTR = 20
SECTIONS = 4
NSUB = 4


def padded_2(block, sides, width):
    for axis, dim in sides:
        count = lax.axis_size(axis)
        forward = [(i, i + 1) for i in range(count - 1)]
        forward.append((count - 1, 0))
        backward = [(target, source) for source, target in forward]
        low = lax.ppermute(
            lax.slice_in_dim(block, block.shape[dim] - width, None, axis=dim), axis, forward
        )
        high = lax.ppermute(lax.slice_in_dim(block, 0, width, axis=dim), axis, backward)
        block = jnp.concatenate([low, block, high], axis=dim)
    return block


def center_of(padded):
    return padded[..., 1:-1, 1:-1]


def grad_x(padded):
    return padded[..., 2:, 1:-1] - padded[..., :-2, 1:-1]


def grad_y(padded):
    return padded[..., 1:-1, 2:] - padded[..., 1:-1, :-2]


def laplace(padded):
    return (
        padded[..., 2:, 1:-1]
        + padded[..., :-2, 1:-1]
        + padded[..., 1:-1, 2:]
        + padded[..., 1:-1, :-2]
        - 4.0 * center_of(padded)
    )


def advance_dynamics(zonal_pad, merid_pad, temp_pad, surf_pad, wet_mask, land_mask, coriolis_rows):
    zonal = center_of(zonal_pad)
    merid = center_of(merid_pad)
    temper = center_of(temp_pad)
    surface = center_of(surf_pad)
    divergence = jnp.sum(grad_x(zonal_pad) + grad_y(merid_pad), axis=0)
    zonal_new = wet_mask * (zonal + coriolis_rows * merid - 0.5 * grad_x(surf_pad))
    merid_new = wet_mask * (merid - coriolis_rows * zonal - 0.5 * grad_y(surf_pad))
    surface_new = land_mask * (surface - 0.25 / zonal.shape[0] * divergence)
    temper_new = wet_mask * (
        temper
        - 0.25 * (zonal * grad_x(temp_pad) + merid * grad_y(temp_pad))
        + 0.1 * laplace(temp_pad)
    )
    return (zonal_new, merid_new, temper_new, surface_new)


def advect_tracers(tracer_pad, zonal, merid, wet_mask):
    return wet_mask * (
        center_of(tracer_pad)
        - 0.25 * (zonal * grad_x(tracer_pad) + merid * grad_y(tracer_pad))
        + 0.1 * laplace(tracer_pad)
    )


def section_rows(padded, wet_mask, land_mask, coriolis_rows):
    levels = (padded.shape[0] - 1) // 3
    results = advance_dynamics(
        padded[:levels],
        padded[levels : 2 * levels],
        padded[2 * levels : 3 * levels],
        padded[3 * levels],
        wet_mask,
        land_mask,
        coriolis_rows,
    )
    return jnp.concatenate([results[0], results[1], results[2], results[3][None]], axis=0)


def fix_rim(padded, width, lat_pos, lat_count):
    length = padded.shape[-1]
    positions = jnp.arange(length)
    lower = (positions < width) & (lat_pos == 0)
    upper = (positions >= length - width) & (lat_pos == lat_count - 1)
    return jnp.where(lower | upper, 0.0, padded)


def body(state, depth, rates, grazing):
    groups = lax.axis_size("grp")
    member = lax.axis_index("grp")
    lat_pos = lax.axis_index("lat")
    lat_count = lax.axis_size("lat")
    local = state[0]
    field_rows, columns, lat_rows = local.shape
    total_levels = LZ * (groups - 1)
    dyn_rows = 3 * total_levels + 1
    lat_total = lat_rows * lat_count
    depth_f = depth.astype(jnp.float32)
    level_index = jnp.arange(total_levels).astype(jnp.float32)[:, None, None]
    fields = local[:dyn_rows]
    wet_local = (level_index < depth_f[None]).astype(jnp.float32)
    land_local = (depth_f > 0).astype(jnp.float32)
    coord = (lat_pos * lat_rows - 0 + jnp.arange(lat_rows + 2 * 0)).astype(jnp.float32)
    coriolis_local = 0.3 * jnp.sin(jnp.pi * (coord + 0.5) / lat_total - jnp.pi / 2)
    current = fields
    for section_index in range(SECTIONS):
        padded = padded_2(current, (("lon", 1), ("lat", 2)), 1)
        padded = fix_rim(padded, 1, lat_pos, lat_count)
        current = section_rows(padded, wet_local, land_local, coriolis_local)
    zonal = current[:total_levels]
    merid = current[total_levels : 2 * total_levels]
    temper = current[2 * total_levels : 3 * total_levels]
    surface = current[3 * total_levels]
    first_level = jnp.maximum(member - 1, 0) * LZ
    forcing = jnp.stack(
        [
            zonal.reshape(groups - 1, LZ, columns, lat_rows),
            merid.reshape(groups - 1, LZ, columns, lat_rows),
            temper.reshape(groups - 1, LZ, columns, lat_rows),
        ],
        axis=1,
    )
    outgoing = jnp.concatenate([jnp.zeros((1,) + forcing.shape[1:], jnp.float32), forcing], axis=0)
    received = lax.all_to_all(outgoing, "grp", split_axis=0, concat_axis=0, tiled=True)
    own_zonal = received[0, 0]
    own_merid = received[0, 1]
    own_temper = received[0, 2]
    member_levels = (first_level + jnp.arange(LZ)).astype(jnp.float32)[:, None, None]
    wet_member = (member_levels < depth_f[None]).astype(jnp.float32)
    advected = local.reshape(NTR, LZ, columns, lat_rows)
    for sub_index in range(NSUB):
        padded = padded_2(
            advected.reshape(field_rows, columns, lat_rows), (("lon", 1), ("lat", 2)), 1
        )
        padded = fix_rim(padded, 1, lat_pos, lat_count)
        advected = advect_tracers(
            padded.reshape(NTR, LZ, columns + 2, lat_rows + 2), own_zonal, own_merid, wet_member
        )
    kinetic = jnp.einsum("ts,szxy->tzxy", rates, advected, precision=lax.Precision.HIGHEST)
    kinetic = kinetic + grazing[:, None, None, None] * (advected[0] * advected[1])[None]
    updated = wet_member[None] * (advected + 0.2 * jnp.exp(0.05 * own_temper)[None] * kinetic)
    light_factor = jnp.exp(-(member_levels + 0.5) / total_levels)
    heating = 0.3 * wet_member * updated[0] * light_factor
    returned = lax.all_gather(heating, "grp", axis=0, tiled=True)
    temper_final = temper + returned[LZ:]
    unused = jnp.zeros((field_rows - dyn_rows, columns, lat_rows), jnp.float32)
    dyn_out = jnp.concatenate([zonal, merid, temper_final, surface[None], unused], axis=0)
    result = jnp.where(member == 0, dyn_out, updated.reshape(field_rows, columns, lat_rows))
    return result[None]


def solution(mesh):
    in_specs = (P("grp", None, "lon", "lat"), P("lon", "lat"), P(), P())
    out_specs = P("grp", None, "lon", "lat")
    return jax.shard_map(body, mesh=mesh, in_specs=in_specs, out_specs=out_specs, check_vma=False)
```

profile of v0, /device:TPU:1, one launch (start us, length us, event | category | flops | bytes accessed | tf_op | source)
XLA Modules:
  0.0 249.5 jit_solution(12287204367169583739)
XLA Ops:
  0.0 1.0 slice_bitcast_fusion
  1.0 4.0 %collective-permute-start = (f32[19,1,128]{2,1,0:T(1,128)S(1)}, f32[19,1,128]{2,1,0:T(1,128)S(1)}, u32[]{:S(2)}, u32[]{:S(2)}) collective-permute-start(f32[19,1,128]{2,1,0:T(1,128)S(1)} %get-tuple-element.55), channel_id=1, source_target_pairs={{0,4},{4,8},{8,12},{12,16},{16,20},{20,24},{24,28},{28,32},{32,36}... | collective-permute-start | bytes 29192 | tf_op jit(solution)/shard_map/ppermute | solution.py:18
  5.0 14.1 %collective-permute-start.1 = (f32[19,1,128]{2,1,0:T(1,128)S(1)}, f32[19,1,128]{2,1,0:T(1,128)S(1)}, u32[]{:S(2)}, u32[]{:S(2)}) collective-permute-start(f32[19,1,128]{2,1,0:T(1,128)S(1)} %get-tuple-element.56), channel_id=1, source_target_pairs={{4,0},{8,4},{12,8},{16,12},{20,16},{24,20},{28,24},{32,28},{36,32}... | collective-permute-start | bytes 29192 | tf_op jit(solution)/shard_map/ppermute | solution.py:21
  19.2 0.7 collective-permute-done.1
  20.1 3.1 %collective-permute-start.2 = (f32[19,26,1]{2,1,0:T(8,128)S(1)}, f32[19,26,1]{2,1,0:T(8,128)S(1)}, u32[]{:S(2)}, u32[]{:S(2)}) collective-permute-start(f32[19,26,1]{2,1,0:T(8,128)S(1)} %get-tuple-element.44), channel_id=1, source_target_pairs={{0,1},{1,2},{2,3},{3,0},{4,5},{5,6},{6,7},{7,4},{8,9},{9,10},{10,1... | collective-permute-start | bytes 5936 | tf_op jit(solution)/shard_map/ppermute | solution.py:18
  23.2 3.4 %collective-permute-start.3 = (f32[19,26,1]{2,1,0:T(8,128)S(1)}, f32[19,26,1]{2,1,0:T(8,128)S(1)}, u32[]{:S(2)}, u32[]{:S(2)}) collective-permute-start(f32[19,26,1]{2,1,0:T(8,128)S(1)} %get-tuple-element.45), channel_id=1, source_target_pairs={{1,0},{2,1},{3,2},{0,3},{5,4},{6,5},{7,6},{4,7},{9,8},{10,9},{11,1... | collective-permute-start | bytes 5936 | tf_op jit(solution)/shard_map/ppermute | solution.py:21
  26.7 2.3 collective-permute-done.2
  29.0 1.9 collective-permute-done.3
  31.7 1.9 collective-permute-start.4
  33.7 10.5 %collective-permute-start.5 = (f32[19,1,128]{2,1,0:T(1,128)S(1)}, f32[19,1,128]{2,1,0:T(1,128)S(1)}, u32[]{:S(2)}, u32[]{:S(2)}) collective-permute-start(f32[19,1,128]{2,1,0:T(1,128)S(1)} %get-tuple-element.54), channel_id=1, source_target_pairs={{4,0},{8,4},{12,8},{16,12},{20,16},{24,20},{28,24},{32,28},{36,32}... | collective-permute-start | bytes 29192 | tf_op jit(solution)/shard_map/ppermute | solution.py:21
  44.2 0.8 collective-permute-done.5
  45.2 4.2 %collective-permute-start.6 = (f32[19,26,1]{2,1,0:T(8,128)S(1)}, f32[19,26,1]{2,1,0:T(8,128)S(1)}, u32[]{:S(2)}, u32[]{:S(2)}) collective-permute-start(f32[19,26,1]{2,1,0:T(8,128)S(1)} %get-tuple-element.42), channel_id=1, source_target_pairs={{0,1},{1,2},{2,3},{3,0},{4,5},{5,6},{6,7},{7,4},{8,9},{9,10},{10,1... | collective-permute-start | bytes 5936 | tf_op jit(solution)/shard_map/ppermute | solution.py:18
  49.4 2.4 collective-permute-start.7
  51.9 2.2 collective-permute-done.6
  54.1 3.1 %collective-permute-done.7 = f32[19,26,1]{2,1,0:T(8,128)S(1)} collective-permute-done((f32[19,26,1]{2,1,0:T(8,128)S(1)}, f32[19,26,1]{2,1,0:T(8,128)S(1)}, u32[]{:S(2)}, u32[]{:S(2)}) %collective-permute-start.7) | collective-permute-done | bytes 2008 | tf_op jit(solution)/shard_map/ppermute | solution.py:21
  58.1 1.9 collective-permute-start.8
  60.0 10.5 %collective-permute-start.9 = (f32[19,1,128]{2,1,0:T(1,128)S(1)}, f32[19,1,128]{2,1,0:T(1,128)S(1)}, u32[]{:S(2)}, u32[]{:S(2)}) collective-permute-start(f32[19,1,128]{2,1,0:T(1,128)S(1)} %get-tuple-element.52), channel_id=1, source_target_pairs={{4,0},{8,4},{12,8},{16,12},{20,16},{24,20},{28,24},{32,28},{36,32}... | collective-permute-start | bytes 29192 | tf_op jit(solution)/shard_map/ppermute | solution.py:21
  70.7 0.7 collective-permute-done.9
  71.5 2.1 collective-permute-start.10
  73.6 4.4 %collective-permute-start.11 = (f32[19,26,1]{2,1,0:T(8,128)S(1)}, f32[19,26,1]{2,1,0:T(8,128)S(1)}, u32[]{:S(2)}, u32[]{:S(2)}) collective-permute-start(f32[19,26,1]{2,1,0:T(8,128)S(1)} %get-tuple-element.41), channel_id=1, source_target_pairs={{1,0},{2,1},{3,2},{0,3},{5,4},{6,5},{7,6},{4,7},{9,8},{10,9},{11,1... | collective-permute-start | bytes 5936 | tf_op jit(solution)/shard_map/ppermute | solution.py:21
  78.1 1.9 collective-permute-start.16
  80.0 10.5 %collective-permute-start.17 = (f32[40,1,128]{2,0,1:T(8,128)S(1)}, f32[40,1,128]{2,0,1:T(8,128)S(1)}, u32[]{:S(2)}, u32[]{:S(2)}) collective-permute-start(f32[40,1,128]{2,0,1:T(8,128)S(1)} %get-tuple-element.37), channel_id=1, source_target_pairs={{4,0},{8,4},{12,8},{16,12},{20,16},{24,20},{28,24},{32,28},{36,32}... | collective-permute-start | bytes 61448 | tf_op jit(solution)/shard_map/ppermute | solution.py:21
  91.4 1.9 collective-permute-start.12
  93.4 10.3 %collective-permute-start.13 = (f32[19,1,128]{2,1,0:T(1,128)S(1)}, f32[19,1,128]{2,1,0:T(1,128)S(1)}, u32[]{:S(2)}, u32[]{:S(2)}) collective-permute-start(f32[19,1,128]{2,1,0:T(1,128)S(1)} %get-tuple-element.50), channel_id=1, source_target_pairs={{4,0},{8,4},{12,8},{16,12},{20,16},{24,20},{28,24},{32,28},{36,32}... | collective-permute-start | bytes 29192 | tf_op jit(solution)/shard_map/ppermute | solution.py:21
  103.7 0.8 collective-permute-done.13
  104.6 1.9 collective-permute-start.14
  106.6 4.6 %collective-permute-start.15 = (f32[19,26,1]{2,1,0:T(8,128)S(1)}, f32[19,26,1]{2,1,0:T(8,128)S(1)}, u32[]{:S(2)}, u32[]{:S(2)}) collective-permute-start(f32[19,26,1]{2,1,0:T(8,128)S(1)} %get-tuple-element.39), channel_id=1, source_target_pairs={{1,0},{2,1},{3,2},{0,3},{5,4},{6,5},{7,6},{4,7},{9,8},{10,9},{11,1... | collective-permute-start | bytes 5936 | tf_op jit(solution)/shard_map/ppermute | solution.py:21
  111.2 2.6 %collective-permute-done.14 = f32[19,26,1]{2,1,0:T(8,128)S(1)} collective-permute-done((f32[19,26,1]{2,1,0:T(8,128)S(1)}, f32[19,26,1]{2,1,0:T(8,128)S(1)}, u32[]{:S(2)}, u32[]{:S(2)}) %collective-permute-start.14) | collective-permute-done | bytes 2008 | tf_op jit(solution)/shard_map/ppermute | solution.py:18
  113.8 1.2 collective-permute-done.15
  115.7 0.8 bitcast_dynamic-update-slice_fusion.1
  116.5 0.7 bitcast_dynamic-update-slice_fusion
  117.2 0.7 select_maximum_fusion
  118.0 19.2 %all-to-all-start = ((f32[4,3,2,24,128]{4,3,2,1,0:T(8,128)}), f32[4,3,2,24,128]{4,3,2,1,0:T(8,128)}, u32[]{:S(2)}, u32[]{:S(2)}) async-start(f32[4,3,2,24,128]{4,3,2,1,0:T(8,128)} %select_maximum_fusion), calls=%async_computation | async-start | bytes 589824 | tf_op jit(solution)/shard_map/all_to_all | solution.py:131
  138.1 5.3 %collective-permute-start.19 = (f32[40,26,1]{1,0,2:T(8,128)S(1)}, f32[40,26,1]{1,0,2:T(8,128)S(1)}, u32[]{:S(2)}, u32[]{:S(2)}) collective-permute-start(f32[40,26,1]{1,0,2:T(8,128)S(1)} %copy.70), channel_id=1, source_target_pairs={{1,0},{2,1},{3,2},{0,3},{5,4},{6,5},{7,6},{4,7},{9,8},{10,9},{11,1... | collective-permute-start | bytes 12488 | tf_op jit(solution)/shard_map/ppermute | solution.py:21
  143.4 1.9 collective-permute-start.18
  145.6 3.9 %collective-permute-done.18 = f32[40,26,1]{1,0,2:T(8,128)S(1)} collective-permute-done((f32[40,26,1]{1,0,2:T(8,128)S(1)}, f32[40,26,1]{1,0,2:T(8,128)S(1)}, u32[]{:S(2)}, u32[]{:S(2)}) %collective-permute-start.18) | collective-permute-done | bytes 4192 | tf_op jit(solution)/shard_map/ppermute | solution.py:18
  150.3 0.6 maximum_select_fusion
  150.9 0.8 fusion.18
  151.7 0.7 add_multiply_fusion.3
  152.6 1.9 collective-permute-start.20
  154.5 10.3 %collective-permute-start.21 = (f32[40,1,128]{2,1,0:T(1,128)S(1)}, f32[40,1,128]{2,1,0:T(1,128)S(1)}, u32[]{:S(2)}, u32[]{:S(2)}) collective-permute-start(f32[40,1,128]{2,1,0:T(1,128)S(1)} %get-tuple-element.35), channel_id=1, source_target_pairs={{4,0},{8,4},{12,8},{16,12},{20,16},{24,20},{28,24},{32,28},{36,32}... | collective-permute-start | bytes 61448 | tf_op jit(solution)/shard_map/ppermute | solution.py:21
  164.8 0.9 collective-permute-done.21
  166.4 1.9 collective-permute-start.22
  168.7 4.6 %collective-permute-start.23 = (f32[40,26,1]{0,2,1:T(1,128)S(1)}, f32[40,26,1]{0,2,1:T(1,128)S(1)}, u32[]{:S(2)}, u32[]{:S(2)}) collective-permute-start(f32[40,26,1]{0,2,1:T(1,128)S(1)} %copy.45), channel_id=1, source_target_pairs={{1,0},{2,1},{3,2},{0,3},{5,4},{6,5},{7,6},{4,7},{9,8},{10,9},{11,1... | collective-permute-start | bytes 12488 | tf_op jit(solution)/shard_map/ppermute | solution.py:21
  174.6 0.6 maximum_select_fusion.1
  175.2 0.7 add_multiply_fusion.2
  176.0 1.9 collective-permute-start.24
  178.0 10.7 %collective-permute-start.25 = (f32[40,1,128]{2,1,0:T(1,128)S(1)}, f32[40,1,128]{2,1,0:T(1,128)S(1)}, u32[]{:S(2)}, u32[]{:S(2)}) collective-permute-start(f32[40,1,128]{2,1,0:T(1,128)S(1)} %get-tuple-element.33), channel_id=1, source_target_pairs={{4,0},{8,4},{12,8},{16,12},{20,16},{24,20},{28,24},{32,28},{36,32}... | collective-permute-start | bytes 61448 | tf_op jit(solution)/shard_map/ppermute | solution.py:21
  188.7 0.7 collective-permute-done.25
  190.1 1.9 collective-permute-start.26
  192.5 4.8 %collective-permute-start.27 = (f32[40,26,1]{0,2,1:T(1,128)S(1)}, f32[40,26,1]{0,2,1:T(1,128)S(1)}, u32[]{:S(2)}, u32[]{:S(2)}) collective-permute-start(f32[40,26,1]{0,2,1:T(1,128)S(1)} %copy.54), channel_id=1, source_target_pairs={{1,0},{2,1},{3,2},{0,3},{5,4},{6,5},{7,6},{4,7},{9,8},{10,9},{11,1... | collective-permute-start | bytes 12488 | tf_op jit(solution)/shard_map/ppermute | solution.py:21
  198.6 0.6 maximum_select_fusion.2
  199.2 0.7 add_multiply_fusion.1
  200.0 1.9 collective-permute-start.28
  201.9 10.5 %collective-permute-start.29 = (f32[40,1,128]{2,1,0:T(1,128)S(1)}, f32[40,1,128]{2,1,0:T(1,128)S(1)}, u32[]{:S(2)}, u32[]{:S(2)}) collective-permute-start(f32[40,1,128]{2,1,0:T(1,128)S(1)} %get-tuple-element.31), channel_id=1, source_target_pairs={{4,0},{8,4},{12,8},{16,12},{20,16},{24,20},{28,24},{32,28},{36,32}... | collective-permute-start | bytes 61448 | tf_op jit(solution)/shard_map/ppermute | solution.py:21
  212.5 0.9 collective-permute-done.29
  214.5 4.8 %collective-permute-start.31 = (f32[40,26,1]{0,2,1:T(1,128)S(1)}, f32[40,26,1]{0,2,1:T(1,128)S(1)}, u32[]{:S(2)}, u32[]{:S(2)}) collective-permute-start(f32[40,26,1]{0,2,1:T(1,128)S(1)} %copy.63), channel_id=1, source_target_pairs={{1,0},{2,1},{3,2},{0,3},{5,4},{6,5},{7,6},{4,7},{9,8},{10,9},{11,1... | collective-permute-start | bytes 12488 | tf_op jit(solution)/shard_map/ppermute | solution.py:21
  219.4 1.9 collective-permute-start.30
  221.3 3.7 %collective-permute-done.30 = f32[40,26,1]{0,2,1:T(1,128)S(1)} collective-permute-done((f32[40,26,1]{0,2,1:T(1,128)S(1)}, f32[40,26,1]{0,2,1:T(1,128)S(1)}, u32[]{:S(2)}, u32[]{:S(2)}) %collective-permute-start.30) | collective-permute-done | bytes 4192 | tf_op jit(solution)/shard_map/ppermute | solution.py:18
  226.0 0.6 maximum_select_fusion.3
  226.6 0.7 add_multiply_fusion
  227.4 0.7 fusion.3
  228.3 20.3 %all_gather.3 = f32[8,24,128]{2,1,0:T(8,128)S(1)} all-gather(f32[2,24,128]{2,1,0:T(8,128)S(1)} %fusion.15), channel_id=1, replica_groups=mesh['grp'=4,'lon'=48,'lat'=4] {'grp'}, dimensions={0}, use_global_device_ids=true | all-gather | bytes 122880 | tf_op jit(solution)/shard_map/all_gather | solution.py:151
  248.7 0.8 bitcast_select_fusion
  (120 shorter events, 13.9 us)
Async XLA Ops:
  0.0 227.3 %copy-start = (f32[20,20]{1,0:T(8,128)S(1)}, f32[20,20]{1,0:T(8,128)}, u32[]{:S(2)}) copy-start(f32[20,20]{1,0:T(8,128)} %param.6) | copy-start | bytes 4804
  0.0 26.6 %copy-start.3 = (s32[24,128]{1,0:T(8,128)S(1)}, s32[24,128]{1,0:T(8,128)}, u32[]{:S(2)}) copy-start(s32[24,128]{1,0:T(8,128)} %param.5) | copy-start | bytes 36868
  1.0 18.2 %collective-permute-start = (f32[19,1,128]{2,1,0:T(1,128)S(1)}, f32[19,1,128]{2,1,0:T(1,128)S(1)}, u32[]{:S(2)}, u32[]{:S(2)}) collective-permute-start(f32[19,1,128]{2,1,0:T(1,128)S(1)} %get-tuple-element.55), channel_id=1, source_target_pairs={{0,4},{4,8},{8,12},{12,16},{16,20},{20,24},{24,28},{28,32},{32,36}... | collective-permute-start | bytes 29192 | tf_op jit(solution)/shard_map/ppermute | solution.py:18
  5.0 14.9 %collective-permute-start.1 = (f32[19,1,128]{2,1,0:T(1,128)S(1)}, f32[19,1,128]{2,1,0:T(1,128)S(1)}, u32[]{:S(2)}, u32[]{:S(2)}) collective-permute-start(f32[19,1,128]{2,1,0:T(1,128)S(1)} %get-tuple-element.56), channel_id=1, source_target_pairs={{4,0},{8,4},{12,8},{16,12},{20,16},{24,20},{28,24},{32,28},{36,32}... | collective-permute-start | bytes 29192 | tf_op jit(solution)/shard_map/ppermute | solution.py:21
  20.1 8.9 %collective-permute-start.2 = (f32[19,26,1]{2,1,0:T(8,128)S(1)}, f32[19,26,1]{2,1,0:T(8,128)S(1)}, u32[]{:S(2)}, u32[]{:S(2)}) collective-permute-start(f32[19,26,1]{2,1,0:T(8,128)S(1)} %get-tuple-element.44), channel_id=1, source_target_pairs={{0,1},{1,2},{2,3},{3,0},{4,5},{5,6},{6,7},{7,4},{8,9},{9,10},{10,1... | collective-permute-start | bytes 5936 | tf_op jit(solution)/shard_map/ppermute | solution.py:18
  23.2 7.6 %collective-permute-start.3 = (f32[19,26,1]{2,1,0:T(8,128)S(1)}, f32[19,26,1]{2,1,0:T(8,128)S(1)}, u32[]{:S(2)}, u32[]{:S(2)}) collective-permute-start(f32[19,26,1]{2,1,0:T(8,128)S(1)} %get-tuple-element.45), channel_id=1, source_target_pairs={{1,0},{2,1},{3,2},{0,3},{5,4},{6,5},{7,6},{4,7},{9,8},{10,9},{11,1... | collective-permute-start | bytes 5936 | tf_op jit(solution)/shard_map/ppermute | solution.py:21
  31.7 12.5 %collective-permute-start.4 = (f32[19,1,128]{2,1,0:T(1,128)S(1)}, f32[19,1,128]{2,1,0:T(1,128)S(1)}, u32[]{:S(2)}, u32[]{:S(2)}) collective-permute-start(f32[19,1,128]{2,1,0:T(1,128)S(1)} %get-tuple-element.53), channel_id=1, source_target_pairs={{0,4},{4,8},{8,12},{12,16},{16,20},{20,24},{24,28},{28,32},{32,36}... | collective-permute-start | bytes 29192 | tf_op jit(solution)/shard_map/ppermute | solution.py:18
  33.7 11.3 %collective-permute-start.5 = (f32[19,1,128]{2,1,0:T(1,128)S(1)}, f32[19,1,128]{2,1,0:T(1,128)S(1)}, u32[]{:S(2)}, u32[]{:S(2)}) collective-permute-start(f32[19,1,128]{2,1,0:T(1,128)S(1)} %get-tuple-element.54), channel_id=1, source_target_pairs={{4,0},{8,4},{12,8},{16,12},{20,16},{24,20},{28,24},{32,28},{36,32}... | collective-permute-start | bytes 29192 | tf_op jit(solution)/shard_map/ppermute | solution.py:21
  45.2 8.9 %collective-permute-start.6 = (f32[19,26,1]{2,1,0:T(8,128)S(1)}, f32[19,26,1]{2,1,0:T(8,128)S(1)}, u32[]{:S(2)}, u32[]{:S(2)}) collective-permute-start(f32[19,26,1]{2,1,0:T(8,128)S(1)} %get-tuple-element.42), channel_id=1, source_target_pairs={{0,1},{1,2},{2,3},{3,0},{4,5},{5,6},{6,7},{7,4},{8,9},{9,10},{10,1... | collective-permute-start | bytes 5936 | tf_op jit(solution)/shard_map/ppermute | solution.py:18
  49.4 21.1 %copy-start.1 = (f32[1,40,24,128]{3,2,1,0:T(8,128)S(1)}, f32[1,40,24,128]{3,2,1,0:T(8,128)}, u32[]{:S(2)}) copy-start(f32[1,40,24,128]{3,2,1,0:T(8,128)} %param.4) | copy-start | bytes 1474564
  49.4 7.8 %collective-permute-start.7 = (f32[19,26,1]{2,1,0:T(8,128)S(1)}, f32[19,26,1]{2,1,0:T(8,128)S(1)}, u32[]{:S(2)}, u32[]{:S(2)}) collective-permute-start(f32[19,26,1]{2,1,0:T(8,128)S(1)} %get-tuple-element.43), channel_id=1, source_target_pairs={{1,0},{2,1},{3,2},{0,3},{5,4},{6,5},{7,6},{4,7},{9,8},{10,9},{11,1... | collective-permute-start | bytes 5936 | tf_op jit(solution)/shard_map/ppermute | solution.py:21
  58.1 12.6 %collective-permute-start.8 = (f32[19,1,128]{2,1,0:T(1,128)S(1)}, f32[19,1,128]{2,1,0:T(1,128)S(1)}, u32[]{:S(2)}, u32[]{:S(2)}) collective-permute-start(f32[19,1,128]{2,1,0:T(1,128)S(1)} %get-tuple-element.51), channel_id=1, source_target_pairs={{0,4},{4,8},{8,12},{12,16},{16,20},{20,24},{24,28},{28,32},{32,36}... | collective-permute-start | bytes 29192 | tf_op jit(solution)/shard_map/ppermute | solution.py:18
  60.0 11.3 %collective-permute-start.9 = (f32[19,1,128]{2,1,0:T(1,128)S(1)}, f32[19,1,128]{2,1,0:T(1,128)S(1)}, u32[]{:S(2)}, u32[]{:S(2)}) collective-permute-start(f32[19,1,128]{2,1,0:T(1,128)S(1)} %get-tuple-element.52), channel_id=1, source_target_pairs={{4,0},{8,4},{12,8},{16,12},{20,16},{24,20},{28,24},{32,28},{36,32}... | collective-permute-start | bytes 29192 | tf_op jit(solution)/shard_map/ppermute | solution.py:21
  71.5 19.0 %collective-permute-start.10 = (f32[19,26,1]{2,1,0:T(8,128)S(1)}, f32[19,26,1]{2,1,0:T(8,128)S(1)}, u32[]{:S(2)}, u32[]{:S(2)}) collective-permute-start(f32[19,26,1]{2,1,0:T(8,128)S(1)} %get-tuple-element.40), channel_id=1, source_target_pairs={{0,1},{1,2},{2,3},{3,0},{4,5},{5,6},{6,7},{7,4},{8,9},{9,10},{10,1... | collective-permute-start | bytes 5936 | tf_op jit(solution)/shard_map/ppermute | solution.py:18
  73.6 17.0 %collective-permute-start.11 = (f32[19,26,1]{2,1,0:T(8,128)S(1)}, f32[19,26,1]{2,1,0:T(8,128)S(1)}, u32[]{:S(2)}, u32[]{:S(2)}) collective-permute-start(f32[19,26,1]{2,1,0:T(8,128)S(1)} %get-tuple-element.41), channel_id=1, source_target_pairs={{1,0},{2,1},{3,2},{0,3},{5,4},{6,5},{7,6},{4,7},{9,8},{10,9},{11,1... | collective-permute-start | bytes 5936 | tf_op jit(solution)/shard_map/ppermute | solution.py:21
  78.1 33.1 %collective-permute-start.16 = (f32[40,1,128]{2,0,1:T(8,128)S(1)}, f32[40,1,128]{2,0,1:T(8,128)S(1)}, u32[]{:S(2)}, u32[]{:S(2)}) collective-permute-start(f32[40,1,128]{2,0,1:T(8,128)S(1)} %get-tuple-element.36), channel_id=1, source_target_pairs={{0,4},{4,8},{8,12},{12,16},{16,20},{20,24},{24,28},{28,32},{32,36}... | collective-permute-start | bytes 61448 | tf_op jit(solution)/shard_map/ppermute | solution.py:18
  80.0 31.2 %collective-permute-start.17 = (f32[40,1,128]{2,0,1:T(8,128)S(1)}, f32[40,1,128]{2,0,1:T(8,128)S(1)}, u32[]{:S(2)}, u32[]{:S(2)}) collective-permute-start(f32[40,1,128]{2,0,1:T(8,128)S(1)} %get-tuple-element.37), channel_id=1, source_target_pairs={{4,0},{8,4},{12,8},{16,12},{20,16},{24,20},{28,24},{32,28},{36,32}... | collective-permute-start | bytes 61448 | tf_op jit(solution)/shard_map/ppermute | solution.py:21
  91.4 12.2 %collective-permute-start.12 = (f32[19,1,128]{2,1,0:T(1,128)S(1)}, f32[19,1,128]{2,1,0:T(1,128)S(1)}, u32[]{:S(2)}, u32[]{:S(2)}) collective-permute-start(f32[19,1,128]{2,1,0:T(1,128)S(1)} %get-tuple-element.49), channel_id=1, source_target_pairs={{0,4},{4,8},{8,12},{12,16},{16,20},{20,24},{24,28},{28,32},{32,36}... | collective-permute-start | bytes 29192 | tf_op jit(solution)/shard_map/ppermute | solution.py:18
  93.4 11.1 %collective-permute-start.13 = (f32[19,1,128]{2,1,0:T(1,128)S(1)}, f32[19,1,128]{2,1,0:T(1,128)S(1)}, u32[]{:S(2)}, u32[]{:S(2)}) collective-permute-start(f32[19,1,128]{2,1,0:T(1,128)S(1)} %get-tuple-element.50), channel_id=1, source_target_pairs={{4,0},{8,4},{12,8},{16,12},{20,16},{24,20},{28,24},{32,28},{36,32}... | collective-permute-start | bytes 29192 | tf_op jit(solution)/shard_map/ppermute | solution.py:21
  104.6 9.1 %collective-permute-start.14 = (f32[19,26,1]{2,1,0:T(8,128)S(1)}, f32[19,26,1]{2,1,0:T(8,128)S(1)}, u32[]{:S(2)}, u32[]{:S(2)}) collective-permute-start(f32[19,26,1]{2,1,0:T(8,128)S(1)} %get-tuple-element.38), channel_id=1, source_target_pairs={{0,1},{1,2},{2,3},{3,0},{4,5},{5,6},{6,7},{7,4},{8,9},{9,10},{10,1... | collective-permute-start | bytes 5936 | tf_op jit(solution)/shard_map/ppermute | solution.py:18
  106.6 8.4 %collective-permute-start.15 = (f32[19,26,1]{2,1,0:T(8,128)S(1)}, f32[19,26,1]{2,1,0:T(8,128)S(1)}, u32[]{:S(2)}, u32[]{:S(2)}) collective-permute-start(f32[19,26,1]{2,1,0:T(8,128)S(1)} %get-tuple-element.39), channel_id=1, source_target_pairs={{1,0},{2,1},{3,2},{0,3},{5,4},{6,5},{7,6},{4,7},{9,8},{10,9},{11,1... | collective-permute-start | bytes 5936 | tf_op jit(solution)/shard_map/ppermute | solution.py:21
  118.0 33.0 %all-to-all-start = ((f32[4,3,2,24,128]{4,3,2,1,0:T(8,128)}), f32[4,3,2,24,128]{4,3,2,1,0:T(8,128)}, u32[]{:S(2)}, u32[]{:S(2)}) async-start(f32[4,3,2,24,128]{4,3,2,1,0:T(8,128)} %select_maximum_fusion), calls=%async_computation | async-start | bytes 589824 | tf_op jit(solution)/shard_map/all_to_all | solution.py:131
  138.1 11.9 %collective-permute-start.19 = (f32[40,26,1]{1,0,2:T(8,128)S(1)}, f32[40,26,1]{1,0,2:T(8,128)S(1)}, u32[]{:S(2)}, u32[]{:S(2)}) collective-permute-start(f32[40,26,1]{1,0,2:T(8,128)S(1)} %copy.70), channel_id=1, source_target_pairs={{1,0},{2,1},{3,2},{0,3},{5,4},{6,5},{7,6},{4,7},{9,8},{10,9},{11,1... | collective-permute-start | bytes 12488 | tf_op jit(solution)/shard_map/ppermute | solution.py:21
  143.4 6.1 %collective-permute-start.18 = (f32[40,26,1]{1,0,2:T(8,128)S(1)}, f32[40,26,1]{1,0,2:T(8,128)S(1)}, u32[]{:S(2)}, u32[]{:S(2)}) collective-permute-start(f32[40,26,1]{1,0,2:T(8,128)S(1)} %copy.69), channel_id=1, source_target_pairs={{0,1},{1,2},{2,3},{3,0},{4,5},{5,6},{6,7},{7,4},{8,9},{9,10},{10,1... | collective-permute-start | bytes 12488 | tf_op jit(solution)/shard_map/ppermute | solution.py:18
  152.6 12.2 %collective-permute-start.20 = (f32[40,1,128]{2,1,0:T(1,128)S(1)}, f32[40,1,128]{2,1,0:T(1,128)S(1)}, u32[]{:S(2)}, u32[]{:S(2)}) collective-permute-start(f32[40,1,128]{2,1,0:T(1,128)S(1)} %get-tuple-element.34), channel_id=1, source_target_pairs={{0,4},{4,8},{8,12},{12,16},{16,20},{20,24},{24,28},{28,32},{32,36}... | collective-permute-start | bytes 61448 | tf_op jit(solution)/shard_map/ppermute | solution.py:18
  154.5 11.2 %collective-permute-start.21 = (f32[40,1,128]{2,1,0:T(1,128)S(1)}, f32[40,1,128]{2,1,0:T(1,128)S(1)}, u32[]{:S(2)}, u32[]{:S(2)}) collective-permute-start(f32[40,1,128]{2,1,0:T(1,128)S(1)} %get-tuple-element.35), channel_id=1, source_target_pairs={{4,0},{8,4},{12,8},{16,12},{20,16},{24,20},{28,24},{32,28},{36,32}... | collective-permute-start | bytes 61448 | tf_op jit(solution)/shard_map/ppermute | solution.py:21
  166.4 6.9 %collective-permute-start.22 = (f32[40,26,1]{0,2,1:T(1,128)S(1)}, f32[40,26,1]{0,2,1:T(1,128)S(1)}, u32[]{:S(2)}, u32[]{:S(2)}) collective-permute-start(f32[40,26,1]{0,2,1:T(1,128)S(1)} %copy.41), channel_id=1, source_target_pairs={{0,1},{1,2},{2,3},{3,0},{4,5},{5,6},{6,7},{7,4},{8,9},{9,10},{10,1... | collective-permute-start | bytes 12488 | tf_op jit(solution)/shard_map/ppermute | solution.py:18
  168.7 5.4 %collective-permute-start.23 = (f32[40,26,1]{0,2,1:T(1,128)S(1)}, f32[40,26,1]{0,2,1:T(1,128)S(1)}, u32[]{:S(2)}, u32[]{:S(2)}) collective-permute-start(f32[40,26,1]{0,2,1:T(1,128)S(1)} %copy.45), channel_id=1, source_target_pairs={{1,0},{2,1},{3,2},{0,3},{5,4},{6,5},{7,6},{4,7},{9,8},{10,9},{11,1... | collective-permute-start | bytes 12488 | tf_op jit(solution)/shard_map/ppermute | solution.py:21
  176.0 12.7 %collective-permute-start.24 = (f32[40,1,128]{2,1,0:T(1,128)S(1)}, f32[40,1,128]{2,1,0:T(1,128)S(1)}, u32[]{:S(2)}, u32[]{:S(2)}) collective-permute-start(f32[40,1,128]{2,1,0:T(1,128)S(1)} %get-tuple-element.32), channel_id=1, source_target_pairs={{0,4},{4,8},{8,12},{12,16},{16,20},{20,24},{24,28},{28,32},{32,36}... | collective-permute-start | bytes 61448 | tf_op jit(solution)/shard_map/ppermute | solution.py:18
  178.0 11.4 %collective-permute-start.25 = (f32[40,1,128]{2,1,0:T(1,128)S(1)}, f32[40,1,128]{2,1,0:T(1,128)S(1)}, u32[]{:S(2)}, u32[]{:S(2)}) collective-permute-start(f32[40,1,128]{2,1,0:T(1,128)S(1)} %get-tuple-element.33), channel_id=1, source_target_pairs={{4,0},{8,4},{12,8},{16,12},{20,16},{24,20},{28,24},{32,28},{36,32}... | collective-permute-start | bytes 61448 | tf_op jit(solution)/shard_map/ppermute | solution.py:21
  190.1 7.2 %collective-permute-start.26 = (f32[40,26,1]{0,2,1:T(1,128)S(1)}, f32[40,26,1]{0,2,1:T(1,128)S(1)}, u32[]{:S(2)}, u32[]{:S(2)}) collective-permute-start(f32[40,26,1]{0,2,1:T(1,128)S(1)} %copy.50), channel_id=1, source_target_pairs={{0,1},{1,2},{2,3},{3,0},{4,5},{5,6},{6,7},{7,4},{8,9},{9,10},{10,1... | collective-permute-start | bytes 12488 | tf_op jit(solution)/shard_map/ppermute | solution.py:18
  192.5 5.7 %collective-permute-start.27 = (f32[40,26,1]{0,2,1:T(1,128)S(1)}, f32[40,26,1]{0,2,1:T(1,128)S(1)}, u32[]{:S(2)}, u32[]{:S(2)}) collective-permute-start(f32[40,26,1]{0,2,1:T(1,128)S(1)} %copy.54), channel_id=1, source_target_pairs={{1,0},{2,1},{3,2},{0,3},{5,4},{6,5},{7,6},{4,7},{9,8},{10,9},{11,1... | collective-permute-start | bytes 12488 | tf_op jit(solution)/shard_map/ppermute | solution.py:21
  200.0 12.5 %collective-permute-start.28 = (f32[40,1,128]{2,1,0:T(1,128)S(1)}, f32[40,1,128]{2,1,0:T(1,128)S(1)}, u32[]{:S(2)}, u32[]{:S(2)}) collective-permute-start(f32[40,1,128]{2,1,0:T(1,128)S(1)} %get-tuple-element.30), channel_id=1, source_target_pairs={{0,4},{4,8},{8,12},{12,16},{16,20},{20,24},{24,28},{28,32},{32,36}... | collective-permute-start | bytes 61448 | tf_op jit(solution)/shard_map/ppermute | solution.py:18
  201.9 11.4 %collective-permute-start.29 = (f32[40,1,128]{2,1,0:T(1,128)S(1)}, f32[40,1,128]{2,1,0:T(1,128)S(1)}, u32[]{:S(2)}, u32[]{:S(2)}) collective-permute-start(f32[40,1,128]{2,1,0:T(1,128)S(1)} %get-tuple-element.31), channel_id=1, source_target_pairs={{4,0},{8,4},{12,8},{16,12},{20,16},{24,20},{28,24},{32,28},{36,32}... | collective-permute-start | bytes 61448 | tf_op jit(solution)/shard_map/ppermute | solution.py:21
  214.5 11.0 %collective-permute-start.31 = (f32[40,26,1]{0,2,1:T(1,128)S(1)}, f32[40,26,1]{0,2,1:T(1,128)S(1)}, u32[]{:S(2)}, u32[]{:S(2)}) collective-permute-start(f32[40,26,1]{0,2,1:T(1,128)S(1)} %copy.63), channel_id=1, source_target_pairs={{1,0},{2,1},{3,2},{0,3},{5,4},{6,5},{7,6},{4,7},{9,8},{10,9},{11,1... | collective-permute-start | bytes 12488 | tf_op jit(solution)/shard_map/ppermute | solution.py:21
  219.4 5.7 %collective-permute-start.30 = (f32[40,26,1]{0,2,1:T(1,128)S(1)}, f32[40,26,1]{0,2,1:T(1,128)S(1)}, u32[]{:S(2)}, u32[]{:S(2)}) collective-permute-start(f32[40,26,1]{0,2,1:T(1,128)S(1)} %copy.59), channel_id=1, source_target_pairs={{0,1},{1,2},{2,3},{3,0},{4,5},{5,6},{6,7},{7,4},{8,9},{9,10},{10,1... | collective-permute-start | bytes 12488 | tf_op jit(solution)/shard_map/ppermute | solution.py:18
  226.6 0.8 copy-start.4
  227.4 21.2 %copy-start.2 = (f32[1,40,24,128]{3,2,1,0:T(8,128)S(1)}, f32[1,40,24,128]{3,2,1,0:T(8,128)}, u32[]{:S(2)}) copy-start(f32[1,40,24,128]{3,2,1,0:T(8,128)} %get-tuple-element.5) | copy-start | bytes 1474564
where the time goes:
time: 251 us; the launch traced here: 250 us
  starting transfers between devices  177 us (71%)
  waiting for transfers between devices  26.9 us (11%)
  blocking collectives  20.3 us (8%)
  other arithmetic  12.9 us (5%)
  local copies, waits for them, and re-layouts  10.3 us (4%)
    ppermute x16, starting transfers between devices, padded_2(): lax.ppermute(lax.slice_in_dim(block, 0, width, axis=dim), axis, backward)  122 us
    ppermute x16, starting transfers between devices, padded_2(): lax.ppermute(lax.slice_in_dim(block, block.shape[dim] - width, None, axis...  36.5 us
    all_gather x1, blocking collectives, body(): returned = lax.all_gather(heating, 'grp', axis=0, tiled=True)  20.3 us
    all_to_all x1, starting transfers between devices, body(): lax.all_to_all(outgoing, 'grp', split_axis=0, concat_axis=0, tiled=True)  19.2 us
    ppermute x16, waiting for transfers between devices, padded_2(): lax.ppermute(lax.slice_in_dim(block, block.shape[dim] - width, None, axis...  14.7 us
    ppermute x16, waiting for transfers between devices, padded_2(): lax.ppermute(lax.slice_in_dim(block, 0, width, axis=dim), axis, backward)  12.2 us
  transfers between devices with their start and end apart: 33, of which 17 were waited for; matrix products, arithmetic and copies ran while one was open for 2% of the time, Pallas kernels for 0%

commit v1 on v0

--- a/solution.py
+++ b/solution.py
@@ -9,18 +9,28 @@
 NSUB = 4
 
 
-def padded_2(block, sides, width):
-    for axis, dim in sides:
+def exchange(block, width, lat_pos, lat_count):
+    for axis, dim in (("lon", 1), ("lat", 2)):
         count = lax.axis_size(axis)
-        forward = [(i, i + 1) for i in range(count - 1)]
-        forward.append((count - 1, 0))
+        forward = [(i, (i + 1) % count) for i in range(count)]
         backward = [(target, source) for source, target in forward]
         low = lax.ppermute(
             lax.slice_in_dim(block, block.shape[dim] - width, None, axis=dim), axis, forward
         )
         high = lax.ppermute(lax.slice_in_dim(block, 0, width, axis=dim), axis, backward)
         block = jnp.concatenate([low, block, high], axis=dim)
-    return block
+    length = block.shape[-1]
+    positions = jnp.arange(length)
+    lower = (positions < width) & (lat_pos == 0)
+    upper = (positions >= length - width) & (lat_pos == lat_count - 1)
+    return jnp.where(lower | upper, 0.0, block)
+
+
+def crop(array, from_radius, to_radius):
+    cut = from_radius - to_radius
+    if cut == 0:
+        return array
+    return array[..., cut : array.shape[-2] - cut, cut : array.shape[-1] - cut]
 
 
 def center_of(padded):
@@ -84,14 +94,6 @@
     return jnp.concatenate([results[0], results[1], results[2], results[3][None]], axis=0)
 
 
-def fix_rim(padded, width, lat_pos, lat_count):
-    length = padded.shape[-1]
-    positions = jnp.arange(length)
-    lower = (positions < width) & (lat_pos == 0)
-    upper = (positions >= length - width) & (lat_pos == lat_count - 1)
-    return jnp.where(lower | upper, 0.0, padded)
-
-
 def body(state, depth, rates, grazing):
     groups = lax.axis_size("grp")
     member = lax.axis_index("grp")
@@ -102,28 +104,47 @@
     total_levels = LZ * (groups - 1)
     dyn_rows = 3 * total_levels + 1
     lat_total = lat_rows * lat_count
+    dyn_halo = SECTIONS + NSUB - 1
+    tracer_halo = NSUB
+    vel_halo = NSUB - 1
+
     depth_f = depth.astype(jnp.float32)
+    block = jnp.concatenate([local, depth_f[None]], axis=0)
+    padded = exchange(block, dyn_halo, lat_pos, lat_count)
+    depth_pad = padded[field_rows]
+
     level_index = jnp.arange(total_levels).astype(jnp.float32)[:, None, None]
-    fields = local[:dyn_rows]
-    wet_local = (level_index < depth_f[None]).astype(jnp.float32)
-    land_local = (depth_f > 0).astype(jnp.float32)
-    coord = (lat_pos * lat_rows - 0 + jnp.arange(lat_rows + 2 * 0)).astype(jnp.float32)
-    coriolis_local = 0.3 * jnp.sin(jnp.pi * (coord + 0.5) / lat_total - jnp.pi / 2)
-    current = fields
+    wet_pad = (level_index < depth_pad[None]).astype(jnp.float32)
+    land_pad = (depth_pad > 0).astype(jnp.float32)
+    coord = (lat_pos * lat_rows - dyn_halo + jnp.arange(lat_rows + 2 * dyn_halo)).astype(jnp.float32)
+    coriolis_pad = 0.3 * jnp.sin(jnp.pi * (coord + 0.5) / lat_total - jnp.pi / 2)
+
+    current = padded[:dyn_rows]
+    radius = dyn_halo
     for section_index in range(SECTIONS):
-        padded = padded_2(current, (("lon", 1), ("lat", 2)), 1)
-        padded = fix_rim(padded, 1, lat_pos, lat_count)
-        current = section_rows(padded, wet_local, land_local, coriolis_local)
-    zonal = current[:total_levels]
-    merid = current[total_levels : 2 * total_levels]
-    temper = current[2 * total_levels : 3 * total_levels]
-    surface = current[3 * total_levels]
+        radius -= 1
+        cut = dyn_halo - radius
+        current = section_rows(
+            current,
+            crop(wet_pad, dyn_halo, radius),
+            crop(land_pad, dyn_halo, radius),
+            coriolis_pad[cut : coriolis_pad.shape[0] - cut],
+        )
+    zonal_r = current[:total_levels]
+    merid_r = current[total_levels : 2 * total_levels]
+    temper_r = current[2 * total_levels : 3 * total_levels]
+    zonal = crop(zonal_r, radius, 0)
+    merid = crop(merid_r, radius, 0)
+    temper = crop(temper_r, radius, 0)
+    surface = crop(current[3 * total_levels], radius, 0)
+
     first_level = jnp.maximum(member - 1, 0) * LZ
+    vcols, vrows = zonal_r.shape[-2:]
     forcing = jnp.stack(
         [
-            zonal.reshape(groups - 1, LZ, columns, lat_rows),
-            merid.reshape(groups - 1, LZ, columns, lat_rows),
-            temper.reshape(groups - 1, LZ, columns, lat_rows),
+            zonal_r.reshape(groups - 1, LZ, vcols, vrows),
+            merid_r.reshape(groups - 1, LZ, vcols, vrows),
+            temper_r.reshape(groups - 1, LZ, vcols, vrows),
         ],
         axis=1,
     )
@@ -131,25 +152,32 @@
     received = lax.all_to_all(outgoing, "grp", split_axis=0, concat_axis=0, tiled=True)
     own_zonal = received[0, 0]
     own_merid = received[0, 1]
-    own_temper = received[0, 2]
+    own_temper = crop(received[0, 2], vel_halo, 0)
+
     member_levels = (first_level + jnp.arange(LZ)).astype(jnp.float32)[:, None, None]
-    wet_member = (member_levels < depth_f[None]).astype(jnp.float32)
-    advected = local.reshape(NTR, LZ, columns, lat_rows)
+    wet_member_pad = (member_levels < depth_pad[None]).astype(jnp.float32)
+    tracers = crop(padded[:field_rows], dyn_halo, tracer_halo)
+    advected = tracers.reshape((NTR, LZ) + tracers.shape[1:])
+    radius = tracer_halo
     for sub_index in range(NSUB):
-        padded = padded_2(
-            advected.reshape(field_rows, columns, lat_rows), (("lon", 1), ("lat", 2)), 1
+        radius -= 1
+        advected = advect_tracers(
+            advected,
+            crop(own_zonal, vel_halo, radius),
+            crop(own_merid, vel_halo, radius),
+            crop(wet_member_pad, dyn_halo, radius),
         )
-        padded = fix_rim(padded, 1, lat_pos, lat_count)
-        advected = advect_tracers(
-            padded.reshape(NTR, LZ, columns + 2, lat_rows + 2), own_zonal, own_merid, wet_member
-        )
+    wet_member = crop(wet_member_pad, dyn_halo, 0)
     kinetic = jnp.einsum("ts,szxy->tzxy", rates, advected, precision=lax.Precision.HIGHEST)
     kinetic = kinetic + grazing[:, None, None, None] * (advected[0] * advected[1])[None]
     updated = wet_member[None] * (advected + 0.2 * jnp.exp(0.05 * own_temper)[None] * kinetic)
     light_factor = jnp.exp(-(member_levels + 0.5) / total_levels)
     heating = 0.3 * wet_member * updated[0] * light_factor
-    returned = lax.all_gather(heating, "grp", axis=0, tiled=True)
-    temper_final = temper + returned[LZ:]
+    heat_out = jnp.concatenate(
+        [heating[None], jnp.zeros((groups - 1,) + heating.shape, jnp.float32)], axis=0
+    )
+    returned = lax.all_to_all(heat_out, "grp", split_axis=0, concat_axis=0, tiled=True)
+    temper_final = temper + returned[1:].reshape(total_levels, columns, lat_rows)
     unused = jnp.zeros((field_rows - dyn_rows, columns, lat_rows), jnp.float32)
     dyn_out = jnp.concatenate([zonal, merid, temper_final, surface[None], unused], axis=0)
     result = jnp.where(member == 0, dyn_out, updated.reshape(field_rows, columns, lat_rows))

time: 251 us -> 118 us (0.47)
  the two profiles are of different devices: /device:TPU:1 before, /device:TPU:6 now
where the time goes in v1:
time: 118 us; the launch traced here: 117 us
  waiting for transfers between devices  38.7 us (33%)
  starting transfers between devices  38.3 us (32%)
  other arithmetic  24.9 us (21%)
  local copies, waits for them, and re-layouts  14 us (12%)
    all_to_all x1, waiting for transfers between devices, body(): lax.all_to_all(outgoing, 'grp', split_axis=0, concat_axis=0, tiled=True)  20.3 us
    ppermute x2, starting transfers between devices, exchange(): lax.ppermute(lax.slice_in_dim(block, 0, width, axis=dim), axis, backward)  16 us
    mul x4, other arithmetic, advect_tracers(): wet_mask * (center_of(tracer_pad) - 0.25 * (zonal * grad_x(tracer_pad) +...  11.1 us
    all_to_all x1, waiting for transfers between devices, body(): lax.all_to_all(heat_out, 'grp', split_axis=0, concat_axis=0, tiled=True)  9.48 us
    ppermute x2, starting transfers between devices, exchange(): lax.ppermute(lax.slice_in_dim(block, block.shape[dim] - width, None, axis...  9.4 us
    all_to_all x1, starting transfers between devices, body(): lax.all_to_all(heat_out, 'grp', split_axis=0, concat_axis=0, tiled=True)  7 us
    ppermute x2, waiting for transfers between devices, exchange(): lax.ppermute(lax.slice_in_dim(block, 0, width, axis=dim), axis, backward)  6.69 us
    all_to_all x1, starting transfers between devices, body(): lax.all_to_all(outgoing, 'grp', split_axis=0, concat_axis=0, tiled=True)  5.9 us
  transfers between devices with their start and end apart: 6, of which 5 were waited for; matrix products, arithmetic and copies ran while one was open for 9% of the time, Pallas kernels for 0%

profile of v1, /device:TPU:6, one launch (start us, length us, event | category | flops | bytes accessed | tf_op | source)
XLA Modules:
  0.0 117.0 jit_solution(14977743393659900843)
XLA Ops:
  0.0 0.7 convert_bitcast_fusion
  0.7 1.0 pad_maximum_fusion.2
  1.7 3.5 %collective-permute-start = (f32[41,7,128]{2,1,0:T(8,128)S(1)}, f32[41,7,128]{2,1,0:T(8,128)S(1)}, u32[]{:S(2)}, u32[]{:S(2)}) collective-permute-start(f32[41,7,128]{2,1,0:T(8,128)S(1)} %get-tuple-element.29), channel_id=1, source_target_pairs={{0,4},{4,8},{8,12},{12,16},{16,20},{20,24},{24,28},{28,32},{32,36}... | collective-permute-start | bytes 440840 | tf_op jit(solution)/shard_map/ppermute | solution.py:17
  5.2 14.1 %collective-permute-start.1 = (f32[41,7,128]{2,1,0:T(8,128)S(1)}, f32[41,7,128]{2,1,0:T(8,128)S(1)}, u32[]{:S(2)}, u32[]{:S(2)}) collective-permute-start(f32[41,7,128]{2,1,0:T(8,128)S(1)} %get-tuple-element.30), channel_id=1, source_target_pairs={{4,0},{8,4},{12,8},{16,12},{20,16},{24,20},{28,24},{32,28},{36,32}... | collective-permute-start | bytes 440840 | tf_op jit(solution)/shard_map/ppermute | solution.py:20
  19.4 2.2 %collective-permute-done = f32[41,7,128]{2,1,0:T(8,128)S(1)} collective-permute-done((f32[41,7,128]{2,1,0:T(8,128)S(1)}, f32[41,7,128]{2,1,0:T(8,128)S(1)}, u32[]{:S(2)}, u32[]{:S(2)}) %collective-permute-start) | collective-permute-done | bytes 146976 | tf_op jit(solution)/shard_map/ppermute | solution.py:17
  21.7 1.2 %collective-permute-done.1 = f32[41,7,128]{2,1,0:T(8,128)S(1)} collective-permute-done((f32[41,7,128]{2,1,0:T(8,128)S(1)}, f32[41,7,128]{2,1,0:T(8,128)S(1)}, u32[]{:S(2)}, u32[]{:S(2)}) %collective-permute-start.1) | collective-permute-done | bytes 146976 | tf_op jit(solution)/shard_map/ppermute | solution.py:20
  22.8 1.1 pad_maximum_fusion
  24.0 0.3 fusion.33
  24.3 0.4 copy.39
  24.7 5.9 %collective-permute-start.2 = (f32[41,38,7]{0,1,2:T(8,128)S(1)}, f32[41,38,7]{0,1,2:T(8,128)S(1)}, u32[]{:S(2)}, u32[]{:S(2)}) collective-permute-start(f32[41,38,7]{0,1,2:T(8,128)S(1)} %copy.39), channel_id=1, source_target_pairs={{0,1},{1,2},{2,3},{3,0},{4,5},{5,6},{6,7},{7,4},{8,9},{9,10},{10,1... | collective-permute-start | bytes 130880 | tf_op jit(solution)/shard_map/ppermute | solution.py:17
  30.6 0.4 copy.40
  31.1 1.9 %collective-permute-start.3 = (f32[41,38,7]{0,1,2:T(8,128)S(1)}, f32[41,38,7]{0,1,2:T(8,128)S(1)}, u32[]{:S(2)}, u32[]{:S(2)}) collective-permute-start(f32[41,38,7]{0,1,2:T(8,128)S(1)} %copy.40), channel_id=1, source_target_pairs={{1,0},{2,1},{3,2},{0,3},{5,4},{6,5},{7,6},{4,7},{9,8},{10,9},{11,1... | collective-permute-start | bytes 130880 | tf_op jit(solution)/shard_map/ppermute | solution.py:20
  33.3 0.5 copy.41
  33.8 5.5 %collective-permute-done.3 = f32[41,38,7]{0,1,2:T(8,128)S(1)} collective-permute-done((f32[41,38,7]{0,1,2:T(8,128)S(1)}, f32[41,38,7]{0,1,2:T(8,128)S(1)}, u32[]{:S(2)}, u32[]{:S(2)}) %collective-permute-start.3) | collective-permute-done | bytes 43656 | tf_op jit(solution)/shard_map/ppermute | solution.py:20
  39.3 1.3 %copy.42 = f32[41,38,7]{2,1,0:T(8,128)} copy(f32[41,38,7]{0,1,2:T(8,128)S(1)} %collective-permute-done.3) | data formatting | bytes 87248 | tf_op jit(solution)/shard_map/ppermute | solution.py:20
  40.6 2.1 %maximum_select_fusion = f32[41,38,142]{2,1,0:T(8,128)S(1)} fusion(f32[41,38,7]{2,1,0:T(8,128)} %copy.42, f32[41,7,128]{2,1,0:T(8,128)S(1)} %collective-permute-done.1, f32[1,24,128]{2,1,0:T(8,128)S(1)} %convert_bitcast_fusion, f32[40,24,128]{2,1,0:T(8,128)S(1)} %bitcast.63, f32[41,7,128]{2,1,0:T(8,128)S(1)} %collective-permute-done, ...), kind=kLoop, calls=%fused_computation | loop fusion | flops 1327416 | bytes 1770030 | tf_op jit(solution)/shard_map/jit(_where)/select_n | solution.py:26
  42.7 0.3 fusion.7
  43.0 0.1 compare_convert_fusion
  43.1 0.1 fusion.19
  43.2 0.5 subtract_multiply_fusion.3
  43.7 0.3 fusion.5
  44.0 0.1 fusion.16
  44.1 0.5 subtract_multiply_fusion.1
  44.7 0.2 fusion.11
  44.9 0.1 fusion.24
  45.0 0.7 fusion.35
  45.7 0.4 subtract_multiply_fusion.7
  46.2 0.4 subtract_multiply_fusion.4
  46.6 0.1 copy.44
  46.8 0.5 copy-done.4
  47.3 0.1 copy.45
  47.4 0.1 copy.46
  47.6 1.2 select_maximum_fusion
  48.8 5.9 %all-to-all-start = ((f32[4,3,2,30,134]{4,2,3,1,0:T(2,128)}), f32[4,3,2,30,134]{4,2,3,1,0:T(2,128)S(1)}, u32[]{:S(2)}, u32[]{:S(2)}) async-start(f32[4,3,2,30,134]{4,2,3,1,0:T(2,128)} %select_maximum_fusion), calls=%async_computation | async-start | bytes 1474560 | tf_op jit(solution)/shard_map/all_to_all | solution.py:152
  54.7 0.5 slice.639
  55.2 0.7 slice.638
  55.9 0.7 slice.637
  56.6 0.1 slice.636
  56.8 0.7 slice.674
  57.5 0.8 fusion.9
  58.3 0.7 fusion.15
  59.0 3.3 %fusion.32 = (f32[20,2,30,134]{3,2,1,0:T(8,128)S(1)}, f32[20,2,30,134]{3,2,1,0:T(8,128)S(1)}, f32[20,2,30,134]{3,2,1,0:T(8,128)}, f32[20,2,30,134]{3,2,1,0:T(8,128)}, f32[20,2,30,134]{3,2,1,0:T(8,128)}) fusion(f32[20,2,32,136]{3,2,1,0:T(8,128)S(1)} %bitcast.60), kind=kLoop, calls=%fused_computation.99 | loop fusion | bytes 6432000 | tf_op jit(solution)/shard_map/slice | solution.py:41
  62.3 20.3 %all-to-all-done = f32[4,3,2,30,134]{4,2,3,1,0:T(2,128)S(1)} async-done(((f32[4,3,2,30,134]{4,2,3,1,0:T(2,128)}), f32[4,3,2,30,134]{4,2,3,1,0:T(2,128)S(1)}, u32[]{:S(2)}, u32[]{:S(2)}) %all-to-all-start) | async-done | bytes 385952 | tf_op jit(solution)/shard_map/all_to_all | solution.py:152
  82.6 0.1 slice.648
  82.7 0.1 slice.651
  82.9 0.1 slice.655
  83.0 0.1 slice.658
  83.1 0.1 slice.662
  83.2 0.1 slice.665
  83.4 0.5 copy-done.1
  83.9 7.5 %add_multiply_fusion = f32[20,2,30,134]{3,0,2,1:T(8,128)S(1)} fusion(f32[20,2,30,134]{3,2,1,0:T(8,128)} %get-tuple-element.13, f32[20,2,30,134]{3,2,1,0:T(8,128)} %get-tuple-element.14, f32[20,2,30,134]{3,2,1,0:T(8,128)S(1)} %get-tuple-element.11, f32[20,2,30,134]{3,2,1,0:T(8,128)S(1)} %copy-done.1, f32[20,2,30,134]{3,2,1,0:T(8,128)S(1)} %get-tuple-element.10, ...), kind=kLoop, calls=%fused_computation.1 | loop fusion | flops 2412000 | bytes 3955680 | tf_op jit(solution)/shard_map/mul | solution.py:76
  91.4 1.5 %add_multiply_fusion.1 = f32[20,2,28,132]{3,0,2,1:T(8,128)S(1)} fusion(f32[20,2,30,134]{3,0,2,1:T(8,128)S(1)} %add_multiply_fusion, f32[2,28,132]{2,1,0:T(8,128)S(1)} %copy.54, f32[2,28,132]{2,1,0:T(8,128)S(1)} %copy.53, f32[2,28,132]{2,1,0:T(8,128)S(1)} %copy-done.6), kind=kLoop, calls=%fused_computation.2 | loop fusion | flops 2217600 | bytes 3636864 | tf_op jit(solution)/shard_map/mul | solution.py:76
  92.9 1.4 %add_multiply_fusion.2 = f32[20,2,26,130]{3,0,2,1:T(8,128)S(1)} fusion(f32[20,2,28,132]{3,0,2,1:T(8,128)S(1)} %add_multiply_fusion.1, f32[2,26,130]{2,1,0:T(8,128)S(1)} %copy.56, f32[2,26,130]{2,1,0:T(8,128)S(1)} %copy.55, f32[2,26,130]{2,1,0:T(8,128)S(1)} %slice.636), kind=kLoop, calls=%fused_computation.3 | loop fusion | flops 2028000 | bytes 3325920 | tf_op jit(solution)/shard_map/mul | solution.py:76
  94.3 0.7 add_multiply_fusion.3
  95.1 0.1 fusion.28
  95.2 0.7 fusion.3
  96.0 0.7 concatenate.39
  96.7 7.0 %all-to-all-start.1 = ((f32[4,2,24,128]{3,2,1,0:T(8,128)}), f32[4,2,24,128]{3,2,1,0:T(8,128)S(1)}, u32[]{:S(2)}, u32[]{:S(2)}) async-start(f32[4,2,24,128]{3,2,1,0:T(8,128)} %concatenate.39), calls=%async_computation.1 | async-start | bytes 196608 | tf_op jit(solution)/shard_map/all_to_all | solution.py:179
  103.7 1.0 fusion.14
  104.7 0.1 copy.60
  104.8 9.5 %all-to-all-done.1 = f32[4,2,24,128]{3,2,1,0:T(8,128)S(1)} async-done(((f32[4,2,24,128]{3,2,1,0:T(8,128)}), f32[4,2,24,128]{3,2,1,0:T(8,128)S(1)}, u32[]{:S(2)}, u32[]{:S(2)}) %all-to-all-start.1) | async-done | bytes 98336 | tf_op jit(solution)/shard_map/all_to_all | solution.py:179
  114.3 1.0 fusion.13
  115.3 0.9 fusion.30
  116.2 0.8 bitcast_select_fusion
  (45 shorter events, 0.8 us)
Async XLA Ops:
  0.0 95.2 %copy-start = (f32[20,20]{1,0:T(8,128)S(1)}, f32[20,20]{1,0:T(8,128)}, u32[]{:S(2)}) copy-start(f32[20,20]{1,0:T(8,128)} %param.6) | copy-start | bytes 4804
  1.7 19.9 %collective-permute-start = (f32[41,7,128]{2,1,0:T(8,128)S(1)}, f32[41,7,128]{2,1,0:T(8,128)S(1)}, u32[]{:S(2)}, u32[]{:S(2)}) collective-permute-start(f32[41,7,128]{2,1,0:T(8,128)S(1)} %get-tuple-element.29), channel_id=1, source_target_pairs={{0,4},{4,8},{8,12},{12,16},{16,20},{20,24},{24,28},{28,32},{32,36}... | collective-permute-start | bytes 440840 | tf_op jit(solution)/shard_map/ppermute | solution.py:17
  5.2 17.6 %collective-permute-start.1 = (f32[41,7,128]{2,1,0:T(8,128)S(1)}, f32[41,7,128]{2,1,0:T(8,128)S(1)}, u32[]{:S(2)}, u32[]{:S(2)}) collective-permute-start(f32[41,7,128]{2,1,0:T(8,128)S(1)} %get-tuple-element.30), channel_id=1, source_target_pairs={{4,0},{8,4},{12,8},{16,12},{20,16},{24,20},{28,24},{32,28},{36,32}... | collective-permute-start | bytes 440840 | tf_op jit(solution)/shard_map/ppermute | solution.py:20
  24.7 8.6 %collective-permute-start.2 = (f32[41,38,7]{0,1,2:T(8,128)S(1)}, f32[41,38,7]{0,1,2:T(8,128)S(1)}, u32[]{:S(2)}, u32[]{:S(2)}) collective-permute-start(f32[41,38,7]{0,1,2:T(8,128)S(1)} %copy.39), channel_id=1, source_target_pairs={{0,1},{1,2},{2,3},{3,0},{4,5},{5,6},{6,7},{7,4},{8,9},{9,10},{10,1... | collective-permute-start | bytes 130880 | tf_op jit(solution)/shard_map/ppermute | solution.py:17
  30.6 10.0 %copy-start.2 = (f32[1,40,24,128]{3,2,1,0:T(8,128)S(1)}, f32[1,40,24,128]{3,2,1,0:T(8,128)}, u32[]{:S(2)}) copy-start(f32[1,40,24,128]{3,2,1,0:T(8,128)} %param.4) | copy-start | bytes 1474564
  31.1 8.2 %collective-permute-start.3 = (f32[41,38,7]{0,1,2:T(8,128)S(1)}, f32[41,38,7]{0,1,2:T(8,128)S(1)}, u32[]{:S(2)}, u32[]{:S(2)}) collective-permute-start(f32[41,38,7]{0,1,2:T(8,128)S(1)} %copy.40), channel_id=1, source_target_pairs={{1,0},{2,1},{3,2},{0,3},{5,4},{6,5},{7,6},{4,7},{9,8},{10,9},{11,1... | collective-permute-start | bytes 130880 | tf_op jit(solution)/shard_map/ppermute | solution.py:20
  46.6 0.7 copy-start.4
  46.6 0.8 copy-start.3
  48.8 33.8 %all-to-all-start = ((f32[4,3,2,30,134]{4,2,3,1,0:T(2,128)}), f32[4,3,2,30,134]{4,2,3,1,0:T(2,128)S(1)}, u32[]{:S(2)}, u32[]{:S(2)}) async-start(f32[4,3,2,30,134]{4,2,3,1,0:T(2,128)} %select_maximum_fusion), calls=%async_computation | async-start | bytes 1474560 | tf_op jit(solution)/shard_map/all_to_all | solution.py:152
  82.6 1.3 %copy-start.1 = (f32[20,2,30,134]{3,2,1,0:T(8,128)S(1)}, f32[20,2,30,134]{3,2,1,0:T(8,128)}, u32[]{:S(2)}) copy-start(f32[20,2,30,134]{3,2,1,0:T(8,128)} %get-tuple-element.12) | copy-start | bytes 1929604
  82.6 1.3 %copy-start.7 = (f32[2,30,134]{2,1,0:T(8,128)S(1)}, f32[2,30,134]{2,1,0:T(8,128)}, u32[]{:S(2)}) copy-start(f32[2,30,134]{2,1,0:T(8,128)} %slice.638) | copy-start | bytes 96484
  83.9 7.5 %copy-start.6 = (f32[2,28,132]{2,1,0:T(8,128)S(1)}, f32[2,28,132]{2,1,0:T(8,128)}, u32[]{:S(2)}) copy-start(f32[2,28,132]{2,1,0:T(8,128)} %slice.637) | copy-start | bytes 88708
  94.3 0.9 copy-start.8
  95.0 8.7 %copy-start.5 = (f32[1,40,24,128]{3,2,1,0:T(8,128)S(1)}, f32[1,40,24,128]{3,2,1,0:T(8,128)}, u32[]{:S(2)}) copy-start(f32[1,40,24,128]{3,2,1,0:T(8,128)} %fusion.15) | copy-start | bytes 1474564
  96.7 17.6 %all-to-all-start.1 = ((f32[4,2,24,128]{3,2,1,0:T(8,128)}), f32[4,2,24,128]{3,2,1,0:T(8,128)S(1)}, u32[]{:S(2)}, u32[]{:S(2)}) async-start(f32[4,2,24,128]{3,2,1,0:T(8,128)} %concatenate.39), calls=%async_computation.1 | async-start | bytes 196608 | tf_op jit(solution)/shard_map/all_to_all | solution.py:179

commit v2 on v1

--- a/solution.py
+++ b/solution.py
@@ -148,11 +148,14 @@
         ],
         axis=1,
     )
-    outgoing = jnp.concatenate([jnp.zeros((1,) + forcing.shape[1:], jnp.float32), forcing], axis=0)
-    received = lax.all_to_all(outgoing, "grp", split_axis=0, concat_axis=0, tiled=True)
-    own_zonal = received[0, 0]
-    own_merid = received[0, 1]
-    own_temper = crop(received[0, 2], vel_halo, 0)
+    own = forcing[0]
+    for shift in range(1, groups):
+        pairs = [(i, (i + shift) % groups) for i in range(groups)]
+        arrived = lax.ppermute(forcing[shift - 1], "grp", pairs)
+        own = jnp.where(member == shift, arrived, own)
+    own_zonal = own[0]
+    own_merid = own[1]
+    own_temper = crop(own[2], vel_halo, 0)
 
     member_levels = (first_level + jnp.arange(LZ)).astype(jnp.float32)[:, None, None]
     wet_member_pad = (member_levels < depth_pad[None]).astype(jnp.float32)
@@ -173,11 +176,12 @@
     updated = wet_member[None] * (advected + 0.2 * jnp.exp(0.05 * own_temper)[None] * kinetic)
     light_factor = jnp.exp(-(member_levels + 0.5) / total_levels)
     heating = 0.3 * wet_member * updated[0] * light_factor
-    heat_out = jnp.concatenate(
-        [heating[None], jnp.zeros((groups - 1,) + heating.shape, jnp.float32)], axis=0
-    )
-    returned = lax.all_to_all(heat_out, "grp", split_axis=0, concat_axis=0, tiled=True)
-    temper_final = temper + returned[1:].reshape(total_levels, columns, lat_rows)
+    returned = []
+    for shift in range(1, groups):
+        pairs = [(i, (i - shift) % groups) for i in range(groups)]
+        returned.append(lax.ppermute(heating, "grp", pairs))
+    returned = jnp.concatenate(returned, axis=0)
+    temper_final = temper + returned
     unused = jnp.zeros((field_rows - dyn_rows, columns, lat_rows), jnp.float32)
     dyn_out = jnp.concatenate([zonal, merid, temper_final, surface[None], unused], axis=0)
     result = jnp.where(member == 0, dyn_out, updated.reshape(field_rows, columns, lat_rows))

time: 118 us -> 108 us (0.915)
  local copies, waits for them, and re-layouts: 14 us -> 5.59 us
  other arithmetic: 24.9 us -> 16.7 us
  starting transfers between devices: 38.3 us -> 46.1 us
    all_to_all x2 -> x0, waiting for transfers between devices: 29.8 us -> none  [the longest x1 20.3 us: body(): lax.all_to_all(outgoing, 'grp', split_axis=0, concat_axis=0, tiled=True)]
    ppermute x0 -> x6, waiting for transfers between devices: none -> 28.9 us  [the longest x3 19.8 us: body(): arrived = lax.ppermute(forcing[shift - 1], 'grp', pairs)]
    ppermute x0 -> x6, starting transfers between devices: none -> 20.7 us  [the longest x3 10.8 us: body(): arrived = lax.ppermute(forcing[shift - 1], 'grp', pairs)]
    all_to_all x2 -> x0, starting transfers between devices: 12.9 us -> none  [the longest x1 7 us: body(): lax.all_to_all(heat_out, 'grp', split_axis=0, concat_axis=0, tiled=True)]
    mul x4, other arithmetic: 11.1 us -> 7.97 us  [advect_tracers(): wet_mask * (center_of(tracer_pad) - 0.25 * (zonal * grad_x(tracer_pad) +...]
    unnamed x21 -> x8, local copies, waits for them, and re-layouts: 2.78 us -> 0.19 us
    slice x18 -> x12, local copies, waits for them, and re-layouts: 3.39 us -> 1.35 us  [crop(): return array[..., cut:array.shape[-2] - cut, cut:array.shape[-1] - cut]]
    slice x1, local copies, waits for them, and re-layouts: 3.28 us -> 1.5 us  [grad_x(): return padded[..., 2:, 1:-1] - padded[..., :-2, 1:-1]]
  transfers between devices with their start and end apart: 6 -> 10, of which waited for: 5 -> 8; matrix products, arithmetic and copies ran while one was open for 9% -> 3% of each run, Pallas kernels for 0% -> 0%
where the time goes in v2:
time: 108 us; the launch traced here: 107 us
  starting transfers between devices  46.1 us (43%)
  waiting for transfers between devices  37.8 us (35%)
  other arithmetic  16.7 us (15%)
  local copies, waits for them, and re-layouts  5.59 us (5%)
    ppermute x3, waiting for transfers between devices, body(): arrived = lax.ppermute(forcing[shift - 1], 'grp', pairs)  19.8 us
    ppermute x2, starting transfers between devices, exchange(): lax.ppermute(lax.slice_in_dim(block, 0, width, axis=dim), axis, backward)  16 us
    ppermute x3, starting transfers between devices, body(): arrived = lax.ppermute(forcing[shift - 1], 'grp', pairs)  10.8 us
    ppermute x3, starting transfers between devices, body(): returned.append(lax.ppermute(heating, 'grp', pairs))  9.98 us
    ppermute x2, starting transfers between devices, exchange(): lax.ppermute(lax.slice_in_dim(block, block.shape[dim] - width, None, axis...  9.4 us
    ppermute x3, waiting for transfers between devices, body(): returned.append(lax.ppermute(heating, 'grp', pairs))  9.11 us
    mul x4, other arithmetic, advect_tracers(): wet_mask * (center_of(tracer_pad) - 0.25 * (zonal * grad_x(tracer_pad) +...  7.97 us
    ppermute x2, waiting for transfers between devices, exchange(): lax.ppermute(lax.slice_in_dim(block, 0, width, axis=dim), axis, backward)  6.69 us
  transfers between devices with their start and end apart: 10, of which 8 were waited for; matrix products, arithmetic and copies ran while one was open for 3% of the time, Pallas kernels for 0%

profile of v2, /device:TPU:6, one launch (start us, length us, event | category | flops | bytes accessed | tf_op | source)
XLA Modules:
  0.0 107.4 jit_solution(2623000540620814578)
XLA Ops:
  0.0 0.7 convert_bitcast_fusion
  0.7 1.0 pad_maximum_fusion.3
  1.7 3.5 %collective-permute-start = (f32[41,7,128]{2,1,0:T(8,128)S(1)}, f32[41,7,128]{2,1,0:T(8,128)S(1)}, u32[]{:S(2)}, u32[]{:S(2)}) collective-permute-start(f32[41,7,128]{2,1,0:T(8,128)S(1)} %get-tuple-element.29), channel_id=1, source_target_pairs={{0,4},{4,8},{8,12},{12,16},{16,20},{20,24},{24,28},{28,32},{32,36}... | collective-permute-start | bytes 440840 | tf_op jit(solution)/shard_map/ppermute | solution.py:17
  5.2 14.1 %collective-permute-start.1 = (f32[41,7,128]{2,1,0:T(8,128)S(1)}, f32[41,7,128]{2,1,0:T(8,128)S(1)}, u32[]{:S(2)}, u32[]{:S(2)}) collective-permute-start(f32[41,7,128]{2,1,0:T(8,128)S(1)} %get-tuple-element.30), channel_id=1, source_target_pairs={{4,0},{8,4},{12,8},{16,12},{20,16},{24,20},{28,24},{32,28},{36,32}... | collective-permute-start | bytes 440840 | tf_op jit(solution)/shard_map/ppermute | solution.py:20
  19.4 2.2 %collective-permute-done = f32[41,7,128]{2,1,0:T(8,128)S(1)} collective-permute-done((f32[41,7,128]{2,1,0:T(8,128)S(1)}, f32[41,7,128]{2,1,0:T(8,128)S(1)}, u32[]{:S(2)}, u32[]{:S(2)}) %collective-permute-start) | collective-permute-done | bytes 146976 | tf_op jit(solution)/shard_map/ppermute | solution.py:17
  21.7 1.2 %collective-permute-done.1 = f32[41,7,128]{2,1,0:T(8,128)S(1)} collective-permute-done((f32[41,7,128]{2,1,0:T(8,128)S(1)}, f32[41,7,128]{2,1,0:T(8,128)S(1)}, u32[]{:S(2)}, u32[]{:S(2)}) %collective-permute-start.1) | collective-permute-done | bytes 146976 | tf_op jit(solution)/shard_map/ppermute | solution.py:20
  22.8 1.1 %pad_maximum_fusion = f32[41,38,128]{2,1,0:T(8,128)S(1)} fusion(f32[41,7,128]{2,1,0:T(8,128)S(1)} %collective-permute-done.1, f32[1,24,128]{2,1,0:T(8,128)S(1)} %convert_bitcast_fusion, f32[40,24,128]{2,1,0:T(8,128)} %bitcast.70, f32[41,7,128]{2,1,0:T(8,128)S(1)} %collective-permute-done), kind=kLoop, calls=%fused_computation.9 | loop fusion | flops 598272 | bytes 1595392 | tf_op jit(solution)/shard_map/concatenate | solution.py:21
  24.0 0.3 fusion.33
  24.3 0.4 copy.20
  24.7 5.9 %collective-permute-start.2 = (f32[41,38,7]{0,1,2:T(8,128)S(1)}, f32[41,38,7]{0,1,2:T(8,128)S(1)}, u32[]{:S(2)}, u32[]{:S(2)}) collective-permute-start(f32[41,38,7]{0,1,2:T(8,128)S(1)} %copy.20), channel_id=1, source_target_pairs={{0,1},{1,2},{2,3},{3,0},{4,5},{5,6},{6,7},{7,4},{8,9},{9,10},{10,1... | collective-permute-start | bytes 130880 | tf_op jit(solution)/shard_map/ppermute | solution.py:17
  30.6 0.4 copy.21
  31.1 1.9 %collective-permute-start.3 = (f32[41,38,7]{0,1,2:T(8,128)S(1)}, f32[41,38,7]{0,1,2:T(8,128)S(1)}, u32[]{:S(2)}, u32[]{:S(2)}) collective-permute-start(f32[41,38,7]{0,1,2:T(8,128)S(1)} %copy.21), channel_id=1, source_target_pairs={{1,0},{2,1},{3,2},{0,3},{5,4},{6,5},{7,6},{4,7},{9,8},{10,9},{11,1... | collective-permute-start | bytes 130880 | tf_op jit(solution)/shard_map/ppermute | solution.py:20
  33.3 0.5 copy.22
  33.8 5.5 %collective-permute-done.3 = f32[41,38,7]{0,1,2:T(8,128)S(1)} collective-permute-done((f32[41,38,7]{0,1,2:T(8,128)S(1)}, f32[41,38,7]{0,1,2:T(8,128)S(1)}, u32[]{:S(2)}, u32[]{:S(2)}) %collective-permute-start.3) | collective-permute-done | bytes 43656 | tf_op jit(solution)/shard_map/ppermute | solution.py:20
  39.3 0.5 copy.23
  39.7 0.9 maximum_select_fusion
  40.7 0.3 fusion.7
  41.0 0.5 slice.648
  41.4 0.1 compare_convert_fusion
  41.5 0.1 fusion.19
  41.6 0.5 subtract_multiply_fusion.3
  42.2 0.3 fusion.5
  42.5 0.1 fusion.16
  42.6 0.5 subtract_multiply_fusion.1
  43.1 0.2 fusion.11
  43.3 0.1 fusion.24
  43.5 0.1 fusion.34
  43.6 0.4 subtract_multiply_fusion.7
  44.0 0.4 subtract_multiply_fusion.4
  44.5 0.1 fusion.15
  44.7 3.4 %collective-permute-start.4 = (f32[3,2,30,134]{3,2,1,0:T(8,128)S(1)}, f32[3,2,30,134]{3,2,1,0:T(8,128)S(1)}, u32[]{:S(2)}, u32[]{:S(2)}) collective-permute-start(f32[3,2,30,134]{3,2,1,0:T(8,128)S(1)} %get-tuple-element.27), channel_id=1, source_target_pairs={{0,576},{192,0},{384,192},{576,384},{1,577},{193,1},{385,193},{577... | collective-permute-start | bytes 289448 | tf_op jit(solution)/shard_map/ppermute | solution.py:154
  48.1 5.0 %collective-permute-start.5 = (f32[3,2,30,134]{3,2,1,0:T(8,128)S(1)}, f32[3,2,30,134]{3,2,1,0:T(8,128)S(1)}, u32[]{:S(2)}, u32[]{:S(2)}) collective-permute-start(f32[3,2,30,134]{3,2,1,0:T(8,128)S(1)} %get-tuple-element.28), channel_id=1, source_target_pairs={{0,384},{192,576},{384,0},{576,192},{1,385},{193,577},{385,1},{577... | collective-permute-start | bytes 289448 | tf_op jit(solution)/shard_map/ppermute | solution.py:154
  53.1 2.3 %collective-permute-start.6 = (f32[3,2,30,134]{3,2,1,0:T(8,128)S(1)}, f32[3,2,30,134]{3,2,1,0:T(8,128)S(1)}, u32[]{:S(2)}, u32[]{:S(2)}) collective-permute-start(f32[3,2,30,134]{3,2,1,0:T(8,128)S(1)} %get-tuple-element.26), channel_id=1, source_target_pairs={{0,192},{192,384},{384,576},{576,0},{1,193},{193,385},{385,577},{5... | collective-permute-start | bytes 289448 | tf_op jit(solution)/shard_map/ppermute | solution.py:154
  55.4 1.5 %fusion.32 = (f32[20,2,30,134]{3,2,1,0:T(8,128)S(1)}, f32[20,2,30,134]{3,2,1,0:T(8,128)S(1)}, f32[20,2,30,134]{3,2,1,0:T(8,128)S(1)}, f32[20,2,30,134]{3,2,1,0:T(8,128)S(1)}, f32[20,2,30,134]{3,2,1,0:T(8,128)S(1)}) fusion(f32[20,2,32,136]{3,2,1,0:T(8,128)S(1)} %bitcast.68), kind=kLoop, calls=%fused_computation.102 | loop fusion | bytes 6432000 | tf_op jit(solution)/shard_map/slice | solution.py:41
  57.0 0.1 fusion.14
  57.1 0.1 slice.647
  57.2 0.1 slice.646
  57.3 0.1 slice.645
  57.4 0.1 slice.644
  57.5 10.0 %collective-permute-done.4 = f32[3,2,30,134]{3,2,1,0:T(8,128)S(1)} collective-permute-done((f32[3,2,30,134]{3,2,1,0:T(8,128)S(1)}, f32[3,2,30,134]{3,2,1,0:T(8,128)S(1)}, u32[]{:S(2)}, u32[]{:S(2)}) %collective-permute-start.4) | collective-permute-done | bytes 96512 | tf_op jit(solution)/shard_map/ppermute | solution.py:154
  67.5 9.4 %collective-permute-done.5 = f32[3,2,30,134]{3,2,1,0:T(8,128)S(1)} collective-permute-done((f32[3,2,30,134]{3,2,1,0:T(8,128)S(1)}, f32[3,2,30,134]{3,2,1,0:T(8,128)S(1)}, u32[]{:S(2)}, u32[]{:S(2)}) %collective-permute-start.5) | collective-permute-done | bytes 96512 | tf_op jit(solution)/shard_map/ppermute | solution.py:154
  76.9 0.4 collective-permute-done.6
  77.4 0.1 slice.660
  77.4 0.1 slice.667
  77.5 0.1 slice.663
  77.6 0.1 slice.670
  77.9 4.4 %add_multiply_fusion = f32[20,2,30,134]{3,0,2,1:T(8,128)S(1)} fusion(f32[20,2,30,134]{3,2,1,0:T(8,128)S(1)} %get-tuple-element.13, f32[20,2,30,134]{3,2,1,0:T(8,128)S(1)} %get-tuple-element.14, f32[20,2,30,134]{3,2,1,0:T(8,128)S(1)} %get-tuple-element.11, f32[20,2,30,134]{3,2,1,0:T(8,128)S(1)} %get-tuple-element.12, ...), kind=kLoop, calls=%fused_computation.1 | loop fusion | flops 2412000 | bytes 3955680 | tf_op jit(solution)/shard_map/mul | solution.py:76
  82.3 1.5 %add_multiply_fusion.1 = f32[20,2,28,132]{3,0,2,1:T(8,128)S(1)} fusion(f32[20,2,30,134]{3,0,2,1:T(8,128)S(1)} %add_multiply_fusion, f32[2,28,132]{2,1,0:T(8,128)S(1)} %slice.663, f32[2,28,132]{2,1,0:T(8,128)S(1)} %slice.660, f32[2,28,132]{2,1,0:T(8,128)S(1)} %slice.646), kind=kLoop, calls=%fused_computation.2 | loop fusion | flops 2217600 | bytes 3636864 | tf_op jit(solution)/shard_map/mul | solution.py:76
  83.8 1.4 %add_multiply_fusion.2 = f32[20,2,26,130]{3,0,2,1:T(8,128)S(1)} fusion(f32[20,2,28,132]{3,0,2,1:T(8,128)S(1)} %add_multiply_fusion.1, f32[2,26,130]{2,1,0:T(8,128)S(1)} %slice.670, f32[2,26,130]{2,1,0:T(8,128)S(1)} %slice.667, f32[2,26,130]{2,1,0:T(8,128)S(1)} %slice.645), kind=kLoop, calls=%fused_computation.3 | loop fusion | flops 2028000 | bytes 3325920 | tf_op jit(solution)/shard_map/mul | solution.py:76
  85.2 0.7 add_multiply_fusion.3
  85.9 0.1 fusion.28
  86.0 0.7 fusion.3
  86.8 0.1 multiply_multiply_fusion
  86.8 1.9 %collective-permute-start.7 = (f32[2,24,128]{2,1,0:T(8,128)S(1)}, f32[2,24,128]{2,1,0:T(8,128)S(1)}, u32[]{:S(2)}, u32[]{:S(2)}) collective-permute-start(f32[2,24,128]{2,1,0:T(8,128)S(1)} %multiply_multiply_fusion), channel_id=1, source_target_pairs={{0,576},{192,0},{384,192},{576,384},{1,577},{193,1},{385,193},{577... | collective-permute-start | bytes 73736 | tf_op jit(solution)/shard_map/ppermute | solution.py:182
  88.8 6.1 %collective-permute-start.8 = (f32[2,24,128]{2,1,0:T(8,128)S(1)}, f32[2,24,128]{2,1,0:T(8,128)S(1)}, u32[]{:S(2)}, u32[]{:S(2)}) collective-permute-start(f32[2,24,128]{2,1,0:T(8,128)S(1)} %multiply_multiply_fusion), channel_id=1, source_target_pairs={{0,384},{192,576},{384,0},{576,192},{1,385},{193,577},{385,1},{577... | collective-permute-start | bytes 73736 | tf_op jit(solution)/shard_map/ppermute | solution.py:182
  94.9 1.9 %collective-permute-start.9 = (f32[2,24,128]{2,1,0:T(8,128)S(1)}, f32[2,24,128]{2,1,0:T(8,128)S(1)}, u32[]{:S(2)}, u32[]{:S(2)}) collective-permute-start(f32[2,24,128]{2,1,0:T(8,128)S(1)} %multiply_multiply_fusion), channel_id=1, source_target_pairs={{0,192},{192,384},{384,576},{576,0},{1,193},{193,385},{385,577},{5... | collective-permute-start | bytes 73736 | tf_op jit(solution)/shard_map/ppermute | solution.py:182
  96.8 0.2 fusion.9
  97.1 0.1 slice.685
  97.2 0.1 copy.31
  97.3 3.5 %collective-permute-done.8 = f32[2,24,128]{2,1,0:T(8,128)S(1)} collective-permute-done((f32[2,24,128]{2,1,0:T(8,128)S(1)}, f32[2,24,128]{2,1,0:T(8,128)S(1)}, u32[]{:S(2)}, u32[]{:S(2)}) %collective-permute-start.8) | collective-permute-done | bytes 24608 | tf_op jit(solution)/shard_map/ppermute | solution.py:182
  100.8 5.6 %collective-permute-done.9 = f32[2,24,128]{2,1,0:T(8,128)S(1)} collective-permute-done((f32[2,24,128]{2,1,0:T(8,128)S(1)}, f32[2,24,128]{2,1,0:T(8,128)S(1)}, u32[]{:S(2)}, u32[]{:S(2)}) %collective-permute-start.9) | collective-permute-done | bytes 24608 | tf_op jit(solution)/shard_map/ppermute | solution.py:182
  106.4 0.1 fusion.13
  106.5 0.1 fusion.30
  106.6 0.8 bitcast_select_fusion
  (29 shorter events, 0.8 us)
Async XLA Ops:
  0.0 86.0 %copy-start = (f32[20,20]{1,0:T(8,128)S(1)}, f32[20,20]{1,0:T(8,128)}, u32[]{:S(2)}) copy-start(f32[20,20]{1,0:T(8,128)} %param.6) | copy-start | bytes 4804
  1.7 19.9 %collective-permute-start = (f32[41,7,128]{2,1,0:T(8,128)S(1)}, f32[41,7,128]{2,1,0:T(8,128)S(1)}, u32[]{:S(2)}, u32[]{:S(2)}) collective-permute-start(f32[41,7,128]{2,1,0:T(8,128)S(1)} %get-tuple-element.29), channel_id=1, source_target_pairs={{0,4},{4,8},{8,12},{12,16},{16,20},{20,24},{24,28},{28,32},{32,36}... | collective-permute-start | bytes 440840 | tf_op jit(solution)/shard_map/ppermute | solution.py:17
  5.2 17.6 %collective-permute-start.1 = (f32[41,7,128]{2,1,0:T(8,128)S(1)}, f32[41,7,128]{2,1,0:T(8,128)S(1)}, u32[]{:S(2)}, u32[]{:S(2)}) collective-permute-start(f32[41,7,128]{2,1,0:T(8,128)S(1)} %get-tuple-element.30), channel_id=1, source_target_pairs={{4,0},{8,4},{12,8},{16,12},{20,16},{24,20},{28,24},{32,28},{36,32}... | collective-permute-start | bytes 440840 | tf_op jit(solution)/shard_map/ppermute | solution.py:20
  24.7 8.6 %collective-permute-start.2 = (f32[41,38,7]{0,1,2:T(8,128)S(1)}, f32[41,38,7]{0,1,2:T(8,128)S(1)}, u32[]{:S(2)}, u32[]{:S(2)}) collective-permute-start(f32[41,38,7]{0,1,2:T(8,128)S(1)} %copy.20), channel_id=1, source_target_pairs={{0,1},{1,2},{2,3},{3,0},{4,5},{5,6},{6,7},{7,4},{8,9},{9,10},{10,1... | collective-permute-start | bytes 130880 | tf_op jit(solution)/shard_map/ppermute | solution.py:17
  30.6 9.1 %copy-start.1 = (f32[1,40,24,128]{3,2,1,0:T(8,128)S(1)}, f32[1,40,24,128]{3,2,1,0:T(8,128)}, u32[]{:S(2)}) copy-start(f32[1,40,24,128]{3,2,1,0:T(8,128)} %param.4) | copy-start | bytes 1474564
  31.1 8.2 %collective-permute-start.3 = (f32[41,38,7]{0,1,2:T(8,128)S(1)}, f32[41,38,7]{0,1,2:T(8,128)S(1)}, u32[]{:S(2)}, u32[]{:S(2)}) collective-permute-start(f32[41,38,7]{0,1,2:T(8,128)S(1)} %copy.21), channel_id=1, source_target_pairs={{1,0},{2,1},{3,2},{0,3},{5,4},{6,5},{7,6},{4,7},{9,8},{10,9},{11,1... | collective-permute-start | bytes 130880 | tf_op jit(solution)/shard_map/ppermute | solution.py:20
  44.7 22.8 %collective-permute-start.4 = (f32[3,2,30,134]{3,2,1,0:T(8,128)S(1)}, f32[3,2,30,134]{3,2,1,0:T(8,128)S(1)}, u32[]{:S(2)}, u32[]{:S(2)}) collective-permute-start(f32[3,2,30,134]{3,2,1,0:T(8,128)S(1)} %get-tuple-element.27), channel_id=1, source_target_pairs={{0,576},{192,0},{384,192},{576,384},{1,577},{193,1},{385,193},{577... | collective-permute-start | bytes 289448 | tf_op jit(solution)/shard_map/ppermute | solution.py:154
  48.1 28.8 %collective-permute-start.5 = (f32[3,2,30,134]{3,2,1,0:T(8,128)S(1)}, f32[3,2,30,134]{3,2,1,0:T(8,128)S(1)}, u32[]{:S(2)}, u32[]{:S(2)}) collective-permute-start(f32[3,2,30,134]{3,2,1,0:T(8,128)S(1)} %get-tuple-element.28), channel_id=1, source_target_pairs={{0,384},{192,576},{384,0},{576,192},{1,385},{193,577},{385,1},{577... | collective-permute-start | bytes 289448 | tf_op jit(solution)/shard_map/ppermute | solution.py:154
  53.1 24.1 %collective-permute-start.6 = (f32[3,2,30,134]{3,2,1,0:T(8,128)S(1)}, f32[3,2,30,134]{3,2,1,0:T(8,128)S(1)}, u32[]{:S(2)}, u32[]{:S(2)}) collective-permute-start(f32[3,2,30,134]{3,2,1,0:T(8,128)S(1)} %get-tuple-element.26), channel_id=1, source_target_pairs={{0,192},{192,384},{384,576},{576,0},{1,193},{193,385},{385,577},{5... | collective-permute-start | bytes 289448 | tf_op jit(solution)/shard_map/ppermute | solution.py:154
  85.2 0.8 copy-start.2
  86.8 10.4 %collective-permute-start.7 = (f32[2,24,128]{2,1,0:T(8,128)S(1)}, f32[2,24,128]{2,1,0:T(8,128)S(1)}, u32[]{:S(2)}, u32[]{:S(2)}) collective-permute-start(f32[2,24,128]{2,1,0:T(8,128)S(1)} %multiply_multiply_fusion), channel_id=1, source_target_pairs={{0,576},{192,0},{384,192},{576,384},{1,577},{193,1},{385,193},{577... | collective-permute-start | bytes 73736 | tf_op jit(solution)/shard_map/ppermute | solution.py:182
  88.8 12.0 %collective-permute-start.8 = (f32[2,24,128]{2,1,0:T(8,128)S(1)}, f32[2,24,128]{2,1,0:T(8,128)S(1)}, u32[]{:S(2)}, u32[]{:S(2)}) collective-permute-start(f32[2,24,128]{2,1,0:T(8,128)S(1)} %multiply_multiply_fusion), channel_id=1, source_target_pairs={{0,384},{192,576},{384,0},{576,192},{1,385},{193,577},{385,1},{577... | collective-permute-start | bytes 73736 | tf_op jit(solution)/shard_map/ppermute | solution.py:182
  94.9 11.5 %collective-permute-start.9 = (f32[2,24,128]{2,1,0:T(8,128)S(1)}, f32[2,24,128]{2,1,0:T(8,128)S(1)}, u32[]{:S(2)}, u32[]{:S(2)}) collective-permute-start(f32[2,24,128]{2,1,0:T(8,128)S(1)} %multiply_multiply_fusion), channel_id=1, source_target_pairs={{0,192},{192,384},{384,576},{576,0},{1,193},{193,385},{385,577},{5... | collective-permute-start | bytes 73736 | tf_op jit(solution)/shard_map/ppermute | solution.py:182

commit v3 on v2

--- a/solution.py
+++ b/solution.py
@@ -150,7 +150,7 @@
     )
     own = forcing[0]
     for shift in range(1, groups):
-        pairs = [(i, (i + shift) % groups) for i in range(groups)]
+        pairs = [(0, shift)]
         arrived = lax.ppermute(forcing[shift - 1], "grp", pairs)
         own = jnp.where(member == shift, arrived, own)
     own_zonal = own[0]
@@ -178,7 +178,7 @@
     heating = 0.3 * wet_member * updated[0] * light_factor
     returned = []
     for shift in range(1, groups):
-        pairs = [(i, (i - shift) % groups) for i in range(groups)]
+        pairs = [(shift, 0)]
         returned.append(lax.ppermute(heating, "grp", pairs))
     returned = jnp.concatenate(returned, axis=0)
     temper_final = temper + returned

time: 108 us -> 83.5 us (0.77)
  the two profiles are of different devices: /device:TPU:6 before, /device:TPU:88 now
where the time goes in v3:
time: 83.5 us; the launch traced here: 83.1 us
  starting transfers between devices  33.9 us (41%)
  waiting for transfers between devices  25.7 us (31%)
  other arithmetic  16.7 us (20%)
  local copies, waits for them, and re-layouts  5.59 us (7%)
    ppermute x3, starting transfers between devices, body(): arrived = lax.ppermute(forcing[shift - 1], 'grp', pairs)  16.4 us
    ppermute x3, waiting for transfers between devices, body(): returned.append(lax.ppermute(heating, 'grp', pairs))  9.74 us
    ppermute x2, starting transfers between devices, exchange(): lax.ppermute(lax.slice_in_dim(block, block.shape[dim] - width, None, axis...  8.1 us
    mul x4, other arithmetic, advect_tracers(): wet_mask * (center_of(tracer_pad) - 0.25 * (zonal * grad_x(tracer_pad) +...  7.97 us
    ppermute x2, waiting for transfers between devices, exchange(): lax.ppermute(lax.slice_in_dim(block, 0, width, axis=dim), axis, backward)  7.51 us
    ppermute x3, waiting for transfers between devices, body(): arrived = lax.ppermute(forcing[shift - 1], 'grp', pairs)  6.58 us
    ppermute x2, starting transfers between devices, exchange(): lax.ppermute(lax.slice_in_dim(block, 0, width, axis=dim), axis, backward)  5.58 us
    ppermute x3, starting transfers between devices, body(): returned.append(lax.ppermute(heating, 'grp', pairs))  3.87 us
  transfers between devices with their start and end apart: 10, of which 8 were waited for; matrix products, arithmetic and copies ran while one was open for 4% of the time, Pallas kernels for 0%

profile of v3, /device:TPU:88, one launch (start us, length us, event | category | flops | bytes accessed | tf_op | source)
XLA Modules:
  0.0 83.1 jit_solution(16813072639361120467)
XLA Ops:
  0.0 0.7 convert_bitcast_fusion
  0.7 1.0 %pad_maximum_fusion.3 = (f32[41,7,128]{2,1,0:T(8,128)S(1)}, f32[41,7,128]{2,1,0:T(8,128)S(1)}) fusion(f32[1,24,128]{2,1,0:T(8,128)S(1)} %convert_bitcast_fusion, f32[40,24,128]{2,1,0:T(8,128)} %bitcast.69), kind=kLoop, calls=%fused_computation.47 | loop fusion | flops 73472 | bytes 797696 | tf_op jit(solution)/shard_map/slice | solution.py:18
  1.7 4.7 %collective-permute-start = (f32[41,7,128]{2,1,0:T(8,128)S(1)}, f32[41,7,128]{2,1,0:T(8,128)S(1)}, u32[]{:S(2)}, u32[]{:S(2)}) collective-permute-start(f32[41,7,128]{2,1,0:T(8,128)S(1)} %get-tuple-element.29), channel_id=1, source_target_pairs={{0,4},{4,8},{8,12},{12,16},{16,20},{20,24},{24,28},{28,32},{32,36}... | collective-permute-start | bytes 440840 | tf_op jit(solution)/shard_map/ppermute | solution.py:17
  6.5 1.9 %collective-permute-start.1 = (f32[41,7,128]{2,1,0:T(8,128)S(1)}, f32[41,7,128]{2,1,0:T(8,128)S(1)}, u32[]{:S(2)}, u32[]{:S(2)}) collective-permute-start(f32[41,7,128]{2,1,0:T(8,128)S(1)} %get-tuple-element.30), channel_id=1, source_target_pairs={{4,0},{8,4},{12,8},{16,12},{20,16},{24,20},{28,24},{32,28},{36,32}... | collective-permute-start | bytes 440840 | tf_op jit(solution)/shard_map/ppermute | solution.py:20
  8.5 1.5 %collective-permute-done = f32[41,7,128]{2,1,0:T(8,128)S(1)} collective-permute-done((f32[41,7,128]{2,1,0:T(8,128)S(1)}, f32[41,7,128]{2,1,0:T(8,128)S(1)}, u32[]{:S(2)}, u32[]{:S(2)}) %collective-permute-start) | collective-permute-done | bytes 146976 | tf_op jit(solution)/shard_map/ppermute | solution.py:17
  10.0 5.3 %collective-permute-done.1 = f32[41,7,128]{2,1,0:T(8,128)S(1)} collective-permute-done((f32[41,7,128]{2,1,0:T(8,128)S(1)}, f32[41,7,128]{2,1,0:T(8,128)S(1)}, u32[]{:S(2)}, u32[]{:S(2)}) %collective-permute-start.1) | collective-permute-done | bytes 146976 | tf_op jit(solution)/shard_map/ppermute | solution.py:20
  15.3 1.1 %pad_maximum_fusion = f32[41,38,128]{2,1,0:T(8,128)S(1)} fusion(f32[41,7,128]{2,1,0:T(8,128)S(1)} %collective-permute-done.1, f32[1,24,128]{2,1,0:T(8,128)S(1)} %convert_bitcast_fusion, f32[40,24,128]{2,1,0:T(8,128)} %bitcast.70, f32[41,7,128]{2,1,0:T(8,128)S(1)} %collective-permute-done), kind=kLoop, calls=%fused_computation.9 | loop fusion | flops 598272 | bytes 1595392 | tf_op jit(solution)/shard_map/concatenate | solution.py:21
  16.4 0.3 fusion.33
  16.7 0.4 copy.20
  17.2 3.4 %collective-permute-start.2 = (f32[41,38,7]{0,1,2:T(8,128)S(1)}, f32[41,38,7]{0,1,2:T(8,128)S(1)}, u32[]{:S(2)}, u32[]{:S(2)}) collective-permute-start(f32[41,38,7]{0,1,2:T(8,128)S(1)} %copy.20), channel_id=1, source_target_pairs={{0,1},{1,2},{2,3},{3,0},{4,5},{5,6},{6,7},{7,4},{8,9},{9,10},{10,1... | collective-permute-start | bytes 130880 | tf_op jit(solution)/shard_map/ppermute | solution.py:17
  20.6 0.4 copy.21
  21.0 3.7 %collective-permute-start.3 = (f32[41,38,7]{0,1,2:T(8,128)S(1)}, f32[41,38,7]{0,1,2:T(8,128)S(1)}, u32[]{:S(2)}, u32[]{:S(2)}) collective-permute-start(f32[41,38,7]{0,1,2:T(8,128)S(1)} %copy.21), channel_id=1, source_target_pairs={{1,0},{2,1},{3,2},{0,3},{5,4},{6,5},{7,6},{4,7},{9,8},{10,9},{11,1... | collective-permute-start | bytes 130880 | tf_op jit(solution)/shard_map/ppermute | solution.py:20
  25.0 0.4 collective-permute-done.2
  25.4 0.5 copy.22
  25.8 2.2 %collective-permute-done.3 = f32[41,38,7]{0,1,2:T(8,128)S(1)} collective-permute-done((f32[41,38,7]{0,1,2:T(8,128)S(1)}, f32[41,38,7]{0,1,2:T(8,128)S(1)}, u32[]{:S(2)}, u32[]{:S(2)}) %collective-permute-start.3) | collective-permute-done | bytes 43656 | tf_op jit(solution)/shard_map/ppermute | solution.py:20
  28.0 0.5 copy.23
  28.5 0.9 %maximum_select_fusion = f32[41,38,142]{2,1,0:T(8,128)S(1)} fusion(f32[41,38,7]{2,1,0:T(8,128)S(1)} %copy.23, f32[41,7,128]{2,1,0:T(8,128)S(1)} %collective-permute-done.1, f32[1,24,128]{2,1,0:T(8,128)S(1)} %convert_bitcast_fusion, f32[40,24,128]{2,1,0:T(8,128)S(1)} %bitcast.71, f32[41,7,128]{2,1,0:T(8,128)S(1)} %collective-permute-done, ...), kind=kLoop, calls=%fused_computation | loop fusion | flops 1327416 | bytes 1770030 | tf_op jit(solution)/shard_map/jit(_where)/select_n | solution.py:26
  29.4 0.3 fusion.7
  29.7 0.5 slice.648
  30.2 0.1 compare_convert_fusion
  30.3 0.1 fusion.19
  30.4 0.5 subtract_multiply_fusion.3
  30.9 0.3 fusion.5
  31.2 0.1 fusion.16
  31.3 0.5 subtract_multiply_fusion.1
  31.8 0.2 fusion.11
  32.1 0.1 fusion.24
  32.2 0.1 fusion.34
  32.3 0.4 subtract_multiply_fusion.7
  32.8 0.4 subtract_multiply_fusion.4
  33.2 0.1 fusion.15
  33.4 11.3 %collective-permute-start.4 = (f32[3,2,30,134]{3,2,1,0:T(8,128)S(1)}, f32[3,2,30,134]{3,2,1,0:T(8,128)S(1)}, u32[]{:S(2)}, u32[]{:S(2)}) collective-permute-start(f32[3,2,30,134]{3,2,1,0:T(8,128)S(1)} %get-tuple-element.27), channel_id=1, source_target_pairs={{0,576},{1,577},{2,578},{3,579},{4,580},{5,581},{6,582},{7,583},{8... | collective-permute-start | bytes 289448 | tf_op jit(solution)/shard_map/ppermute | solution.py:154
  44.7 3.6 %collective-permute-start.5 = (f32[3,2,30,134]{3,2,1,0:T(8,128)S(1)}, f32[3,2,30,134]{3,2,1,0:T(8,128)S(1)}, u32[]{:S(2)}, u32[]{:S(2)}) collective-permute-start(f32[3,2,30,134]{3,2,1,0:T(8,128)S(1)} %get-tuple-element.28), channel_id=1, source_target_pairs={{0,384},{1,385},{2,386},{3,387},{4,388},{5,389},{6,390},{7,391},{8... | collective-permute-start | bytes 289448 | tf_op jit(solution)/shard_map/ppermute | solution.py:154
  48.3 1.5 %collective-permute-start.6 = (f32[3,2,30,134]{3,2,1,0:T(8,128)S(1)}, f32[3,2,30,134]{3,2,1,0:T(8,128)S(1)}, u32[]{:S(2)}, u32[]{:S(2)}) collective-permute-start(f32[3,2,30,134]{3,2,1,0:T(8,128)S(1)} %get-tuple-element.26), channel_id=1, source_target_pairs={{0,192},{1,193},{2,194},{3,195},{4,196},{5,197},{6,198},{7,199},{8... | collective-permute-start | bytes 289448 | tf_op jit(solution)/shard_map/ppermute | solution.py:154
  49.8 1.5 %fusion.32 = (f32[20,2,30,134]{3,2,1,0:T(8,128)S(1)}, f32[20,2,30,134]{3,2,1,0:T(8,128)S(1)}, f32[20,2,30,134]{3,2,1,0:T(8,128)S(1)}, f32[20,2,30,134]{3,2,1,0:T(8,128)S(1)}, f32[20,2,30,134]{3,2,1,0:T(8,128)S(1)}) fusion(f32[20,2,32,136]{3,2,1,0:T(8,128)S(1)} %bitcast.68), kind=kLoop, calls=%fused_computation.102 | loop fusion | bytes 6432000 | tf_op jit(solution)/shard_map/slice | solution.py:41
  51.3 0.1 fusion.14
  51.5 0.1 slice.647
  51.6 0.1 slice.646
  51.7 0.1 slice.645
  51.8 4.5 %collective-permute-done.4 = f32[3,2,30,134]{3,2,1,0:T(8,128)S(1)} collective-permute-done((f32[3,2,30,134]{3,2,1,0:T(8,128)S(1)}, f32[3,2,30,134]{3,2,1,0:T(8,128)S(1)}, u32[]{:S(2)}, u32[]{:S(2)}) %collective-permute-start.4) | collective-permute-done | bytes 96512 | tf_op jit(solution)/shard_map/ppermute | solution.py:154
  56.3 2.1 %collective-permute-done.5 = f32[3,2,30,134]{3,2,1,0:T(8,128)S(1)} collective-permute-done((f32[3,2,30,134]{3,2,1,0:T(8,128)S(1)}, f32[3,2,30,134]{3,2,1,0:T(8,128)S(1)}, u32[]{:S(2)}, u32[]{:S(2)}) %collective-permute-start.5) | collective-permute-done | bytes 96512 | tf_op jit(solution)/shard_map/ppermute | solution.py:154
  58.5 0.1 slice.660
  58.6 0.1 slice.667
  58.7 0.1 slice.663
  58.8 0.1 slice.670
  58.9 0.1 slice.674
  59.0 4.4 %add_multiply_fusion = f32[20,2,30,134]{3,0,2,1:T(8,128)S(1)} fusion(f32[20,2,30,134]{3,2,1,0:T(8,128)S(1)} %get-tuple-element.13, f32[20,2,30,134]{3,2,1,0:T(8,128)S(1)} %get-tuple-element.14, f32[20,2,30,134]{3,2,1,0:T(8,128)S(1)} %get-tuple-element.11, f32[20,2,30,134]{3,2,1,0:T(8,128)S(1)} %get-tuple-element.12, ...), kind=kLoop, calls=%fused_computation.1 | loop fusion | flops 2412000 | bytes 3955680 | tf_op jit(solution)/shard_map/mul | solution.py:76
  63.4 1.5 %add_multiply_fusion.1 = f32[20,2,28,132]{3,0,2,1:T(8,128)S(1)} fusion(f32[20,2,30,134]{3,0,2,1:T(8,128)S(1)} %add_multiply_fusion, f32[2,28,132]{2,1,0:T(8,128)S(1)} %slice.663, f32[2,28,132]{2,1,0:T(8,128)S(1)} %slice.660, f32[2,28,132]{2,1,0:T(8,128)S(1)} %slice.646), kind=kLoop, calls=%fused_computation.2 | loop fusion | flops 2217600 | bytes 3636864 | tf_op jit(solution)/shard_map/mul | solution.py:76
  64.9 1.4 %add_multiply_fusion.2 = f32[20,2,26,130]{3,0,2,1:T(8,128)S(1)} fusion(f32[20,2,28,132]{3,0,2,1:T(8,128)S(1)} %add_multiply_fusion.1, f32[2,26,130]{2,1,0:T(8,128)S(1)} %slice.670, f32[2,26,130]{2,1,0:T(8,128)S(1)} %slice.667, f32[2,26,130]{2,1,0:T(8,128)S(1)} %slice.645), kind=kLoop, calls=%fused_computation.3 | loop fusion | flops 2028000 | bytes 3325920 | tf_op jit(solution)/shard_map/mul | solution.py:76
  66.3 0.7 add_multiply_fusion.3
  67.0 0.1 fusion.28
  67.2 0.7 fusion.3
  67.9 0.1 multiply_multiply_fusion
  68.0 1.3 %collective-permute-start.7 = (f32[2,24,128]{2,1,0:T(8,128)S(1)}, f32[2,24,128]{2,1,0:T(8,128)S(1)}, u32[]{:S(2)}, u32[]{:S(2)}) collective-permute-start(f32[2,24,128]{2,1,0:T(8,128)S(1)} %multiply_multiply_fusion), channel_id=1, source_target_pairs={{192,0},{193,1},{194,2},{195,3},{196,4},{197,5},{198,6},{199,7},{2... | collective-permute-start | bytes 73736 | tf_op jit(solution)/shard_map/ppermute | solution.py:182
  69.3 1.3 %collective-permute-start.8 = (f32[2,24,128]{2,1,0:T(8,128)S(1)}, f32[2,24,128]{2,1,0:T(8,128)S(1)}, u32[]{:S(2)}, u32[]{:S(2)}) collective-permute-start(f32[2,24,128]{2,1,0:T(8,128)S(1)} %multiply_multiply_fusion), channel_id=1, source_target_pairs={{384,0},{385,1},{386,2},{387,3},{388,4},{389,5},{390,6},{391,7},{3... | collective-permute-start | bytes 73736 | tf_op jit(solution)/shard_map/ppermute | solution.py:182
  70.6 1.3 %collective-permute-start.9 = (f32[2,24,128]{2,1,0:T(8,128)S(1)}, f32[2,24,128]{2,1,0:T(8,128)S(1)}, u32[]{:S(2)}, u32[]{:S(2)}) collective-permute-start(f32[2,24,128]{2,1,0:T(8,128)S(1)} %multiply_multiply_fusion), channel_id=1, source_target_pairs={{576,0},{577,1},{578,2},{579,3},{580,4},{581,5},{582,6},{583,7},{5... | collective-permute-start | bytes 73736 | tf_op jit(solution)/shard_map/ppermute | solution.py:182
  71.9 0.2 fusion.9
  72.1 0.1 slice.685
  72.2 0.1 copy.31
  72.3 9.0 %collective-permute-done.8 = f32[2,24,128]{2,1,0:T(8,128)S(1)} collective-permute-done((f32[2,24,128]{2,1,0:T(8,128)S(1)}, f32[2,24,128]{2,1,0:T(8,128)S(1)}, u32[]{:S(2)}, u32[]{:S(2)}) %collective-permute-start.8) | collective-permute-done | bytes 24608 | tf_op jit(solution)/shard_map/ppermute | solution.py:182
  81.3 0.7 collective-permute-done.9
  82.0 0.1 fusion.13
  82.1 0.1 fusion.30
  82.2 0.8 %bitcast_select_fusion = f32[1,40,24,128]{3,2,1,0:T(8,128)} fusion(f32[1,40,24,128]{3,2,1,0:T(8,128)S(1)} %broadcast_dynamic-update-slice_fusion, pred[]{:T(512)S(6)} %eq.18, f32[1,40,24,128]{3,2,1,0:T(8,128)S(1)} %bitcast.72), kind=kLoop, calls=%fused_computation.12 | loop fusion | flops 122880 | bytes 1474561 | tf_op jit(solution)/shard_map/jit(_where)/select_n | solution.py:187
  (29 shorter events, 0.8 us)
Async XLA Ops:
  0.0 67.1 %copy-start = (f32[20,20]{1,0:T(8,128)S(1)}, f32[20,20]{1,0:T(8,128)}, u32[]{:S(2)}) copy-start(f32[20,20]{1,0:T(8,128)} %param.6) | copy-start | bytes 4804
  1.7 8.2 %collective-permute-start = (f32[41,7,128]{2,1,0:T(8,128)S(1)}, f32[41,7,128]{2,1,0:T(8,128)S(1)}, u32[]{:S(2)}, u32[]{:S(2)}) collective-permute-start(f32[41,7,128]{2,1,0:T(8,128)S(1)} %get-tuple-element.29), channel_id=1, source_target_pairs={{0,4},{4,8},{8,12},{12,16},{16,20},{20,24},{24,28},{28,32},{32,36}... | collective-permute-start | bytes 440840 | tf_op jit(solution)/shard_map/ppermute | solution.py:17
  6.5 8.9 %collective-permute-start.1 = (f32[41,7,128]{2,1,0:T(8,128)S(1)}, f32[41,7,128]{2,1,0:T(8,128)S(1)}, u32[]{:S(2)}, u32[]{:S(2)}) collective-permute-start(f32[41,7,128]{2,1,0:T(8,128)S(1)} %get-tuple-element.30), channel_id=1, source_target_pairs={{4,0},{8,4},{12,8},{16,12},{20,16},{24,20},{28,24},{32,28},{36,32}... | collective-permute-start | bytes 440840 | tf_op jit(solution)/shard_map/ppermute | solution.py:20
  17.2 8.2 %collective-permute-start.2 = (f32[41,38,7]{0,1,2:T(8,128)S(1)}, f32[41,38,7]{0,1,2:T(8,128)S(1)}, u32[]{:S(2)}, u32[]{:S(2)}) collective-permute-start(f32[41,38,7]{0,1,2:T(8,128)S(1)} %copy.20), channel_id=1, source_target_pairs={{0,1},{1,2},{2,3},{3,0},{4,5},{5,6},{6,7},{7,4},{8,9},{9,10},{10,1... | collective-permute-start | bytes 130880 | tf_op jit(solution)/shard_map/ppermute | solution.py:17
  20.6 7.9 %copy-start.1 = (f32[1,40,24,128]{3,2,1,0:T(8,128)S(1)}, f32[1,40,24,128]{3,2,1,0:T(8,128)}, u32[]{:S(2)}) copy-start(f32[1,40,24,128]{3,2,1,0:T(8,128)} %param.4) | copy-start | bytes 1474564
  21.0 7.0 %collective-permute-start.3 = (f32[41,38,7]{0,1,2:T(8,128)S(1)}, f32[41,38,7]{0,1,2:T(8,128)S(1)}, u32[]{:S(2)}, u32[]{:S(2)}) collective-permute-start(f32[41,38,7]{0,1,2:T(8,128)S(1)} %copy.21), channel_id=1, source_target_pairs={{1,0},{2,1},{3,2},{0,3},{5,4},{6,5},{7,6},{4,7},{9,8},{10,9},{11,1... | collective-permute-start | bytes 130880 | tf_op jit(solution)/shard_map/ppermute | solution.py:20
  33.4 22.9 %collective-permute-start.4 = (f32[3,2,30,134]{3,2,1,0:T(8,128)S(1)}, f32[3,2,30,134]{3,2,1,0:T(8,128)S(1)}, u32[]{:S(2)}, u32[]{:S(2)}) collective-permute-start(f32[3,2,30,134]{3,2,1,0:T(8,128)S(1)} %get-tuple-element.27), channel_id=1, source_target_pairs={{0,576},{1,577},{2,578},{3,579},{4,580},{5,581},{6,582},{7,583},{8... | collective-permute-start | bytes 289448 | tf_op jit(solution)/shard_map/ppermute | solution.py:154
  44.7 13.7 %collective-permute-start.5 = (f32[3,2,30,134]{3,2,1,0:T(8,128)S(1)}, f32[3,2,30,134]{3,2,1,0:T(8,128)S(1)}, u32[]{:S(2)}, u32[]{:S(2)}) collective-permute-start(f32[3,2,30,134]{3,2,1,0:T(8,128)S(1)} %get-tuple-element.28), channel_id=1, source_target_pairs={{0,384},{1,385},{2,386},{3,387},{4,388},{5,389},{6,390},{7,391},{8... | collective-permute-start | bytes 289448 | tf_op jit(solution)/shard_map/ppermute | solution.py:154
  48.3 10.1 %collective-permute-start.6 = (f32[3,2,30,134]{3,2,1,0:T(8,128)S(1)}, f32[3,2,30,134]{3,2,1,0:T(8,128)S(1)}, u32[]{:S(2)}, u32[]{:S(2)}) collective-permute-start(f32[3,2,30,134]{3,2,1,0:T(8,128)S(1)} %get-tuple-element.26), channel_id=1, source_target_pairs={{0,192},{1,193},{2,194},{3,195},{4,196},{5,197},{6,198},{7,199},{8... | collective-permute-start | bytes 289448 | tf_op jit(solution)/shard_map/ppermute | solution.py:154
  66.3 0.8 %copy-start.2 = (f32[20]{0:T(128)S(1)}, f32[20]{0:T(128)}, u32[]{:S(2)}) copy-start(f32[20]{0:T(128)} %param.7) | copy-start | bytes 244
  68.0 4.3 %collective-permute-start.7 = (f32[2,24,128]{2,1,0:T(8,128)S(1)}, f32[2,24,128]{2,1,0:T(8,128)S(1)}, u32[]{:S(2)}, u32[]{:S(2)}) collective-permute-start(f32[2,24,128]{2,1,0:T(8,128)S(1)} %multiply_multiply_fusion), channel_id=1, source_target_pairs={{192,0},{193,1},{194,2},{195,3},{196,4},{197,5},{198,6},{199,7},{2... | collective-permute-start | bytes 73736 | tf_op jit(solution)/shard_map/ppermute | solution.py:182
  69.3 12.0 %collective-permute-start.8 = (f32[2,24,128]{2,1,0:T(8,128)S(1)}, f32[2,24,128]{2,1,0:T(8,128)S(1)}, u32[]{:S(2)}, u32[]{:S(2)}) collective-permute-start(f32[2,24,128]{2,1,0:T(8,128)S(1)} %multiply_multiply_fusion), channel_id=1, source_target_pairs={{384,0},{385,1},{386,2},{387,3},{388,4},{389,5},{390,6},{391,7},{3... | collective-permute-start | bytes 73736 | tf_op jit(solution)/shard_map/ppermute | solution.py:182
  70.6 11.5 %collective-permute-start.9 = (f32[2,24,128]{2,1,0:T(8,128)S(1)}, f32[2,24,128]{2,1,0:T(8,128)S(1)}, u32[]{:S(2)}, u32[]{:S(2)}) collective-permute-start(f32[2,24,128]{2,1,0:T(8,128)S(1)} %multiply_multiply_fusion), channel_id=1, source_target_pairs={{576,0},{577,1},{578,2},{579,3},{580,4},{581,5},{582,6},{583,7},{5... | collective-permute-start | bytes 73736 | tf_op jit(solution)/shard_map/ppermute | solution.py:182

commit v4 on v3

--- a/solution.py
+++ b/solution.py
@@ -10,20 +10,45 @@
 
 
 def exchange(block, width, lat_pos, lat_count):
-    for axis, dim in (("lon", 1), ("lat", 2)):
-        count = lax.axis_size(axis)
-        forward = [(i, (i + 1) % count) for i in range(count)]
-        backward = [(target, source) for source, target in forward]
-        low = lax.ppermute(
-            lax.slice_in_dim(block, block.shape[dim] - width, None, axis=dim), axis, forward
-        )
-        high = lax.ppermute(lax.slice_in_dim(block, 0, width, axis=dim), axis, backward)
-        block = jnp.concatenate([low, block, high], axis=dim)
-    length = block.shape[-1]
+    lon_count = lax.axis_size("lon")
+
+    def shifted(piece, d_lon, d_lat):
+        if d_lat == 0:
+            pairs = [(i, (i + d_lon) % lon_count) for i in range(lon_count)]
+            return lax.ppermute(piece, "lon", pairs)
+        if d_lon == 0:
+            pairs = [(j, (j + d_lat) % lat_count) for j in range(lat_count)]
+            return lax.ppermute(piece, "lat", pairs)
+        pairs = [
+            (i * lat_count + j, ((i + d_lon) % lon_count) * lat_count + (j + d_lat) % lat_count)
+            for i in range(lon_count)
+            for j in range(lat_count)
+        ]
+        return lax.ppermute(piece, ("lon", "lat"), pairs)
+
+    columns, rows = block.shape[1], block.shape[2]
+    low_x, high_x = slice(columns - width, columns), slice(0, width)
+    low_y, high_y = slice(rows - width, rows), slice(0, width)
+    every = slice(None)
+    parts = {}
+    for d_lon, xs in ((1, low_x), (0, every), (-1, high_x)):
+        for d_lat, ys in ((1, low_y), (0, every), (-1, high_y)):
+            if d_lon == 0 and d_lat == 0:
+                parts[(d_lon, d_lat)] = block
+            else:
+                parts[(d_lon, d_lat)] = shifted(block[:, xs, ys], d_lon, d_lat)
+    padded = jnp.concatenate(
+        [
+            jnp.concatenate([parts[(d_lon, 1)], parts[(d_lon, 0)], parts[(d_lon, -1)]], axis=2)
+            for d_lon in (1, 0, -1)
+        ],
+        axis=1,
+    )
+    length = padded.shape[-1]
     positions = jnp.arange(length)
     lower = (positions < width) & (lat_pos == 0)
     upper = (positions >= length - width) & (lat_pos == lat_count - 1)
-    return jnp.where(lower | upper, 0.0, block)
+    return jnp.where(lower | upper, 0.0, padded)
 
 
 def crop(array, from_radius, to_radius):

time: 83.5 us -> 109 us (1.31)
  the two profiles are of different devices: /device:TPU:88 before, /device:TPU:6 now
where the time goes in v4:
time: 109 us; the launch traced here: 108 us
  starting transfers between devices  63.8 us (59%)
  other arithmetic  20.4 us (19%)
  waiting for transfers between devices  18.1 us (17%)
  local copies, waits for them, and re-layouts  4.46 us (4%)
    ppermute x4, starting transfers between devices, shifted(): return lax.ppermute(piece, ('lon', 'lat'), pairs)  26.4 us
    ppermute x3, starting transfers between devices, body(): arrived = lax.ppermute(forcing[shift - 1], 'grp', pairs)  15 us
    ppermute x2, starting transfers between devices, shifted(): return lax.ppermute(piece, 'lon', pairs)  12.7 us
    ppermute x3, waiting for transfers between devices, body(): returned.append(lax.ppermute(heating, 'grp', pairs))  9.74 us
    mul x4, other arithmetic, advect_tracers(): wet_mask * (center_of(tracer_pad) - 0.25 * (zonal * grad_x(tracer_pad) +...  7.97 us
    ppermute x2, waiting for transfers between devices, shifted(): return lax.ppermute(piece, 'lat', pairs)  7.39 us
    ppermute x2, starting transfers between devices, shifted(): return lax.ppermute(piece, 'lat', pairs)  5.84 us
    ppermute x3, starting transfers between devices, body(): returned.append(lax.ppermute(heating, 'grp', pairs))  3.87 us
  transfers between devices with their start and end apart: 14, of which 5 were waited for; matrix products, arithmetic and copies ran while one was open for 6% of the time, Pallas kernels for 0%

profile of v4, /device:TPU:6, one launch (start us, length us, event | category | flops | bytes accessed | tf_op | source)
XLA Modules:
  0.0 107.9 jit_solution(2949721683907842400)
XLA Ops:
  0.0 0.8 convert_bitcast_fusion
  0.8 1.9 %fusion.15 = (f32[41,7,7]{2,1,0:T(8,128)S(1)}, f32[41,7,7]{2,1,0:T(8,128)S(1)}, f32[41,7,7]{2,1,0:T(8,128)S(1)}, f32[41,7,7]{2,1,0:T(8,128)}) fusion(f32[40,24,128]{2,1,0:T(8,128)} %bitcast.69, f32[1,24,128]{2,1,0:T(8,128)S(1)} %convert_bitcast_fusion), kind=kLoop, calls=%fused_computation.60 | loop fusion | flops 8036 | bytes 535952 | tf_op jit(solution)/shard_map/concatenate | solution.py:137
  2.7 3.4 %collective-permute-start = (f32[41,7,7]{2,1,0:T(8,128)S(1)}, f32[41,7,7]{2,1,0:T(8,128)S(1)}, u32[]{:S(2)}, u32[]{:S(2)}) collective-permute-start(f32[41,7,7]{2,1,0:T(8,128)S(1)} %get-tuple-element.27), channel_id=1, source_target_pairs={{0,5},{1,6},{2,7},{3,4},{4,9},{5,10},{6,11},{7,8},{8,13},{9,14},{1... | collective-permute-start | bytes 24116 | tf_op jit(solution)/shard_map/ppermute | solution.py:27
  6.1 4.5 %collective-permute-start.2 = (f32[41,7,7]{2,1,0:T(8,128)S(1)}, f32[41,7,7]{2,1,0:T(8,128)S(1)}, u32[]{:S(2)}, u32[]{:S(2)}) collective-permute-start(f32[41,7,7]{2,1,0:T(8,128)S(1)} %get-tuple-element.28), channel_id=1, source_target_pairs={{0,7},{1,4},{2,5},{3,6},{4,11},{5,8},{6,9},{7,10},{8,15},{9,12},{1... | collective-permute-start | bytes 24116 | tf_op jit(solution)/shard_map/ppermute | solution.py:27
  10.6 11.5 %collective-permute-start.5 = (f32[41,7,7]{2,1,0:T(8,128)S(1)}, f32[41,7,7]{2,1,0:T(8,128)S(1)}, u32[]{:S(2)}, u32[]{:S(2)}) collective-permute-start(f32[41,7,7]{2,1,0:T(8,128)S(1)} %get-tuple-element.29), channel_id=1, source_target_pairs={{0,189},{1,190},{2,191},{3,188},{4,1},{5,2},{6,3},{7,0},{8,5},{9,6... | collective-permute-start | bytes 24116 | tf_op jit(solution)/shard_map/ppermute | solution.py:27
  22.1 0.7 fusion.16
  22.9 1.9 %collective-permute-start.1 = (f32[41,7,128]{2,1,0:T(8,128)}, f32[41,7,128]{2,1,0:T(8,128)S(1)}, u32[]{:S(2)}, u32[]{:S(2)}) collective-permute-start(f32[41,7,128]{2,1,0:T(8,128)} %get-tuple-element.31), channel_id=1, source_target_pairs={{0,4},{4,8},{8,12},{12,16},{16,20},{20,24},{24,28},{28,32},{32,36}... | collective-permute-start | bytes 440840 | tf_op jit(solution)/shard_map/ppermute | solution.py:18
  24.8 10.8 %collective-permute-start.6 = (f32[41,7,128]{2,1,0:T(8,128)}, f32[41,7,128]{2,1,0:T(8,128)S(1)}, u32[]{:S(2)}, u32[]{:S(2)}) collective-permute-start(f32[41,7,128]{2,1,0:T(8,128)} %get-tuple-element.32), channel_id=1, source_target_pairs={{0,188},{4,0},{8,4},{12,8},{16,12},{20,16},{24,20},{28,24},{32,28}... | collective-permute-start | bytes 440840 | tf_op jit(solution)/shard_map/ppermute | solution.py:18
  35.6 0.2 fusion.4
  35.8 0.5 iota_convert_fusion
  36.4 0.6 add_convert_fusion
  37.0 0.5 multiply_exponential_fusion
  37.5 7.0 %collective-permute-start.7 = (f32[41,7,7]{2,1,0:T(8,128)}, f32[41,7,7]{2,1,0:T(8,128)S(1)}, u32[]{:S(2)}, u32[]{:S(2)}) collective-permute-start(f32[41,7,7]{2,1,0:T(8,128)} %get-tuple-element.30), channel_id=1, source_target_pairs={{0,191},{1,188},{2,189},{3,190},{4,3},{5,0},{6,1},{7,2},{8,7},{9,4... | collective-permute-start | bytes 24116 | tf_op jit(solution)/shard_map/ppermute | solution.py:27
  44.5 2.5 %collective-permute-start.3 = (f32[41,24,7]{2,1,0:T(8,128)S(1)}, f32[41,24,7]{2,1,0:T(8,128)S(1)}, u32[]{:S(2)}, u32[]{:S(2)}) collective-permute-start(f32[41,24,7]{2,1,0:T(8,128)S(1)} %get-tuple-element.33), channel_id=1, source_target_pairs={{0,1},{1,2},{2,3},{3,0},{4,5},{5,6},{6,7},{7,4},{8,9},{9,10},{10,1... | collective-permute-start | bytes 82664 | tf_op jit(solution)/shard_map/ppermute | solution.py:21
  47.0 3.4 %collective-permute-start.4 = (f32[41,24,7]{2,1,0:T(8,128)S(1)}, f32[41,24,7]{2,1,0:T(8,128)S(1)}, u32[]{:S(2)}, u32[]{:S(2)}) collective-permute-start(f32[41,24,7]{2,1,0:T(8,128)S(1)} %get-tuple-element.34), channel_id=1, source_target_pairs={{0,3},{1,0},{2,1},{3,2},{4,7},{5,4},{6,5},{7,6},{8,11},{9,8},{10,9... | collective-permute-start | bytes 82664 | tf_op jit(solution)/shard_map/ppermute | solution.py:21
  50.4 0.6 and_or_fusion
  51.1 0.7 slice.489
  51.8 3.5 %collective-permute-done.3 = f32[41,24,7]{2,1,0:T(8,128)S(1)} collective-permute-done((f32[41,24,7]{2,1,0:T(8,128)S(1)}, f32[41,24,7]{2,1,0:T(8,128)S(1)}, u32[]{:S(2)}, u32[]{:S(2)}) %collective-permute-start.3) | collective-permute-done | bytes 27584 | tf_op jit(solution)/shard_map/ppermute | solution.py:21
  55.4 3.9 %collective-permute-done.4 = f32[41,24,7]{2,1,0:T(8,128)S(1)} collective-permute-done((f32[41,24,7]{2,1,0:T(8,128)S(1)}, f32[41,24,7]{2,1,0:T(8,128)S(1)}, u32[]{:S(2)}, u32[]{:S(2)}) %collective-permute-start.4) | collective-permute-done | bytes 27584 | tf_op jit(solution)/shard_map/ppermute | solution.py:21
  59.2 1.7 %maximum_select_fusion = f32[41,38,142]{2,1,0:T(8,128)S(1)} fusion(f32[41,7,7]{2,1,0:T(8,128)S(1)} %collective-permute-done.7, f32[41,7,128]{2,1,0:T(8,128)S(1)} %collective-permute-done.6, f32[41,7,7]{2,1,0:T(8,128)S(1)} %collective-permute-done.5, f32[41,24,7]{2,1,0:T(8,128)S(1)} %collective-permute-done.4, f32[1,24,128]{2,1,0:T(8,128)S(1)} %convert_bitcast_fusion, ...), kind=kLoop, calls=%fused_computation.7 | loop fusion | flops 2212360 | bytes 1770030 | tf_op jit(solution)/shard_map/jit(_where)/select_n | solution.py:51
  60.9 0.3 fusion.9
  61.2 0.5 slice.676
  61.7 0.1 copy-done.6
  61.8 0.1 compare_convert_fusion
  61.9 0.1 fusion.26
  62.0 0.5 subtract_multiply_fusion.3
  62.6 0.3 fusion.7
  62.8 0.1 fusion.23
  63.0 0.5 subtract_multiply_fusion.1
  63.5 0.2 fusion.13
  63.7 0.1 fusion.31
  63.9 0.1 fusion.40
  64.0 0.2 copy-done.2
  64.2 0.4 subtract_multiply_fusion.7
  64.6 0.4 subtract_multiply_fusion.4
  65.1 0.1 fusion.22
  65.3 1.3 %collective-permute-start.10 = (f32[3,2,30,134]{3,2,1,0:T(8,128)S(1)}, f32[3,2,30,134]{3,2,1,0:T(8,128)S(1)}, u32[]{:S(2)}, u32[]{:S(2)}) collective-permute-start(f32[3,2,30,134]{3,2,1,0:T(8,128)S(1)} %get-tuple-element.24), channel_id=1, source_target_pairs={{0,192},{1,193},{2,194},{3,195},{4,196},{5,197},{6,198},{7,199},{8... | collective-permute-start | bytes 289448 | tf_op jit(solution)/shard_map/ppermute | solution.py:179
  66.6 9.7 %collective-permute-start.8 = (f32[3,2,30,134]{3,2,1,0:T(8,128)S(1)}, f32[3,2,30,134]{3,2,1,0:T(8,128)S(1)}, u32[]{:S(2)}, u32[]{:S(2)}) collective-permute-start(f32[3,2,30,134]{3,2,1,0:T(8,128)S(1)} %get-tuple-element.25), channel_id=1, source_target_pairs={{0,576},{1,577},{2,578},{3,579},{4,580},{5,581},{6,582},{7,583},{8... | collective-permute-start | bytes 289448 | tf_op jit(solution)/shard_map/ppermute | solution.py:179
  76.3 4.0 %collective-permute-start.9 = (f32[3,2,30,134]{3,2,1,0:T(8,128)S(1)}, f32[3,2,30,134]{3,2,1,0:T(8,128)S(1)}, u32[]{:S(2)}, u32[]{:S(2)}) collective-permute-start(f32[3,2,30,134]{3,2,1,0:T(8,128)S(1)} %get-tuple-element.26), channel_id=1, source_target_pairs={{0,384},{1,385},{2,386},{3,387},{4,388},{5,389},{6,390},{7,391},{8... | collective-permute-start | bytes 289448 | tf_op jit(solution)/shard_map/ppermute | solution.py:179
  80.3 1.5 %fusion.39 = (f32[20,2,30,134]{3,2,1,0:T(8,128)S(1)}, f32[20,2,30,134]{3,2,1,0:T(8,128)S(1)}, f32[20,2,30,134]{3,2,1,0:T(8,128)S(1)}, f32[20,2,30,134]{3,2,1,0:T(8,128)S(1)}, f32[20,2,30,134]{3,2,1,0:T(8,128)S(1)}) fusion(f32[20,2,32,136]{3,2,1,0:T(8,128)S(1)} %bitcast.68), kind=kLoop, calls=%fused_computation.119 | loop fusion | bytes 6432000 | tf_op jit(solution)/shard_map/slice | solution.py:66
  81.8 0.1 fusion.21
  82.0 0.1 slice.675
  82.1 0.1 slice.674
  82.2 0.1 slice.673
  82.3 0.9 collective-permute-done.9
  83.3 0.1 slice.688
  83.4 0.1 slice.695
  83.5 0.1 slice.691
  83.6 0.1 slice.698
  83.8 4.4 %add_multiply_fusion = f32[20,2,30,134]{3,0,2,1:T(8,128)S(1)} fusion(f32[20,2,30,134]{3,2,1,0:T(8,128)S(1)} %get-tuple-element.13, f32[20,2,30,134]{3,2,1,0:T(8,128)S(1)} %get-tuple-element.14, f32[20,2,30,134]{3,2,1,0:T(8,128)S(1)} %get-tuple-element.11, f32[20,2,30,134]{3,2,1,0:T(8,128)S(1)} %get-tuple-element.12, ...), kind=kLoop, calls=%fused_computation.8 | loop fusion | flops 2412000 | bytes 3955680 | tf_op jit(solution)/shard_map/mul | solution.py:101
  88.2 1.5 %add_multiply_fusion.1 = f32[20,2,28,132]{3,0,2,1:T(8,128)S(1)} fusion(f32[20,2,30,134]{3,0,2,1:T(8,128)S(1)} %add_multiply_fusion, f32[2,28,132]{2,1,0:T(8,128)S(1)} %slice.691, f32[2,28,132]{2,1,0:T(8,128)S(1)} %slice.688, f32[2,28,132]{2,1,0:T(8,128)S(1)} %slice.674), kind=kLoop, calls=%fused_computation.9 | loop fusion | flops 2217600 | bytes 3636864 | tf_op jit(solution)/shard_map/mul | solution.py:101
  89.7 1.4 %add_multiply_fusion.2 = f32[20,2,26,130]{3,0,2,1:T(8,128)S(1)} fusion(f32[20,2,28,132]{3,0,2,1:T(8,128)S(1)} %add_multiply_fusion.1, f32[2,26,130]{2,1,0:T(8,128)S(1)} %slice.698, f32[2,26,130]{2,1,0:T(8,128)S(1)} %slice.695, f32[2,26,130]{2,1,0:T(8,128)S(1)} %slice.673), kind=kLoop, calls=%fused_computation.10 | loop fusion | flops 2028000 | bytes 3325920 | tf_op jit(solution)/shard_map/mul | solution.py:101
  91.1 0.7 add_multiply_fusion.3
  91.9 0.1 fusion.35
  92.0 0.7 fusion.3
  92.8 1.3 %collective-permute-start.11 = (f32[2,24,128]{2,1,0:T(8,128)S(1)}, f32[2,24,128]{2,1,0:T(8,128)S(1)}, u32[]{:S(2)}, u32[]{:S(2)}) collective-permute-start(f32[2,24,128]{2,1,0:T(8,128)S(1)} %multiply_multiply_fusion), channel_id=1, source_target_pairs={{192,0},{193,1},{194,2},{195,3},{196,4},{197,5},{198,6},{199,7},{2... | collective-permute-start | bytes 73736 | tf_op jit(solution)/shard_map/ppermute | solution.py:207
  94.1 1.3 %collective-permute-start.12 = (f32[2,24,128]{2,1,0:T(8,128)S(1)}, f32[2,24,128]{2,1,0:T(8,128)S(1)}, u32[]{:S(2)}, u32[]{:S(2)}) collective-permute-start(f32[2,24,128]{2,1,0:T(8,128)S(1)} %multiply_multiply_fusion), channel_id=1, source_target_pairs={{384,0},{385,1},{386,2},{387,3},{388,4},{389,5},{390,6},{391,7},{3... | collective-permute-start | bytes 73736 | tf_op jit(solution)/shard_map/ppermute | solution.py:207
  95.4 1.3 %collective-permute-start.13 = (f32[2,24,128]{2,1,0:T(8,128)S(1)}, f32[2,24,128]{2,1,0:T(8,128)S(1)}, u32[]{:S(2)}, u32[]{:S(2)}) collective-permute-start(f32[2,24,128]{2,1,0:T(8,128)S(1)} %multiply_multiply_fusion), channel_id=1, source_target_pairs={{576,0},{577,1},{578,2},{579,3},{580,4},{581,5},{582,6},{583,7},{5... | collective-permute-start | bytes 73736 | tf_op jit(solution)/shard_map/ppermute | solution.py:207
  96.7 0.2 fusion.11
  97.0 0.1 copy.19
  97.2 9.0 %collective-permute-done.12 = f32[2,24,128]{2,1,0:T(8,128)S(1)} collective-permute-done((f32[2,24,128]{2,1,0:T(8,128)S(1)}, f32[2,24,128]{2,1,0:T(8,128)S(1)}, u32[]{:S(2)}, u32[]{:S(2)}) %collective-permute-start.12) | collective-permute-done | bytes 24608 | tf_op jit(solution)/shard_map/ppermute | solution.py:207
  106.2 0.7 collective-permute-done.13
  106.9 0.1 fusion.20
  107.1 0.8 bitcast_select_fusion
  (41 shorter events, 1.1 us)
Async XLA Ops:
  0.0 92.0 %copy-start = (f32[20,20]{1,0:T(8,128)S(1)}, f32[20,20]{1,0:T(8,128)}, u32[]{:S(2)}) copy-start(f32[20,20]{1,0:T(8,128)} %param.6) | copy-start | bytes 4804
  0.0 22.1 %copy-start.1 = (f32[1,40,24,128]{3,2,1,0:T(8,128)S(1)}, f32[1,40,24,128]{3,2,1,0:T(8,128)}, u32[]{:S(2)}) copy-start(f32[1,40,24,128]{3,2,1,0:T(8,128)} %param.4) | copy-start | bytes 1474564
  2.7 34.8 %collective-permute-start = (f32[41,7,7]{2,1,0:T(8,128)S(1)}, f32[41,7,7]{2,1,0:T(8,128)S(1)}, u32[]{:S(2)}, u32[]{:S(2)}) collective-permute-start(f32[41,7,7]{2,1,0:T(8,128)S(1)} %get-tuple-element.27), channel_id=1, source_target_pairs={{0,5},{1,6},{2,7},{3,4},{4,9},{5,10},{6,11},{7,8},{8,13},{9,14},{1... | collective-permute-start | bytes 24116 | tf_op jit(solution)/shard_map/ppermute | solution.py:27
  6.1 38.4 %collective-permute-start.2 = (f32[41,7,7]{2,1,0:T(8,128)S(1)}, f32[41,7,7]{2,1,0:T(8,128)S(1)}, u32[]{:S(2)}, u32[]{:S(2)}) collective-permute-start(f32[41,7,7]{2,1,0:T(8,128)S(1)} %get-tuple-element.28), channel_id=1, source_target_pairs={{0,7},{1,4},{2,5},{3,6},{4,11},{5,8},{6,9},{7,10},{8,15},{9,12},{1... | collective-permute-start | bytes 24116 | tf_op jit(solution)/shard_map/ppermute | solution.py:27
  10.6 36.4 %collective-permute-start.5 = (f32[41,7,7]{2,1,0:T(8,128)S(1)}, f32[41,7,7]{2,1,0:T(8,128)S(1)}, u32[]{:S(2)}, u32[]{:S(2)}) collective-permute-start(f32[41,7,7]{2,1,0:T(8,128)S(1)} %get-tuple-element.29), channel_id=1, source_target_pairs={{0,189},{1,190},{2,191},{3,188},{4,1},{5,2},{6,3},{7,0},{8,5},{9,6... | collective-permute-start | bytes 24116 | tf_op jit(solution)/shard_map/ppermute | solution.py:27
  22.9 36.4 %collective-permute-start.1 = (f32[41,7,128]{2,1,0:T(8,128)}, f32[41,7,128]{2,1,0:T(8,128)S(1)}, u32[]{:S(2)}, u32[]{:S(2)}) collective-permute-start(f32[41,7,128]{2,1,0:T(8,128)} %get-tuple-element.31), channel_id=1, source_target_pairs={{0,4},{4,8},{8,12},{12,16},{16,20},{20,24},{24,28},{28,32},{32,36}... | collective-permute-start | bytes 440840 | tf_op jit(solution)/shard_map/ppermute | solution.py:18
  24.8 34.5 %collective-permute-start.6 = (f32[41,7,128]{2,1,0:T(8,128)}, f32[41,7,128]{2,1,0:T(8,128)S(1)}, u32[]{:S(2)}, u32[]{:S(2)}) collective-permute-start(f32[41,7,128]{2,1,0:T(8,128)} %get-tuple-element.32), channel_id=1, source_target_pairs={{0,188},{4,0},{8,4},{12,8},{16,12},{20,16},{24,20},{28,24},{32,28}... | collective-permute-start | bytes 440840 | tf_op jit(solution)/shard_map/ppermute | solution.py:18
  37.5 14.3 %collective-permute-start.7 = (f32[41,7,7]{2,1,0:T(8,128)}, f32[41,7,7]{2,1,0:T(8,128)S(1)}, u32[]{:S(2)}, u32[]{:S(2)}) collective-permute-start(f32[41,7,7]{2,1,0:T(8,128)} %get-tuple-element.30), channel_id=1, source_target_pairs={{0,191},{1,188},{2,189},{3,190},{4,3},{5,0},{6,1},{7,2},{8,7},{9,4... | collective-permute-start | bytes 24116 | tf_op jit(solution)/shard_map/ppermute | solution.py:27
  44.5 10.9 %collective-permute-start.3 = (f32[41,24,7]{2,1,0:T(8,128)S(1)}, f32[41,24,7]{2,1,0:T(8,128)S(1)}, u32[]{:S(2)}, u32[]{:S(2)}) collective-permute-start(f32[41,24,7]{2,1,0:T(8,128)S(1)} %get-tuple-element.33), channel_id=1, source_target_pairs={{0,1},{1,2},{2,3},{3,0},{4,5},{5,6},{6,7},{7,4},{8,9},{9,10},{10,1... | collective-permute-start | bytes 82664 | tf_op jit(solution)/shard_map/ppermute | solution.py:21
  47.0 12.2 %collective-permute-start.4 = (f32[41,24,7]{2,1,0:T(8,128)S(1)}, f32[41,24,7]{2,1,0:T(8,128)S(1)}, u32[]{:S(2)}, u32[]{:S(2)}) collective-permute-start(f32[41,24,7]{2,1,0:T(8,128)S(1)} %get-tuple-element.34), channel_id=1, source_target_pairs={{0,3},{1,0},{2,1},{3,2},{4,7},{5,4},{6,5},{7,6},{8,11},{9,8},{10,9... | collective-permute-start | bytes 82664 | tf_op jit(solution)/shard_map/ppermute | solution.py:21
  61.2 0.6 copy-start.6
  63.5 0.7 copy-start.2
  65.3 17.1 %collective-permute-start.10 = (f32[3,2,30,134]{3,2,1,0:T(8,128)S(1)}, f32[3,2,30,134]{3,2,1,0:T(8,128)S(1)}, u32[]{:S(2)}, u32[]{:S(2)}) collective-permute-start(f32[3,2,30,134]{3,2,1,0:T(8,128)S(1)} %get-tuple-element.24), channel_id=1, source_target_pairs={{0,192},{1,193},{2,194},{3,195},{4,196},{5,197},{6,198},{7,199},{8... | collective-permute-start | bytes 289448 | tf_op jit(solution)/shard_map/ppermute | solution.py:179
  66.6 15.8 %collective-permute-start.8 = (f32[3,2,30,134]{3,2,1,0:T(8,128)S(1)}, f32[3,2,30,134]{3,2,1,0:T(8,128)S(1)}, u32[]{:S(2)}, u32[]{:S(2)}) collective-permute-start(f32[3,2,30,134]{3,2,1,0:T(8,128)S(1)} %get-tuple-element.25), channel_id=1, source_target_pairs={{0,576},{1,577},{2,578},{3,579},{4,580},{5,581},{6,582},{7,583},{8... | collective-permute-start | bytes 289448 | tf_op jit(solution)/shard_map/ppermute | solution.py:179
  76.3 6.9 %collective-permute-start.9 = (f32[3,2,30,134]{3,2,1,0:T(8,128)S(1)}, f32[3,2,30,134]{3,2,1,0:T(8,128)S(1)}, u32[]{:S(2)}, u32[]{:S(2)}) collective-permute-start(f32[3,2,30,134]{3,2,1,0:T(8,128)S(1)} %get-tuple-element.26), channel_id=1, source_target_pairs={{0,384},{1,385},{2,386},{3,387},{4,388},{5,389},{6,390},{7,391},{8... | collective-permute-start | bytes 289448 | tf_op jit(solution)/shard_map/ppermute | solution.py:179
  80.3 1.6 %copy-start.5 = (f32[2]{0:T(128)S(1)}, f32[2]{0:T(128)}, u32[]{:S(2)}) copy-start(f32[2]{0:T(128)} %add_convert_fusion) | copy-start | bytes 28
  91.1 0.9 copy-start.3
  91.8 0.9 copy-start.4
  92.8 4.3 %collective-permute-start.11 = (f32[2,24,128]{2,1,0:T(8,128)S(1)}, f32[2,24,128]{2,1,0:T(8,128)S(1)}, u32[]{:S(2)}, u32[]{:S(2)}) collective-permute-start(f32[2,24,128]{2,1,0:T(8,128)S(1)} %multiply_multiply_fusion), channel_id=1, source_target_pairs={{192,0},{193,1},{194,2},{195,3},{196,4},{197,5},{198,6},{199,7},{2... | collective-permute-start | bytes 73736 | tf_op jit(solution)/shard_map/ppermute | solution.py:207
  94.1 12.0 %collective-permute-start.12 = (f32[2,24,128]{2,1,0:T(8,128)S(1)}, f32[2,24,128]{2,1,0:T(8,128)S(1)}, u32[]{:S(2)}, u32[]{:S(2)}) collective-permute-start(f32[2,24,128]{2,1,0:T(8,128)S(1)} %multiply_multiply_fusion), channel_id=1, source_target_pairs={{384,0},{385,1},{386,2},{387,3},{388,4},{389,5},{390,6},{391,7},{3... | collective-permute-start | bytes 73736 | tf_op jit(solution)/shard_map/ppermute | solution.py:207
  95.4 11.5 %collective-permute-start.13 = (f32[2,24,128]{2,1,0:T(8,128)S(1)}, f32[2,24,128]{2,1,0:T(8,128)S(1)}, u32[]{:S(2)}, u32[]{:S(2)}) collective-permute-start(f32[2,24,128]{2,1,0:T(8,128)S(1)} %multiply_multiply_fusion), channel_id=1, source_target_pairs={{576,0},{577,1},{578,2},{579,3},{580,4},{581,5},{582,6},{583,7},{5... | collective-permute-start | bytes 73736 | tf_op jit(solution)/shard_map/ppermute | solution.py:207

commit v5 on v3

--- a/solution.py
+++ b/solution.py
@@ -171,8 +171,9 @@
             crop(wet_member_pad, dyn_halo, radius),
         )
     wet_member = crop(wet_member_pad, dyn_halo, 0)
-    kinetic = jnp.einsum("ts,szxy->tzxy", rates, advected, precision=lax.Precision.HIGHEST)
-    kinetic = kinetic + grazing[:, None, None, None] * (advected[0] * advected[1])[None]
+    kinetic = grazing[:, None, None, None] * (advected[0] * advected[1])[None]
+    for source in range(NTR):
+        kinetic = kinetic + rates[:, source, None, None, None] * advected[source][None]
     updated = wet_member[None] * (advected + 0.2 * jnp.exp(0.05 * own_temper)[None] * kinetic)
     light_factor = jnp.exp(-(member_levels + 0.5) / total_levels)
     heating = 0.3 * wet_member * updated[0] * light_factor

time: 83.5 us -> 80.1 us (0.959)
  other arithmetic: 16.7 us -> 14.3 us
  waiting for transfers between devices: 25.7 us -> 24 us
  local copies, waits for them, and re-layouts: 5.59 us -> 6.83 us
    mul x4, other arithmetic: 7.97 us -> 4.93 us  [advect_tracers(): wet_mask * (center_of(tracer_pad) - 0.25 * (zonal * grad_x(tracer_pad) +...]
    mul x1 -> x2, other arithmetic: 0.02 us -> 1.76 us  [the longest x1 1.72 us: body(): wet_member[None]]
    ppermute x2, waiting for transfers between devices: 1.87 us -> 0.41 us  [exchange(): lax.ppermute(lax.slice_in_dim(block, block.shape[dim] - width, None, axis...]
    ppermute x2, waiting for transfers between devices: 7.51 us -> 6.12 us  [exchange(): lax.ppermute(lax.slice_in_dim(block, 0, width, axis=dim), axis, backward)]
    slice x2, local copies, waits for them, and re-layouts: 1.51 us -> 2.85 us  [body(): rates[:, source, None, None, None] * advected[source][None]]
    ppermute x3, waiting for transfers between devices: 6.58 us -> 7.65 us  [body(): arrived = lax.ppermute(forcing[shift - 1], 'grp', pairs)]
    concatenate x1, other arithmetic: 1.14 us -> 0.1 us  [exchange(): block = jnp.concatenate([low, block, high], axis=dim)]
  transfers between devices with their start and end apart: 10 -> 10, of which waited for: 8 -> 7; matrix products, arithmetic and copies ran while one was open for 4% -> 7% of each run, Pallas kernels for 0% -> 0%
where the time goes in v5:
time: 80.1 us; the launch traced here: 79.6 us
  starting transfers between devices  33.9 us (42%)
  waiting for transfers between devices  24 us (30%)
  other arithmetic  14.3 us (18%)
  local copies, waits for them, and re-layouts  6.83 us (9%)
    ppermute x3, starting transfers between devices, body(): arrived = lax.ppermute(forcing[shift - 1], 'grp', pairs)  16.4 us
    ppermute x3, waiting for transfers between devices, body(): returned.append(lax.ppermute(heating, 'grp', pairs))  9.85 us
    ppermute x2, starting transfers between devices, exchange(): lax.ppermute(lax.slice_in_dim(block, block.shape[dim] - width, None, axis...  8.1 us
    ppermute x3, waiting for transfers between devices, body(): arrived = lax.ppermute(forcing[shift - 1], 'grp', pairs)  7.65 us
    ppermute x2, waiting for transfers between devices, exchange(): lax.ppermute(lax.slice_in_dim(block, 0, width, axis=dim), axis, backward)  6.12 us
    ppermute x2, starting transfers between devices, exchange(): lax.ppermute(lax.slice_in_dim(block, 0, width, axis=dim), axis, backward)  5.58 us
    mul x4, other arithmetic, advect_tracers(): wet_mask * (center_of(tracer_pad) - 0.25 * (zonal * grad_x(tracer_pad) +...  4.93 us
    ppermute x3, starting transfers between devices, body(): returned.append(lax.ppermute(heating, 'grp', pairs))  3.87 us
  transfers between devices with their start and end apart: 10, of which 7 were waited for; matrix products, arithmetic and copies ran while one was open for 7% of the time, Pallas kernels for 0%

profile of v5, /device:TPU:88, one launch (start us, length us, event | category | flops | bytes accessed | tf_op | source)
XLA Modules:
  0.0 79.6 jit_solution(11761582816004577867)
XLA Ops:
  0.0 0.8 convert_bitcast_fusion
  0.8 1.0 %pad_maximum_fusion.3 = (f32[41,7,128]{2,1,0:T(8,128)S(1)}, f32[41,7,128]{2,1,0:T(8,128)S(1)}) fusion(f32[1,24,128]{2,1,0:T(8,128)S(1)} %convert_bitcast_fusion, f32[40,24,128]{2,1,0:T(8,128)} %bitcast.97), kind=kLoop, calls=%fused_computation.43 | loop fusion | flops 73472 | bytes 797696 | tf_op jit(solution)/shard_map/slice | solution.py:18
  1.8 4.7 %collective-permute-start = (f32[41,7,128]{2,1,0:T(8,128)S(1)}, f32[41,7,128]{2,1,0:T(8,128)S(1)}, u32[]{:S(2)}, u32[]{:S(2)}) collective-permute-start(f32[41,7,128]{2,1,0:T(8,128)S(1)} %get-tuple-element.43), channel_id=1, source_target_pairs={{0,4},{4,8},{8,12},{12,16},{16,20},{20,24},{24,28},{28,32},{32,36}... | collective-permute-start | bytes 440840 | tf_op jit(solution)/shard_map/ppermute | solution.py:17
  6.5 1.9 %collective-permute-start.1 = (f32[41,7,128]{2,1,0:T(8,128)S(1)}, f32[41,7,128]{2,1,0:T(8,128)S(1)}, u32[]{:S(2)}, u32[]{:S(2)}) collective-permute-start(f32[41,7,128]{2,1,0:T(8,128)S(1)} %get-tuple-element.44), channel_id=1, source_target_pairs={{4,0},{8,4},{12,8},{16,12},{20,16},{24,20},{28,24},{32,28},{36,32}... | collective-permute-start | bytes 440840 | tf_op jit(solution)/shard_map/ppermute | solution.py:20
  8.5 0.9 %slice_reduce_fusion.1 = f32[20]{0:T(128)S(1)} fusion(f32[20,20]{1,0:T(8,128)} %param.6), kind=kLoop, calls=%fused_computation.114 | loop fusion | bytes 160 | tf_op jit(solution)/shard_map/slice | solution.py:176
  9.4 2.0 %slice_reduce_fusion.19 = (f32[20]{0:T(128)S(1)}, f32[20]{0:T(128)S(1)}, f32[20]{0:T(128)S(1)}, f32[20]{0:T(128)S(1)}, f32[20]{0:T(128)S(1)}, /*index=5*/f32[20]...) fusion(f32[20,20]{1,0:T(8,128)} %param.6), kind=kLoop, calls=%fused_computation.132 | loop fusion | bytes 3040 | tf_op jit(solution)/shard_map/slice | solution.py:176
  11.4 4.0 %collective-permute-done.1 = f32[41,7,128]{2,1,0:T(8,128)S(1)} collective-permute-done((f32[41,7,128]{2,1,0:T(8,128)S(1)}, f32[41,7,128]{2,1,0:T(8,128)S(1)}, u32[]{:S(2)}, u32[]{:S(2)}) %collective-permute-start.1) | collective-permute-done | bytes 146976 | tf_op jit(solution)/shard_map/ppermute | solution.py:20
  15.3 0.1 pad_maximum_fusion
  15.5 0.3 fusion.29
  15.7 0.4 copy.23
  16.2 3.4 %collective-permute-start.2 = (f32[41,38,7]{0,1,2:T(8,128)S(1)}, f32[41,38,7]{0,1,2:T(8,128)S(1)}, u32[]{:S(2)}, u32[]{:S(2)}) collective-permute-start(f32[41,38,7]{0,1,2:T(8,128)S(1)} %copy.23), channel_id=1, source_target_pairs={{0,1},{1,2},{2,3},{3,0},{4,5},{5,6},{6,7},{7,4},{8,9},{9,10},{10,1... | collective-permute-start | bytes 130880 | tf_op jit(solution)/shard_map/ppermute | solution.py:17
  19.6 0.4 copy.24
  20.0 3.7 %collective-permute-start.3 = (f32[41,38,7]{0,1,2:T(8,128)S(1)}, f32[41,38,7]{0,1,2:T(8,128)S(1)}, u32[]{:S(2)}, u32[]{:S(2)}) collective-permute-start(f32[41,38,7]{0,1,2:T(8,128)S(1)} %copy.24), channel_id=1, source_target_pairs={{1,0},{2,1},{3,2},{0,3},{5,4},{6,5},{7,6},{4,7},{9,8},{10,9},{11,1... | collective-permute-start | bytes 130880 | tf_op jit(solution)/shard_map/ppermute | solution.py:20
  24.0 0.4 collective-permute-done.2
  24.4 0.5 copy.25
  24.8 2.2 %collective-permute-done.3 = f32[41,38,7]{0,1,2:T(8,128)S(1)} collective-permute-done((f32[41,38,7]{0,1,2:T(8,128)S(1)}, f32[41,38,7]{0,1,2:T(8,128)S(1)}, u32[]{:S(2)}, u32[]{:S(2)}) %collective-permute-start.3) | collective-permute-done | bytes 43656 | tf_op jit(solution)/shard_map/ppermute | solution.py:20
  27.0 0.5 copy.26
  27.5 0.9 %maximum_select_fusion = f32[41,38,142]{2,1,0:T(8,128)S(1)} fusion(f32[41,38,7]{2,1,0:T(8,128)S(1)} %copy.26, f32[41,7,128]{2,1,0:T(8,128)S(1)} %collective-permute-done.1, f32[1,24,128]{2,1,0:T(8,128)S(1)} %convert_bitcast_fusion, f32[40,24,128]{2,1,0:T(8,128)S(1)} %bitcast.99, f32[41,7,128]{2,1,0:T(8,128)S(1)} %collective-permute-done, ...), kind=kLoop, calls=%fused_computation | loop fusion | flops 1327416 | bytes 1770030 | tf_op jit(solution)/shard_map/jit(_where)/select_n | solution.py:26
  28.4 0.3 fusion.3
  28.7 0.1 compare_convert_fusion
  28.8 0.1 fusion.15
  28.9 0.5 subtract_multiply_fusion.3
  29.4 0.3 fusion.1
  29.7 0.1 fusion.12
  29.8 0.5 subtract_multiply_fusion.1
  30.4 0.2 fusion.7
  30.6 0.1 fusion.20
  30.7 0.1 fusion.30
  30.8 0.4 subtract_multiply_fusion.7
  31.3 0.4 subtract_multiply_fusion.4
  31.7 0.1 fusion.11
  31.9 11.3 %collective-permute-start.4 = (f32[3,2,30,134]{3,2,1,0:T(8,128)S(1)}, f32[3,2,30,134]{3,2,1,0:T(8,128)S(1)}, u32[]{:S(2)}, u32[]{:S(2)}) collective-permute-start(f32[3,2,30,134]{3,2,1,0:T(8,128)S(1)} %get-tuple-element.42), channel_id=1, source_target_pairs={{0,576},{1,577},{2,578},{3,579},{4,580},{5,581},{6,582},{7,583},{8... | collective-permute-start | bytes 289448 | tf_op jit(solution)/shard_map/ppermute | solution.py:154
  43.3 3.6 %collective-permute-start.5 = (f32[3,2,30,134]{3,2,1,0:T(8,128)S(1)}, f32[3,2,30,134]{3,2,1,0:T(8,128)S(1)}, u32[]{:S(2)}, u32[]{:S(2)}) collective-permute-start(f32[3,2,30,134]{3,2,1,0:T(8,128)S(1)} %get-tuple-element.41), channel_id=1, source_target_pairs={{0,384},{1,385},{2,386},{3,387},{4,388},{5,389},{6,390},{7,391},{8... | collective-permute-start | bytes 289448 | tf_op jit(solution)/shard_map/ppermute | solution.py:154
  46.8 1.5 %collective-permute-start.6 = (f32[3,2,30,134]{3,2,1,0:T(8,128)S(1)}, f32[3,2,30,134]{3,2,1,0:T(8,128)S(1)}, u32[]{:S(2)}, u32[]{:S(2)}) collective-permute-start(f32[3,2,30,134]{3,2,1,0:T(8,128)S(1)} %get-tuple-element.40), channel_id=1, source_target_pairs={{0,192},{1,193},{2,194},{3,195},{4,196},{5,197},{6,198},{7,199},{8... | collective-permute-start | bytes 289448 | tf_op jit(solution)/shard_map/ppermute | solution.py:154
  48.3 0.1 fusion.10
  48.4 0.1 compare_convert_fusion.1
  48.5 0.5 slice.802
  49.0 0.1 slice.801
  49.1 0.1 slice.800
  49.1 0.1 slice.799
  49.2 0.1 slice.798
  49.3 5.6 %collective-permute-done.4 = f32[3,2,30,134]{3,2,1,0:T(8,128)S(1)} collective-permute-done((f32[3,2,30,134]{3,2,1,0:T(8,128)S(1)}, f32[3,2,30,134]{3,2,1,0:T(8,128)S(1)}, u32[]{:S(2)}, u32[]{:S(2)}) %collective-permute-start.4) | collective-permute-done | bytes 96512 | tf_op jit(solution)/shard_map/ppermute | solution.py:154
  54.9 2.1 %collective-permute-done.5 = f32[3,2,30,134]{3,2,1,0:T(8,128)S(1)} collective-permute-done((f32[3,2,30,134]{3,2,1,0:T(8,128)S(1)}, f32[3,2,30,134]{3,2,1,0:T(8,128)S(1)}, u32[]{:S(2)}, u32[]{:S(2)}) %collective-permute-start.5) | collective-permute-done | bytes 96512 | tf_op jit(solution)/shard_map/ppermute | solution.py:154
  57.0 0.1 slice.814
  57.1 0.1 slice.821
  57.2 0.1 slice.817
  57.3 0.1 slice.824
  57.5 1.4 %add_multiply_fusion.2 = f32[20,2,30,134]{3,2,1,0:T(8,128)S(1)} fusion(f32[20,2,32,136]{3,2,1,0:T(8,128)S(1)} %bitcast.96, f32[2,30,134]{2,1,0:T(8,128)S(1)} %get-tuple-element.67, f32[2,30,134]{2,1,0:T(8,128)S(1)} %get-tuple-element.68, f32[2,30,134]{2,1,0:T(8,128)S(1)} %slice.801), kind=kLoop, calls=%fused_computation.3 | loop fusion | flops 2412000 | bytes 3955680 | tf_op jit(solution)/shard_map/mul | solution.py:76
  59.0 1.5 %add_multiply_fusion.1 = f32[20,2,28,132]{3,2,1,0:T(8,128)S(1)} fusion(f32[20,2,30,134]{3,2,1,0:T(8,128)S(1)} %add_multiply_fusion.2, f32[2,28,132]{2,1,0:T(8,128)S(1)} %slice.817, f32[2,28,132]{2,1,0:T(8,128)S(1)} %slice.814, f32[2,28,132]{2,1,0:T(8,128)S(1)} %slice.800), kind=kLoop, calls=%fused_computation.2 | loop fusion | flops 2217600 | bytes 3636864 | tf_op jit(solution)/shard_map/mul | solution.py:76
  60.5 1.5 %add_multiply_fusion = f32[20,2,26,130]{3,2,1,0:T(8,128)S(1)} fusion(f32[20,2,28,132]{3,2,1,0:T(8,128)S(1)} %add_multiply_fusion.1, f32[2,26,130]{2,1,0:T(8,128)S(1)} %slice.824, f32[2,26,130]{2,1,0:T(8,128)S(1)} %slice.821, f32[2,26,130]{2,1,0:T(8,128)S(1)} %slice.799), kind=kLoop, calls=%fused_computation.1 | loop fusion | flops 2028000 | bytes 3325920 | tf_op jit(solution)/shard_map/mul | solution.py:76
  61.9 0.6 add_multiply_fusion.4
  62.6 0.1 fusion.26
  62.7 1.7 %add_multiply_fusion.3 = f32[20,2,24,128]{3,2,1,0:T(8,128)S(1)} fusion(f32[2,24,128]{2,1,0:T(8,128)S(1)} %get-tuple-element.47, f32[20]{0:T(128)S(1)} %get-tuple-element.23, f32[2,24,128]{2,1,0:T(8,128)S(1)} %get-tuple-element.48, f32[20]{0:T(128)S(1)} %slice_reduce_fusion.1, f32[2,24,128]{2,1,0:T(8,128)S(1)} %get-tuple-element.49, ...), kind=kLoop, calls=%fused_computation.7 | loop fusion | flops 7249920 | bytes 3565200 | tf_op jit(solution)/shard_map/mul | solution.py:177
  64.4 0.1 fusion.24
  64.5 1.3 %collective-permute-start.7 = (f32[2,24,128]{2,1,0:T(8,128)S(1)}, f32[2,24,128]{2,1,0:T(8,128)S(1)}, u32[]{:S(2)}, u32[]{:S(2)}) collective-permute-start(f32[2,24,128]{2,1,0:T(8,128)S(1)} %fusion.24), channel_id=1, source_target_pairs={{192,0},{193,1},{194,2},{195,3},{196,4},{197,5},{198,6},{199,7},{2... | collective-permute-start | bytes 73736 | tf_op jit(solution)/shard_map/ppermute | solution.py:183
  65.8 1.3 %collective-permute-start.8 = (f32[2,24,128]{2,1,0:T(8,128)S(1)}, f32[2,24,128]{2,1,0:T(8,128)S(1)}, u32[]{:S(2)}, u32[]{:S(2)}) collective-permute-start(f32[2,24,128]{2,1,0:T(8,128)S(1)} %fusion.24), channel_id=1, source_target_pairs={{384,0},{385,1},{386,2},{387,3},{388,4},{389,5},{390,6},{391,7},{3... | collective-permute-start | bytes 73736 | tf_op jit(solution)/shard_map/ppermute | solution.py:183
  67.1 1.3 %collective-permute-start.9 = (f32[2,24,128]{2,1,0:T(8,128)S(1)}, f32[2,24,128]{2,1,0:T(8,128)S(1)}, u32[]{:S(2)}, u32[]{:S(2)}) collective-permute-start(f32[2,24,128]{2,1,0:T(8,128)S(1)} %fusion.24), channel_id=1, source_target_pairs={{576,0},{577,1},{578,2},{579,3},{580,4},{581,5},{582,6},{583,7},{5... | collective-permute-start | bytes 73736 | tf_op jit(solution)/shard_map/ppermute | solution.py:183
  68.4 0.2 fusion.5
  68.6 0.1 slice.857
  68.7 9.1 %collective-permute-done.8 = f32[2,24,128]{2,1,0:T(8,128)S(1)} collective-permute-done((f32[2,24,128]{2,1,0:T(8,128)S(1)}, f32[2,24,128]{2,1,0:T(8,128)S(1)}, u32[]{:S(2)}, u32[]{:S(2)}) %collective-permute-start.8) | collective-permute-done | bytes 24608 | tf_op jit(solution)/shard_map/ppermute | solution.py:183
  77.8 0.7 collective-permute-done.9
  78.5 0.1 fusion.9
  78.6 0.1 fusion.28
  78.7 0.8 %bitcast_select_fusion = f32[1,40,24,128]{3,2,1,0:T(8,128)} fusion(f32[1,40,24,128]{3,2,1,0:T(8,128)S(1)} %broadcast_dynamic-update-slice_fusion, pred[]{:T(512)S(6)} %eq.18, f32[1,40,24,128]{3,2,1,0:T(8,128)S(1)} %bitcast.100), kind=kLoop, calls=%fused_computation.6 | loop fusion | flops 122880 | bytes 1474561 | tf_op jit(solution)/shard_map/jit(_where)/select_n | solution.py:188
  (27 shorter events, 0.8 us)
Async XLA Ops:
  0.0 15.3 %copy-start = (f32[1,40,24,128]{3,2,1,0:T(8,128)S(1)}, f32[1,40,24,128]{3,2,1,0:T(8,128)}, u32[]{:S(2)}) copy-start(f32[1,40,24,128]{3,2,1,0:T(8,128)} %param.4) | copy-start | bytes 1474564
  1.8 9.6 %collective-permute-start = (f32[41,7,128]{2,1,0:T(8,128)S(1)}, f32[41,7,128]{2,1,0:T(8,128)S(1)}, u32[]{:S(2)}, u32[]{:S(2)}) collective-permute-start(f32[41,7,128]{2,1,0:T(8,128)S(1)} %get-tuple-element.43), channel_id=1, source_target_pairs={{0,4},{4,8},{8,12},{12,16},{16,20},{20,24},{24,28},{28,32},{32,36}... | collective-permute-start | bytes 440840 | tf_op jit(solution)/shard_map/ppermute | solution.py:17
  6.5 8.9 %collective-permute-start.1 = (f32[41,7,128]{2,1,0:T(8,128)S(1)}, f32[41,7,128]{2,1,0:T(8,128)S(1)}, u32[]{:S(2)}, u32[]{:S(2)}) collective-permute-start(f32[41,7,128]{2,1,0:T(8,128)S(1)} %get-tuple-element.44), channel_id=1, source_target_pairs={{4,0},{8,4},{12,8},{16,12},{20,16},{24,20},{28,24},{32,28},{36,32}... | collective-permute-start | bytes 440840 | tf_op jit(solution)/shard_map/ppermute | solution.py:20
  16.2 8.2 %collective-permute-start.2 = (f32[41,38,7]{0,1,2:T(8,128)S(1)}, f32[41,38,7]{0,1,2:T(8,128)S(1)}, u32[]{:S(2)}, u32[]{:S(2)}) collective-permute-start(f32[41,38,7]{0,1,2:T(8,128)S(1)} %copy.23), channel_id=1, source_target_pairs={{0,1},{1,2},{2,3},{3,0},{4,5},{5,6},{6,7},{7,4},{8,9},{9,10},{10,1... | collective-permute-start | bytes 130880 | tf_op jit(solution)/shard_map/ppermute | solution.py:17
  20.0 7.0 %collective-permute-start.3 = (f32[41,38,7]{0,1,2:T(8,128)S(1)}, f32[41,38,7]{0,1,2:T(8,128)S(1)}, u32[]{:S(2)}, u32[]{:S(2)}) collective-permute-start(f32[41,38,7]{0,1,2:T(8,128)S(1)} %copy.24), channel_id=1, source_target_pairs={{1,0},{2,1},{3,2},{0,3},{5,4},{6,5},{7,6},{4,7},{9,8},{10,9},{11,1... | collective-permute-start | bytes 130880 | tf_op jit(solution)/shard_map/ppermute | solution.py:20
  31.9 23.0 %collective-permute-start.4 = (f32[3,2,30,134]{3,2,1,0:T(8,128)S(1)}, f32[3,2,30,134]{3,2,1,0:T(8,128)S(1)}, u32[]{:S(2)}, u32[]{:S(2)}) collective-permute-start(f32[3,2,30,134]{3,2,1,0:T(8,128)S(1)} %get-tuple-element.42), channel_id=1, source_target_pairs={{0,576},{1,577},{2,578},{3,579},{4,580},{5,581},{6,582},{7,583},{8... | collective-permute-start | bytes 289448 | tf_op jit(solution)/shard_map/ppermute | solution.py:154
  43.3 13.7 %collective-permute-start.5 = (f32[3,2,30,134]{3,2,1,0:T(8,128)S(1)}, f32[3,2,30,134]{3,2,1,0:T(8,128)S(1)}, u32[]{:S(2)}, u32[]{:S(2)}) collective-permute-start(f32[3,2,30,134]{3,2,1,0:T(8,128)S(1)} %get-tuple-element.41), channel_id=1, source_target_pairs={{0,384},{1,385},{2,386},{3,387},{4,388},{5,389},{6,390},{7,391},{8... | collective-permute-start | bytes 289448 | tf_op jit(solution)/shard_map/ppermute | solution.py:154
  46.8 10.1 %collective-permute-start.6 = (f32[3,2,30,134]{3,2,1,0:T(8,128)S(1)}, f32[3,2,30,134]{3,2,1,0:T(8,128)S(1)}, u32[]{:S(2)}, u32[]{:S(2)}) collective-permute-start(f32[3,2,30,134]{3,2,1,0:T(8,128)S(1)} %get-tuple-element.40), channel_id=1, source_target_pairs={{0,192},{1,193},{2,194},{3,195},{4,196},{5,197},{6,198},{7,199},{8... | collective-permute-start | bytes 289448 | tf_op jit(solution)/shard_map/ppermute | solution.py:154
  61.9 0.8 copy-start.1
  64.5 4.2 %collective-permute-start.7 = (f32[2,24,128]{2,1,0:T(8,128)S(1)}, f32[2,24,128]{2,1,0:T(8,128)S(1)}, u32[]{:S(2)}, u32[]{:S(2)}) collective-permute-start(f32[2,24,128]{2,1,0:T(8,128)S(1)} %fusion.24), channel_id=1, source_target_pairs={{192,0},{193,1},{194,2},{195,3},{196,4},{197,5},{198,6},{199,7},{2... | collective-permute-start | bytes 73736 | tf_op jit(solution)/shard_map/ppermute | solution.py:183
  65.8 12.0 %collective-permute-start.8 = (f32[2,24,128]{2,1,0:T(8,128)S(1)}, f32[2,24,128]{2,1,0:T(8,128)S(1)}, u32[]{:S(2)}, u32[]{:S(2)}) collective-permute-start(f32[2,24,128]{2,1,0:T(8,128)S(1)} %fusion.24), channel_id=1, source_target_pairs={{384,0},{385,1},{386,2},{387,3},{388,4},{389,5},{390,6},{391,7},{3... | collective-permute-start | bytes 73736 | tf_op jit(solution)/shard_map/ppermute | solution.py:183
  67.1 11.5 %collective-permute-start.9 = (f32[2,24,128]{2,1,0:T(8,128)S(1)}, f32[2,24,128]{2,1,0:T(8,128)S(1)}, u32[]{:S(2)}, u32[]{:S(2)}) collective-permute-start(f32[2,24,128]{2,1,0:T(8,128)S(1)} %fusion.24), channel_id=1, source_target_pairs={{576,0},{577,1},{578,2},{579,3},{580,4},{581,5},{582,6},{583,7},{5... | collective-permute-start | bytes 73736 | tf_op jit(solution)/shard_map/ppermute | solution.py:183

commit v6 on v5

--- a/solution.py
+++ b/solution.py
@@ -140,22 +140,18 @@
 
     first_level = jnp.maximum(member - 1, 0) * LZ
     vcols, vrows = zonal_r.shape[-2:]
-    forcing = jnp.stack(
-        [
-            zonal_r.reshape(groups - 1, LZ, vcols, vrows),
-            merid_r.reshape(groups - 1, LZ, vcols, vrows),
-            temper_r.reshape(groups - 1, LZ, vcols, vrows),
-        ],
-        axis=1,
-    )
-    own = forcing[0]
+    own = None
     for shift in range(1, groups):
-        pairs = [(0, shift)]
-        arrived = lax.ppermute(forcing[shift - 1], "grp", pairs)
-        own = jnp.where(member == shift, arrived, own)
-    own_zonal = own[0]
-    own_merid = own[1]
-    own_temper = crop(own[2], vel_halo, 0)
+        levels = slice((shift - 1) * LZ, shift * LZ)
+        payload = jnp.concatenate(
+            [zonal_r[levels].reshape(-1), merid_r[levels].reshape(-1), temper[levels].reshape(-1)]
+        )
+        arrived = lax.ppermute(payload, "grp", [(0, shift)])
+        own = arrived if own is None else jnp.where(member == shift, arrived, own)
+    vel_size = LZ * vcols * vrows
+    own_zonal = own[:vel_size].reshape(LZ, vcols, vrows)
+    own_merid = own[vel_size : 2 * vel_size].reshape(LZ, vcols, vrows)
+    own_temper = own[2 * vel_size :].reshape(LZ, columns, lat_rows)
 
     member_levels = (first_level + jnp.arange(LZ)).astype(jnp.float32)[:, None, None]
     wet_member_pad = (member_levels < depth_pad[None]).astype(jnp.float32)

time: 80.1 us -> 90.6 us (1.13)
  the two profiles are of different devices: /device:TPU:88 before, /device:TPU:6 now
where the time goes in v6:
time: 90.6 us; the launch traced here: 89.5 us
  starting transfers between devices  42.3 us (47%)
  other arithmetic  19.1 us (21%)
  local copies, waits for them, and re-layouts  15.9 us (18%)
  waiting for transfers between devices  11.4 us (13%)
    ppermute x2, starting transfers between devices, exchange(): lax.ppermute(lax.slice_in_dim(block, 0, width, axis=dim), axis, backward)  16.8 us
    ppermute x3, starting transfers between devices, body(): arrived = lax.ppermute(payload, 'grp', [(0, shift)])  12.3 us
    ppermute x2, starting transfers between devices, exchange(): lax.ppermute(lax.slice_in_dim(block, block.shape[dim] - width, None, axis...  9.25 us
    ppermute x3, waiting for transfers between devices, body(): returned.append(lax.ppermute(heating, 'grp', pairs))  9.12 us
    mul x4, other arithmetic, advect_tracers(): wet_mask * (center_of(tracer_pad) - 0.25 * (zonal * grad_x(tracer_pad) +...  4.93 us
    slice x2, local copies, waits for them, and re-layouts, body(): rates[:, source, None, None, None] * advected[source][None]  4 us
    ppermute x3, starting transfers between devices, body(): returned.append(lax.ppermute(heating, 'grp', pairs))  3.87 us
    slice x12, local copies, waits for them, and re-layouts, crop(): return array[..., cut:array.shape[-2] - cut, cut:array.shape[-1] - cut]  3.19 us
  transfers between devices with their start and end apart: 10, of which 3 were waited for; matrix products, arithmetic and copies ran while one was open for 12% of the time, Pallas kernels for 0%

profile of v6, /device:TPU:6, one launch (start us, length us, event | category | flops | bytes accessed | tf_op | source)
XLA Modules:
  0.0 89.5 jit_solution(1685121985472908231)
XLA Ops:
  0.0 0.8 convert_bitcast_fusion
  0.8 1.0 %pad_maximum_fusion.2 = (f32[41,7,128]{2,1,0:T(8,128)S(1)}, f32[41,7,128]{2,1,0:T(8,128)S(1)}) fusion(f32[1,24,128]{2,1,0:T(8,128)S(1)} %convert_bitcast_fusion, f32[40,24,128]{2,1,0:T(8,128)} %bitcast.82), kind=kLoop, calls=%fused_computation.38 | loop fusion | flops 73472 | bytes 797696 | tf_op jit(solution)/shard_map/slice | solution.py:18
  1.8 3.5 %collective-permute-start = (f32[41,7,128]{2,1,0:T(8,128)S(1)}, f32[41,7,128]{2,1,0:T(8,128)S(1)}, u32[]{:S(2)}, u32[]{:S(2)}) collective-permute-start(f32[41,7,128]{2,1,0:T(8,128)S(1)} %get-tuple-element.40), channel_id=1, source_target_pairs={{0,4},{4,8},{8,12},{12,16},{16,20},{20,24},{24,28},{28,32},{32,36}... | collective-permute-start | bytes 440840 | tf_op jit(solution)/shard_map/ppermute | solution.py:17
  5.3 14.1 %collective-permute-start.1 = (f32[41,7,128]{2,1,0:T(8,128)S(1)}, f32[41,7,128]{2,1,0:T(8,128)S(1)}, u32[]{:S(2)}, u32[]{:S(2)}) collective-permute-start(f32[41,7,128]{2,1,0:T(8,128)S(1)} %get-tuple-element.41), channel_id=1, source_target_pairs={{4,0},{8,4},{12,8},{16,12},{20,16},{24,20},{28,24},{32,28},{36,32}... | collective-permute-start | bytes 440840 | tf_op jit(solution)/shard_map/ppermute | solution.py:20
  19.4 0.6 multiply_exponential_fusion
  20.0 1.5 %slice_reduce_fusion.1 = f32[20]{0:T(128)} fusion(f32[20,20]{1,0:T(8,128)} %param.6), kind=kLoop, calls=%fused_computation.107 | loop fusion | bytes 160 | tf_op jit(solution)/shard_map/slice | solution.py:172
  21.4 2.5 %slice_reduce_fusion.19 = (f32[20]{0:T(128)S(1)}, f32[20]{0:T(128)S(1)}, f32[20]{0:T(128)S(1)}, f32[20]{0:T(128)S(1)}, f32[20]{0:T(128)S(1)}, /*index=5*/f32[20]...) fusion(f32[20,20]{1,0:T(8,128)} %param.6), kind=kLoop, calls=%fused_computation.125 | loop fusion | bytes 3040 | tf_op jit(solution)/shard_map/slice | solution.py:172
  24.0 0.1 pad_maximum_fusion
  24.1 0.3 fusion.29
  24.4 0.4 copy.31
  24.8 0.4 copy.32
  25.3 2.7 %collective-permute-start.3 = (f32[41,38,7]{0,1,2:T(8,128)S(1)}, f32[41,38,7]{0,1,2:T(8,128)S(1)}, u32[]{:S(2)}, u32[]{:S(2)}) collective-permute-start(f32[41,38,7]{0,1,2:T(8,128)S(1)} %copy.32), channel_id=1, source_target_pairs={{1,0},{2,1},{3,2},{0,3},{5,4},{6,5},{7,6},{4,7},{9,8},{10,9},{11,1... | collective-permute-start | bytes 130880 | tf_op jit(solution)/shard_map/ppermute | solution.py:20
  28.0 5.8 %collective-permute-start.2 = (f32[41,38,7]{0,1,2:T(8,128)S(1)}, f32[41,38,7]{0,1,2:T(8,128)S(1)}, u32[]{:S(2)}, u32[]{:S(2)}) collective-permute-start(f32[41,38,7]{0,1,2:T(8,128)S(1)} %copy.31), channel_id=1, source_target_pairs={{0,1},{1,2},{2,3},{3,0},{4,5},{5,6},{6,7},{7,4},{8,9},{9,10},{10,1... | collective-permute-start | bytes 130880 | tf_op jit(solution)/shard_map/ppermute | solution.py:17
  34.1 2.3 %collective-permute-done.2 = f32[41,38,7]{0,1,2:T(8,128)S(1)} collective-permute-done((f32[41,38,7]{0,1,2:T(8,128)S(1)}, f32[41,38,7]{0,1,2:T(8,128)S(1)}, u32[]{:S(2)}, u32[]{:S(2)}) %collective-permute-start.2) | collective-permute-done | bytes 43656 | tf_op jit(solution)/shard_map/ppermute | solution.py:17
  36.4 0.5 copy.33
  36.9 1.4 %copy.34 = f32[41,38,7]{2,1,0:T(8,128)} copy(f32[41,38,7]{0,1,2:T(8,128)S(1)} %collective-permute-done.3) | data formatting | bytes 87248 | tf_op jit(solution)/shard_map/ppermute | solution.py:20
  38.2 2.0 %maximum_select_fusion = f32[41,38,142]{2,1,0:T(8,128)S(1)} fusion(f32[41,38,7]{2,1,0:T(8,128)} %copy.34, f32[41,7,128]{2,1,0:T(8,128)S(1)} %collective-permute-done.1, f32[1,24,128]{2,1,0:T(8,128)S(1)} %convert_bitcast_fusion, f32[40,24,128]{2,1,0:T(8,128)S(1)} %bitcast.84, f32[41,7,128]{2,1,0:T(8,128)S(1)} %collective-permute-done, ...), kind=kLoop, calls=%fused_computation | loop fusion | flops 1327416 | bytes 1770030 | tf_op jit(solution)/shard_map/jit(_where)/select_n | solution.py:26
  40.3 0.3 fusion.3
  40.7 0.1 fusion.15
  40.8 0.5 subtract_multiply_fusion.3
  41.3 0.3 fusion.1
  41.6 0.1 fusion.12
  41.7 0.5 subtract_multiply_fusion.1
  42.2 0.2 fusion.7
  42.5 0.1 fusion.20
  42.6 0.7 fusion.34
  43.3 0.4 subtract_multiply_fusion.7
  43.7 0.4 subtract_multiply_fusion.4
  44.2 0.1 fusion.30
  44.3 0.7 fusion.11
  45.0 0.2 reshape.191
  45.2 0.2 reshape.188
  45.4 0.2 reshape.185
  45.6 0.2 reshape.184
  45.8 0.2 reshape.187
  46.0 0.2 reshape.190
  46.2 0.7 concatenate.46
  47.0 1.9 %collective-permute-start.6 = (f32[22224]{0:T(1024)}, f32[22224]{0:T(1024)}, u32[]{:S(2)}, u32[]{:S(2)}) collective-permute-start(f32[22224]{0:T(1024)} %concatenate.46), channel_id=1, source_target_pairs={{0,192},{1,193},{2,194},{3,195},{4,196},{5,197},{6,198},{7,199},{8... | collective-permute-start | bytes 266696 | tf_op jit(solution)/shard_map/ppermute | solution.py:149
  48.9 0.7 concatenate.45
  49.6 9.0 %collective-permute-start.5 = (f32[22224]{0:T(1024)}, f32[22224]{0:T(1024)}, u32[]{:S(2)}, u32[]{:S(2)}) collective-permute-start(f32[22224]{0:T(1024)} %concatenate.45), channel_id=1, source_target_pairs={{0,384},{1,385},{2,386},{3,387},{4,388},{5,389},{6,390},{7,391},{8... | collective-permute-start | bytes 266696 | tf_op jit(solution)/shard_map/ppermute | solution.py:149
  58.6 0.7 concatenate.44
  59.3 1.5 %collective-permute-start.4 = (f32[22224]{0:T(1024)}, f32[22224]{0:T(1024)S(1)}, u32[]{:S(2)}, u32[]{:S(2)}) collective-permute-start(f32[22224]{0:T(1024)} %concatenate.44), channel_id=1, source_target_pairs={{0,576},{1,577},{2,578},{3,579},{4,580},{5,581},{6,582},{7,583},{8... | collective-permute-start | bytes 266696 | tf_op jit(solution)/shard_map/ppermute | solution.py:149
  60.7 0.7 fusion.10
  61.6 0.7 slice.823
  62.3 0.7 slice.822
  63.0 0.7 slice.821
  63.7 0.4 slice.824
  64.2 0.9 %select_select_fusion = f32[22224]{0:T(1024)S(1)} fusion(f32[22224]{0:T(1024)S(1)} %collective-permute-done.4, f32[22224]{0:T(1024)} %collective-permute-done.5, f32[22224]{0:T(1024)} %collective-permute-done.6, pred[]{:T(512)S(6)} %eq.19, pred[]{:T(512)S(6)} %eq.18), kind=kLoop, calls=%fused_computation.40 | loop fusion | flops 44448 | bytes 355586 | tf_op jit(solution)/shard_map/jit(_where)/select_n | solution.py:150
  65.3 0.2 mul.935
  65.8 0.2 mul.932
  66.2 1.5 %add_multiply_fusion.2 = f32[20,2,30,134]{3,2,1,0:T(8,128)S(1)} fusion(f32[20,2,32,136]{3,2,1,0:T(8,128)S(1)} %bitcast.81, f32[2,30,134]{2,1,0:T(8,128)S(1)} %mul.935, f32[2,30,134]{2,1,0:T(8,128)S(1)} %mul.932, f32[2,30,134]{2,1,0:T(8,128)S(1)} %copy-done.5), kind=kLoop, calls=%fused_computation.3 | loop fusion | flops 2412000 | bytes 3955680 | tf_op jit(solution)/shard_map/mul | solution.py:76
  67.7 1.4 %add_multiply_fusion.1 = f32[20,2,28,132]{3,2,1,0:T(8,128)S(1)} fusion(f32[20,2,30,134]{3,2,1,0:T(8,128)S(1)} %add_multiply_fusion.2, f32[2,28,132]{2,1,0:T(8,128)S(1)} %slice.845, f32[2,28,132]{2,1,0:T(8,128)S(1)} %slice.842, f32[2,28,132]{2,1,0:T(8,128)S(1)} %copy-done.4), kind=kLoop, calls=%fused_computation.2 | loop fusion | flops 2217600 | bytes 3636864 | tf_op jit(solution)/shard_map/mul | solution.py:76
  69.2 1.4 %add_multiply_fusion = f32[20,2,26,130]{3,2,1,0:T(8,128)S(1)} fusion(f32[20,2,28,132]{3,2,1,0:T(8,128)S(1)} %add_multiply_fusion.1, f32[2,26,130]{2,1,0:T(8,128)S(1)} %slice.852, f32[2,26,130]{2,1,0:T(8,128)S(1)} %slice.849, f32[2,26,130]{2,1,0:T(8,128)S(1)} %copy-done.3), kind=kLoop, calls=%fused_computation.1 | loop fusion | flops 2028000 | bytes 3325920 | tf_op jit(solution)/shard_map/mul | solution.py:76
  70.8 0.6 add_multiply_fusion.4
  71.6 1.7 %add_multiply_fusion.3 = f32[20,2,24,128]{3,2,1,0:T(8,128)S(1)} fusion(f32[2,24,128]{2,1,0:T(8,128)S(1)} %get-tuple-element.44, f32[20]{0:T(128)S(1)} %copy-done.18, f32[2,24,128]{2,1,0:T(8,128)S(1)} %get-tuple-element.45, f32[20]{0:T(128)S(1)} %copy-done.19, f32[2,24,128]{2,1,0:T(8,128)S(1)} %get-tuple-element.46, f32[20]{0:T(128)S(1)} %get-tuple-element.6, ...), kind=kLoop, calls=%fused_computation.6 | loop fusion | flops 7249920 | bytes 3565200 | tf_op jit(solution)/shard_map/mul | solution.py:173
  73.4 1.3 %collective-permute-start.9 = (f32[2,24,128]{2,1,0:T(8,128)S(1)}, f32[2,24,128]{2,1,0:T(8,128)S(1)}, u32[]{:S(2)}, u32[]{:S(2)}) collective-permute-start(f32[2,24,128]{2,1,0:T(8,128)S(1)} %fusion.24), channel_id=1, source_target_pairs={{576,0},{577,1},{578,2},{579,3},{580,4},{581,5},{582,6},{583,7},{5... | collective-permute-start | bytes 73736 | tf_op jit(solution)/shard_map/ppermute | solution.py:179
  74.7 1.3 %collective-permute-start.8 = (f32[2,24,128]{2,1,0:T(8,128)S(1)}, f32[2,24,128]{2,1,0:T(8,128)S(1)}, u32[]{:S(2)}, u32[]{:S(2)}) collective-permute-start(f32[2,24,128]{2,1,0:T(8,128)S(1)} %fusion.24), channel_id=1, source_target_pairs={{384,0},{385,1},{386,2},{387,3},{388,4},{389,5},{390,6},{391,7},{3... | collective-permute-start | bytes 73736 | tf_op jit(solution)/shard_map/ppermute | solution.py:179
  76.0 1.3 %collective-permute-start.7 = (f32[2,24,128]{2,1,0:T(8,128)S(1)}, f32[2,24,128]{2,1,0:T(8,128)S(1)}, u32[]{:S(2)}, u32[]{:S(2)}) collective-permute-start(f32[2,24,128]{2,1,0:T(8,128)S(1)} %fusion.24), channel_id=1, source_target_pairs={{192,0},{193,1},{194,2},{195,3},{196,4},{197,5},{198,6},{199,7},{2... | collective-permute-start | bytes 73736 | tf_op jit(solution)/shard_map/ppermute | solution.py:179
  77.3 0.2 fusion.5
  77.6 7.2 %collective-permute-done.9 = f32[2,24,128]{2,1,0:T(8,128)S(1)} collective-permute-done((f32[2,24,128]{2,1,0:T(8,128)S(1)}, f32[2,24,128]{2,1,0:T(8,128)S(1)}, u32[]{:S(2)}, u32[]{:S(2)}) %collective-permute-start.9) | collective-permute-done | bytes 24608 | tf_op jit(solution)/shard_map/ppermute | solution.py:179
  84.9 1.9 %collective-permute-done.8 = f32[2,24,128]{2,1,0:T(8,128)S(1)} collective-permute-done((f32[2,24,128]{2,1,0:T(8,128)S(1)}, f32[2,24,128]{2,1,0:T(8,128)S(1)}, u32[]{:S(2)}, u32[]{:S(2)}) %collective-permute-start.8) | collective-permute-done | bytes 24608 | tf_op jit(solution)/shard_map/ppermute | solution.py:179
  86.8 1.0 %fusion.9 = f32[1,40,24,128]{3,2,1,0:T(8,128)S(1)} fusion(f32[1,40,24,128]{3,2,1,0:T(8,128)S(1)} %copy-done.1, f32[6,30,134]{2,1,0:T(8,128)} %copy-done.2, f32[2,24,128]{2,1,0:T(8,128)S(1)} %collective-permute-done.9, f32[2,24,128]{2,1,0:T(8,128)S(1)} %collective-permute-done.8, f32[2,24,128]{2,1,0:T(8,128)S(1)} %collective-permute-done.7), kind=kLoop, calls=%fused_computation.44 | loop fusion | flops 55296 | bytes 221184
  87.8 0.8 fusion.28
  88.6 0.8 bitcast_select_fusion
  (78 shorter events, 1.6 us)
Async XLA Ops:
  0.0 24.0 %copy-start = (f32[1,40,24,128]{3,2,1,0:T(8,128)S(1)}, f32[1,40,24,128]{3,2,1,0:T(8,128)}, u32[]{:S(2)}) copy-start(f32[1,40,24,128]{3,2,1,0:T(8,128)} %param.4) | copy-start | bytes 1474564
  1.8 22.2 %collective-permute-start = (f32[41,7,128]{2,1,0:T(8,128)S(1)}, f32[41,7,128]{2,1,0:T(8,128)S(1)}, u32[]{:S(2)}, u32[]{:S(2)}) collective-permute-start(f32[41,7,128]{2,1,0:T(8,128)S(1)} %get-tuple-element.40), channel_id=1, source_target_pairs={{0,4},{4,8},{8,12},{12,16},{16,20},{20,24},{24,28},{28,32},{32,36}... | collective-permute-start | bytes 440840 | tf_op jit(solution)/shard_map/ppermute | solution.py:17
  5.3 18.7 %collective-permute-start.1 = (f32[41,7,128]{2,1,0:T(8,128)S(1)}, f32[41,7,128]{2,1,0:T(8,128)S(1)}, u32[]{:S(2)}, u32[]{:S(2)}) collective-permute-start(f32[41,7,128]{2,1,0:T(8,128)S(1)} %get-tuple-element.41), channel_id=1, source_target_pairs={{4,0},{8,4},{12,8},{16,12},{20,16},{24,20},{28,24},{32,28},{36,32}... | collective-permute-start | bytes 440840 | tf_op jit(solution)/shard_map/ppermute | solution.py:20
  25.3 11.6 %collective-permute-start.3 = (f32[41,38,7]{0,1,2:T(8,128)S(1)}, f32[41,38,7]{0,1,2:T(8,128)S(1)}, u32[]{:S(2)}, u32[]{:S(2)}) collective-permute-start(f32[41,38,7]{0,1,2:T(8,128)S(1)} %copy.32), channel_id=1, source_target_pairs={{1,0},{2,1},{3,2},{0,3},{5,4},{6,5},{7,6},{4,7},{9,8},{10,9},{11,1... | collective-permute-start | bytes 130880 | tf_op jit(solution)/shard_map/ppermute | solution.py:20
  28.0 8.4 %collective-permute-start.2 = (f32[41,38,7]{0,1,2:T(8,128)S(1)}, f32[41,38,7]{0,1,2:T(8,128)S(1)}, u32[]{:S(2)}, u32[]{:S(2)}) collective-permute-start(f32[41,38,7]{0,1,2:T(8,128)S(1)} %copy.31), channel_id=1, source_target_pairs={{0,1},{1,2},{2,3},{3,0},{4,5},{5,6},{6,7},{7,4},{8,9},{9,10},{10,1... | collective-permute-start | bytes 130880 | tf_op jit(solution)/shard_map/ppermute | solution.py:17
  44.2 18.2 %copy-start.2 = (f32[6,30,134]{2,1,0:T(8,128)}, f32[6,30,134]{2,1,0:T(8,128)S(1)}, u32[]{:S(2)}) copy-start(f32[6,30,134]{2,1,0:T(8,128)S(1)} %get-tuple-element.39) | copy-start | bytes 289444
  47.0 17.2 %collective-permute-start.6 = (f32[22224]{0:T(1024)}, f32[22224]{0:T(1024)}, u32[]{:S(2)}, u32[]{:S(2)}) collective-permute-start(f32[22224]{0:T(1024)} %concatenate.46), channel_id=1, source_target_pairs={{0,192},{1,193},{2,194},{3,195},{4,196},{5,197},{6,198},{7,199},{8... | collective-permute-start | bytes 266696 | tf_op jit(solution)/shard_map/ppermute | solution.py:149
  49.6 14.6 %collective-permute-start.5 = (f32[22224]{0:T(1024)}, f32[22224]{0:T(1024)}, u32[]{:S(2)}, u32[]{:S(2)}) collective-permute-start(f32[22224]{0:T(1024)} %concatenate.45), channel_id=1, source_target_pairs={{0,384},{1,385},{2,386},{3,387},{4,388},{5,389},{6,390},{7,391},{8... | collective-permute-start | bytes 266696 | tf_op jit(solution)/shard_map/ppermute | solution.py:149
  59.3 4.9 %collective-permute-start.4 = (f32[22224]{0:T(1024)}, f32[22224]{0:T(1024)S(1)}, u32[]{:S(2)}, u32[]{:S(2)}) collective-permute-start(f32[22224]{0:T(1024)} %concatenate.44), channel_id=1, source_target_pairs={{0,576},{1,577},{2,578},{3,579},{4,580},{5,581},{6,582},{7,583},{8... | collective-permute-start | bytes 266696 | tf_op jit(solution)/shard_map/ppermute | solution.py:149
  64.2 2.0 %copy-start.5 = (f32[2,30,134]{2,1,0:T(8,128)S(1)}, f32[2,30,134]{2,1,0:T(8,128)}, u32[]{:S(2)}) copy-start(f32[2,30,134]{2,1,0:T(8,128)} %slice.823) | copy-start | bytes 96484
  66.2 1.5 %copy-start.4 = (f32[2,28,132]{2,1,0:T(8,128)S(1)}, f32[2,28,132]{2,1,0:T(8,128)}, u32[]{:S(2)}) copy-start(f32[2,28,132]{2,1,0:T(8,128)} %slice.822) | copy-start | bytes 88708
  67.7 1.5 %copy-start.3 = (f32[2,26,130]{2,1,0:T(8,128)S(1)}, f32[2,26,130]{2,1,0:T(8,128)}, u32[]{:S(2)}) copy-start(f32[2,26,130]{2,1,0:T(8,128)} %slice.821) | copy-start | bytes 81124
  70.6 0.8 copy-start.6
  70.6 0.8 copy-start.7
  70.7 0.8 copy-start.8
  70.7 0.8 copy-start.9
  70.7 0.8 copy-start.10
  70.7 0.8 copy-start.11
  70.7 0.8 copy-start.12
  70.7 0.8 copy-start.13
  70.7 0.8 copy-start.14
  70.7 0.8 copy-start.15
  70.7 0.8 copy-start.16
  70.7 0.8 copy-start.17
  70.8 0.8 copy-start.18
  70.8 0.8 copy-start.19
  70.8 0.8 copy-start.20
  71.6 1.8 %copy-start.21 = (f32[2]{0:T(128)S(1)}, f32[2]{0:T(128)}, u32[]{:S(2)}) copy-start(f32[2]{0:T(128)} %multiply_exponential_fusion) | copy-start | bytes 28
  71.6 15.2 %copy-start.1 = (f32[1,40,24,128]{3,2,1,0:T(8,128)S(1)}, f32[1,40,24,128]{3,2,1,0:T(8,128)}, u32[]{:S(2)}) copy-start(f32[1,40,24,128]{3,2,1,0:T(8,128)} %fusion.10) | copy-start | bytes 1474564
  73.4 11.5 %collective-permute-start.9 = (f32[2,24,128]{2,1,0:T(8,128)S(1)}, f32[2,24,128]{2,1,0:T(8,128)S(1)}, u32[]{:S(2)}, u32[]{:S(2)}) collective-permute-start(f32[2,24,128]{2,1,0:T(8,128)S(1)} %fusion.24), channel_id=1, source_target_pairs={{576,0},{577,1},{578,2},{579,3},{580,4},{581,5},{582,6},{583,7},{5... | collective-permute-start | bytes 73736 | tf_op jit(solution)/shard_map/ppermute | solution.py:179
  74.7 12.0 %collective-permute-start.8 = (f32[2,24,128]{2,1,0:T(8,128)S(1)}, f32[2,24,128]{2,1,0:T(8,128)S(1)}, u32[]{:S(2)}, u32[]{:S(2)}) collective-permute-start(f32[2,24,128]{2,1,0:T(8,128)S(1)} %fusion.24), channel_id=1, source_target_pairs={{384,0},{385,1},{386,2},{387,3},{388,4},{389,5},{390,6},{391,7},{3... | collective-permute-start | bytes 73736 | tf_op jit(solution)/shard_map/ppermute | solution.py:179
  76.0 10.7 %collective-permute-start.7 = (f32[2,24,128]{2,1,0:T(8,128)S(1)}, f32[2,24,128]{2,1,0:T(8,128)S(1)}, u32[]{:S(2)}, u32[]{:S(2)}) collective-permute-start(f32[2,24,128]{2,1,0:T(8,128)S(1)} %fusion.24), channel_id=1, source_target_pairs={{192,0},{193,1},{194,2},{195,3},{196,4},{197,5},{198,6},{199,7},{2... | collective-permute-start | bytes 73736 | tf_op jit(solution)/shard_map/ppermute | solution.py:179

commit v7 on v6

--- a/solution.py
+++ b/solution.py
@@ -2,6 +2,7 @@
 import jax.numpy as jnp
 from jax import lax
 from jax.sharding import PartitionSpec as P
+
 
 LZ = 2
 NTR = 20
@@ -94,7 +95,7 @@
     return jnp.concatenate([results[0], results[1], results[2], results[3][None]], axis=0)
 
 
-def body(state, depth, rates, grazing):
+def step_body(state, depth, rates, grazing):
     groups = lax.axis_size("grp")
     member = lax.axis_index("grp")
     lat_pos = lax.axis_index("lat")
@@ -121,7 +122,7 @@
 
     current = padded[:dyn_rows]
     radius = dyn_halo
-    for section_index in range(SECTIONS):
+    for _ in range(SECTIONS):
         radius -= 1
         cut = dyn_halo - radius
         current = section_rows(
@@ -139,26 +140,26 @@
     surface = crop(current[3 * total_levels], radius, 0)
 
     first_level = jnp.maximum(member - 1, 0) * LZ
-    vcols, vrows = zonal_r.shape[-2:]
-    own = None
+    own_wind = None
+    own_temper = None
     for shift in range(1, groups):
         levels = slice((shift - 1) * LZ, shift * LZ)
-        payload = jnp.concatenate(
-            [zonal_r[levels].reshape(-1), merid_r[levels].reshape(-1), temper[levels].reshape(-1)]
-        )
-        arrived = lax.ppermute(payload, "grp", [(0, shift)])
-        own = arrived if own is None else jnp.where(member == shift, arrived, own)
-    vel_size = LZ * vcols * vrows
-    own_zonal = own[:vel_size].reshape(LZ, vcols, vrows)
-    own_merid = own[vel_size : 2 * vel_size].reshape(LZ, vcols, vrows)
-    own_temper = own[2 * vel_size :].reshape(LZ, columns, lat_rows)
+        wind = jnp.stack([zonal_r[levels], merid_r[levels]])
+        arrived = lax.ppermute(wind, "grp", [(0, shift)])
+        own_wind = arrived if own_wind is None else jnp.where(member == shift, arrived, own_wind)
+    for shift in range(1, groups):
+        levels = slice((shift - 1) * LZ, shift * LZ)
+        arrived = lax.ppermute(temper[levels], "grp", [(0, shift)])
+        own_temper = arrived if own_temper is None else jnp.where(member == shift, arrived, own_temper)
+    own_zonal = own_wind[0]
+    own_merid = own_wind[1]
 
     member_levels = (first_level + jnp.arange(LZ)).astype(jnp.float32)[:, None, None]
     wet_member_pad = (member_levels < depth_pad[None]).astype(jnp.float32)
     tracers = crop(padded[:field_rows], dyn_halo, tracer_halo)
     advected = tracers.reshape((NTR, LZ) + tracers.shape[1:])
     radius = tracer_halo
-    for sub_index in range(NSUB):
+    for _ in range(NSUB):
         radius -= 1
         advected = advect_tracers(
             advected,
@@ -188,4 +189,4 @@
 def solution(mesh):
     in_specs = (P("grp", None, "lon", "lat"), P("lon", "lat"), P(), P())
     out_specs = P("grp", None, "lon", "lat")
-    return jax.shard_map(body, mesh=mesh, in_specs=in_specs, out_specs=out_specs, check_vma=False)
+    return jax.shard_map(step_body, mesh=mesh, in_specs=in_specs, out_specs=out_specs, check_vma=False)

time: 90.6 us -> 85.2 us (0.940)
  local copies, waits for them, and re-layouts: 15.9 us -> 6.9 us
  waiting for transfers between devices: 11.4 us -> 18.2 us
  other arithmetic: 19.1 us -> 14.2 us
  starting transfers between devices: 42.3 us -> 44.3 us
    ppermute x2, waiting for transfers between devices: 0.01 us -> 6.06 us  [exchange(): lax.ppermute(lax.slice_in_dim(block, 0, width, axis=dim), axis, backward)]
    ppermute x6 -> x9, waiting for transfers between devices: 9.13 us -> 12.1 us  [the longest x3 9.85 us: step_body(): returned.append(lax.ppermute(heating, 'grp', pairs))]
    ppermute x6 -> x9, starting transfers between devices: 16.2 us -> 18.8 us  [the longest x3 8.36 us: step_body(): arrived = lax.ppermute(temper[levels], 'grp', [(0, shift)])]
    ppermute x2, waiting for transfers between devices: 2.31 us -> 0.01 us  [exchange(): lax.ppermute(lax.slice_in_dim(block, block.shape[dim] - width, None, axis...]
    concatenate x4 -> x1, local copies, waits for them, and re-layouts: 2.18 us -> 0.02 us  [step_body(): jnp.concatenate([zonal, merid, temper_final, surface[None], unused], axis=0)]
    slice x12, local copies, waits for them, and re-layouts: 3.19 us -> 1.35 us  [crop(): return array[..., cut:array.shape[-2] - cut, cut:array.shape[-1] - cut]]
    unnamed x2, other arithmetic: 1.86 us -> 0.17 us
    unnamed x46 -> x6, local copies, waits for them, and re-layouts: 1.54 us -> 0.18 us
  transfers between devices with their start and end apart: 10 -> 13, of which waited for: 3 -> 5; matrix products, arithmetic and copies ran while one was open for 12% -> 6% of each run, Pallas kernels for 0% -> 0%
where the time goes in v7:
time: 85.2 us; the launch traced here: 84.1 us
  starting transfers between devices  44.3 us (52%)
  waiting for transfers between devices  18.2 us (21%)
  other arithmetic  14.2 us (17%)
  local copies, waits for them, and re-layouts  6.9 us (8%)
    ppermute x2, starting transfers between devices, exchange(): lax.ppermute(lax.slice_in_dim(block, 0, width, axis=dim), axis, backward)  16 us
    ppermute x3, waiting for transfers between devices, step_body(): returned.append(lax.ppermute(heating, 'grp', pairs))  9.85 us
    ppermute x2, starting transfers between devices, exchange(): lax.ppermute(lax.slice_in_dim(block, block.shape[dim] - width, None, axis...  9.53 us
    ppermute x3, starting transfers between devices, step_body(): arrived = lax.ppermute(temper[levels], 'grp', [(0, shift)])  8.36 us
    ppermute x3, starting transfers between devices, step_body(): arrived = lax.ppermute(wind, 'grp', [(0, shift)])  6.54 us
    ppermute x2, waiting for transfers between devices, exchange(): lax.ppermute(lax.slice_in_dim(block, 0, width, axis=dim), axis, backward)  6.06 us
    mul x4, other arithmetic, advect_tracers(): wet_mask * (center_of(tracer_pad) - 0.25 * (zonal * grad_x(tracer_pad) +...  4.93 us
    ppermute x3, starting transfers between devices, step_body(): returned.append(lax.ppermute(heating, 'grp', pairs))  3.87 us
  transfers between devices with their start and end apart: 13, of which 5 were waited for; matrix products, arithmetic and copies ran while one was open for 6% of the time, Pallas kernels for 0%

profile of v7, /device:TPU:6, one launch (start us, length us, event | category | flops | bytes accessed | tf_op | source)
XLA Modules:
  0.0 84.1 jit_solution(12990763737305545127)
XLA Ops:
  0.0 0.8 convert_bitcast_fusion
  0.8 1.0 %pad_maximum_fusion.2 = (f32[41,7,128]{2,1,0:T(8,128)S(1)}, f32[41,7,128]{2,1,0:T(8,128)S(1)}) fusion(f32[1,24,128]{2,1,0:T(8,128)S(1)} %convert_bitcast_fusion, f32[40,24,128]{2,1,0:T(8,128)} %bitcast.94), kind=kLoop, calls=%fused_computation.38 | loop fusion | flops 73472 | bytes 797696 | tf_op jit(solution)/shard_map/slice | solution.py:19
  1.8 3.5 %collective-permute-start = (f32[41,7,128]{2,1,0:T(8,128)S(1)}, f32[41,7,128]{2,1,0:T(8,128)S(1)}, u32[]{:S(2)}, u32[]{:S(2)}) collective-permute-start(f32[41,7,128]{2,1,0:T(8,128)S(1)} %get-tuple-element.40), channel_id=1, source_target_pairs={{0,4},{4,8},{8,12},{12,16},{16,20},{20,24},{24,28},{28,32},{32,36}... | collective-permute-start | bytes 440840 | tf_op jit(solution)/shard_map/ppermute | solution.py:18
  5.3 14.1 %collective-permute-start.1 = (f32[41,7,128]{2,1,0:T(8,128)S(1)}, f32[41,7,128]{2,1,0:T(8,128)S(1)}, u32[]{:S(2)}, u32[]{:S(2)}) collective-permute-start(f32[41,7,128]{2,1,0:T(8,128)S(1)} %get-tuple-element.41), channel_id=1, source_target_pairs={{4,0},{8,4},{12,8},{16,12},{20,16},{24,20},{28,24},{32,28},{36,32}... | collective-permute-start | bytes 440840 | tf_op jit(solution)/shard_map/ppermute | solution.py:21
  19.4 0.9 %slice_reduce_fusion.1 = f32[20]{0:T(128)S(1)} fusion(f32[20,20]{1,0:T(8,128)} %param.6), kind=kLoop, calls=%fused_computation.116 | loop fusion | bytes 160 | tf_op jit(solution)/shard_map/slice | solution.py:173
  20.4 2.0 %slice_reduce_fusion.19 = (f32[20]{0:T(128)S(1)}, f32[20]{0:T(128)S(1)}, f32[20]{0:T(128)S(1)}, f32[20]{0:T(128)S(1)}, f32[20]{0:T(128)S(1)}, /*index=5*/f32[20]...) fusion(f32[20,20]{1,0:T(8,128)} %param.6), kind=kLoop, calls=%fused_computation.134 | loop fusion | bytes 3040 | tf_op jit(solution)/shard_map/slice | solution.py:173
  22.3 0.6 collective-permute-done.1
  22.9 0.1 pad_maximum_fusion
  23.0 0.3 fusion.27
  23.3 0.4 copy.17
  23.7 6.0 %collective-permute-start.2 = (f32[41,38,7]{0,1,2:T(8,128)S(1)}, f32[41,38,7]{0,1,2:T(8,128)S(1)}, u32[]{:S(2)}, u32[]{:S(2)}) collective-permute-start(f32[41,38,7]{0,1,2:T(8,128)S(1)} %copy.17), channel_id=1, source_target_pairs={{0,1},{1,2},{2,3},{3,0},{4,5},{5,6},{6,7},{7,4},{8,9},{9,10},{10,1... | collective-permute-start | bytes 130880 | tf_op jit(solution)/shard_map/ppermute | solution.py:18
  29.8 0.4 copy.18
  30.2 1.9 %collective-permute-start.3 = (f32[41,38,7]{0,1,2:T(8,128)S(1)}, f32[41,38,7]{0,1,2:T(8,128)S(1)}, u32[]{:S(2)}, u32[]{:S(2)}) collective-permute-start(f32[41,38,7]{0,1,2:T(8,128)S(1)} %copy.18), channel_id=1, source_target_pairs={{1,0},{2,1},{3,2},{0,3},{5,4},{6,5},{7,6},{4,7},{9,8},{10,9},{11,1... | collective-permute-start | bytes 130880 | tf_op jit(solution)/shard_map/ppermute | solution.py:21
  32.4 0.5 copy.19
  32.9 5.5 %collective-permute-done.3 = f32[41,38,7]{0,1,2:T(8,128)S(1)} collective-permute-done((f32[41,38,7]{0,1,2:T(8,128)S(1)}, f32[41,38,7]{0,1,2:T(8,128)S(1)}, u32[]{:S(2)}, u32[]{:S(2)}) %collective-permute-start.3) | collective-permute-done | bytes 43656 | tf_op jit(solution)/shard_map/ppermute | solution.py:21
  38.4 0.5 copy.20
  38.9 0.9 %maximum_select_fusion = f32[41,38,142]{2,1,0:T(8,128)S(1)} fusion(f32[41,38,7]{2,1,0:T(8,128)S(1)} %copy.20, f32[41,7,128]{2,1,0:T(8,128)S(1)} %collective-permute-done.1, f32[1,24,128]{2,1,0:T(8,128)S(1)} %convert_bitcast_fusion, f32[40,24,128]{2,1,0:T(8,128)S(1)} %bitcast.96, f32[41,7,128]{2,1,0:T(8,128)S(1)} %collective-permute-done, ...), kind=kLoop, calls=%fused_computation | loop fusion | flops 1327416 | bytes 1770030 | tf_op jit(solution)/shard_map/jit(_where)/select_n | solution.py:27
  39.8 0.3 fusion.3
  40.1 0.5 slice.820
  40.6 0.1 slice.819
  40.7 0.1 slice.818
  40.8 0.1 slice.817
  40.9 0.1 slice.816
  41.0 0.1 compare_convert_fusion
  41.0 0.1 fusion.15
  41.2 0.5 subtract_multiply_fusion.3
  41.7 0.3 fusion.1
  42.0 0.1 fusion.12
  42.1 0.5 subtract_multiply_fusion.1
  42.6 0.2 fusion.7
  42.9 0.1 fusion.20
  43.0 0.1 fusion.29
  43.1 0.4 subtract_multiply_fusion.7
  43.5 0.4 subtract_multiply_fusion.4
  44.0 0.1 fusion.28
  44.1 3.6 %collective-permute-start.7 = (f32[2,24,128]{2,1,0:T(8,128)S(1)}, f32[2,24,128]{2,1,0:T(8,128)S(1)}, u32[]{:S(2)}, u32[]{:S(2)}) collective-permute-start(f32[2,24,128]{2,1,0:T(8,128)S(1)} %get-tuple-element.65), channel_id=1, source_target_pairs={{0,576},{1,577},{2,578},{3,579},{4,580},{5,581},{6,582},{7,583},{8... | collective-permute-start | bytes 73736 | tf_op jit(solution)/shard_map/ppermute | solution.py:152
  47.7 3.5 %collective-permute-start.8 = (f32[2,24,128]{2,1,0:T(8,128)S(1)}, f32[2,24,128]{2,1,0:T(8,128)S(1)}, u32[]{:S(2)}, u32[]{:S(2)}) collective-permute-start(f32[2,24,128]{2,1,0:T(8,128)S(1)} %get-tuple-element.64), channel_id=1, source_target_pairs={{0,384},{1,385},{2,386},{3,387},{4,388},{5,389},{6,390},{7,391},{8... | collective-permute-start | bytes 73736 | tf_op jit(solution)/shard_map/ppermute | solution.py:152
  51.1 1.3 %collective-permute-start.9 = (f32[2,24,128]{2,1,0:T(8,128)S(1)}, f32[2,24,128]{2,1,0:T(8,128)S(1)}, u32[]{:S(2)}, u32[]{:S(2)}) collective-permute-start(f32[2,24,128]{2,1,0:T(8,128)S(1)} %get-tuple-element.63), channel_id=1, source_target_pairs={{0,192},{1,193},{2,194},{3,195},{4,196},{5,197},{6,198},{7,199},{8... | collective-permute-start | bytes 73736 | tf_op jit(solution)/shard_map/ppermute | solution.py:152
  52.4 0.1 fusion.11
  52.6 1.3 %collective-permute-start.6 = (f32[2,2,30,134]{3,2,1,0:T(8,128)S(1)}, f32[2,2,30,134]{3,2,1,0:T(8,128)S(1)}, u32[]{:S(2)}, u32[]{:S(2)}) collective-permute-start(f32[2,2,30,134]{3,2,1,0:T(8,128)S(1)} %pad_maximum_fusion.5), channel_id=1, source_target_pairs={{0,192},{1,193},{2,194},{3,195},{4,196},{5,197},{6,198},{7,199},{8... | collective-permute-start | bytes 192968 | tf_op jit(solution)/shard_map/ppermute | solution.py:148
  53.9 1.3 %collective-permute-start.5 = (f32[2,2,30,134]{3,2,1,0:T(8,128)S(1)}, f32[2,2,30,134]{3,2,1,0:T(8,128)S(1)}, u32[]{:S(2)}, u32[]{:S(2)}) collective-permute-start(f32[2,2,30,134]{3,2,1,0:T(8,128)S(1)} %pad_maximum_fusion.4), channel_id=1, source_target_pairs={{0,384},{1,385},{2,386},{3,387},{4,388},{5,389},{6,390},{7,391},{8... | collective-permute-start | bytes 192968 | tf_op jit(solution)/shard_map/ppermute | solution.py:148
  55.2 0.1 fusion.10
  55.4 3.9 %collective-permute-start.4 = (f32[2,2,30,134]{3,2,1,0:T(8,128)S(1)}, f32[2,2,30,134]{3,2,1,0:T(8,128)S(1)}, u32[]{:S(2)}, u32[]{:S(2)}) collective-permute-start(f32[2,2,30,134]{3,2,1,0:T(8,128)S(1)} %pad_maximum_fusion.3), channel_id=1, source_target_pairs={{0,576},{1,577},{2,578},{3,579},{4,580},{5,581},{6,582},{7,583},{8... | collective-permute-start | bytes 192968 | tf_op jit(solution)/shard_map/ppermute | solution.py:148
  59.4 2.2 %collective-permute-done.4 = f32[2,2,30,134]{3,2,1,0:T(8,128)S(1)} collective-permute-done((f32[2,2,30,134]{3,2,1,0:T(8,128)S(1)}, f32[2,2,30,134]{3,2,1,0:T(8,128)S(1)}, u32[]{:S(2)}, u32[]{:S(2)}) %collective-permute-start.4) | collective-permute-done | bytes 64352 | tf_op jit(solution)/shard_map/ppermute | solution.py:148
  61.7 0.1 slice.835
  61.8 0.1 slice.842
  61.8 0.1 slice.838
  61.9 0.1 slice.845
  62.2 1.4 %add_multiply_fusion.2 = f32[20,2,30,134]{3,2,1,0:T(8,128)S(1)} fusion(f32[20,2,32,136]{3,2,1,0:T(8,128)S(1)} %bitcast.93, f32[2,30,134]{2,1,0:T(8,128)S(1)} %get-tuple-element.73, f32[2,30,134]{2,1,0:T(8,128)S(1)} %get-tuple-element.72, f32[2,30,134]{2,1,0:T(8,128)S(1)} %slice.819), kind=kLoop, calls=%fused_computation.3 | loop fusion | flops 2412000 | bytes 3955680 | tf_op jit(solution)/shard_map/mul | solution.py:77
  63.6 1.5 %add_multiply_fusion.1 = f32[20,2,28,132]{3,2,1,0:T(8,128)S(1)} fusion(f32[20,2,30,134]{3,2,1,0:T(8,128)S(1)} %add_multiply_fusion.2, f32[2,28,132]{2,1,0:T(8,128)S(1)} %slice.838, f32[2,28,132]{2,1,0:T(8,128)S(1)} %slice.835, f32[2,28,132]{2,1,0:T(8,128)S(1)} %slice.818), kind=kLoop, calls=%fused_computation.2 | loop fusion | flops 2217600 | bytes 3636864 | tf_op jit(solution)/shard_map/mul | solution.py:77
  65.1 1.5 %add_multiply_fusion = f32[20,2,26,130]{3,2,1,0:T(8,128)S(1)} fusion(f32[20,2,28,132]{3,2,1,0:T(8,128)S(1)} %add_multiply_fusion.1, f32[2,26,130]{2,1,0:T(8,128)S(1)} %slice.845, f32[2,26,130]{2,1,0:T(8,128)S(1)} %slice.842, f32[2,26,130]{2,1,0:T(8,128)S(1)} %slice.817), kind=kLoop, calls=%fused_computation.1 | loop fusion | flops 2028000 | bytes 3325920 | tf_op jit(solution)/shard_map/mul | solution.py:77
  66.6 0.6 add_multiply_fusion.4
  67.2 1.7 %add_multiply_fusion.3 = f32[20,2,24,128]{3,2,1,0:T(8,128)S(1)} fusion(f32[2,24,128]{2,1,0:T(8,128)S(1)} %get-tuple-element.44, f32[20]{0:T(128)S(1)} %get-tuple-element.23, f32[2,24,128]{2,1,0:T(8,128)S(1)} %get-tuple-element.45, f32[20]{0:T(128)S(1)} %slice_reduce_fusion.1, f32[2,24,128]{2,1,0:T(8,128)S(1)} %get-tuple-element.46, ...), kind=kLoop, calls=%fused_computation.6 | loop fusion | flops 7249920 | bytes 3565200 | tf_op jit(solution)/shard_map/mul | solution.py:174
  68.9 0.1 fusion.24
  69.0 1.3 %collective-permute-start.10 = (f32[2,24,128]{2,1,0:T(8,128)S(1)}, f32[2,24,128]{2,1,0:T(8,128)S(1)}, u32[]{:S(2)}, u32[]{:S(2)}) collective-permute-start(f32[2,24,128]{2,1,0:T(8,128)S(1)} %fusion.24), channel_id=1, source_target_pairs={{192,0},{193,1},{194,2},{195,3},{196,4},{197,5},{198,6},{199,7},{2... | collective-permute-start | bytes 73736 | tf_op jit(solution)/shard_map/ppermute | solution.py:180
  70.3 1.3 %collective-permute-start.11 = (f32[2,24,128]{2,1,0:T(8,128)S(1)}, f32[2,24,128]{2,1,0:T(8,128)S(1)}, u32[]{:S(2)}, u32[]{:S(2)}) collective-permute-start(f32[2,24,128]{2,1,0:T(8,128)S(1)} %fusion.24), channel_id=1, source_target_pairs={{384,0},{385,1},{386,2},{387,3},{388,4},{389,5},{390,6},{391,7},{3... | collective-permute-start | bytes 73736 | tf_op jit(solution)/shard_map/ppermute | solution.py:180
  71.6 1.3 %collective-permute-start.12 = (f32[2,24,128]{2,1,0:T(8,128)S(1)}, f32[2,24,128]{2,1,0:T(8,128)S(1)}, u32[]{:S(2)}, u32[]{:S(2)}) collective-permute-start(f32[2,24,128]{2,1,0:T(8,128)S(1)} %fusion.24), channel_id=1, source_target_pairs={{576,0},{577,1},{578,2},{579,3},{580,4},{581,5},{582,6},{583,7},{5... | collective-permute-start | bytes 73736 | tf_op jit(solution)/shard_map/ppermute | solution.py:180
  72.9 0.2 fusion.5
  73.2 0.1 slice.879
  73.2 9.1 %collective-permute-done.11 = f32[2,24,128]{2,1,0:T(8,128)S(1)} collective-permute-done((f32[2,24,128]{2,1,0:T(8,128)S(1)}, f32[2,24,128]{2,1,0:T(8,128)S(1)}, u32[]{:S(2)}, u32[]{:S(2)}) %collective-permute-start.11) | collective-permute-done | bytes 24608 | tf_op jit(solution)/shard_map/ppermute | solution.py:180
  82.4 0.7 collective-permute-done.12
  83.1 0.1 fusion.9
  83.2 0.1 fusion.26
  83.3 0.8 bitcast_select_fusion
  (36 shorter events, 0.8 us)
Async XLA Ops:
  0.0 22.9 %copy-start = (f32[1,40,24,128]{3,2,1,0:T(8,128)S(1)}, f32[1,40,24,128]{3,2,1,0:T(8,128)}, u32[]{:S(2)}) copy-start(f32[1,40,24,128]{3,2,1,0:T(8,128)} %param.4) | copy-start | bytes 1474564
  1.8 20.5 %collective-permute-start = (f32[41,7,128]{2,1,0:T(8,128)S(1)}, f32[41,7,128]{2,1,0:T(8,128)S(1)}, u32[]{:S(2)}, u32[]{:S(2)}) collective-permute-start(f32[41,7,128]{2,1,0:T(8,128)S(1)} %get-tuple-element.40), channel_id=1, source_target_pairs={{0,4},{4,8},{8,12},{12,16},{16,20},{20,24},{24,28},{28,32},{32,36}... | collective-permute-start | bytes 440840 | tf_op jit(solution)/shard_map/ppermute | solution.py:18
  5.3 17.6 %collective-permute-start.1 = (f32[41,7,128]{2,1,0:T(8,128)S(1)}, f32[41,7,128]{2,1,0:T(8,128)S(1)}, u32[]{:S(2)}, u32[]{:S(2)}) collective-permute-start(f32[41,7,128]{2,1,0:T(8,128)S(1)} %get-tuple-element.41), channel_id=1, source_target_pairs={{4,0},{8,4},{12,8},{16,12},{20,16},{24,20},{28,24},{32,28},{36,32}... | collective-permute-start | bytes 440840 | tf_op jit(solution)/shard_map/ppermute | solution.py:21
  23.7 8.7 %collective-permute-start.2 = (f32[41,38,7]{0,1,2:T(8,128)S(1)}, f32[41,38,7]{0,1,2:T(8,128)S(1)}, u32[]{:S(2)}, u32[]{:S(2)}) collective-permute-start(f32[41,38,7]{0,1,2:T(8,128)S(1)} %copy.17), channel_id=1, source_target_pairs={{0,1},{1,2},{2,3},{3,0},{4,5},{5,6},{6,7},{7,4},{8,9},{9,10},{10,1... | collective-permute-start | bytes 130880 | tf_op jit(solution)/shard_map/ppermute | solution.py:18
  30.2 8.2 %collective-permute-start.3 = (f32[41,38,7]{0,1,2:T(8,128)S(1)}, f32[41,38,7]{0,1,2:T(8,128)S(1)}, u32[]{:S(2)}, u32[]{:S(2)}) collective-permute-start(f32[41,38,7]{0,1,2:T(8,128)S(1)} %copy.18), channel_id=1, source_target_pairs={{1,0},{2,1},{3,2},{0,3},{5,4},{6,5},{7,6},{4,7},{9,8},{10,9},{11,1... | collective-permute-start | bytes 130880 | tf_op jit(solution)/shard_map/ppermute | solution.py:21
  44.1 11.3 %collective-permute-start.7 = (f32[2,24,128]{2,1,0:T(8,128)S(1)}, f32[2,24,128]{2,1,0:T(8,128)S(1)}, u32[]{:S(2)}, u32[]{:S(2)}) collective-permute-start(f32[2,24,128]{2,1,0:T(8,128)S(1)} %get-tuple-element.65), channel_id=1, source_target_pairs={{0,576},{1,577},{2,578},{3,579},{4,580},{5,581},{6,582},{7,583},{8... | collective-permute-start | bytes 73736 | tf_op jit(solution)/shard_map/ppermute | solution.py:152
  47.7 11.6 %collective-permute-start.8 = (f32[2,24,128]{2,1,0:T(8,128)S(1)}, f32[2,24,128]{2,1,0:T(8,128)S(1)}, u32[]{:S(2)}, u32[]{:S(2)}) collective-permute-start(f32[2,24,128]{2,1,0:T(8,128)S(1)} %get-tuple-element.64), channel_id=1, source_target_pairs={{0,384},{1,385},{2,386},{3,387},{4,388},{5,389},{6,390},{7,391},{8... | collective-permute-start | bytes 73736 | tf_op jit(solution)/shard_map/ppermute | solution.py:152
  51.1 8.2 %collective-permute-start.9 = (f32[2,24,128]{2,1,0:T(8,128)S(1)}, f32[2,24,128]{2,1,0:T(8,128)S(1)}, u32[]{:S(2)}, u32[]{:S(2)}) collective-permute-start(f32[2,24,128]{2,1,0:T(8,128)S(1)} %get-tuple-element.63), channel_id=1, source_target_pairs={{0,192},{1,193},{2,194},{3,195},{4,196},{5,197},{6,198},{7,199},{8... | collective-permute-start | bytes 73736 | tf_op jit(solution)/shard_map/ppermute | solution.py:152
  52.6 6.8 %collective-permute-start.6 = (f32[2,2,30,134]{3,2,1,0:T(8,128)S(1)}, f32[2,2,30,134]{3,2,1,0:T(8,128)S(1)}, u32[]{:S(2)}, u32[]{:S(2)}) collective-permute-start(f32[2,2,30,134]{3,2,1,0:T(8,128)S(1)} %pad_maximum_fusion.5), channel_id=1, source_target_pairs={{0,192},{1,193},{2,194},{3,195},{4,196},{5,197},{6,198},{7,199},{8... | collective-permute-start | bytes 192968 | tf_op jit(solution)/shard_map/ppermute | solution.py:148
  53.9 5.4 %collective-permute-start.5 = (f32[2,2,30,134]{3,2,1,0:T(8,128)S(1)}, f32[2,2,30,134]{3,2,1,0:T(8,128)S(1)}, u32[]{:S(2)}, u32[]{:S(2)}) collective-permute-start(f32[2,2,30,134]{3,2,1,0:T(8,128)S(1)} %pad_maximum_fusion.4), channel_id=1, source_target_pairs={{0,384},{1,385},{2,386},{3,387},{4,388},{5,389},{6,390},{7,391},{8... | collective-permute-start | bytes 192968 | tf_op jit(solution)/shard_map/ppermute | solution.py:148
  55.4 6.3 %collective-permute-start.4 = (f32[2,2,30,134]{3,2,1,0:T(8,128)S(1)}, f32[2,2,30,134]{3,2,1,0:T(8,128)S(1)}, u32[]{:S(2)}, u32[]{:S(2)}) collective-permute-start(f32[2,2,30,134]{3,2,1,0:T(8,128)S(1)} %pad_maximum_fusion.3), channel_id=1, source_target_pairs={{0,576},{1,577},{2,578},{3,579},{4,580},{5,581},{6,582},{7,583},{8... | collective-permute-start | bytes 192968 | tf_op jit(solution)/shard_map/ppermute | solution.py:148
  66.5 0.7 copy-start.1
  69.0 4.2 %collective-permute-start.10 = (f32[2,24,128]{2,1,0:T(8,128)S(1)}, f32[2,24,128]{2,1,0:T(8,128)S(1)}, u32[]{:S(2)}, u32[]{:S(2)}) collective-permute-start(f32[2,24,128]{2,1,0:T(8,128)S(1)} %fusion.24), channel_id=1, source_target_pairs={{192,0},{193,1},{194,2},{195,3},{196,4},{197,5},{198,6},{199,7},{2... | collective-permute-start | bytes 73736 | tf_op jit(solution)/shard_map/ppermute | solution.py:180
  70.3 12.0 %collective-permute-start.11 = (f32[2,24,128]{2,1,0:T(8,128)S(1)}, f32[2,24,128]{2,1,0:T(8,128)S(1)}, u32[]{:S(2)}, u32[]{:S(2)}) collective-permute-start(f32[2,24,128]{2,1,0:T(8,128)S(1)} %fusion.24), channel_id=1, source_target_pairs={{384,0},{385,1},{386,2},{387,3},{388,4},{389,5},{390,6},{391,7},{3... | collective-permute-start | bytes 73736 | tf_op jit(solution)/shard_map/ppermute | solution.py:180
  71.6 11.5 %collective-permute-start.12 = (f32[2,24,128]{2,1,0:T(8,128)S(1)}, f32[2,24,128]{2,1,0:T(8,128)S(1)}, u32[]{:S(2)}, u32[]{:S(2)}) collective-permute-start(f32[2,24,128]{2,1,0:T(8,128)S(1)} %fusion.24), channel_id=1, source_target_pairs={{576,0},{577,1},{578,2},{579,3},{580,4},{581,5},{582,6},{583,7},{5... | collective-permute-start | bytes 73736 | tf_op jit(solution)/shard_map/ppermute | solution.py:180

commit v8 on v5

--- a/solution.py
+++ b/solution.py
@@ -10,15 +10,22 @@
 
 
 def exchange(block, width, lat_pos, lat_count):
-    for axis, dim in (("lon", 1), ("lat", 2)):
-        count = lax.axis_size(axis)
-        forward = [(i, (i + 1) % count) for i in range(count)]
-        backward = [(target, source) for source, target in forward]
-        low = lax.ppermute(
-            lax.slice_in_dim(block, block.shape[dim] - width, None, axis=dim), axis, forward
-        )
-        high = lax.ppermute(lax.slice_in_dim(block, 0, width, axis=dim), axis, backward)
-        block = jnp.concatenate([low, block, high], axis=dim)
+    count = lax.axis_size("lon")
+    forward = [(i, (i + 1) % count) for i in range(count)]
+    backward = [(target, source) for source, target in forward]
+    low = lax.ppermute(lax.slice_in_dim(block, block.shape[1] - width, None, axis=1), "lon", forward)
+    high = lax.ppermute(lax.slice_in_dim(block, 0, width, axis=1), "lon", backward)
+    block = jnp.concatenate([low, block, high], axis=1)
+    to_up = lax.slice_in_dim(block, block.shape[2] - width, None, axis=2)
+    to_down = lax.slice_in_dim(block, 0, width, axis=2)
+    chunk = jnp.arange(lat_count)[:, None, None, None]
+    up = (lat_pos + 1) % lat_count
+    down = (lat_pos + lat_count - 1) % lat_count
+    outgoing = jnp.where(chunk == up, to_up[None], jnp.where(chunk == down, to_down[None], 0.0))
+    received = lax.all_to_all(outgoing, "lat", split_axis=0, concat_axis=0, tiled=True)
+    low = jnp.sum(jnp.where(chunk == down, received, 0.0), axis=0)
+    high = jnp.sum(jnp.where(chunk == up, received, 0.0), axis=0)
+    block = jnp.concatenate([low, block, high], axis=2)
     length = block.shape[-1]
     positions = jnp.arange(length)
     lower = (positions < width) & (lat_pos == 0)

time: 80.1 us -> 85 us (1.061)
  waiting for transfers between devices: 24 us -> 28.6 us
  starting transfers between devices: 33.9 us -> 31.2 us
  other arithmetic: 14.3 us -> 16.8 us
    ppermute x4 -> x2, starting transfers between devices: 13.7 us -> 6.62 us  [the longest x1 4.7 us: exchange(): lax.ppermute(lax.slice_in_dim(block, block.shape[1] - width, None, axis=1...]
    all_to_all x0 -> x1, waiting for transfers between devices: none -> 5.41 us  [exchange(): lax.all_to_all(outgoing, 'lat', split_axis=0, concat_axis=0, tiled=True)]
    all_to_all x0 -> x1, starting transfers between devices: none -> 4.29 us  [exchange(): lax.all_to_all(outgoing, 'lat', split_axis=0, concat_axis=0, tiled=True)]
    unnamed x6 -> x10, local copies, waits for them, and re-layouts: 0.18 us -> 1.78 us
    slice x2, local copies, waits for them, and re-layouts: 2.85 us -> 1.39 us  [body(): rates[:, source, None, None, None] * advected[source][None]]
    all_to_all x0 -> x1, other arithmetic: none -> 1.12 us  [exchange(): lax.all_to_all(outgoing, 'lat', split_axis=0, concat_axis=0, tiled=True)]
    concatenate x1, other arithmetic: 0.1 us -> 1.14 us  [exchange(): block = jnp.concatenate([low, block, high], axis=1)]
    reduce_sum x0 -> x2, local copies, waits for them, and re-layouts: none -> 0.93 us  [the longest x1 0.46 us: exchange(): low = jnp.sum(jnp.where(chunk == down, received, 0.0), axis=0)]
  transfers between devices with their start and end apart: 10 -> 9, of which waited for: 7 -> 7; matrix products, arithmetic and copies ran while one was open for 7% -> 4% of each run, Pallas kernels for 0% -> 0%
where the time goes in v8:
time: 85 us; the launch traced here: 84.5 us
  starting transfers between devices  31.2 us (37%)
  waiting for transfers between devices  28.6 us (34%)
  other arithmetic  16.8 us (20%)
  local copies, waits for them, and re-layouts  7.49 us (9%)
    ppermute x3, starting transfers between devices, body(): arrived = lax.ppermute(forcing[shift - 1], 'grp', pairs)  16.4 us
    ppermute x3, waiting for transfers between devices, body(): returned.append(lax.ppermute(heating, 'grp', pairs))  9.85 us
    ppermute x3, waiting for transfers between devices, body(): arrived = lax.ppermute(forcing[shift - 1], 'grp', pairs)  7.43 us
    all_to_all x1, waiting for transfers between devices, exchange(): lax.all_to_all(outgoing, 'lat', split_axis=0, concat_axis=0, tiled=True)  5.41 us
    ppermute x1, waiting for transfers between devices, exchange(): lax.ppermute(lax.slice_in_dim(block, 0, width, axis=1), 'lon', backward)  5.33 us
    mul x4, other arithmetic, advect_tracers(): wet_mask * (center_of(tracer_pad) - 0.25 * (zonal * grad_x(tracer_pad) +...  4.93 us
    ppermute x1, starting transfers between devices, exchange(): lax.ppermute(lax.slice_in_dim(block, block.shape[1] - width, None, axis=1...  4.7 us
    all_to_all x1, starting transfers between devices, exchange(): lax.all_to_all(outgoing, 'lat', split_axis=0, concat_axis=0, tiled=True)  4.29 us
  transfers between devices with their start and end apart: 9, of which 7 were waited for; matrix products, arithmetic and copies ran while one was open for 4% of the time, Pallas kernels for 0%

profile of v8, /device:TPU:88, one launch (start us, length us, event | category | flops | bytes accessed | tf_op | source)
XLA Modules:
  0.0 84.5 jit_solution(15639151181307985593)
XLA Ops:
  0.0 0.7 convert_bitcast_fusion
  0.7 1.0 %pad_maximum_fusion.3 = (f32[41,7,128]{2,1,0:T(8,128)S(1)}, f32[41,7,128]{2,1,0:T(8,128)S(1)}) fusion(f32[1,24,128]{2,1,0:T(8,128)S(1)} %convert_bitcast_fusion, f32[40,24,128]{2,1,0:T(8,128)} %bitcast.103), kind=kLoop, calls=%fused_computation.46 | loop fusion | flops 73472 | bytes 797696 | tf_op jit(solution)/shard_map/slice | solution.py:16
  1.7 4.7 %collective-permute-start = (f32[41,7,128]{2,1,0:T(8,128)S(1)}, f32[41,7,128]{2,1,0:T(8,128)S(1)}, u32[]{:S(2)}, u32[]{:S(2)}) collective-permute-start(f32[41,7,128]{2,1,0:T(8,128)S(1)} %get-tuple-element.45), channel_id=1, source_target_pairs={{0,4},{4,8},{8,12},{12,16},{16,20},{20,24},{24,28},{28,32},{32,36}... | collective-permute-start | bytes 440840 | tf_op jit(solution)/shard_map/ppermute | solution.py:16
  6.4 1.9 %collective-permute-start.1 = (f32[41,7,128]{2,1,0:T(8,128)S(1)}, f32[41,7,128]{2,1,0:T(8,128)S(1)}, u32[]{:S(2)}, u32[]{:S(2)}) collective-permute-start(f32[41,7,128]{2,1,0:T(8,128)S(1)} %get-tuple-element.46), channel_id=1, source_target_pairs={{4,0},{8,4},{12,8},{16,12},{20,16},{24,20},{28,24},{32,28},{36,32}... | collective-permute-start | bytes 440840 | tf_op jit(solution)/shard_map/ppermute | solution.py:17
  8.5 0.9 %slice_reduce_fusion.1 = f32[20]{0:T(128)S(1)} fusion(f32[20,20]{1,0:T(8,128)} %param.6), kind=kLoop, calls=%fused_computation.117 | loop fusion | bytes 160 | tf_op jit(solution)/shard_map/slice | solution.py:183
  9.4 0.5 collective-permute-done
  10.0 5.3 %collective-permute-done.1 = f32[41,7,128]{2,1,0:T(8,128)S(1)} collective-permute-done((f32[41,7,128]{2,1,0:T(8,128)S(1)}, f32[41,7,128]{2,1,0:T(8,128)S(1)}, u32[]{:S(2)}, u32[]{:S(2)}) %collective-permute-start.1) | collective-permute-done | bytes 146976 | tf_op jit(solution)/shard_map/ppermute | solution.py:17
  15.3 1.1 %pad_maximum_fusion = f32[41,38,128]{2,1,0:T(8,128)S(1)} fusion(f32[41,7,128]{2,1,0:T(8,128)S(1)} %collective-permute-done.1, f32[1,24,128]{2,1,0:T(8,128)S(1)} %convert_bitcast_fusion, f32[40,24,128]{2,1,0:T(8,128)} %bitcast.104, f32[41,7,128]{2,1,0:T(8,128)S(1)} %collective-permute-done), kind=kLoop, calls=%fused_computation.4 | loop fusion | flops 598272 | bytes 1595392 | tf_op jit(solution)/shard_map/concatenate | solution.py:18
  16.4 0.3 fusion.29
  16.7 0.4 copy.13
  17.1 0.4 copy.14
  17.6 0.1 fusion.31
  17.7 1.2 %reshape.174 = f32[4,1,10906]{2,1,0:T(1,128)} reshape(f32[4,7,38,41]{3,2,1,0:T(8,128)S(1)} %fusion.31) | data formatting | bytes 348992
  18.9 4.3 %all-to-all-start = ((f32[4,1,10906]{2,1,0:T(1,128)}), f32[4,1,10906]{2,1,0:T(1,128)S(1)}, u32[]{:S(2)}, u32[]{:S(2)}) async-start(f32[4,1,10906]{2,1,0:T(1,128)} %reshape.174), calls=%async_computation | async-start | bytes 352256 | tf_op jit(solution)/shard_map/all_to_all | solution.py:25
  23.5 0.5 slice_reduce_fusion.19
  24.0 5.4 %all-to-all-done = f32[4,1,10906]{2,1,0:T(1,128)S(1)} async-done(((f32[4,1,10906]{2,1,0:T(1,128)}), f32[4,1,10906]{2,1,0:T(1,128)S(1)}, u32[]{:S(2)}, u32[]{:S(2)}) %all-to-all-start) | async-done | bytes 174528 | tf_op jit(solution)/shard_map/all_to_all | solution.py:25
  29.4 0.5 broadcast.132
  29.9 1.1 %reduce.40 = f32[4,10906]{1,0:T(4,128)S(1)} reduce(f32[4,1,10906]{2,1,0:T(1,128)S(1)} %all-to-all-done, f32[]{:T(128)} %broadcast.132), dimensions={1}, to_apply=%all_to_all.3.reduce_sub_computation | reduce | bytes 348996 | tf_op jit(solution)/shard_map/all_to_all | solution.py:25
  31.1 0.4 reshape.175
  31.5 0.2 select_reduce_fusion.1
  31.7 0.5 copy.15
  32.1 0.5 copy.16
  32.6 0.9 %maximum_select_fusion = f32[41,38,142]{2,1,0:T(8,128)S(1)} fusion(f32[41,38,7]{2,1,0:T(8,128)S(1)} %copy.16, f32[41,7,128]{2,1,0:T(8,128)S(1)} %collective-permute-done.1, f32[1,24,128]{2,1,0:T(8,128)S(1)} %convert_bitcast_fusion, f32[40,24,128]{2,1,0:T(8,128)S(1)} %bitcast.105, f32[41,7,128]{2,1,0:T(8,128)S(1)} %collective-permute-done, ...), kind=kLoop, calls=%fused_computation | loop fusion | flops 1327416 | bytes 1770030 | tf_op jit(solution)/shard_map/jit(_where)/select_n | solution.py:33
  33.6 0.3 fusion.3
  33.8 0.1 compare_convert_fusion
  33.9 0.1 fusion.15
  34.1 0.5 subtract_multiply_fusion.3
  34.6 0.3 fusion.1
  34.9 0.1 fusion.12
  35.0 0.5 subtract_multiply_fusion.1
  35.5 0.2 fusion.7
  35.8 0.1 fusion.20
  35.9 0.1 fusion.30
  36.0 0.4 subtract_multiply_fusion.7
  36.4 0.4 subtract_multiply_fusion.4
  36.8 0.1 fusion.11
  37.1 11.1 %collective-permute-start.2 = (f32[3,2,30,134]{3,2,1,0:T(8,128)S(1)}, f32[3,2,30,134]{3,2,1,0:T(8,128)S(1)}, u32[]{:S(2)}, u32[]{:S(2)}) collective-permute-start(f32[3,2,30,134]{3,2,1,0:T(8,128)S(1)} %get-tuple-element.43), channel_id=1, source_target_pairs={{0,576},{1,577},{2,578},{3,579},{4,580},{5,581},{6,582},{7,583},{8... | collective-permute-start | bytes 289448 | tf_op jit(solution)/shard_map/ppermute | solution.py:161
  48.2 3.8 %collective-permute-start.3 = (f32[3,2,30,134]{3,2,1,0:T(8,128)S(1)}, f32[3,2,30,134]{3,2,1,0:T(8,128)S(1)}, u32[]{:S(2)}, u32[]{:S(2)}) collective-permute-start(f32[3,2,30,134]{3,2,1,0:T(8,128)S(1)} %get-tuple-element.44), channel_id=1, source_target_pairs={{0,384},{1,385},{2,386},{3,387},{4,388},{5,389},{6,390},{7,391},{8... | collective-permute-start | bytes 289448 | tf_op jit(solution)/shard_map/ppermute | solution.py:161
  52.0 1.5 %collective-permute-start.4 = (f32[3,2,30,134]{3,2,1,0:T(8,128)S(1)}, f32[3,2,30,134]{3,2,1,0:T(8,128)S(1)}, u32[]{:S(2)}, u32[]{:S(2)}) collective-permute-start(f32[3,2,30,134]{3,2,1,0:T(8,128)S(1)} %get-tuple-element.42), channel_id=1, source_target_pairs={{0,192},{1,193},{2,194},{3,195},{4,196},{5,197},{6,198},{7,199},{8... | collective-permute-start | bytes 289448 | tf_op jit(solution)/shard_map/ppermute | solution.py:161
  53.5 0.1 fusion.10
  53.6 0.5 slice.802
  54.1 0.1 slice.801
  54.2 0.1 slice.800
  54.3 0.1 slice.799
  54.5 5.3 %collective-permute-done.2 = f32[3,2,30,134]{3,2,1,0:T(8,128)S(1)} collective-permute-done((f32[3,2,30,134]{3,2,1,0:T(8,128)S(1)}, f32[3,2,30,134]{3,2,1,0:T(8,128)S(1)}, u32[]{:S(2)}, u32[]{:S(2)}) %collective-permute-start.2) | collective-permute-done | bytes 96512 | tf_op jit(solution)/shard_map/ppermute | solution.py:161
  59.8 2.1 %collective-permute-done.3 = f32[3,2,30,134]{3,2,1,0:T(8,128)S(1)} collective-permute-done((f32[3,2,30,134]{3,2,1,0:T(8,128)S(1)}, f32[3,2,30,134]{3,2,1,0:T(8,128)S(1)}, u32[]{:S(2)}, u32[]{:S(2)}) %collective-permute-start.3) | collective-permute-done | bytes 96512 | tf_op jit(solution)/shard_map/ppermute | solution.py:161
  62.0 0.1 slice.814
  62.0 0.1 slice.821
  62.1 0.1 slice.817
  62.2 0.1 slice.824
  62.5 1.4 %add_multiply_fusion.2 = f32[20,2,30,134]{3,2,1,0:T(8,128)S(1)} fusion(f32[20,2,32,136]{3,2,1,0:T(8,128)S(1)} %bitcast.102, f32[2,30,134]{2,1,0:T(8,128)S(1)} %get-tuple-element.69, f32[2,30,134]{2,1,0:T(8,128)S(1)} %get-tuple-element.70, f32[2,30,134]{2,1,0:T(8,128)S(1)} %slice.801), kind=kLoop, calls=%fused_computation.3 | loop fusion | flops 2412000 | bytes 3955680 | tf_op jit(solution)/shard_map/mul | solution.py:83
  63.9 1.5 %add_multiply_fusion.1 = f32[20,2,28,132]{3,2,1,0:T(8,128)S(1)} fusion(f32[20,2,30,134]{3,2,1,0:T(8,128)S(1)} %add_multiply_fusion.2, f32[2,28,132]{2,1,0:T(8,128)S(1)} %slice.817, f32[2,28,132]{2,1,0:T(8,128)S(1)} %slice.814, f32[2,28,132]{2,1,0:T(8,128)S(1)} %slice.800), kind=kLoop, calls=%fused_computation.2 | loop fusion | flops 2217600 | bytes 3636864 | tf_op jit(solution)/shard_map/mul | solution.py:83
  65.4 1.5 %add_multiply_fusion = f32[20,2,26,130]{3,2,1,0:T(8,128)S(1)} fusion(f32[20,2,28,132]{3,2,1,0:T(8,128)S(1)} %add_multiply_fusion.1, f32[2,26,130]{2,1,0:T(8,128)S(1)} %slice.824, f32[2,26,130]{2,1,0:T(8,128)S(1)} %slice.821, f32[2,26,130]{2,1,0:T(8,128)S(1)} %slice.799), kind=kLoop, calls=%fused_computation.1 | loop fusion | flops 2028000 | bytes 3325920 | tf_op jit(solution)/shard_map/mul | solution.py:83
  66.8 0.6 add_multiply_fusion.4
  67.5 0.1 fusion.26
  67.6 1.7 %add_multiply_fusion.3 = f32[20,2,24,128]{3,2,1,0:T(8,128)S(1)} fusion(f32[2,24,128]{2,1,0:T(8,128)S(1)} %get-tuple-element.49, f32[20]{0:T(128)S(1)} %get-tuple-element.25, f32[2,24,128]{2,1,0:T(8,128)S(1)} %get-tuple-element.50, f32[20]{0:T(128)S(1)} %slice_reduce_fusion.1, f32[2,24,128]{2,1,0:T(8,128)S(1)} %get-tuple-element.51, ...), kind=kLoop, calls=%fused_computation.10 | loop fusion | flops 7249920 | bytes 3565200 | tf_op jit(solution)/shard_map/mul | solution.py:184
  69.4 1.3 %collective-permute-start.5 = (f32[2,24,128]{2,1,0:T(8,128)S(1)}, f32[2,24,128]{2,1,0:T(8,128)S(1)}, u32[]{:S(2)}, u32[]{:S(2)}) collective-permute-start(f32[2,24,128]{2,1,0:T(8,128)S(1)} %fusion.24), channel_id=1, source_target_pairs={{192,0},{193,1},{194,2},{195,3},{196,4},{197,5},{198,6},{199,7},{2... | collective-permute-start | bytes 73736 | tf_op jit(solution)/shard_map/ppermute | solution.py:190
  70.7 1.3 %collective-permute-start.6 = (f32[2,24,128]{2,1,0:T(8,128)S(1)}, f32[2,24,128]{2,1,0:T(8,128)S(1)}, u32[]{:S(2)}, u32[]{:S(2)}) collective-permute-start(f32[2,24,128]{2,1,0:T(8,128)S(1)} %fusion.24), channel_id=1, source_target_pairs={{384,0},{385,1},{386,2},{387,3},{388,4},{389,5},{390,6},{391,7},{3... | collective-permute-start | bytes 73736 | tf_op jit(solution)/shard_map/ppermute | solution.py:190
  72.0 1.3 %collective-permute-start.7 = (f32[2,24,128]{2,1,0:T(8,128)S(1)}, f32[2,24,128]{2,1,0:T(8,128)S(1)}, u32[]{:S(2)}, u32[]{:S(2)}) collective-permute-start(f32[2,24,128]{2,1,0:T(8,128)S(1)} %fusion.24), channel_id=1, source_target_pairs={{576,0},{577,1},{578,2},{579,3},{580,4},{581,5},{582,6},{583,7},{5... | collective-permute-start | bytes 73736 | tf_op jit(solution)/shard_map/ppermute | solution.py:190
  73.3 0.2 fusion.5
  73.6 9.1 %collective-permute-done.6 = f32[2,24,128]{2,1,0:T(8,128)S(1)} collective-permute-done((f32[2,24,128]{2,1,0:T(8,128)S(1)}, f32[2,24,128]{2,1,0:T(8,128)S(1)}, u32[]{:S(2)}, u32[]{:S(2)}) %collective-permute-start.6) | collective-permute-done | bytes 24608 | tf_op jit(solution)/shard_map/ppermute | solution.py:190
  82.7 0.7 collective-permute-done.7
  83.5 0.1 fusion.9
  83.7 0.8 bitcast_select_fusion
  (34 shorter events, 1.2 us)
Async XLA Ops:
  1.7 8.2 %collective-permute-start = (f32[41,7,128]{2,1,0:T(8,128)S(1)}, f32[41,7,128]{2,1,0:T(8,128)S(1)}, u32[]{:S(2)}, u32[]{:S(2)}) collective-permute-start(f32[41,7,128]{2,1,0:T(8,128)S(1)} %get-tuple-element.45), channel_id=1, source_target_pairs={{0,4},{4,8},{8,12},{12,16},{16,20},{20,24},{24,28},{28,32},{32,36}... | collective-permute-start | bytes 440840 | tf_op jit(solution)/shard_map/ppermute | solution.py:16
  6.4 8.9 %collective-permute-start.1 = (f32[41,7,128]{2,1,0:T(8,128)S(1)}, f32[41,7,128]{2,1,0:T(8,128)S(1)}, u32[]{:S(2)}, u32[]{:S(2)}) collective-permute-start(f32[41,7,128]{2,1,0:T(8,128)S(1)} %get-tuple-element.46), channel_id=1, source_target_pairs={{4,0},{8,4},{12,8},{16,12},{20,16},{24,20},{28,24},{32,28},{36,32}... | collective-permute-start | bytes 440840 | tf_op jit(solution)/shard_map/ppermute | solution.py:17
  17.1 6.4 %copy-start = (f32[20,20]{1,0:T(8,128)S(1)}, f32[20,20]{1,0:T(8,128)}, u32[]{:S(2)}) copy-start(f32[20,20]{1,0:T(8,128)} %param.6) | copy-start | bytes 4804
  18.9 10.5 %all-to-all-start = ((f32[4,1,10906]{2,1,0:T(1,128)}), f32[4,1,10906]{2,1,0:T(1,128)S(1)}, u32[]{:S(2)}, u32[]{:S(2)}) async-start(f32[4,1,10906]{2,1,0:T(1,128)} %reshape.174), calls=%async_computation | async-start | bytes 352256 | tf_op jit(solution)/shard_map/all_to_all | solution.py:25
  31.5 1.1 %copy-start.1 = (f32[1,40,24,128]{3,2,1,0:T(8,128)S(1)}, f32[1,40,24,128]{3,2,1,0:T(8,128)}, u32[]{:S(2)}) copy-start(f32[1,40,24,128]{3,2,1,0:T(8,128)} %param.4) | copy-start | bytes 1474564
  37.1 22.7 %collective-permute-start.2 = (f32[3,2,30,134]{3,2,1,0:T(8,128)S(1)}, f32[3,2,30,134]{3,2,1,0:T(8,128)S(1)}, u32[]{:S(2)}, u32[]{:S(2)}) collective-permute-start(f32[3,2,30,134]{3,2,1,0:T(8,128)S(1)} %get-tuple-element.43), channel_id=1, source_target_pairs={{0,576},{1,577},{2,578},{3,579},{4,580},{5,581},{6,582},{7,583},{8... | collective-permute-start | bytes 289448 | tf_op jit(solution)/shard_map/ppermute | solution.py:161
  48.2 13.7 %collective-permute-start.3 = (f32[3,2,30,134]{3,2,1,0:T(8,128)S(1)}, f32[3,2,30,134]{3,2,1,0:T(8,128)S(1)}, u32[]{:S(2)}, u32[]{:S(2)}) collective-permute-start(f32[3,2,30,134]{3,2,1,0:T(8,128)S(1)} %get-tuple-element.44), channel_id=1, source_target_pairs={{0,384},{1,385},{2,386},{3,387},{4,388},{5,389},{6,390},{7,391},{8... | collective-permute-start | bytes 289448 | tf_op jit(solution)/shard_map/ppermute | solution.py:161
  52.0 9.9 %collective-permute-start.4 = (f32[3,2,30,134]{3,2,1,0:T(8,128)S(1)}, f32[3,2,30,134]{3,2,1,0:T(8,128)S(1)}, u32[]{:S(2)}, u32[]{:S(2)}) collective-permute-start(f32[3,2,30,134]{3,2,1,0:T(8,128)S(1)} %get-tuple-element.42), channel_id=1, source_target_pairs={{0,192},{1,193},{2,194},{3,195},{4,196},{5,197},{6,198},{7,199},{8... | collective-permute-start | bytes 289448 | tf_op jit(solution)/shard_map/ppermute | solution.py:161
  66.8 0.8 copy-start.2
  69.4 4.2 %collective-permute-start.5 = (f32[2,24,128]{2,1,0:T(8,128)S(1)}, f32[2,24,128]{2,1,0:T(8,128)S(1)}, u32[]{:S(2)}, u32[]{:S(2)}) collective-permute-start(f32[2,24,128]{2,1,0:T(8,128)S(1)} %fusion.24), channel_id=1, source_target_pairs={{192,0},{193,1},{194,2},{195,3},{196,4},{197,5},{198,6},{199,7},{2... | collective-permute-start | bytes 73736 | tf_op jit(solution)/shard_map/ppermute | solution.py:190
  70.7 12.0 %collective-permute-start.6 = (f32[2,24,128]{2,1,0:T(8,128)S(1)}, f32[2,24,128]{2,1,0:T(8,128)S(1)}, u32[]{:S(2)}, u32[]{:S(2)}) collective-permute-start(f32[2,24,128]{2,1,0:T(8,128)S(1)} %fusion.24), channel_id=1, source_target_pairs={{384,0},{385,1},{386,2},{387,3},{388,4},{389,5},{390,6},{391,7},{3... | collective-permute-start | bytes 73736 | tf_op jit(solution)/shard_map/ppermute | solution.py:190
  72.0 11.5 %collective-permute-start.7 = (f32[2,24,128]{2,1,0:T(8,128)S(1)}, f32[2,24,128]{2,1,0:T(8,128)S(1)}, u32[]{:S(2)}, u32[]{:S(2)}) collective-permute-start(f32[2,24,128]{2,1,0:T(8,128)S(1)} %fusion.24), channel_id=1, source_target_pairs={{576,0},{577,1},{578,2},{579,3},{580,4},{581,5},{582,6},{583,7},{5... | collective-permute-start | bytes 73736 | tf_op jit(solution)/shard_map/ppermute | solution.py:190

commit v9 on v3

--- a/solution.py
+++ b/solution.py
@@ -119,17 +119,26 @@
     coord = (lat_pos * lat_rows - dyn_halo + jnp.arange(lat_rows + 2 * dyn_halo)).astype(jnp.float32)
     coriolis_pad = 0.3 * jnp.sin(jnp.pi * (coord + 0.5) / lat_total - jnp.pi / 2)
 
-    current = padded[:dyn_rows]
-    radius = dyn_halo
-    for section_index in range(SECTIONS):
-        radius -= 1
-        cut = dyn_halo - radius
-        current = section_rows(
-            current,
-            crop(wet_pad, dyn_halo, radius),
-            crop(land_pad, dyn_halo, radius),
-            coriolis_pad[cut : coriolis_pad.shape[0] - cut],
-        )
+    def dynamics(fields, wet_pad, land_pad, coriolis_pad):
+        radius = dyn_halo
+        for section_index in range(SECTIONS):
+            radius -= 1
+            cut = dyn_halo - radius
+            fields = section_rows(
+                fields,
+                crop(wet_pad, dyn_halo, radius),
+                crop(land_pad, dyn_halo, radius),
+                coriolis_pad[cut : coriolis_pad.shape[0] - cut],
+            )
+        return fields
+
+    def no_dynamics(fields, wet_pad, land_pad, coriolis_pad):
+        return jnp.zeros(fields.shape[:1] + crop(fields, dyn_halo, vel_halo).shape[1:], fields.dtype)
+
+    current = lax.cond(
+        member == 0, dynamics, no_dynamics, padded[:dyn_rows], wet_pad, land_pad, coriolis_pad
+    )
+    radius = vel_halo
     zonal_r = current[:total_levels]
     merid_r = current[total_levels : 2 * total_levels]
     temper_r = current[2 * total_levels : 3 * total_levels]
@@ -160,22 +169,45 @@
     member_levels = (first_level + jnp.arange(LZ)).astype(jnp.float32)[:, None, None]
     wet_member_pad = (member_levels < depth_pad[None]).astype(jnp.float32)
     tracers = crop(padded[:field_rows], dyn_halo, tracer_halo)
-    advected = tracers.reshape((NTR, LZ) + tracers.shape[1:])
-    radius = tracer_halo
-    for sub_index in range(NSUB):
-        radius -= 1
-        advected = advect_tracers(
-            advected,
-            crop(own_zonal, vel_halo, radius),
-            crop(own_merid, vel_halo, radius),
-            crop(wet_member_pad, dyn_halo, radius),
+    light_factor = jnp.exp(-(member_levels + 0.5) / total_levels)
+
+    def transport(tracers, own_zonal, own_merid, own_temper, wet_member_pad, rates, grazing):
+        advected = tracers.reshape((NTR, LZ) + tracers.shape[1:])
+        radius = tracer_halo
+        for sub_index in range(NSUB):
+            radius -= 1
+            advected = advect_tracers(
+                advected,
+                crop(own_zonal, vel_halo, radius),
+                crop(own_merid, vel_halo, radius),
+                crop(wet_member_pad, dyn_halo, radius),
+            )
+        wet_member = crop(wet_member_pad, dyn_halo, 0)
+        kinetic = grazing[:, None, None, None] * (advected[0] * advected[1])[None]
+        for source in range(NTR):
+            kinetic = kinetic + rates[:, source, None, None, None] * advected[source][None]
+        updated = wet_member[None] * (advected + 0.2 * jnp.exp(0.05 * own_temper)[None] * kinetic)
+        heating = 0.3 * wet_member * updated[0] * light_factor
+        return updated, heating
+
+    def no_transport(tracers, own_zonal, own_merid, own_temper, wet_member_pad, rates, grazing):
+        return (
+            jnp.zeros((NTR, LZ, columns, lat_rows), jnp.float32),
+            jnp.zeros((LZ, columns, lat_rows), jnp.float32),
         )
-    wet_member = crop(wet_member_pad, dyn_halo, 0)
-    kinetic = jnp.einsum("ts,szxy->tzxy", rates, advected, precision=lax.Precision.HIGHEST)
-    kinetic = kinetic + grazing[:, None, None, None] * (advected[0] * advected[1])[None]
-    updated = wet_member[None] * (advected + 0.2 * jnp.exp(0.05 * own_temper)[None] * kinetic)
-    light_factor = jnp.exp(-(member_levels + 0.5) / total_levels)
-    heating = 0.3 * wet_member * updated[0] * light_factor
+
+    updated, heating = lax.cond(
+        member == 0,
+        no_transport,
+        transport,
+        tracers,
+        own_zonal,
+        own_merid,
+        own_temper,
+        wet_member_pad,
+        rates,
+        grazing,
+    )
     returned = []
     for shift in range(1, groups):
         pairs = [(shift, 0)]

time: 83.5 us -> 82.9 us (level)
  the two profiles are of different devices: /device:TPU:88 before, /device:TPU:126 now
where the time goes in v9:
time: 82.9 us; the launch traced here: 82.4 us
  waiting for transfers between devices  40.5 us (49%)
  starting transfers between devices  28.3 us (34%)
  other arithmetic  9.59 us (12%)
  local copies, waits for them, and re-layouts  3.65 us (4%)
    ppermute x3, waiting for transfers between devices, body(): returned.append(lax.ppermute(heating, 'grp', pairs))  16.7 us
    ppermute x3, starting transfers between devices, body(): arrived = lax.ppermute(forcing[shift - 1], 'grp', pairs)  12.8 us
    ppermute x3, waiting for transfers between devices, body(): arrived = lax.ppermute(forcing[shift - 1], 'grp', pairs)  12.3 us
    ppermute x2, waiting for transfers between devices, exchange(): lax.ppermute(lax.slice_in_dim(block, 0, width, axis=dim), axis, backward)  8.9 us
    ppermute x2, starting transfers between devices, exchange(): lax.ppermute(lax.slice_in_dim(block, block.shape[dim] - width, None, axis...  5.87 us
    ppermute x2, starting transfers between devices, exchange(): lax.ppermute(lax.slice_in_dim(block, 0, width, axis=dim), axis, backward)  5.82 us
    ppermute x3, starting transfers between devices, body(): returned.append(lax.ppermute(heating, 'grp', pairs))  3.88 us
    ppermute x2, waiting for transfers between devices, exchange(): lax.ppermute(lax.slice_in_dim(block, block.shape[dim] - width, None, axis...  2.58 us
  transfers between devices with their start and end apart: 10, of which 8 were waited for; matrix products, arithmetic and copies ran while one was open for 1% of the time, Pallas kernels for 0%

profile of v9, /device:TPU:126, one launch (start us, length us, event | category | flops | bytes accessed | tf_op | source)
XLA Modules:
  0.0 82.4 jit_solution(885285936379037650)
XLA Ops:
  0.0 0.7 convert_bitcast_fusion
  0.7 1.0 %pad_maximum_fusion.4 = (f32[41,7,128]{2,1,0:T(8,128)S(1)}, f32[41,7,128]{2,1,0:T(8,128)S(1)}) fusion(f32[1,24,128]{2,1,0:T(8,128)S(1)} %convert_bitcast_fusion, f32[40,24,128]{2,1,0:T(8,128)} %bitcast.127), kind=kLoop, calls=%fused_computation.119 | loop fusion | flops 73472 | bytes 797696 | tf_op jit(solution)/shard_map/slice | solution.py:18
  1.7 3.5 %collective-permute-start = (f32[41,7,128]{2,1,0:T(8,128)S(1)}, f32[41,7,128]{2,1,0:T(8,128)S(1)}, u32[]{:S(2)}, u32[]{:S(2)}) collective-permute-start(f32[41,7,128]{2,1,0:T(8,128)S(1)} %get-tuple-element.296), channel_id=1, source_target_pairs={{0,4},{4,8},{8,12},{12,16},{16,20},{20,24},{24,28},{28,32},{32,36}... | collective-permute-start | bytes 440840 | tf_op jit(solution)/shard_map/ppermute | solution.py:17
  5.2 2.4 %collective-permute-start.1 = (f32[41,7,128]{2,1,0:T(8,128)S(1)}, f32[41,7,128]{2,1,0:T(8,128)S(1)}, u32[]{:S(2)}, u32[]{:S(2)}) collective-permute-start(f32[41,7,128]{2,1,0:T(8,128)S(1)} %get-tuple-element.297), channel_id=1, source_target_pairs={{4,0},{8,4},{12,8},{16,12},{20,16},{24,20},{28,24},{32,28},{36,32}... | collective-permute-start | bytes 440840 | tf_op jit(solution)/shard_map/ppermute | solution.py:20
  7.7 2.0 %collective-permute-done = f32[41,7,128]{2,1,0:T(8,128)S(1)} collective-permute-done((f32[41,7,128]{2,1,0:T(8,128)S(1)}, f32[41,7,128]{2,1,0:T(8,128)S(1)}, u32[]{:S(2)}, u32[]{:S(2)}) %collective-permute-start) | collective-permute-done | bytes 146976 | tf_op jit(solution)/shard_map/ppermute | solution.py:17
  9.7 5.3 %collective-permute-done.1 = f32[41,7,128]{2,1,0:T(8,128)S(1)} collective-permute-done((f32[41,7,128]{2,1,0:T(8,128)S(1)}, f32[41,7,128]{2,1,0:T(8,128)S(1)}, u32[]{:S(2)}, u32[]{:S(2)}) %collective-permute-start.1) | collective-permute-done | bytes 146976 | tf_op jit(solution)/shard_map/ppermute | solution.py:20
  15.0 1.1 %pad_maximum_fusion.1 = f32[41,38,128]{2,1,0:T(8,128)S(1)} fusion(f32[41,7,128]{2,1,0:T(8,128)S(1)} %collective-permute-done.1, f32[1,24,128]{2,1,0:T(8,128)S(1)} %convert_bitcast_fusion, f32[40,24,128]{2,1,0:T(8,128)} %bitcast.128, f32[41,7,128]{2,1,0:T(8,128)S(1)} %collective-permute-done), kind=kLoop, calls=%fused_computation.111 | loop fusion | flops 598272 | bytes 1595392 | tf_op jit(solution)/shard_map/concatenate | solution.py:21
  16.1 0.3 fusion.24
  16.4 0.4 copy.16
  16.8 2.4 %collective-permute-start.2 = (f32[41,38,7]{0,1,2:T(8,128)S(1)}, f32[41,38,7]{0,1,2:T(8,128)S(1)}, u32[]{:S(2)}, u32[]{:S(2)}) collective-permute-start(f32[41,38,7]{0,1,2:T(8,128)S(1)} %copy.16), channel_id=1, source_target_pairs={{0,1},{1,2},{2,3},{3,0},{4,5},{5,6},{6,7},{7,4},{8,9},{9,10},{10,1... | collective-permute-start | bytes 130880 | tf_op jit(solution)/shard_map/ppermute | solution.py:17
  19.2 0.0 copy-start
  19.2 0.4 copy.17
  19.7 3.5 %collective-permute-start.3 = (f32[41,38,7]{0,1,2:T(8,128)S(1)}, f32[41,38,7]{0,1,2:T(8,128)S(1)}, u32[]{:S(2)}, u32[]{:S(2)}) collective-permute-start(f32[41,38,7]{0,1,2:T(8,128)S(1)} %copy.17), channel_id=1, source_target_pairs={{1,0},{2,1},{3,2},{0,3},{5,4},{6,5},{7,6},{4,7},{9,8},{10,9},{11,1... | collective-permute-start | bytes 130880 | tf_op jit(solution)/shard_map/ppermute | solution.py:20
  23.2 0.1 pad.7.clone
  23.2 0.6 collective-permute-done.2
  23.8 0.5 copy.18
  24.3 3.6 %collective-permute-done.3 = f32[41,38,7]{0,1,2:T(8,128)S(1)} collective-permute-done((f32[41,38,7]{0,1,2:T(8,128)S(1)}, f32[41,38,7]{0,1,2:T(8,128)S(1)}, u32[]{:S(2)}, u32[]{:S(2)}) %collective-permute-start.3) | collective-permute-done | bytes 43656 | tf_op jit(solution)/shard_map/ppermute | solution.py:20
  27.9 1.3 %copy.19 = f32[41,38,7]{2,1,0:T(8,128)} copy(f32[41,38,7]{0,1,2:T(8,128)S(1)} %collective-permute-done.3) | data formatting | bytes 87248 | tf_op jit(solution)/shard_map/ppermute | solution.py:20
  29.2 0.0 copy-done
  29.2 2.1 %maximum_select_fusion = f32[41,38,142]{2,1,0:T(8,128)S(1)} fusion(f32[41,38,7]{2,1,0:T(8,128)} %copy.19, f32[41,7,128]{2,1,0:T(8,128)S(1)} %collective-permute-done.1, f32[1,24,128]{2,1,0:T(8,128)S(1)} %convert_bitcast_fusion, f32[40,24,128]{2,1,0:T(8,128)S(1)} %bitcast.129, f32[41,7,128]{2,1,0:T(8,128)S(1)} %collective-permute-done, ...), kind=kLoop, calls=%fused_computation.110 | loop fusion | flops 1327416 | bytes 1770030 | tf_op jit(solution)/shard_map/jit(_where)/select_n | solution.py:26
  31.3 0.1 compare_convert_fusion
  31.4 3.8 %conditional.2 = (f32[19,30,134]{2,1,0:T(8,128)S(1)}) conditional(s32[]{:T(128)} %convert_element_type.40, () %tuple.46, (f32[6,38,142]{2,1,0:T(8,128)S(1)}, f32[41,38,142]{2,1,0:T(8,128)S(1)}, f32[142]{0:T(256)S(1)}, f32[38,142]{1,0:T(8,128)S(1)}) %tuple.47), branch_computations={%region_0.1_spmd, %region_1.6_spmd} | conditional | flops 3271180 | bytes 8120776 | solution.py:138
  31.4 0.3 add_reduce_fusion
  31.7 0.1 fusion.11
  31.9 0.1 slice.741
  32.0 0.5 subtract_multiply_fusion.3
  32.5 0.3 fusion.1
  32.8 0.1 fusion.8
  32.9 0.1 slice.747
  33.0 0.5 subtract_multiply_fusion.1
  33.5 0.2 fusion.5
  33.7 0.1 fusion.18
  33.8 0.1 slice.760
  33.9 0.4 subtract_multiply_fusion.7
  34.3 0.2 fusion.3
  34.6 0.1 fusion.15
  34.7 0.1 slice.773
  34.8 0.4 subtract_multiply_fusion.5
  35.3 0.1 slice_bitcast_fusion.48
  35.4 0.0 copy-start.1
  35.4 0.0 copy-start.2
  35.4 0.1 pad_maximum_fusion.2
  35.5 1.3 %collective-permute-start.4 = (f32[3,2,30,134]{3,2,1,0:T(8,128)S(1)}, f32[3,2,30,134]{3,2,1,0:T(8,128)S(1)}, u32[]{:S(2)}, u32[]{:S(2)}) collective-permute-start(f32[3,2,30,134]{3,2,1,0:T(8,128)S(1)} %get-tuple-element.295), channel_id=1, source_target_pairs={{0,192},{1,193},{2,194},{3,195},{4,196},{5,197},{6,198},{7,199},{8... | collective-permute-start | bytes 289448 | tf_op jit(solution)/shard_map/ppermute | solution.py:163
  36.9 10.2 %collective-permute-start.5 = (f32[3,2,30,134]{3,2,1,0:T(8,128)S(1)}, f32[3,2,30,134]{3,2,1,0:T(8,128)S(1)}, u32[]{:S(2)}, u32[]{:S(2)}) collective-permute-start(f32[3,2,30,134]{3,2,1,0:T(8,128)S(1)} %get-tuple-element.294), channel_id=1, source_target_pairs={{0,384},{1,385},{2,386},{3,387},{4,388},{5,389},{6,390},{7,391},{8... | collective-permute-start | bytes 289448 | tf_op jit(solution)/shard_map/ppermute | solution.py:163
  47.0 1.3 %collective-permute-start.6 = (f32[3,2,30,134]{3,2,1,0:T(8,128)S(1)}, f32[3,2,30,134]{3,2,1,0:T(8,128)S(1)}, u32[]{:S(2)}, u32[]{:S(2)}) collective-permute-start(f32[3,2,30,134]{3,2,1,0:T(8,128)S(1)} %get-tuple-element.293), channel_id=1, source_target_pairs={{0,576},{1,577},{2,578},{3,579},{4,580},{5,581},{6,582},{7,583},{8... | collective-permute-start | bytes 289448 | tf_op jit(solution)/shard_map/ppermute | solution.py:163
  48.3 0.1 compare_convert_fusion.1
  48.4 0.0 collective-permute-done.4
  48.4 6.0 %collective-permute-done.5 = f32[3,2,30,134]{3,2,1,0:T(8,128)S(1)} collective-permute-done((f32[3,2,30,134]{3,2,1,0:T(8,128)S(1)}, f32[3,2,30,134]{3,2,1,0:T(8,128)S(1)}, u32[]{:S(2)}, u32[]{:S(2)}) %collective-permute-start.5) | collective-permute-done | bytes 96512 | tf_op jit(solution)/shard_map/ppermute | solution.py:163
  54.4 6.3 %collective-permute-done.6 = f32[3,2,30,134]{3,2,1,0:T(8,128)S(1)} collective-permute-done((f32[3,2,30,134]{3,2,1,0:T(8,128)S(1)}, f32[3,2,30,134]{3,2,1,0:T(8,128)S(1)}, u32[]{:S(2)}, u32[]{:S(2)}) %collective-permute-start.6) | collective-permute-done | bytes 96512 | tf_op jit(solution)/shard_map/ppermute | solution.py:163
  60.7 0.0 copy-done.1
  60.7 0.0 copy-done.2
  60.8 1.3 %collective-permute-start.7 = (f32[2,24,128]{2,1,0:T(8,128)S(1)}, f32[2,24,128]{2,1,0:T(8,128)S(1)}, u32[]{:S(2)}, u32[]{:S(2)}) collective-permute-start(f32[2,24,128]{2,1,0:T(8,128)S(1)} %get-tuple-element.181), channel_id=1, source_target_pairs={{192,0},{193,1},{194,2},{195,3},{196,4},{197,5},{198,6},{199,7},{2... | collective-permute-start | bytes 73736 | tf_op jit(solution)/shard_map/ppermute | solution.py:214
  62.1 1.3 %collective-permute-start.8 = (f32[2,24,128]{2,1,0:T(8,128)S(1)}, f32[2,24,128]{2,1,0:T(8,128)S(1)}, u32[]{:S(2)}, u32[]{:S(2)}) collective-permute-start(f32[2,24,128]{2,1,0:T(8,128)S(1)} %get-tuple-element.181), channel_id=1, source_target_pairs={{384,0},{385,1},{386,2},{387,3},{388,4},{389,5},{390,6},{391,7},{3... | collective-permute-start | bytes 73736 | tf_op jit(solution)/shard_map/ppermute | solution.py:214
  63.4 1.3 %collective-permute-start.9 = (f32[2,24,128]{2,1,0:T(8,128)S(1)}, f32[2,24,128]{2,1,0:T(8,128)S(1)}, u32[]{:S(2)}, u32[]{:S(2)}) collective-permute-start(f32[2,24,128]{2,1,0:T(8,128)S(1)} %get-tuple-element.181), channel_id=1, source_target_pairs={{576,0},{577,1},{578,2},{579,3},{580,4},{581,5},{582,6},{583,7},{5... | collective-permute-start | bytes 73736 | tf_op jit(solution)/shard_map/ppermute | solution.py:214
  64.7 0.1 slice_bitcast_fusion.51
  64.8 0.0 collective-permute-done.7
  64.8 10.8 %collective-permute-done.8 = f32[2,24,128]{2,1,0:T(8,128)S(1)} collective-permute-done((f32[2,24,128]{2,1,0:T(8,128)S(1)}, f32[2,24,128]{2,1,0:T(8,128)S(1)}, u32[]{:S(2)}, u32[]{:S(2)}) %collective-permute-start.8) | collective-permute-done | bytes 24608 | tf_op jit(solution)/shard_map/ppermute | solution.py:214
  75.5 5.9 %collective-permute-done.9 = f32[2,24,128]{2,1,0:T(8,128)S(1)} collective-permute-done((f32[2,24,128]{2,1,0:T(8,128)S(1)}, f32[2,24,128]{2,1,0:T(8,128)S(1)}, u32[]{:S(2)}, u32[]{:S(2)}) %collective-permute-start.9) | collective-permute-done | bytes 24608 | tf_op jit(solution)/shard_map/ppermute | solution.py:214
  81.5 0.1 fusion.23
  81.6 0.9 %maximum_select_fusion.1 = f32[1,40,24,128]{3,2,1,0:T(8,128)} fusion(f32[1,40,24,128]{3,2,1,0:T(8,128)S(1)} %get-tuple-element.182, f32[1,1,24,128]{3,2,1,0:T(8,128)S(1)} %slice_bitcast_fusion.51, f32[1,6,24,128]{3,2,1,0:T(8,128)S(1)} %fusion.23, f32[1,12,24,128]{3,2,1,0:T(8,128)S(1)} %slice_bitcast_fusion.48, f32[40]{0:T(128)S(1)} %pad.7.clone, pred[]{:T(512)S(6)} %eq.26), kind=kLoop, calls=%fused_computation.113 | loop fusion | flops 491520 | bytes 1216673 | tf_op jit(solution)/shard_map/jit(_where)/select_n | solution.py:219
  (17 shorter events, 0.3 us)
Async XLA Ops:
  1.7 7.9 %collective-permute-start = (f32[41,7,128]{2,1,0:T(8,128)S(1)}, f32[41,7,128]{2,1,0:T(8,128)S(1)}, u32[]{:S(2)}, u32[]{:S(2)}) collective-permute-start(f32[41,7,128]{2,1,0:T(8,128)S(1)} %get-tuple-element.296), channel_id=1, source_target_pairs={{0,4},{4,8},{8,12},{12,16},{16,20},{20,24},{24,28},{28,32},{32,36}... | collective-permute-start | bytes 440840 | tf_op jit(solution)/shard_map/ppermute | solution.py:17
  5.2 9.8 %collective-permute-start.1 = (f32[41,7,128]{2,1,0:T(8,128)S(1)}, f32[41,7,128]{2,1,0:T(8,128)S(1)}, u32[]{:S(2)}, u32[]{:S(2)}) collective-permute-start(f32[41,7,128]{2,1,0:T(8,128)S(1)} %get-tuple-element.297), channel_id=1, source_target_pairs={{4,0},{8,4},{12,8},{16,12},{20,16},{24,20},{28,24},{32,28},{36,32}... | collective-permute-start | bytes 440840 | tf_op jit(solution)/shard_map/ppermute | solution.py:20
  16.8 7.0 %collective-permute-start.2 = (f32[41,38,7]{0,1,2:T(8,128)S(1)}, f32[41,38,7]{0,1,2:T(8,128)S(1)}, u32[]{:S(2)}, u32[]{:S(2)}) collective-permute-start(f32[41,38,7]{0,1,2:T(8,128)S(1)} %copy.16), channel_id=1, source_target_pairs={{0,1},{1,2},{2,3},{3,0},{4,5},{5,6},{6,7},{7,4},{8,9},{9,10},{10,1... | collective-permute-start | bytes 130880 | tf_op jit(solution)/shard_map/ppermute | solution.py:17
  19.2 10.0 %copy-start = (f32[1,40,24,128]{3,2,1,0:T(8,128)S(1)}, f32[1,40,24,128]{3,2,1,0:T(8,128)}, u32[]{:S(2)}) copy-start(f32[1,40,24,128]{3,2,1,0:T(8,128)} %param.8) | copy-start | bytes 1474564
  19.7 8.2 %collective-permute-start.3 = (f32[41,38,7]{0,1,2:T(8,128)S(1)}, f32[41,38,7]{0,1,2:T(8,128)S(1)}, u32[]{:S(2)}, u32[]{:S(2)}) collective-permute-start(f32[41,38,7]{0,1,2:T(8,128)S(1)} %copy.17), channel_id=1, source_target_pairs={{1,0},{2,1},{3,2},{0,3},{5,4},{6,5},{7,6},{4,7},{9,8},{10,9},{11,1... | collective-permute-start | bytes 130880 | tf_op jit(solution)/shard_map/ppermute | solution.py:20
  35.4 25.3 %copy-start.1 = (f32[20,20]{1,0:T(8,128)S(1)}, f32[20,20]{1,0:T(8,128)}, u32[]{:S(2)}) copy-start(f32[20,20]{1,0:T(8,128)} %param.10) | copy-start | bytes 4804
  35.4 25.3 %copy-start.2 = (f32[20]{0:T(128)S(1)}, f32[20]{0:T(128)}, u32[]{:S(2)}) copy-start(f32[20]{0:T(128)} %param.11) | copy-start | bytes 244
  35.5 12.9 %collective-permute-start.4 = (f32[3,2,30,134]{3,2,1,0:T(8,128)S(1)}, f32[3,2,30,134]{3,2,1,0:T(8,128)S(1)}, u32[]{:S(2)}, u32[]{:S(2)}) collective-permute-start(f32[3,2,30,134]{3,2,1,0:T(8,128)S(1)} %get-tuple-element.295), channel_id=1, source_target_pairs={{0,192},{1,193},{2,194},{3,195},{4,196},{5,197},{6,198},{7,199},{8... | collective-permute-start | bytes 289448 | tf_op jit(solution)/shard_map/ppermute | solution.py:163
  36.9 17.5 %collective-permute-start.5 = (f32[3,2,30,134]{3,2,1,0:T(8,128)S(1)}, f32[3,2,30,134]{3,2,1,0:T(8,128)S(1)}, u32[]{:S(2)}, u32[]{:S(2)}) collective-permute-start(f32[3,2,30,134]{3,2,1,0:T(8,128)S(1)} %get-tuple-element.294), channel_id=1, source_target_pairs={{0,384},{1,385},{2,386},{3,387},{4,388},{5,389},{6,390},{7,391},{8... | collective-permute-start | bytes 289448 | tf_op jit(solution)/shard_map/ppermute | solution.py:163
  47.0 13.7 %collective-permute-start.6 = (f32[3,2,30,134]{3,2,1,0:T(8,128)S(1)}, f32[3,2,30,134]{3,2,1,0:T(8,128)S(1)}, u32[]{:S(2)}, u32[]{:S(2)}) collective-permute-start(f32[3,2,30,134]{3,2,1,0:T(8,128)S(1)} %get-tuple-element.293), channel_id=1, source_target_pairs={{0,576},{1,577},{2,578},{3,579},{4,580},{5,581},{6,582},{7,583},{8... | collective-permute-start | bytes 289448 | tf_op jit(solution)/shard_map/ppermute | solution.py:163
  60.8 4.0 %collective-permute-start.7 = (f32[2,24,128]{2,1,0:T(8,128)S(1)}, f32[2,24,128]{2,1,0:T(8,128)S(1)}, u32[]{:S(2)}, u32[]{:S(2)}) collective-permute-start(f32[2,24,128]{2,1,0:T(8,128)S(1)} %get-tuple-element.181), channel_id=1, source_target_pairs={{192,0},{193,1},{194,2},{195,3},{196,4},{197,5},{198,6},{199,7},{2... | collective-permute-start | bytes 73736 | tf_op jit(solution)/shard_map/ppermute | solution.py:214
  62.1 13.5 %collective-permute-start.8 = (f32[2,24,128]{2,1,0:T(8,128)S(1)}, f32[2,24,128]{2,1,0:T(8,128)S(1)}, u32[]{:S(2)}, u32[]{:S(2)}) collective-permute-start(f32[2,24,128]{2,1,0:T(8,128)S(1)} %get-tuple-element.181), channel_id=1, source_target_pairs={{384,0},{385,1},{386,2},{387,3},{388,4},{389,5},{390,6},{391,7},{3... | collective-permute-start | bytes 73736 | tf_op jit(solution)/shard_map/ppermute | solution.py:214
  63.4 18.1 %collective-permute-start.9 = (f32[2,24,128]{2,1,0:T(8,128)S(1)}, f32[2,24,128]{2,1,0:T(8,128)S(1)}, u32[]{:S(2)}, u32[]{:S(2)}) collective-permute-start(f32[2,24,128]{2,1,0:T(8,128)S(1)} %get-tuple-element.181), channel_id=1, source_target_pairs={{576,0},{577,1},{578,2},{579,3},{580,4},{581,5},{582,6},{583,7},{5... | collective-permute-start | bytes 73736 | tf_op jit(solution)/shard_map/ppermute | solution.py:214

commit v10 on v9

--- a/solution.py
+++ b/solution.py
@@ -149,22 +149,18 @@
 
     first_level = jnp.maximum(member - 1, 0) * LZ
     vcols, vrows = zonal_r.shape[-2:]
-    forcing = jnp.stack(
-        [
-            zonal_r.reshape(groups - 1, LZ, vcols, vrows),
-            merid_r.reshape(groups - 1, LZ, vcols, vrows),
-            temper_r.reshape(groups - 1, LZ, vcols, vrows),
-        ],
-        axis=1,
-    )
-    own = forcing[0]
+    own = None
     for shift in range(1, groups):
-        pairs = [(0, shift)]
-        arrived = lax.ppermute(forcing[shift - 1], "grp", pairs)
-        own = jnp.where(member == shift, arrived, own)
-    own_zonal = own[0]
-    own_merid = own[1]
-    own_temper = crop(own[2], vel_halo, 0)
+        levels = slice((shift - 1) * LZ, shift * LZ)
+        payload = jnp.concatenate(
+            [zonal_r[levels].reshape(-1), merid_r[levels].reshape(-1), temper[levels].reshape(-1)]
+        )
+        arrived = lax.ppermute(payload, "grp", [(0, shift)])
+        own = arrived if own is None else jnp.where(member == shift, arrived, own)
+    vel_size = LZ * vcols * vrows
+    own_zonal = own[:vel_size].reshape(LZ, vcols, vrows)
+    own_merid = own[vel_size : 2 * vel_size].reshape(LZ, vcols, vrows)
+    own_temper = own[2 * vel_size :].reshape(LZ, columns, lat_rows)
 
     member_levels = (first_level + jnp.arange(LZ)).astype(jnp.float32)[:, None, None]
     wet_member_pad = (member_levels < depth_pad[None]).astype(jnp.float32)

time: 82.9 us -> 77.4 us (0.934)
  the two profiles are of different devices: /device:TPU:126 before, /device:TPU:6 now
where the time goes in v10:
time: 77.4 us; the launch traced here: 76.9 us
  starting transfers between devices  33.4 us (43%)
  waiting for transfers between devices  28 us (36%)
  other arithmetic  10 us (13%)
  local copies, waits for them, and re-layouts  5.11 us (7%)
    ppermute x3, waiting for transfers between devices, body(): returned.append(lax.ppermute(heating, 'grp', pairs))  17.3 us
    ppermute x2, starting transfers between devices, exchange(): lax.ppermute(lax.slice_in_dim(block, 0, width, axis=dim), axis, backward)  16 us
    ppermute x2, starting transfers between devices, exchange(): lax.ppermute(lax.slice_in_dim(block, block.shape[dim] - width, None, axis...  9.4 us
    ppermute x2, waiting for transfers between devices, exchange(): lax.ppermute(lax.slice_in_dim(block, 0, width, axis=dim), axis, backward)  6.75 us
    ppermute x3, starting transfers between devices, body(): arrived = lax.ppermute(payload, 'grp', [(0, shift)])  4.1 us
    ppermute x3, starting transfers between devices, body(): returned.append(lax.ppermute(heating, 'grp', pairs))  3.88 us
    select_n x1, other arithmetic, exchange(): return jnp.where(lower | upper, 0.0, block)  2.05 us
    ppermute x3, waiting for transfers between devices, body(): arrived = lax.ppermute(payload, 'grp', [(0, shift)])  2.01 us
  transfers between devices with their start and end apart: 10, of which 7 were waited for; matrix products, arithmetic and copies ran while one was open for 3% of the time, Pallas kernels for 0%

profile of v10, /device:TPU:6, one launch (start us, length us, event | category | flops | bytes accessed | tf_op | source)
XLA Modules:
  0.0 76.9 jit_solution(8249517921731103403)
XLA Ops:
  0.0 0.7 convert_bitcast_fusion
  0.7 1.0 %pad_maximum_fusion.3 = (f32[41,7,128]{2,1,0:T(8,128)S(1)}, f32[41,7,128]{2,1,0:T(8,128)S(1)}) fusion(f32[1,24,128]{2,1,0:T(8,128)S(1)} %convert_bitcast_fusion, f32[40,24,128]{2,1,0:T(8,128)} %bitcast.116), kind=kLoop, calls=%fused_computation.112 | loop fusion | flops 73472 | bytes 797696 | tf_op jit(solution)/shard_map/slice | solution.py:18
  1.7 3.5 %collective-permute-start = (f32[41,7,128]{2,1,0:T(8,128)S(1)}, f32[41,7,128]{2,1,0:T(8,128)S(1)}, u32[]{:S(2)}, u32[]{:S(2)}) collective-permute-start(f32[41,7,128]{2,1,0:T(8,128)S(1)} %get-tuple-element.265), channel_id=1, source_target_pairs={{0,4},{4,8},{8,12},{12,16},{16,20},{20,24},{24,28},{28,32},{32,36}... | collective-permute-start | bytes 440840 | tf_op jit(solution)/shard_map/ppermute | solution.py:17
  5.2 14.1 %collective-permute-start.1 = (f32[41,7,128]{2,1,0:T(8,128)S(1)}, f32[41,7,128]{2,1,0:T(8,128)S(1)}, u32[]{:S(2)}, u32[]{:S(2)}) collective-permute-start(f32[41,7,128]{2,1,0:T(8,128)S(1)} %get-tuple-element.266), channel_id=1, source_target_pairs={{4,0},{8,4},{12,8},{16,12},{20,16},{24,20},{28,24},{32,28},{36,32}... | collective-permute-start | bytes 440840 | tf_op jit(solution)/shard_map/ppermute | solution.py:20
  19.3 0.5 add_convert_fusion.1
  19.9 1.8 %collective-permute-done = f32[41,7,128]{2,1,0:T(8,128)S(1)} collective-permute-done((f32[41,7,128]{2,1,0:T(8,128)S(1)}, f32[41,7,128]{2,1,0:T(8,128)S(1)}, u32[]{:S(2)}, u32[]{:S(2)}) %collective-permute-start) | collective-permute-done | bytes 146976 | tf_op jit(solution)/shard_map/ppermute | solution.py:17
  21.6 1.2 %collective-permute-done.1 = f32[41,7,128]{2,1,0:T(8,128)S(1)} collective-permute-done((f32[41,7,128]{2,1,0:T(8,128)S(1)}, f32[41,7,128]{2,1,0:T(8,128)S(1)}, u32[]{:S(2)}, u32[]{:S(2)}) %collective-permute-start.1) | collective-permute-done | bytes 146976 | tf_op jit(solution)/shard_map/ppermute | solution.py:20
  22.8 1.1 %pad_maximum_fusion.1 = f32[41,38,128]{2,1,0:T(8,128)S(1)} fusion(f32[41,7,128]{2,1,0:T(8,128)S(1)} %collective-permute-done.1, f32[1,24,128]{2,1,0:T(8,128)S(1)} %convert_bitcast_fusion, f32[40,24,128]{2,1,0:T(8,128)} %bitcast.117, f32[41,7,128]{2,1,0:T(8,128)S(1)} %collective-permute-done), kind=kLoop, calls=%fused_computation.108 | loop fusion | flops 598272 | bytes 1595392 | tf_op jit(solution)/shard_map/concatenate | solution.py:21
  24.0 0.3 fusion.25
  24.2 0.4 copy.17
  24.7 5.9 %collective-permute-start.2 = (f32[41,38,7]{0,1,2:T(8,128)S(1)}, f32[41,38,7]{0,1,2:T(8,128)S(1)}, u32[]{:S(2)}, u32[]{:S(2)}) collective-permute-start(f32[41,38,7]{0,1,2:T(8,128)S(1)} %copy.17), channel_id=1, source_target_pairs={{0,1},{1,2},{2,3},{3,0},{4,5},{5,6},{6,7},{7,4},{8,9},{9,10},{10,1... | collective-permute-start | bytes 130880 | tf_op jit(solution)/shard_map/ppermute | solution.py:17
  30.6 0.0 copy-start
  30.6 0.4 copy.18
  31.0 1.9 %collective-permute-start.3 = (f32[41,38,7]{0,1,2:T(8,128)S(1)}, f32[41,38,7]{0,1,2:T(8,128)S(1)}, u32[]{:S(2)}, u32[]{:S(2)}) collective-permute-start(f32[41,38,7]{0,1,2:T(8,128)S(1)} %copy.18), channel_id=1, source_target_pairs={{1,0},{2,1},{3,2},{0,3},{5,4},{6,5},{7,6},{4,7},{9,8},{10,9},{11,1... | collective-permute-start | bytes 130880 | tf_op jit(solution)/shard_map/ppermute | solution.py:20
  33.0 0.1 pad.7.clone
  33.1 0.1 collective-permute-done.2
  33.2 0.5 copy.19
  33.7 5.6 %collective-permute-done.3 = f32[41,38,7]{0,1,2:T(8,128)S(1)} collective-permute-done((f32[41,38,7]{0,1,2:T(8,128)S(1)}, f32[41,38,7]{0,1,2:T(8,128)S(1)}, u32[]{:S(2)}, u32[]{:S(2)}) %collective-permute-start.3) | collective-permute-done | bytes 43656 | tf_op jit(solution)/shard_map/ppermute | solution.py:20
  39.3 1.4 %copy.20 = f32[41,38,7]{2,1,0:T(8,128)} copy(f32[41,38,7]{0,1,2:T(8,128)S(1)} %collective-permute-done.3) | data formatting | bytes 87248 | tf_op jit(solution)/shard_map/ppermute | solution.py:20
  40.6 2.1 %maximum_select_fusion = f32[41,38,142]{2,1,0:T(8,128)S(1)} fusion(f32[41,38,7]{2,1,0:T(8,128)} %copy.20, f32[41,7,128]{2,1,0:T(8,128)S(1)} %collective-permute-done.1, f32[1,24,128]{2,1,0:T(8,128)S(1)} %convert_bitcast_fusion, f32[40,24,128]{2,1,0:T(8,128)S(1)} %bitcast.118, f32[41,7,128]{2,1,0:T(8,128)S(1)} %collective-permute-done, ...), kind=kLoop, calls=%fused_computation.107 | loop fusion | flops 1327416 | bytes 1770030 | tf_op jit(solution)/shard_map/jit(_where)/select_n | solution.py:26
  42.7 0.1 compare_convert_fusion
  42.8 3.8 %conditional.2 = (f32[19,30,134]{2,1,0:T(8,128)S(1)}) conditional(s32[]{:T(128)} %convert_element_type.40, () %tuple.43, (f32[6,38,142]{2,1,0:T(8,128)S(1)}, f32[41,38,142]{2,1,0:T(8,128)S(1)}, f32[142]{0:T(256)S(1)}, f32[38,142]{1,0:T(8,128)S(1)}) %tuple.44), branch_computations={%region_0.1_spmd, %region_1.6_spmd} | conditional | flops 3271180 | bytes 8120776 | solution.py:138
  42.8 0.3 add_reduce_fusion
  43.1 0.1 fusion.11
  43.3 0.1 slice.677
  43.3 0.5 subtract_multiply_fusion.3
  43.9 0.3 fusion.1
  44.1 0.1 fusion.8
  44.3 0.1 slice.683
  44.3 0.5 subtract_multiply_fusion.1
  44.9 0.2 fusion.5
  45.1 0.1 fusion.18
  45.2 0.1 slice.696
  45.3 0.4 subtract_multiply_fusion.7
  45.7 0.2 fusion.3
  46.0 0.1 fusion.15
  46.1 0.1 slice.709
  46.1 0.4 subtract_multiply_fusion.5
  46.6 0.1 pad_maximum_fusion
  46.6 0.0 copy-start.2
  46.7 0.1 fusion.26
  46.8 0.1 slice_bitcast_fusion.42
  46.9 0.2 reshape.137
  47.1 0.2 reshape.138
  47.3 0.1 concatenate.42
  47.4 1.3 %collective-permute-start.6 = (f32[22224]{0:T(1024)S(1)}, f32[22224]{0:T(1024)S(1)}, u32[]{:S(2)}, u32[]{:S(2)}) collective-permute-start(f32[22224]{0:T(1024)S(1)} %concatenate.42), channel_id=1, source_target_pairs={{0,576},{1,577},{2,578},{3,579},{4,580},{5,581},{6,582},{7,583},{8... | collective-permute-start | bytes 266696 | tf_op jit(solution)/shard_map/ppermute | solution.py:158
  48.7 0.2 reshape.134
  48.9 0.2 reshape.135
  49.1 0.1 concatenate.41
  49.2 1.3 %collective-permute-start.5 = (f32[22224]{0:T(1024)S(1)}, f32[22224]{0:T(1024)S(1)}, u32[]{:S(2)}, u32[]{:S(2)}) collective-permute-start(f32[22224]{0:T(1024)S(1)} %concatenate.41), channel_id=1, source_target_pairs={{0,192},{1,193},{2,194},{3,195},{4,196},{5,197},{6,198},{7,199},{8... | collective-permute-start | bytes 266696 | tf_op jit(solution)/shard_map/ppermute | solution.py:158
  50.5 0.2 reshape.131
  50.7 0.2 reshape.132
  50.9 0.1 concatenate.40
  51.0 1.5 %collective-permute-start.4 = (f32[22224]{0:T(1024)S(1)}, f32[22224]{0:T(1024)S(1)}, u32[]{:S(2)}, u32[]{:S(2)}) collective-permute-start(f32[22224]{0:T(1024)S(1)} %concatenate.40), channel_id=1, source_target_pairs={{0,384},{1,385},{2,386},{3,387},{4,388},{5,389},{6,390},{7,391},{8... | collective-permute-start | bytes 266696 | tf_op jit(solution)/shard_map/ppermute | solution.py:158
  52.5 0.1 compare_convert_fusion.1
  52.6 2.0 %collective-permute-done.4 = f32[22224]{0:T(1024)S(1)} collective-permute-done((f32[22224]{0:T(1024)S(1)}, f32[22224]{0:T(1024)S(1)}, u32[]{:S(2)}, u32[]{:S(2)}) %collective-permute-start.4) | collective-permute-done | bytes 88928 | tf_op jit(solution)/shard_map/ppermute | solution.py:158
  54.7 1.3 %collective-permute-start.7 = (f32[2,24,128]{2,1,0:T(8,128)S(1)}, f32[2,24,128]{2,1,0:T(8,128)S(1)}, u32[]{:S(2)}, u32[]{:S(2)}) collective-permute-start(f32[2,24,128]{2,1,0:T(8,128)S(1)} %get-tuple-element.142), channel_id=1, source_target_pairs={{192,0},{193,1},{194,2},{195,3},{196,4},{197,5},{198,6},{199,7},{2... | collective-permute-start | bytes 73736 | tf_op jit(solution)/shard_map/ppermute | solution.py:210
  56.0 1.3 %collective-permute-start.8 = (f32[2,24,128]{2,1,0:T(8,128)S(1)}, f32[2,24,128]{2,1,0:T(8,128)S(1)}, u32[]{:S(2)}, u32[]{:S(2)}) collective-permute-start(f32[2,24,128]{2,1,0:T(8,128)S(1)} %get-tuple-element.142), channel_id=1, source_target_pairs={{384,0},{385,1},{386,2},{387,3},{388,4},{389,5},{390,6},{391,7},{3... | collective-permute-start | bytes 73736 | tf_op jit(solution)/shard_map/ppermute | solution.py:210
  57.3 1.3 %collective-permute-start.9 = (f32[2,24,128]{2,1,0:T(8,128)S(1)}, f32[2,24,128]{2,1,0:T(8,128)S(1)}, u32[]{:S(2)}, u32[]{:S(2)}) collective-permute-start(f32[2,24,128]{2,1,0:T(8,128)S(1)} %get-tuple-element.142), channel_id=1, source_target_pairs={{576,0},{577,1},{578,2},{579,3},{580,4},{581,5},{582,6},{583,7},{5... | collective-permute-start | bytes 73736 | tf_op jit(solution)/shard_map/ppermute | solution.py:210
  58.6 0.1 slice_bitcast_fusion.45
  58.6 4.0 %collective-permute-done.7 = f32[2,24,128]{2,1,0:T(8,128)S(1)} collective-permute-done((f32[2,24,128]{2,1,0:T(8,128)S(1)}, f32[2,24,128]{2,1,0:T(8,128)S(1)}, u32[]{:S(2)}, u32[]{:S(2)}) %collective-permute-start.7) | collective-permute-done | bytes 24608 | tf_op jit(solution)/shard_map/ppermute | solution.py:210
  62.6 13.3 %collective-permute-done.8 = f32[2,24,128]{2,1,0:T(8,128)S(1)} collective-permute-done((f32[2,24,128]{2,1,0:T(8,128)S(1)}, f32[2,24,128]{2,1,0:T(8,128)S(1)}, u32[]{:S(2)}, u32[]{:S(2)}) %collective-permute-start.8) | collective-permute-done | bytes 24608 | tf_op jit(solution)/shard_map/ppermute | solution.py:210
  76.0 0.1 fusion.23
  76.1 0.9 %maximum_select_fusion.1 = f32[1,40,24,128]{3,2,1,0:T(8,128)} fusion(f32[1,40,24,128]{3,2,1,0:T(8,128)S(1)} %get-tuple-element.143, f32[1,1,24,128]{3,2,1,0:T(8,128)S(1)} %slice_bitcast_fusion.45, f32[1,6,24,128]{3,2,1,0:T(8,128)S(1)} %fusion.23, f32[1,12,24,128]{3,2,1,0:T(8,128)S(1)} %slice_bitcast_fusion.42, f32[40]{0:T(128)S(1)} %pad.7.clone, pred[]{:T(512)S(6)} %eq.19), kind=kLoop, calls=%fused_computation.109 | loop fusion | flops 491520 | bytes 1216673 | tf_op jit(solution)/shard_map/jit(_where)/select_n | solution.py:215
  (19 shorter events, 0.2 us)
Async XLA Ops:
  1.7 19.9 %collective-permute-start = (f32[41,7,128]{2,1,0:T(8,128)S(1)}, f32[41,7,128]{2,1,0:T(8,128)S(1)}, u32[]{:S(2)}, u32[]{:S(2)}) collective-permute-start(f32[41,7,128]{2,1,0:T(8,128)S(1)} %get-tuple-element.265), channel_id=1, source_target_pairs={{0,4},{4,8},{8,12},{12,16},{16,20},{20,24},{24,28},{28,32},{32,36}... | collective-permute-start | bytes 440840 | tf_op jit(solution)/shard_map/ppermute | solution.py:17
  5.2 17.6 %collective-permute-start.1 = (f32[41,7,128]{2,1,0:T(8,128)S(1)}, f32[41,7,128]{2,1,0:T(8,128)S(1)}, u32[]{:S(2)}, u32[]{:S(2)}) collective-permute-start(f32[41,7,128]{2,1,0:T(8,128)S(1)} %get-tuple-element.266), channel_id=1, source_target_pairs={{4,0},{8,4},{12,8},{16,12},{20,16},{24,20},{28,24},{32,28},{36,32}... | collective-permute-start | bytes 440840 | tf_op jit(solution)/shard_map/ppermute | solution.py:20
  24.7 8.5 %collective-permute-start.2 = (f32[41,38,7]{0,1,2:T(8,128)S(1)}, f32[41,38,7]{0,1,2:T(8,128)S(1)}, u32[]{:S(2)}, u32[]{:S(2)}) collective-permute-start(f32[41,38,7]{0,1,2:T(8,128)S(1)} %copy.17), channel_id=1, source_target_pairs={{0,1},{1,2},{2,3},{3,0},{4,5},{5,6},{6,7},{7,4},{8,9},{9,10},{10,1... | collective-permute-start | bytes 130880 | tf_op jit(solution)/shard_map/ppermute | solution.py:17
  30.6 10.0 %copy-start = (f32[1,40,24,128]{3,2,1,0:T(8,128)S(1)}, f32[1,40,24,128]{3,2,1,0:T(8,128)}, u32[]{:S(2)}) copy-start(f32[1,40,24,128]{3,2,1,0:T(8,128)} %param.8) | copy-start | bytes 1474564
  31.0 8.2 %collective-permute-start.3 = (f32[41,38,7]{0,1,2:T(8,128)S(1)}, f32[41,38,7]{0,1,2:T(8,128)S(1)}, u32[]{:S(2)}, u32[]{:S(2)}) collective-permute-start(f32[41,38,7]{0,1,2:T(8,128)S(1)} %copy.18), channel_id=1, source_target_pairs={{1,0},{2,1},{3,2},{0,3},{5,4},{6,5},{7,6},{4,7},{9,8},{10,9},{11,1... | collective-permute-start | bytes 130880 | tf_op jit(solution)/shard_map/ppermute | solution.py:20
  46.6 8.0 %copy-start.2 = (f32[20]{0:T(128)S(1)}, f32[20]{0:T(128)}, u32[]{:S(2)}) copy-start(f32[20]{0:T(128)} %param.11) | copy-start | bytes 244
  47.4 5.2 %collective-permute-start.6 = (f32[22224]{0:T(1024)S(1)}, f32[22224]{0:T(1024)S(1)}, u32[]{:S(2)}, u32[]{:S(2)}) collective-permute-start(f32[22224]{0:T(1024)S(1)} %concatenate.42), channel_id=1, source_target_pairs={{0,576},{1,577},{2,578},{3,579},{4,580},{5,581},{6,582},{7,583},{8... | collective-permute-start | bytes 266696 | tf_op jit(solution)/shard_map/ppermute | solution.py:158
  49.2 3.4 %collective-permute-start.5 = (f32[22224]{0:T(1024)S(1)}, f32[22224]{0:T(1024)S(1)}, u32[]{:S(2)}, u32[]{:S(2)}) collective-permute-start(f32[22224]{0:T(1024)S(1)} %concatenate.41), channel_id=1, source_target_pairs={{0,192},{1,193},{2,194},{3,195},{4,196},{5,197},{6,198},{7,199},{8... | collective-permute-start | bytes 266696 | tf_op jit(solution)/shard_map/ppermute | solution.py:158
  51.0 3.6 %collective-permute-start.4 = (f32[22224]{0:T(1024)S(1)}, f32[22224]{0:T(1024)S(1)}, u32[]{:S(2)}, u32[]{:S(2)}) collective-permute-start(f32[22224]{0:T(1024)S(1)} %concatenate.40), channel_id=1, source_target_pairs={{0,384},{1,385},{2,386},{3,387},{4,388},{5,389},{6,390},{7,391},{8... | collective-permute-start | bytes 266696 | tf_op jit(solution)/shard_map/ppermute | solution.py:158
  54.7 7.9 %collective-permute-start.7 = (f32[2,24,128]{2,1,0:T(8,128)S(1)}, f32[2,24,128]{2,1,0:T(8,128)S(1)}, u32[]{:S(2)}, u32[]{:S(2)}) collective-permute-start(f32[2,24,128]{2,1,0:T(8,128)S(1)} %get-tuple-element.142), channel_id=1, source_target_pairs={{192,0},{193,1},{194,2},{195,3},{196,4},{197,5},{198,6},{199,7},{2... | collective-permute-start | bytes 73736 | tf_op jit(solution)/shard_map/ppermute | solution.py:210
  56.0 20.0 %collective-permute-start.8 = (f32[2,24,128]{2,1,0:T(8,128)S(1)}, f32[2,24,128]{2,1,0:T(8,128)S(1)}, u32[]{:S(2)}, u32[]{:S(2)}) collective-permute-start(f32[2,24,128]{2,1,0:T(8,128)S(1)} %get-tuple-element.142), channel_id=1, source_target_pairs={{384,0},{385,1},{386,2},{387,3},{388,4},{389,5},{390,6},{391,7},{3... | collective-permute-start | bytes 73736 | tf_op jit(solution)/shard_map/ppermute | solution.py:210
  57.3 18.7 %collective-permute-start.9 = (f32[2,24,128]{2,1,0:T(8,128)S(1)}, f32[2,24,128]{2,1,0:T(8,128)S(1)}, u32[]{:S(2)}, u32[]{:S(2)}) collective-permute-start(f32[2,24,128]{2,1,0:T(8,128)S(1)} %get-tuple-element.142), channel_id=1, source_target_pairs={{576,0},{577,1},{578,2},{579,3},{580,4},{581,5},{582,6},{583,7},{5... | collective-permute-start | bytes 73736 | tf_op jit(solution)/shard_map/ppermute | solution.py:210

commit v11 on v10

--- a/solution.py
+++ b/solution.py
@@ -10,7 +10,7 @@
 
 
 def exchange(block, width, lat_pos, lat_count):
-    for axis, dim in (("lon", 1), ("lat", 2)):
+    for axis, dim in (("lat", 2), ("lon", 1)):
         count = lax.axis_size(axis)
         forward = [(i, (i + 1) % count) for i in range(count)]
         backward = [(target, source) for source, target in forward]

time: 77.4 us -> 84.5 us (1.092)
  waiting for transfers between devices: 28 us -> 34.5 us
  starting transfers between devices: 33.4 us -> 37.6 us
  local copies, waits for them, and re-layouts: 5.11 us -> 2.14 us
    ppermute x2, waiting for transfers between devices: 1.93 us -> 8.42 us  [exchange(): lax.ppermute(lax.slice_in_dim(block, block.shape[dim] - width, None, axis...]
    ppermute x2, starting transfers between devices: 9.4 us -> 13.3 us  [exchange(): lax.ppermute(lax.slice_in_dim(block, block.shape[dim] - width, None, axis...]
    ppermute x3, starting transfers between devices: 4.1 us -> 7.63 us  [body(): arrived = lax.ppermute(payload, 'grp', [(0, shift)])]
    ppermute x2, starting transfers between devices: 16 us -> 12.8 us  [exchange(): lax.ppermute(lax.slice_in_dim(block, 0, width, axis=dim), axis, backward)]
    ppermute x2 -> x0, local copies, waits for them, and re-layouts: 1.82 us -> none  [the longest x1 1.36 us: exchange(): lax.ppermute(lax.slice_in_dim(block, 0, width, axis=dim), axis, backward)]
    slice x3 -> x0, local copies, waits for them, and re-layouts: 1.15 us -> none  [the longest x2 0.72 us: exchange(): lax.slice_in_dim(block, block.shape[dim] - width, None, axis=dim)]
  transfers between devices with their start and end apart: 10 -> 10, of which waited for: 7 -> 7; matrix products, arithmetic and copies ran while one was open for 3% -> 2% of each run, Pallas kernels for 0% -> 0%
where the time goes in v11:
time: 84.5 us; the launch traced here: 84 us
  starting transfers between devices  37.6 us (44%)
  waiting for transfers between devices  34.5 us (41%)
  other arithmetic  9.4 us (11%)
  local copies, waits for them, and re-layouts  2.14 us (3%)
    ppermute x3, waiting for transfers between devices, body(): returned.append(lax.ppermute(heating, 'grp', pairs))  17.3 us
    ppermute x2, starting transfers between devices, exchange(): lax.ppermute(lax.slice_in_dim(block, block.shape[dim] - width, None, axis...  13.3 us
    ppermute x2, starting transfers between devices, exchange(): lax.ppermute(lax.slice_in_dim(block, 0, width, axis=dim), axis, backward)  12.8 us
    ppermute x2, waiting for transfers between devices, exchange(): lax.ppermute(lax.slice_in_dim(block, block.shape[dim] - width, None, axis...  8.42 us
    ppermute x3, starting transfers between devices, body(): arrived = lax.ppermute(payload, 'grp', [(0, shift)])  7.63 us
    ppermute x2, waiting for transfers between devices, exchange(): lax.ppermute(lax.slice_in_dim(block, 0, width, axis=dim), axis, backward)  6.79 us
    ppermute x3, starting transfers between devices, body(): returned.append(lax.ppermute(heating, 'grp', pairs))  3.88 us
    ppermute x3, waiting for transfers between devices, body(): arrived = lax.ppermute(payload, 'grp', [(0, shift)])  2.01 us
  transfers between devices with their start and end apart: 10, of which 7 were waited for; matrix products, arithmetic and copies ran while one was open for 2% of the time, Pallas kernels for 0%

profile of v11, /device:TPU:6, one launch (start us, length us, event | category | flops | bytes accessed | tf_op | source)
XLA Modules:
  0.0 84.0 jit_solution(11918516742615395802)
XLA Ops:
  0.0 0.0 copy-start
  0.0 0.8 convert_bitcast_fusion
  0.8 1.5 %slice_maximum_fusion = (f32[41,24,7]{2,1,0:T(8,128)S(1)}, f32[41,24,7]{2,1,0:T(8,128)S(1)}) fusion(f32[1,24,128]{2,1,0:T(8,128)S(1)} %convert_bitcast_fusion, f32[40,24,128]{2,1,0:T(8,128)} %bitcast.116), kind=kLoop, calls=%fused_computation.109 | loop fusion | flops 13776 | bytes 558912 | tf_op jit(solution)/shard_map/concatenate | solution.py:112
  2.2 11.4 %collective-permute-start = (f32[41,24,7]{2,1,0:T(8,128)S(1)}, f32[41,24,7]{2,1,0:T(8,128)S(1)}, u32[]{:S(2)}, u32[]{:S(2)}) collective-permute-start(f32[41,24,7]{2,1,0:T(8,128)S(1)} %get-tuple-element.243), channel_id=1, source_target_pairs={{0,1},{1,2},{2,3},{3,0},{4,5},{5,6},{6,7},{7,4},{8,9},{9,10},{10,1... | collective-permute-start | bytes 82664 | tf_op jit(solution)/shard_map/ppermute | solution.py:17
  13.6 1.9 %collective-permute-start.1 = (f32[41,24,7]{2,1,0:T(8,128)S(1)}, f32[41,24,7]{2,1,0:T(8,128)S(1)}, u32[]{:S(2)}, u32[]{:S(2)}) collective-permute-start(f32[41,24,7]{2,1,0:T(8,128)S(1)} %get-tuple-element.244), channel_id=1, source_target_pairs={{1,0},{2,1},{3,2},{0,3},{5,4},{6,5},{7,6},{4,7},{9,8},{10,9},{11,1... | collective-permute-start | bytes 82664 | tf_op jit(solution)/shard_map/ppermute | solution.py:20
  15.6 0.6 add_convert_fusion.1
  16.1 3.9 %collective-permute-done = f32[41,24,7]{2,1,0:T(8,128)S(1)} collective-permute-done((f32[41,24,7]{2,1,0:T(8,128)S(1)}, f32[41,24,7]{2,1,0:T(8,128)S(1)}, u32[]{:S(2)}, u32[]{:S(2)}) %collective-permute-start) | collective-permute-done | bytes 27584 | tf_op jit(solution)/shard_map/ppermute | solution.py:17
  20.1 5.6 %collective-permute-done.1 = f32[41,24,7]{2,1,0:T(8,128)S(1)} collective-permute-done((f32[41,24,7]{2,1,0:T(8,128)S(1)}, f32[41,24,7]{2,1,0:T(8,128)S(1)}, u32[]{:S(2)}, u32[]{:S(2)}) %collective-permute-start.1) | collective-permute-done | bytes 27584 | tf_op jit(solution)/shard_map/ppermute | solution.py:20
  25.7 0.0 copy-done
  25.7 0.3 pad_maximum_fusion.5
  26.0 1.9 %collective-permute-start.2 = (f32[41,7,142]{2,1,0:T(8,128)S(1)}, f32[41,7,142]{2,1,0:T(8,128)S(1)}, u32[]{:S(2)}, u32[]{:S(2)}) collective-permute-start(f32[41,7,142]{2,1,0:T(8,128)S(1)} %get-tuple-element.232), channel_id=1, source_target_pairs={{0,4},{4,8},{8,12},{12,16},{16,20},{20,24},{24,28},{28,32},{32,36}... | collective-permute-start | bytes 489056 | tf_op jit(solution)/shard_map/ppermute | solution.py:17
  28.0 10.8 %collective-permute-start.3 = (f32[41,7,142]{2,1,0:T(8,128)S(1)}, f32[41,7,142]{2,1,0:T(8,128)}, u32[]{:S(2)}, u32[]{:S(2)}) collective-permute-start(f32[41,7,142]{2,1,0:T(8,128)S(1)} %get-tuple-element.233), channel_id=1, source_target_pairs={{4,0},{8,4},{12,8},{16,12},{20,16},{24,20},{28,24},{32,28},{36,32}... | collective-permute-start | bytes 489056 | tf_op jit(solution)/shard_map/ppermute | solution.py:20
  38.8 0.1 pad.7.clone
  38.9 4.5 %collective-permute-done.2 = f32[41,7,142]{2,1,0:T(8,128)S(1)} collective-permute-done((f32[41,7,142]{2,1,0:T(8,128)S(1)}, f32[41,7,142]{2,1,0:T(8,128)S(1)}, u32[]{:S(2)}, u32[]{:S(2)}) %collective-permute-start.2) | collective-permute-done | bytes 163048 | tf_op jit(solution)/shard_map/ppermute | solution.py:17
  43.4 1.2 %collective-permute-done.3 = f32[41,7,142]{2,1,0:T(8,128)} collective-permute-done((f32[41,7,142]{2,1,0:T(8,128)S(1)}, f32[41,7,142]{2,1,0:T(8,128)}, u32[]{:S(2)}, u32[]{:S(2)}) %collective-permute-start.3) | collective-permute-done | bytes 163048 | tf_op jit(solution)/shard_map/ppermute | solution.py:20
  44.6 1.7 %maximum_select_fusion = f32[41,38,142]{2,1,0:T(8,128)S(1)} fusion(f32[41,7,142]{2,1,0:T(8,128)} %collective-permute-done.3, f32[41,24,7]{2,1,0:T(8,128)S(1)} %collective-permute-done.1, f32[1,24,128]{2,1,0:T(8,128)S(1)} %convert_bitcast_fusion, f32[40,24,128]{2,1,0:T(8,128)S(1)} %bitcast.118, f32[41,24,7]{2,1,0:T(8,128)S(1)} %collective-permute-done, ...), kind=kLoop, calls=%fused_computation.107 | loop fusion | flops 1327416 | bytes 1770030 | tf_op jit(solution)/shard_map/jit(_where)/select_n | solution.py:26
  46.3 0.1 compare_convert_fusion
  46.4 3.8 %conditional.2 = (f32[19,30,134]{2,1,0:T(8,128)S(1)}) conditional(s32[]{:T(128)} %convert_element_type.40, () %tuple.43, (f32[6,38,142]{2,1,0:T(8,128)S(1)}, f32[41,38,142]{2,1,0:T(8,128)S(1)}, f32[142]{0:T(256)S(1)}, f32[38,142]{1,0:T(8,128)S(1)}) %tuple.44), branch_computations={%region_0.1_spmd, %region_1.6_spmd} | conditional | flops 3271180 | bytes 8120776 | solution.py:138
  46.4 0.3 add_reduce_fusion
  46.7 0.1 fusion.11
  46.8 0.1 slice.677
  46.9 0.5 subtract_multiply_fusion.3
  47.4 0.3 fusion.1
  47.7 0.1 fusion.8
  47.8 0.1 slice.683
  47.9 0.5 subtract_multiply_fusion.1
  48.4 0.2 fusion.5
  48.7 0.1 fusion.18
  48.8 0.1 slice.696
  48.9 0.4 subtract_multiply_fusion.7
  49.3 0.2 fusion.3
  49.5 0.1 fusion.15
  49.6 0.1 slice.709
  49.7 0.4 subtract_multiply_fusion.5
  50.2 0.1 pad_maximum_fusion
  50.2 0.0 copy-start.2
  50.3 0.1 fusion.25
  50.4 0.1 slice_bitcast_fusion.42
  50.5 0.2 reshape.137
  50.7 0.2 reshape.138
  50.9 0.1 concatenate.42
  51.0 3.5 %collective-permute-start.6 = (f32[22224]{0:T(1024)S(1)}, f32[22224]{0:T(1024)S(1)}, u32[]{:S(2)}, u32[]{:S(2)}) collective-permute-start(f32[22224]{0:T(1024)S(1)} %concatenate.42), channel_id=1, source_target_pairs={{0,576},{1,577},{2,578},{3,579},{4,580},{5,581},{6,582},{7,583},{8... | collective-permute-start | bytes 266696 | tf_op jit(solution)/shard_map/ppermute | solution.py:158
  54.4 0.2 reshape.134
  54.6 0.2 reshape.135
  54.8 0.1 concatenate.41
  54.9 1.3 %collective-permute-start.5 = (f32[22224]{0:T(1024)S(1)}, f32[22224]{0:T(1024)S(1)}, u32[]{:S(2)}, u32[]{:S(2)}) collective-permute-start(f32[22224]{0:T(1024)S(1)} %concatenate.41), channel_id=1, source_target_pairs={{0,192},{1,193},{2,194},{3,195},{4,196},{5,197},{6,198},{7,199},{8... | collective-permute-start | bytes 266696 | tf_op jit(solution)/shard_map/ppermute | solution.py:158
  56.2 0.2 reshape.131
  56.4 0.2 reshape.132
  56.6 0.1 concatenate.40
  56.7 2.9 %collective-permute-start.4 = (f32[22224]{0:T(1024)S(1)}, f32[22224]{0:T(1024)S(1)}, u32[]{:S(2)}, u32[]{:S(2)}) collective-permute-start(f32[22224]{0:T(1024)S(1)} %concatenate.40), channel_id=1, source_target_pairs={{0,384},{1,385},{2,386},{3,387},{4,388},{5,389},{6,390},{7,391},{8... | collective-permute-start | bytes 266696 | tf_op jit(solution)/shard_map/ppermute | solution.py:158
  59.6 0.1 compare_convert_fusion.1
  59.7 0.0 collective-permute-done.6
  59.7 0.0 collective-permute-done.5
  59.7 2.0 %collective-permute-done.4 = f32[22224]{0:T(1024)S(1)} collective-permute-done((f32[22224]{0:T(1024)S(1)}, f32[22224]{0:T(1024)S(1)}, u32[]{:S(2)}, u32[]{:S(2)}) %collective-permute-start.4) | collective-permute-done | bytes 88928 | tf_op jit(solution)/shard_map/ppermute | solution.py:158
  61.7 0.0 copy-done.2
  61.8 1.3 %collective-permute-start.7 = (f32[2,24,128]{2,1,0:T(8,128)S(1)}, f32[2,24,128]{2,1,0:T(8,128)S(1)}, u32[]{:S(2)}, u32[]{:S(2)}) collective-permute-start(f32[2,24,128]{2,1,0:T(8,128)S(1)} %get-tuple-element.142), channel_id=1, source_target_pairs={{192,0},{193,1},{194,2},{195,3},{196,4},{197,5},{198,6},{199,7},{2... | collective-permute-start | bytes 73736 | tf_op jit(solution)/shard_map/ppermute | solution.py:210
  63.1 1.3 %collective-permute-start.8 = (f32[2,24,128]{2,1,0:T(8,128)S(1)}, f32[2,24,128]{2,1,0:T(8,128)S(1)}, u32[]{:S(2)}, u32[]{:S(2)}) collective-permute-start(f32[2,24,128]{2,1,0:T(8,128)S(1)} %get-tuple-element.142), channel_id=1, source_target_pairs={{384,0},{385,1},{386,2},{387,3},{388,4},{389,5},{390,6},{391,7},{3... | collective-permute-start | bytes 73736 | tf_op jit(solution)/shard_map/ppermute | solution.py:210
  64.4 1.3 %collective-permute-start.9 = (f32[2,24,128]{2,1,0:T(8,128)S(1)}, f32[2,24,128]{2,1,0:T(8,128)S(1)}, u32[]{:S(2)}, u32[]{:S(2)}) collective-permute-start(f32[2,24,128]{2,1,0:T(8,128)S(1)} %get-tuple-element.142), channel_id=1, source_target_pairs={{576,0},{577,1},{578,2},{579,3},{580,4},{581,5},{582,6},{583,7},{5... | collective-permute-start | bytes 73736 | tf_op jit(solution)/shard_map/ppermute | solution.py:210
  65.7 0.1 slice_bitcast_fusion.45
  65.7 2.6 %collective-permute-done.7 = f32[2,24,128]{2,1,0:T(8,128)S(1)} collective-permute-done((f32[2,24,128]{2,1,0:T(8,128)S(1)}, f32[2,24,128]{2,1,0:T(8,128)S(1)}, u32[]{:S(2)}, u32[]{:S(2)}) %collective-permute-start.7) | collective-permute-done | bytes 24608 | tf_op jit(solution)/shard_map/ppermute | solution.py:210
  68.4 14.7 %collective-permute-done.8 = f32[2,24,128]{2,1,0:T(8,128)S(1)} collective-permute-done((f32[2,24,128]{2,1,0:T(8,128)S(1)}, f32[2,24,128]{2,1,0:T(8,128)S(1)}, u32[]{:S(2)}, u32[]{:S(2)}) %collective-permute-start.8) | collective-permute-done | bytes 24608 | tf_op jit(solution)/shard_map/ppermute | solution.py:210
  83.1 0.0 collective-permute-done.9
  83.1 0.1 fusion.23
  83.2 0.9 %maximum_select_fusion.1 = f32[1,40,24,128]{3,2,1,0:T(8,128)} fusion(f32[1,40,24,128]{3,2,1,0:T(8,128)S(1)} %get-tuple-element.143, f32[1,1,24,128]{3,2,1,0:T(8,128)S(1)} %slice_bitcast_fusion.45, f32[1,6,24,128]{3,2,1,0:T(8,128)S(1)} %fusion.23, f32[1,12,24,128]{3,2,1,0:T(8,128)S(1)} %slice_bitcast_fusion.42, f32[40]{0:T(128)S(1)} %pad.7.clone, pred[]{:T(512)S(6)} %eq.19), kind=kLoop, calls=%fused_computation.110 | loop fusion | flops 491520 | bytes 1216673 | tf_op jit(solution)/shard_map/jit(_where)/select_n | solution.py:215
  (14 shorter events, 0.2 us)
Async XLA Ops:
  0.0 25.7 %copy-start = (f32[1,40,24,128]{3,2,1,0:T(8,128)S(1)}, f32[1,40,24,128]{3,2,1,0:T(8,128)}, u32[]{:S(2)}) copy-start(f32[1,40,24,128]{3,2,1,0:T(8,128)} %param.8) | copy-start | bytes 1474564
  2.2 17.8 %collective-permute-start = (f32[41,24,7]{2,1,0:T(8,128)S(1)}, f32[41,24,7]{2,1,0:T(8,128)S(1)}, u32[]{:S(2)}, u32[]{:S(2)}) collective-permute-start(f32[41,24,7]{2,1,0:T(8,128)S(1)} %get-tuple-element.243), channel_id=1, source_target_pairs={{0,1},{1,2},{2,3},{3,0},{4,5},{5,6},{6,7},{7,4},{8,9},{9,10},{10,1... | collective-permute-start | bytes 82664 | tf_op jit(solution)/shard_map/ppermute | solution.py:17
  13.6 12.1 %collective-permute-start.1 = (f32[41,24,7]{2,1,0:T(8,128)S(1)}, f32[41,24,7]{2,1,0:T(8,128)S(1)}, u32[]{:S(2)}, u32[]{:S(2)}) collective-permute-start(f32[41,24,7]{2,1,0:T(8,128)S(1)} %get-tuple-element.244), channel_id=1, source_target_pairs={{1,0},{2,1},{3,2},{0,3},{5,4},{6,5},{7,6},{4,7},{9,8},{10,9},{11,1... | collective-permute-start | bytes 82664 | tf_op jit(solution)/shard_map/ppermute | solution.py:20
  26.0 17.4 %collective-permute-start.2 = (f32[41,7,142]{2,1,0:T(8,128)S(1)}, f32[41,7,142]{2,1,0:T(8,128)S(1)}, u32[]{:S(2)}, u32[]{:S(2)}) collective-permute-start(f32[41,7,142]{2,1,0:T(8,128)S(1)} %get-tuple-element.232), channel_id=1, source_target_pairs={{0,4},{4,8},{8,12},{12,16},{16,20},{20,24},{24,28},{28,32},{32,36}... | collective-permute-start | bytes 489056 | tf_op jit(solution)/shard_map/ppermute | solution.py:17
  28.0 16.6 %collective-permute-start.3 = (f32[41,7,142]{2,1,0:T(8,128)S(1)}, f32[41,7,142]{2,1,0:T(8,128)}, u32[]{:S(2)}, u32[]{:S(2)}) collective-permute-start(f32[41,7,142]{2,1,0:T(8,128)S(1)} %get-tuple-element.233), channel_id=1, source_target_pairs={{4,0},{8,4},{12,8},{16,12},{20,16},{24,20},{28,24},{32,28},{36,32}... | collective-permute-start | bytes 489056 | tf_op jit(solution)/shard_map/ppermute | solution.py:20
  50.2 11.5 %copy-start.2 = (f32[20]{0:T(128)S(1)}, f32[20]{0:T(128)}, u32[]{:S(2)}) copy-start(f32[20]{0:T(128)} %param.11) | copy-start | bytes 244
  51.0 8.7 %collective-permute-start.6 = (f32[22224]{0:T(1024)S(1)}, f32[22224]{0:T(1024)S(1)}, u32[]{:S(2)}, u32[]{:S(2)}) collective-permute-start(f32[22224]{0:T(1024)S(1)} %concatenate.42), channel_id=1, source_target_pairs={{0,576},{1,577},{2,578},{3,579},{4,580},{5,581},{6,582},{7,583},{8... | collective-permute-start | bytes 266696 | tf_op jit(solution)/shard_map/ppermute | solution.py:158
  54.9 4.8 %collective-permute-start.5 = (f32[22224]{0:T(1024)S(1)}, f32[22224]{0:T(1024)S(1)}, u32[]{:S(2)}, u32[]{:S(2)}) collective-permute-start(f32[22224]{0:T(1024)S(1)} %concatenate.41), channel_id=1, source_target_pairs={{0,192},{1,193},{2,194},{3,195},{4,196},{5,197},{6,198},{7,199},{8... | collective-permute-start | bytes 266696 | tf_op jit(solution)/shard_map/ppermute | solution.py:158
  56.7 5.0 %collective-permute-start.4 = (f32[22224]{0:T(1024)S(1)}, f32[22224]{0:T(1024)S(1)}, u32[]{:S(2)}, u32[]{:S(2)}) collective-permute-start(f32[22224]{0:T(1024)S(1)} %concatenate.40), channel_id=1, source_target_pairs={{0,384},{1,385},{2,386},{3,387},{4,388},{5,389},{6,390},{7,391},{8... | collective-permute-start | bytes 266696 | tf_op jit(solution)/shard_map/ppermute | solution.py:158
  61.8 6.6 %collective-permute-start.7 = (f32[2,24,128]{2,1,0:T(8,128)S(1)}, f32[2,24,128]{2,1,0:T(8,128)S(1)}, u32[]{:S(2)}, u32[]{:S(2)}) collective-permute-start(f32[2,24,128]{2,1,0:T(8,128)S(1)} %get-tuple-element.142), channel_id=1, source_target_pairs={{192,0},{193,1},{194,2},{195,3},{196,4},{197,5},{198,6},{199,7},{2... | collective-permute-start | bytes 73736 | tf_op jit(solution)/shard_map/ppermute | solution.py:210
  63.1 20.0 %collective-permute-start.8 = (f32[2,24,128]{2,1,0:T(8,128)S(1)}, f32[2,24,128]{2,1,0:T(8,128)S(1)}, u32[]{:S(2)}, u32[]{:S(2)}) collective-permute-start(f32[2,24,128]{2,1,0:T(8,128)S(1)} %get-tuple-element.142), channel_id=1, source_target_pairs={{384,0},{385,1},{386,2},{387,3},{388,4},{389,5},{390,6},{391,7},{3... | collective-permute-start | bytes 73736 | tf_op jit(solution)/shard_map/ppermute | solution.py:210
  64.4 18.7 %collective-permute-start.9 = (f32[2,24,128]{2,1,0:T(8,128)S(1)}, f32[2,24,128]{2,1,0:T(8,128)S(1)}, u32[]{:S(2)}, u32[]{:S(2)}) collective-permute-start(f32[2,24,128]{2,1,0:T(8,128)S(1)} %get-tuple-element.142), channel_id=1, source_target_pairs={{576,0},{577,1},{578,2},{579,3},{580,4},{581,5},{582,6},{583,7},{5... | collective-permute-start | bytes 73736 | tf_op jit(solution)/shard_map/ppermute | solution.py:210

commit v12 on v10

--- a/solution.py
+++ b/solution.py
@@ -2,6 +2,7 @@
 import jax.numpy as jnp
 from jax import lax
 from jax.sharding import PartitionSpec as P
+
 
 LZ = 2
 NTR = 20
@@ -94,7 +95,7 @@
     return jnp.concatenate([results[0], results[1], results[2], results[3][None]], axis=0)
 
 
-def body(state, depth, rates, grazing):
+def step_body(state, depth, rates, grazing):
     groups = lax.axis_size("grp")
     member = lax.axis_index("grp")
     lat_pos = lax.axis_index("lat")
@@ -121,7 +122,7 @@
 
     def dynamics(fields, wet_pad, land_pad, coriolis_pad):
         radius = dyn_halo
-        for section_index in range(SECTIONS):
+        for _ in range(SECTIONS):
             radius -= 1
             cut = dyn_halo - radius
             fields = section_rows(
@@ -170,7 +171,7 @@
     def transport(tracers, own_zonal, own_merid, own_temper, wet_member_pad, rates, grazing):
         advected = tracers.reshape((NTR, LZ) + tracers.shape[1:])
         radius = tracer_halo
-        for sub_index in range(NSUB):
+        for _ in range(NSUB):
             radius -= 1
             advected = advect_tracers(
                 advected,
@@ -219,4 +220,4 @@
 def solution(mesh):
     in_specs = (P("grp", None, "lon", "lat"), P("lon", "lat"), P(), P())
     out_specs = P("grp", None, "lon", "lat")
-    return jax.shard_map(body, mesh=mesh, in_specs=in_specs, out_specs=out_specs, check_vma=False)
+    return jax.shard_map(step_body, mesh=mesh, in_specs=in_specs, out_specs=out_specs, check_vma=False)

time: 77.4 us -> 77.4 us (level)
  no operation moved by 1% of the time
where the time goes in v12:
time: 77.4 us; the launch traced here: 76.9 us
  starting transfers between devices  33.4 us (43%)
  waiting for transfers between devices  28 us (36%)
  other arithmetic  10 us (13%)
  local copies, waits for them, and re-layouts  5.11 us (7%)
    ppermute x3, waiting for transfers between devices, step_body(): returned.append(lax.ppermute(heating, 'grp', pairs))  17.3 us
    ppermute x2, starting transfers between devices, exchange(): lax.ppermute(lax.slice_in_dim(block, 0, width, axis=dim), axis, backward)  16 us
    ppermute x2, starting transfers between devices, exchange(): lax.ppermute(lax.slice_in_dim(block, block.shape[dim] - width, None, axis...  9.4 us
    ppermute x2, waiting for transfers between devices, exchange(): lax.ppermute(lax.slice_in_dim(block, 0, width, axis=dim), axis, backward)  6.75 us
    ppermute x3, starting transfers between devices, step_body(): arrived = lax.ppermute(payload, 'grp', [(0, shift)])  4.1 us
    ppermute x3, starting transfers between devices, step_body(): returned.append(lax.ppermute(heating, 'grp', pairs))  3.88 us
    select_n x1, other arithmetic, exchange(): return jnp.where(lower | upper, 0.0, block)  2.05 us
    ppermute x3, waiting for transfers between devices, step_body(): arrived = lax.ppermute(payload, 'grp', [(0, shift)])  2.01 us
  transfers between devices with their start and end apart: 10, of which 7 were waited for; matrix products, arithmetic and copies ran while one was open for 3% of the time, Pallas kernels for 0%

profile of v12, /device:TPU:6, one launch (start us, length us, event | category | flops | bytes accessed | tf_op | source)
XLA Modules:
  0.0 76.9 jit_solution(8249517921731103403)
XLA Ops:
  0.0 0.7 convert_bitcast_fusion
  0.7 1.0 %pad_maximum_fusion.3 = (f32[41,7,128]{2,1,0:T(8,128)S(1)}, f32[41,7,128]{2,1,0:T(8,128)S(1)}) fusion(f32[1,24,128]{2,1,0:T(8,128)S(1)} %convert_bitcast_fusion, f32[40,24,128]{2,1,0:T(8,128)} %bitcast.116), kind=kLoop, calls=%fused_computation.112 | loop fusion | flops 73472 | bytes 797696 | tf_op jit(solution)/shard_map/slice | solution.py:19
  1.7 3.5 %collective-permute-start = (f32[41,7,128]{2,1,0:T(8,128)S(1)}, f32[41,7,128]{2,1,0:T(8,128)S(1)}, u32[]{:S(2)}, u32[]{:S(2)}) collective-permute-start(f32[41,7,128]{2,1,0:T(8,128)S(1)} %get-tuple-element.265), channel_id=1, source_target_pairs={{0,4},{4,8},{8,12},{12,16},{16,20},{20,24},{24,28},{28,32},{32,36}... | collective-permute-start | bytes 440840 | tf_op jit(solution)/shard_map/ppermute | solution.py:18
  5.2 14.1 %collective-permute-start.1 = (f32[41,7,128]{2,1,0:T(8,128)S(1)}, f32[41,7,128]{2,1,0:T(8,128)S(1)}, u32[]{:S(2)}, u32[]{:S(2)}) collective-permute-start(f32[41,7,128]{2,1,0:T(8,128)S(1)} %get-tuple-element.266), channel_id=1, source_target_pairs={{4,0},{8,4},{12,8},{16,12},{20,16},{24,20},{28,24},{32,28},{36,32}... | collective-permute-start | bytes 440840 | tf_op jit(solution)/shard_map/ppermute | solution.py:21
  19.3 0.5 add_convert_fusion.1
  19.9 1.8 %collective-permute-done = f32[41,7,128]{2,1,0:T(8,128)S(1)} collective-permute-done((f32[41,7,128]{2,1,0:T(8,128)S(1)}, f32[41,7,128]{2,1,0:T(8,128)S(1)}, u32[]{:S(2)}, u32[]{:S(2)}) %collective-permute-start) | collective-permute-done | bytes 146976 | tf_op jit(solution)/shard_map/ppermute | solution.py:18
  21.6 1.2 %collective-permute-done.1 = f32[41,7,128]{2,1,0:T(8,128)S(1)} collective-permute-done((f32[41,7,128]{2,1,0:T(8,128)S(1)}, f32[41,7,128]{2,1,0:T(8,128)S(1)}, u32[]{:S(2)}, u32[]{:S(2)}) %collective-permute-start.1) | collective-permute-done | bytes 146976 | tf_op jit(solution)/shard_map/ppermute | solution.py:21
  22.8 1.1 %pad_maximum_fusion.1 = f32[41,38,128]{2,1,0:T(8,128)S(1)} fusion(f32[41,7,128]{2,1,0:T(8,128)S(1)} %collective-permute-done.1, f32[1,24,128]{2,1,0:T(8,128)S(1)} %convert_bitcast_fusion, f32[40,24,128]{2,1,0:T(8,128)} %bitcast.117, f32[41,7,128]{2,1,0:T(8,128)S(1)} %collective-permute-done), kind=kLoop, calls=%fused_computation.108 | loop fusion | flops 598272 | bytes 1595392 | tf_op jit(solution)/shard_map/concatenate | solution.py:22
  24.0 0.3 fusion.25
  24.2 0.4 copy.17
  24.7 5.9 %collective-permute-start.2 = (f32[41,38,7]{0,1,2:T(8,128)S(1)}, f32[41,38,7]{0,1,2:T(8,128)S(1)}, u32[]{:S(2)}, u32[]{:S(2)}) collective-permute-start(f32[41,38,7]{0,1,2:T(8,128)S(1)} %copy.17), channel_id=1, source_target_pairs={{0,1},{1,2},{2,3},{3,0},{4,5},{5,6},{6,7},{7,4},{8,9},{9,10},{10,1... | collective-permute-start | bytes 130880 | tf_op jit(solution)/shard_map/ppermute | solution.py:18
  30.6 0.0 copy-start
  30.6 0.4 copy.18
  31.0 1.9 %collective-permute-start.3 = (f32[41,38,7]{0,1,2:T(8,128)S(1)}, f32[41,38,7]{0,1,2:T(8,128)S(1)}, u32[]{:S(2)}, u32[]{:S(2)}) collective-permute-start(f32[41,38,7]{0,1,2:T(8,128)S(1)} %copy.18), channel_id=1, source_target_pairs={{1,0},{2,1},{3,2},{0,3},{5,4},{6,5},{7,6},{4,7},{9,8},{10,9},{11,1... | collective-permute-start | bytes 130880 | tf_op jit(solution)/shard_map/ppermute | solution.py:21
  33.0 0.1 pad.7.clone
  33.1 0.1 collective-permute-done.2
  33.2 0.5 copy.19
  33.7 5.6 %collective-permute-done.3 = f32[41,38,7]{0,1,2:T(8,128)S(1)} collective-permute-done((f32[41,38,7]{0,1,2:T(8,128)S(1)}, f32[41,38,7]{0,1,2:T(8,128)S(1)}, u32[]{:S(2)}, u32[]{:S(2)}) %collective-permute-start.3) | collective-permute-done | bytes 43656 | tf_op jit(solution)/shard_map/ppermute | solution.py:21
  39.3 1.4 %copy.20 = f32[41,38,7]{2,1,0:T(8,128)} copy(f32[41,38,7]{0,1,2:T(8,128)S(1)} %collective-permute-done.3) | data formatting | bytes 87248 | tf_op jit(solution)/shard_map/ppermute | solution.py:21
  40.6 2.1 %maximum_select_fusion = f32[41,38,142]{2,1,0:T(8,128)S(1)} fusion(f32[41,38,7]{2,1,0:T(8,128)} %copy.20, f32[41,7,128]{2,1,0:T(8,128)S(1)} %collective-permute-done.1, f32[1,24,128]{2,1,0:T(8,128)S(1)} %convert_bitcast_fusion, f32[40,24,128]{2,1,0:T(8,128)S(1)} %bitcast.118, f32[41,7,128]{2,1,0:T(8,128)S(1)} %collective-permute-done, ...), kind=kLoop, calls=%fused_computation.107 | loop fusion | flops 1327416 | bytes 1770030 | tf_op jit(solution)/shard_map/jit(_where)/select_n | solution.py:27
  42.7 0.1 compare_convert_fusion
  42.8 3.8 %conditional.2 = (f32[19,30,134]{2,1,0:T(8,128)S(1)}) conditional(s32[]{:T(128)} %convert_element_type.40, () %tuple.43, (f32[6,38,142]{2,1,0:T(8,128)S(1)}, f32[41,38,142]{2,1,0:T(8,128)S(1)}, f32[142]{0:T(256)S(1)}, f32[38,142]{1,0:T(8,128)S(1)}) %tuple.44), branch_computations={%region_0.1_spmd, %region_1.6_spmd} | conditional | flops 3271180 | bytes 8120776 | solution.py:139
  42.8 0.3 add_reduce_fusion
  43.1 0.1 fusion.11
  43.3 0.1 slice.677
  43.3 0.5 subtract_multiply_fusion.3
  43.9 0.3 fusion.1
  44.1 0.1 fusion.8
  44.3 0.1 slice.683
  44.3 0.5 subtract_multiply_fusion.1
  44.9 0.2 fusion.5
  45.1 0.1 fusion.18
  45.2 0.1 slice.696
  45.3 0.4 subtract_multiply_fusion.7
  45.7 0.2 fusion.3
  46.0 0.1 fusion.15
  46.1 0.1 slice.709
  46.1 0.4 subtract_multiply_fusion.5
  46.6 0.1 pad_maximum_fusion
  46.6 0.0 copy-start.2
  46.7 0.1 fusion.26
  46.8 0.1 slice_bitcast_fusion.42
  46.9 0.2 reshape.137
  47.1 0.2 reshape.138
  47.3 0.1 concatenate.42
  47.4 1.3 %collective-permute-start.6 = (f32[22224]{0:T(1024)S(1)}, f32[22224]{0:T(1024)S(1)}, u32[]{:S(2)}, u32[]{:S(2)}) collective-permute-start(f32[22224]{0:T(1024)S(1)} %concatenate.42), channel_id=1, source_target_pairs={{0,576},{1,577},{2,578},{3,579},{4,580},{5,581},{6,582},{7,583},{8... | collective-permute-start | bytes 266696 | tf_op jit(solution)/shard_map/ppermute | solution.py:159
  48.7 0.2 reshape.134
  48.9 0.2 reshape.135
  49.1 0.1 concatenate.41
  49.2 1.3 %collective-permute-start.5 = (f32[22224]{0:T(1024)S(1)}, f32[22224]{0:T(1024)S(1)}, u32[]{:S(2)}, u32[]{:S(2)}) collective-permute-start(f32[22224]{0:T(1024)S(1)} %concatenate.41), channel_id=1, source_target_pairs={{0,192},{1,193},{2,194},{3,195},{4,196},{5,197},{6,198},{7,199},{8... | collective-permute-start | bytes 266696 | tf_op jit(solution)/shard_map/ppermute | solution.py:159
  50.5 0.2 reshape.131
  50.7 0.2 reshape.132
  50.9 0.1 concatenate.40
  51.0 1.5 %collective-permute-start.4 = (f32[22224]{0:T(1024)S(1)}, f32[22224]{0:T(1024)S(1)}, u32[]{:S(2)}, u32[]{:S(2)}) collective-permute-start(f32[22224]{0:T(1024)S(1)} %concatenate.40), channel_id=1, source_target_pairs={{0,384},{1,385},{2,386},{3,387},{4,388},{5,389},{6,390},{7,391},{8... | collective-permute-start | bytes 266696 | tf_op jit(solution)/shard_map/ppermute | solution.py:159
  52.5 0.1 compare_convert_fusion.1
  52.6 2.0 %collective-permute-done.4 = f32[22224]{0:T(1024)S(1)} collective-permute-done((f32[22224]{0:T(1024)S(1)}, f32[22224]{0:T(1024)S(1)}, u32[]{:S(2)}, u32[]{:S(2)}) %collective-permute-start.4) | collective-permute-done | bytes 88928 | tf_op jit(solution)/shard_map/ppermute | solution.py:159
  54.7 1.3 %collective-permute-start.7 = (f32[2,24,128]{2,1,0:T(8,128)S(1)}, f32[2,24,128]{2,1,0:T(8,128)S(1)}, u32[]{:S(2)}, u32[]{:S(2)}) collective-permute-start(f32[2,24,128]{2,1,0:T(8,128)S(1)} %get-tuple-element.142), channel_id=1, source_target_pairs={{192,0},{193,1},{194,2},{195,3},{196,4},{197,5},{198,6},{199,7},{2... | collective-permute-start | bytes 73736 | tf_op jit(solution)/shard_map/ppermute | solution.py:211
  56.0 1.3 %collective-permute-start.8 = (f32[2,24,128]{2,1,0:T(8,128)S(1)}, f32[2,24,128]{2,1,0:T(8,128)S(1)}, u32[]{:S(2)}, u32[]{:S(2)}) collective-permute-start(f32[2,24,128]{2,1,0:T(8,128)S(1)} %get-tuple-element.142), channel_id=1, source_target_pairs={{384,0},{385,1},{386,2},{387,3},{388,4},{389,5},{390,6},{391,7},{3... | collective-permute-start | bytes 73736 | tf_op jit(solution)/shard_map/ppermute | solution.py:211
  57.3 1.3 %collective-permute-start.9 = (f32[2,24,128]{2,1,0:T(8,128)S(1)}, f32[2,24,128]{2,1,0:T(8,128)S(1)}, u32[]{:S(2)}, u32[]{:S(2)}) collective-permute-start(f32[2,24,128]{2,1,0:T(8,128)S(1)} %get-tuple-element.142), channel_id=1, source_target_pairs={{576,0},{577,1},{578,2},{579,3},{580,4},{581,5},{582,6},{583,7},{5... | collective-permute-start | bytes 73736 | tf_op jit(solution)/shard_map/ppermute | solution.py:211
  58.6 0.1 slice_bitcast_fusion.45
  58.6 4.0 %collective-permute-done.7 = f32[2,24,128]{2,1,0:T(8,128)S(1)} collective-permute-done((f32[2,24,128]{2,1,0:T(8,128)S(1)}, f32[2,24,128]{2,1,0:T(8,128)S(1)}, u32[]{:S(2)}, u32[]{:S(2)}) %collective-permute-start.7) | collective-permute-done | bytes 24608 | tf_op jit(solution)/shard_map/ppermute | solution.py:211
  62.6 13.3 %collective-permute-done.8 = f32[2,24,128]{2,1,0:T(8,128)S(1)} collective-permute-done((f32[2,24,128]{2,1,0:T(8,128)S(1)}, f32[2,24,128]{2,1,0:T(8,128)S(1)}, u32[]{:S(2)}, u32[]{:S(2)}) %collective-permute-start.8) | collective-permute-done | bytes 24608 | tf_op jit(solution)/shard_map/ppermute | solution.py:211
  76.0 0.1 fusion.23
  76.1 0.9 %maximum_select_fusion.1 = f32[1,40,24,128]{3,2,1,0:T(8,128)} fusion(f32[1,40,24,128]{3,2,1,0:T(8,128)S(1)} %get-tuple-element.143, f32[1,1,24,128]{3,2,1,0:T(8,128)S(1)} %slice_bitcast_fusion.45, f32[1,6,24,128]{3,2,1,0:T(8,128)S(1)} %fusion.23, f32[1,12,24,128]{3,2,1,0:T(8,128)S(1)} %slice_bitcast_fusion.42, f32[40]{0:T(128)S(1)} %pad.7.clone, pred[]{:T(512)S(6)} %eq.19), kind=kLoop, calls=%fused_computation.109 | loop fusion | flops 491520 | bytes 1216673 | tf_op jit(solution)/shard_map/jit(_where)/select_n | solution.py:216
  (19 shorter events, 0.2 us)
Async XLA Ops:
  1.7 19.9 %collective-permute-start = (f32[41,7,128]{2,1,0:T(8,128)S(1)}, f32[41,7,128]{2,1,0:T(8,128)S(1)}, u32[]{:S(2)}, u32[]{:S(2)}) collective-permute-start(f32[41,7,128]{2,1,0:T(8,128)S(1)} %get-tuple-element.265), channel_id=1, source_target_pairs={{0,4},{4,8},{8,12},{12,16},{16,20},{20,24},{24,28},{28,32},{32,36}... | collective-permute-start | bytes 440840 | tf_op jit(solution)/shard_map/ppermute | solution.py:18
  5.2 17.6 %collective-permute-start.1 = (f32[41,7,128]{2,1,0:T(8,128)S(1)}, f32[41,7,128]{2,1,0:T(8,128)S(1)}, u32[]{:S(2)}, u32[]{:S(2)}) collective-permute-start(f32[41,7,128]{2,1,0:T(8,128)S(1)} %get-tuple-element.266), channel_id=1, source_target_pairs={{4,0},{8,4},{12,8},{16,12},{20,16},{24,20},{28,24},{32,28},{36,32}... | collective-permute-start | bytes 440840 | tf_op jit(solution)/shard_map/ppermute | solution.py:21
  24.7 8.5 %collective-permute-start.2 = (f32[41,38,7]{0,1,2:T(8,128)S(1)}, f32[41,38,7]{0,1,2:T(8,128)S(1)}, u32[]{:S(2)}, u32[]{:S(2)}) collective-permute-start(f32[41,38,7]{0,1,2:T(8,128)S(1)} %copy.17), channel_id=1, source_target_pairs={{0,1},{1,2},{2,3},{3,0},{4,5},{5,6},{6,7},{7,4},{8,9},{9,10},{10,1... | collective-permute-start | bytes 130880 | tf_op jit(solution)/shard_map/ppermute | solution.py:18
  30.6 10.0 %copy-start = (f32[1,40,24,128]{3,2,1,0:T(8,128)S(1)}, f32[1,40,24,128]{3,2,1,0:T(8,128)}, u32[]{:S(2)}) copy-start(f32[1,40,24,128]{3,2,1,0:T(8,128)} %param.8) | copy-start | bytes 1474564
  31.0 8.2 %collective-permute-start.3 = (f32[41,38,7]{0,1,2:T(8,128)S(1)}, f32[41,38,7]{0,1,2:T(8,128)S(1)}, u32[]{:S(2)}, u32[]{:S(2)}) collective-permute-start(f32[41,38,7]{0,1,2:T(8,128)S(1)} %copy.18), channel_id=1, source_target_pairs={{1,0},{2,1},{3,2},{0,3},{5,4},{6,5},{7,6},{4,7},{9,8},{10,9},{11,1... | collective-permute-start | bytes 130880 | tf_op jit(solution)/shard_map/ppermute | solution.py:21
  46.6 8.0 %copy-start.2 = (f32[20]{0:T(128)S(1)}, f32[20]{0:T(128)}, u32[]{:S(2)}) copy-start(f32[20]{0:T(128)} %param.11) | copy-start | bytes 244
  47.4 5.2 %collective-permute-start.6 = (f32[22224]{0:T(1024)S(1)}, f32[22224]{0:T(1024)S(1)}, u32[]{:S(2)}, u32[]{:S(2)}) collective-permute-start(f32[22224]{0:T(1024)S(1)} %concatenate.42), channel_id=1, source_target_pairs={{0,576},{1,577},{2,578},{3,579},{4,580},{5,581},{6,582},{7,583},{8... | collective-permute-start | bytes 266696 | tf_op jit(solution)/shard_map/ppermute | solution.py:159
  49.2 3.4 %collective-permute-start.5 = (f32[22224]{0:T(1024)S(1)}, f32[22224]{0:T(1024)S(1)}, u32[]{:S(2)}, u32[]{:S(2)}) collective-permute-start(f32[22224]{0:T(1024)S(1)} %concatenate.41), channel_id=1, source_target_pairs={{0,192},{1,193},{2,194},{3,195},{4,196},{5,197},{6,198},{7,199},{8... | collective-permute-start | bytes 266696 | tf_op jit(solution)/shard_map/ppermute | solution.py:159
  51.0 3.6 %collective-permute-start.4 = (f32[22224]{0:T(1024)S(1)}, f32[22224]{0:T(1024)S(1)}, u32[]{:S(2)}, u32[]{:S(2)}) collective-permute-start(f32[22224]{0:T(1024)S(1)} %concatenate.40), channel_id=1, source_target_pairs={{0,384},{1,385},{2,386},{3,387},{4,388},{5,389},{6,390},{7,391},{8... | collective-permute-start | bytes 266696 | tf_op jit(solution)/shard_map/ppermute | solution.py:159
  54.7 7.9 %collective-permute-start.7 = (f32[2,24,128]{2,1,0:T(8,128)S(1)}, f32[2,24,128]{2,1,0:T(8,128)S(1)}, u32[]{:S(2)}, u32[]{:S(2)}) collective-permute-start(f32[2,24,128]{2,1,0:T(8,128)S(1)} %get-tuple-element.142), channel_id=1, source_target_pairs={{192,0},{193,1},{194,2},{195,3},{196,4},{197,5},{198,6},{199,7},{2... | collective-permute-start | bytes 73736 | tf_op jit(solution)/shard_map/ppermute | solution.py:211
  56.0 20.0 %collective-permute-start.8 = (f32[2,24,128]{2,1,0:T(8,128)S(1)}, f32[2,24,128]{2,1,0:T(8,128)S(1)}, u32[]{:S(2)}, u32[]{:S(2)}) collective-permute-start(f32[2,24,128]{2,1,0:T(8,128)S(1)} %get-tuple-element.142), channel_id=1, source_target_pairs={{384,0},{385,1},{386,2},{387,3},{388,4},{389,5},{390,6},{391,7},{3... | collective-permute-start | bytes 73736 | tf_op jit(solution)/shard_map/ppermute | solution.py:211
  57.3 18.7 %collective-permute-start.9 = (f32[2,24,128]{2,1,0:T(8,128)S(1)}, f32[2,24,128]{2,1,0:T(8,128)S(1)}, u32[]{:S(2)}, u32[]{:S(2)}) collective-permute-start(f32[2,24,128]{2,1,0:T(8,128)S(1)} %get-tuple-element.142), channel_id=1, source_target_pairs={{576,0},{577,1},{578,2},{579,3},{580,4},{581,5},{582,6},{583,7},{5... | collective-permute-start | bytes 73736 | tf_op jit(solution)/shard_map/ppermute | solution.py:211

commit v13 on v10

--- a/solution.py
+++ b/solution.py
@@ -209,10 +209,17 @@
         pairs = [(shift, 0)]
         returned.append(lax.ppermute(heating, "grp", pairs))
     returned = jnp.concatenate(returned, axis=0)
-    temper_final = temper + returned
-    unused = jnp.zeros((field_rows - dyn_rows, columns, lat_rows), jnp.float32)
-    dyn_out = jnp.concatenate([zonal, merid, temper_final, surface[None], unused], axis=0)
-    result = jnp.where(member == 0, dyn_out, updated.reshape(field_rows, columns, lat_rows))
+
+    def dynamics_out(zonal, merid, temper, surface, returned, updated):
+        unused = jnp.zeros((field_rows - dyn_rows, columns, lat_rows), jnp.float32)
+        return jnp.concatenate([zonal, merid, temper + returned, surface[None], unused], axis=0)
+
+    def tracer_out(zonal, merid, temper, surface, returned, updated):
+        return updated.reshape(field_rows, columns, lat_rows)
+
+    result = lax.cond(
+        member == 0, dynamics_out, tracer_out, zonal, merid, temper, surface, returned, updated
+    )
     return result[None]
 
 

time: 77.4 us -> 77.5 us (level)
  other arithmetic: 10 us -> 8.76 us
    select_n x1 -> x0, other arithmetic: 0.89 us -> none  [body(): jnp.where(member == 0, dyn_out, updated.reshape(field_rows, columns, lat_...]
    unnamed x4 -> x8, local copies, waits for them, and re-layouts: 0.01 us -> 0.79 us
where the time goes in v13:
time: 77.5 us; the launch traced here: 77.1 us
  starting transfers between devices  33.4 us (43%)
  waiting for transfers between devices  28.6 us (37%)
  other arithmetic  8.76 us (11%)
  local copies, waits for them, and re-layouts  5.88 us (8%)
    ppermute x3, waiting for transfers between devices, body(): returned.append(lax.ppermute(heating, 'grp', pairs))  17.3 us
    ppermute x2, starting transfers between devices, exchange(): lax.ppermute(lax.slice_in_dim(block, 0, width, axis=dim), axis, backward)  16 us
    ppermute x2, starting transfers between devices, exchange(): lax.ppermute(lax.slice_in_dim(block, block.shape[dim] - width, None, axis...  9.4 us
    ppermute x2, waiting for transfers between devices, exchange(): lax.ppermute(lax.slice_in_dim(block, 0, width, axis=dim), axis, backward)  6.75 us
    ppermute x3, starting transfers between devices, body(): arrived = lax.ppermute(payload, 'grp', [(0, shift)])  4.11 us
    ppermute x3, starting transfers between devices, body(): returned.append(lax.ppermute(heating, 'grp', pairs))  3.88 us
    ppermute x2, waiting for transfers between devices, exchange(): lax.ppermute(lax.slice_in_dim(block, block.shape[dim] - width, None, axis...  2.5 us
    select_n x1, other arithmetic, exchange(): return jnp.where(lower | upper, 0.0, block)  2.05 us
  transfers between devices with their start and end apart: 10, of which 7 were waited for; matrix products, arithmetic and copies ran while one was open for 3% of the time, Pallas kernels for 0%

profile of v13, /device:TPU:6, one launch (start us, length us, event | category | flops | bytes accessed | tf_op | source)
XLA Modules:
  0.0 77.1 jit_solution(14065372821568501702)
XLA Ops:
  0.0 0.7 convert_bitcast_fusion
  0.7 1.0 %pad_maximum_fusion.3 = (f32[41,7,128]{2,1,0:T(8,128)S(1)}, f32[41,7,128]{2,1,0:T(8,128)S(1)}) fusion(f32[1,24,128]{2,1,0:T(8,128)S(1)} %convert_bitcast_fusion, f32[40,24,128]{2,1,0:T(8,128)} %bitcast.114), kind=kLoop, calls=%fused_computation.115 | loop fusion | flops 73472 | bytes 797696 | tf_op jit(solution)/shard_map/slice | solution.py:18
  1.7 3.5 %collective-permute-start = (f32[41,7,128]{2,1,0:T(8,128)S(1)}, f32[41,7,128]{2,1,0:T(8,128)S(1)}, u32[]{:S(2)}, u32[]{:S(2)}) collective-permute-start(f32[41,7,128]{2,1,0:T(8,128)S(1)} %get-tuple-element.286), channel_id=1, source_target_pairs={{0,4},{4,8},{8,12},{12,16},{16,20},{20,24},{24,28},{28,32},{32,36}... | collective-permute-start | bytes 440840 | tf_op jit(solution)/shard_map/ppermute | solution.py:17
  5.2 14.1 %collective-permute-start.1 = (f32[41,7,128]{2,1,0:T(8,128)S(1)}, f32[41,7,128]{2,1,0:T(8,128)S(1)}, u32[]{:S(2)}, u32[]{:S(2)}) collective-permute-start(f32[41,7,128]{2,1,0:T(8,128)S(1)} %get-tuple-element.287), channel_id=1, source_target_pairs={{4,0},{8,4},{12,8},{16,12},{20,16},{24,20},{28,24},{32,28},{36,32}... | collective-permute-start | bytes 440840 | tf_op jit(solution)/shard_map/ppermute | solution.py:20
  19.4 2.3 %collective-permute-done = f32[41,7,128]{2,1,0:T(8,128)S(1)} collective-permute-done((f32[41,7,128]{2,1,0:T(8,128)S(1)}, f32[41,7,128]{2,1,0:T(8,128)S(1)}, u32[]{:S(2)}, u32[]{:S(2)}) %collective-permute-start) | collective-permute-done | bytes 146976 | tf_op jit(solution)/shard_map/ppermute | solution.py:17
  21.6 1.2 %collective-permute-done.1 = f32[41,7,128]{2,1,0:T(8,128)S(1)} collective-permute-done((f32[41,7,128]{2,1,0:T(8,128)S(1)}, f32[41,7,128]{2,1,0:T(8,128)S(1)}, u32[]{:S(2)}, u32[]{:S(2)}) %collective-permute-start.1) | collective-permute-done | bytes 146976 | tf_op jit(solution)/shard_map/ppermute | solution.py:20
  22.8 1.1 %pad_maximum_fusion.1 = f32[41,38,128]{2,1,0:T(8,128)S(1)} fusion(f32[41,7,128]{2,1,0:T(8,128)S(1)} %collective-permute-done.1, f32[1,24,128]{2,1,0:T(8,128)S(1)} %convert_bitcast_fusion, f32[40,24,128]{2,1,0:T(8,128)} %bitcast.115, f32[41,7,128]{2,1,0:T(8,128)S(1)} %collective-permute-done), kind=kLoop, calls=%fused_computation.112 | loop fusion | flops 598272 | bytes 1595392 | tf_op jit(solution)/shard_map/concatenate | solution.py:21
  24.0 0.3 fusion.24
  24.2 0.4 copy.19
  24.7 5.9 %collective-permute-start.2 = (f32[41,38,7]{0,1,2:T(8,128)S(1)}, f32[41,38,7]{0,1,2:T(8,128)S(1)}, u32[]{:S(2)}, u32[]{:S(2)}) collective-permute-start(f32[41,38,7]{0,1,2:T(8,128)S(1)} %copy.19), channel_id=1, source_target_pairs={{0,1},{1,2},{2,3},{3,0},{4,5},{5,6},{6,7},{7,4},{8,9},{9,10},{10,1... | collective-permute-start | bytes 130880 | tf_op jit(solution)/shard_map/ppermute | solution.py:17
  30.6 0.0 copy-start
  30.6 0.4 copy.20
  31.0 1.9 %collective-permute-start.3 = (f32[41,38,7]{0,1,2:T(8,128)S(1)}, f32[41,38,7]{0,1,2:T(8,128)S(1)}, u32[]{:S(2)}, u32[]{:S(2)}) collective-permute-start(f32[41,38,7]{0,1,2:T(8,128)S(1)} %copy.20), channel_id=1, source_target_pairs={{1,0},{2,1},{3,2},{0,3},{5,4},{6,5},{7,6},{4,7},{9,8},{10,9},{11,1... | collective-permute-start | bytes 130880 | tf_op jit(solution)/shard_map/ppermute | solution.py:20
  33.0 0.2 collective-permute-done.2
  33.2 0.5 copy.21
  33.7 5.6 %collective-permute-done.3 = f32[41,38,7]{0,1,2:T(8,128)S(1)} collective-permute-done((f32[41,38,7]{0,1,2:T(8,128)S(1)}, f32[41,38,7]{0,1,2:T(8,128)S(1)}, u32[]{:S(2)}, u32[]{:S(2)}) %collective-permute-start.3) | collective-permute-done | bytes 43656 | tf_op jit(solution)/shard_map/ppermute | solution.py:20
  39.3 1.3 %copy.22 = f32[41,38,7]{2,1,0:T(8,128)} copy(f32[41,38,7]{0,1,2:T(8,128)S(1)} %collective-permute-done.3) | data formatting | bytes 87248 | tf_op jit(solution)/shard_map/ppermute | solution.py:20
  40.6 2.1 %maximum_select_fusion = f32[41,38,142]{2,1,0:T(8,128)S(1)} fusion(f32[41,38,7]{2,1,0:T(8,128)} %copy.22, f32[41,7,128]{2,1,0:T(8,128)S(1)} %collective-permute-done.1, f32[1,24,128]{2,1,0:T(8,128)S(1)} %convert_bitcast_fusion, f32[40,24,128]{2,1,0:T(8,128)S(1)} %bitcast.116, f32[41,7,128]{2,1,0:T(8,128)S(1)} %collective-permute-done, ...), kind=kLoop, calls=%fused_computation.111 | loop fusion | flops 1327416 | bytes 1770030 | tf_op jit(solution)/shard_map/jit(_where)/select_n | solution.py:26
  42.7 0.1 compare_convert_fusion
  42.8 3.8 %conditional.3 = (f32[19,30,134]{2,1,0:T(8,128)S(1)}) conditional(s32[]{:T(128)} %convert_element_type.41, () %tuple.55, (f32[6,38,142]{2,1,0:T(8,128)S(1)}, f32[41,38,142]{2,1,0:T(8,128)S(1)}, f32[142]{0:T(256)S(1)}, f32[38,142]{1,0:T(8,128)S(1)}) %tuple.56), branch_computations={%region_0.1_spmd, %region_1.6_spmd} | conditional | flops 3271180 | bytes 8120776 | solution.py:138
  42.8 0.3 add_reduce_fusion
  43.1 0.1 fusion.11
  43.3 0.1 slice.682
  43.3 0.5 subtract_multiply_fusion.3
  43.9 0.3 fusion.1
  44.1 0.1 fusion.8
  44.3 0.1 slice.688
  44.3 0.5 subtract_multiply_fusion.1
  44.9 0.2 fusion.5
  45.1 0.1 fusion.18
  45.2 0.1 slice.701
  45.3 0.4 subtract_multiply_fusion.7
  45.7 0.2 fusion.3
  45.9 0.1 fusion.15
  46.1 0.1 slice.714
  46.1 0.4 subtract_multiply_fusion.5
  46.6 0.1 pad_maximum_fusion
  46.7 0.1 fusion.25
  46.8 0.2 reshape.124
  47.0 0.2 reshape.125
  47.2 0.1 concatenate.33
  47.3 1.3 %collective-permute-start.6 = (f32[22224]{0:T(1024)S(1)}, f32[22224]{0:T(1024)S(1)}, u32[]{:S(2)}, u32[]{:S(2)}) collective-permute-start(f32[22224]{0:T(1024)S(1)} %concatenate.33), channel_id=1, source_target_pairs={{0,576},{1,577},{2,578},{3,579},{4,580},{5,581},{6,582},{7,583},{8... | collective-permute-start | bytes 266696 | tf_op jit(solution)/shard_map/ppermute | solution.py:158
  48.6 0.2 reshape.121
  48.8 0.2 reshape.122
  49.0 0.1 concatenate.32
  49.1 1.3 %collective-permute-start.5 = (f32[22224]{0:T(1024)S(1)}, f32[22224]{0:T(1024)S(1)}, u32[]{:S(2)}, u32[]{:S(2)}) collective-permute-start(f32[22224]{0:T(1024)S(1)} %concatenate.32), channel_id=1, source_target_pairs={{0,192},{1,193},{2,194},{3,195},{4,196},{5,197},{6,198},{7,199},{8... | collective-permute-start | bytes 266696 | tf_op jit(solution)/shard_map/ppermute | solution.py:158
  50.4 0.2 reshape.118
  50.6 0.2 reshape.119
  50.8 0.1 concatenate.31
  50.9 1.5 %collective-permute-start.4 = (f32[22224]{0:T(1024)S(1)}, f32[22224]{0:T(1024)S(1)}, u32[]{:S(2)}, u32[]{:S(2)}) collective-permute-start(f32[22224]{0:T(1024)S(1)} %concatenate.31), channel_id=1, source_target_pairs={{0,384},{1,385},{2,386},{3,387},{4,388},{5,389},{6,390},{7,391},{8... | collective-permute-start | bytes 266696 | tf_op jit(solution)/shard_map/ppermute | solution.py:158
  52.4 0.1 compare_convert_fusion.1
  52.5 2.0 %collective-permute-done.4 = f32[22224]{0:T(1024)S(1)} collective-permute-done((f32[22224]{0:T(1024)S(1)}, f32[22224]{0:T(1024)S(1)}, u32[]{:S(2)}, u32[]{:S(2)}) %collective-permute-start.4) | collective-permute-done | bytes 88928 | tf_op jit(solution)/shard_map/ppermute | solution.py:158
  54.6 1.3 %collective-permute-start.7 = (f32[2,24,128]{2,1,0:T(8,128)S(1)}, f32[2,24,128]{2,1,0:T(8,128)S(1)}, u32[]{:S(2)}, u32[]{:S(2)}) collective-permute-start(f32[2,24,128]{2,1,0:T(8,128)S(1)} %get-tuple-element.163), channel_id=1, source_target_pairs={{192,0},{193,1},{194,2},{195,3},{196,4},{197,5},{198,6},{199,7},{2... | collective-permute-start | bytes 73736 | tf_op jit(solution)/shard_map/ppermute | solution.py:210
  55.9 1.3 %collective-permute-start.8 = (f32[2,24,128]{2,1,0:T(8,128)S(1)}, f32[2,24,128]{2,1,0:T(8,128)S(1)}, u32[]{:S(2)}, u32[]{:S(2)}) collective-permute-start(f32[2,24,128]{2,1,0:T(8,128)S(1)} %get-tuple-element.163), channel_id=1, source_target_pairs={{384,0},{385,1},{386,2},{387,3},{388,4},{389,5},{390,6},{391,7},{3... | collective-permute-start | bytes 73736 | tf_op jit(solution)/shard_map/ppermute | solution.py:210
  57.2 1.3 %collective-permute-start.9 = (f32[2,24,128]{2,1,0:T(8,128)S(1)}, f32[2,24,128]{2,1,0:T(8,128)S(1)}, u32[]{:S(2)}, u32[]{:S(2)}) collective-permute-start(f32[2,24,128]{2,1,0:T(8,128)S(1)} %get-tuple-element.163), channel_id=1, source_target_pairs={{576,0},{577,1},{578,2},{579,3},{580,4},{581,5},{582,6},{583,7},{5... | collective-permute-start | bytes 73736 | tf_op jit(solution)/shard_map/ppermute | solution.py:210
  58.5 4.2 %collective-permute-done.7 = f32[2,24,128]{2,1,0:T(8,128)S(1)} collective-permute-done((f32[2,24,128]{2,1,0:T(8,128)S(1)}, f32[2,24,128]{2,1,0:T(8,128)S(1)}, u32[]{:S(2)}, u32[]{:S(2)}) %collective-permute-start.7) | collective-permute-done | bytes 24608 | tf_op jit(solution)/shard_map/ppermute | solution.py:210
  62.6 13.1 %collective-permute-done.8 = f32[2,24,128]{2,1,0:T(8,128)S(1)} collective-permute-done((f32[2,24,128]{2,1,0:T(8,128)S(1)}, f32[2,24,128]{2,1,0:T(8,128)S(1)}, u32[]{:S(2)}, u32[]{:S(2)}) %collective-permute-start.8) | collective-permute-done | bytes 24608 | tf_op jit(solution)/shard_map/ppermute | solution.py:210
  75.8 0.5 conditional.5
  75.8 0.1 slice.862
  75.9 0.1 slice_add_fusion
  76.0 0.1 slice_bitcast_fusion.43
  76.1 0.1 pad.7.clone
  76.2 0.1 maximum_bitcast_fusion
  76.3 0.8 copy-done.1
  (25 shorter events, 0.2 us)
Async XLA Ops:
  1.7 19.9 %collective-permute-start = (f32[41,7,128]{2,1,0:T(8,128)S(1)}, f32[41,7,128]{2,1,0:T(8,128)S(1)}, u32[]{:S(2)}, u32[]{:S(2)}) collective-permute-start(f32[41,7,128]{2,1,0:T(8,128)S(1)} %get-tuple-element.286), channel_id=1, source_target_pairs={{0,4},{4,8},{8,12},{12,16},{16,20},{20,24},{24,28},{28,32},{32,36}... | collective-permute-start | bytes 440840 | tf_op jit(solution)/shard_map/ppermute | solution.py:17
  5.2 17.6 %collective-permute-start.1 = (f32[41,7,128]{2,1,0:T(8,128)S(1)}, f32[41,7,128]{2,1,0:T(8,128)S(1)}, u32[]{:S(2)}, u32[]{:S(2)}) collective-permute-start(f32[41,7,128]{2,1,0:T(8,128)S(1)} %get-tuple-element.287), channel_id=1, source_target_pairs={{4,0},{8,4},{12,8},{16,12},{20,16},{24,20},{28,24},{32,28},{36,32}... | collective-permute-start | bytes 440840 | tf_op jit(solution)/shard_map/ppermute | solution.py:20
  24.7 8.5 %collective-permute-start.2 = (f32[41,38,7]{0,1,2:T(8,128)S(1)}, f32[41,38,7]{0,1,2:T(8,128)S(1)}, u32[]{:S(2)}, u32[]{:S(2)}) collective-permute-start(f32[41,38,7]{0,1,2:T(8,128)S(1)} %copy.19), channel_id=1, source_target_pairs={{0,1},{1,2},{2,3},{3,0},{4,5},{5,6},{6,7},{7,4},{8,9},{9,10},{10,1... | collective-permute-start | bytes 130880 | tf_op jit(solution)/shard_map/ppermute | solution.py:17
  30.6 10.0 %copy-start = (f32[1,40,24,128]{3,2,1,0:T(8,128)S(1)}, f32[1,40,24,128]{3,2,1,0:T(8,128)}, u32[]{:S(2)}) copy-start(f32[1,40,24,128]{3,2,1,0:T(8,128)} %param.10) | copy-start | bytes 1474564
  31.0 8.2 %collective-permute-start.3 = (f32[41,38,7]{0,1,2:T(8,128)S(1)}, f32[41,38,7]{0,1,2:T(8,128)S(1)}, u32[]{:S(2)}, u32[]{:S(2)}) collective-permute-start(f32[41,38,7]{0,1,2:T(8,128)S(1)} %copy.20), channel_id=1, source_target_pairs={{1,0},{2,1},{3,2},{0,3},{5,4},{6,5},{7,6},{4,7},{9,8},{10,9},{11,1... | collective-permute-start | bytes 130880 | tf_op jit(solution)/shard_map/ppermute | solution.py:20
  46.6 7.9 %copy-start.2 = (f32[20,20]{1,0:T(8,128)S(1)}, f32[20,20]{1,0:T(8,128)}, u32[]{:S(2)}) copy-start(f32[20,20]{1,0:T(8,128)} %param.12) | copy-start | bytes 4804
  46.6 7.9 %copy-start.3 = (f32[20]{0:T(128)S(1)}, f32[20]{0:T(128)}, u32[]{:S(2)}) copy-start(f32[20]{0:T(128)} %param.13) | copy-start | bytes 244
  47.3 5.2 %collective-permute-start.6 = (f32[22224]{0:T(1024)S(1)}, f32[22224]{0:T(1024)S(1)}, u32[]{:S(2)}, u32[]{:S(2)}) collective-permute-start(f32[22224]{0:T(1024)S(1)} %concatenate.33), channel_id=1, source_target_pairs={{0,576},{1,577},{2,578},{3,579},{4,580},{5,581},{6,582},{7,583},{8... | collective-permute-start | bytes 266696 | tf_op jit(solution)/shard_map/ppermute | solution.py:158
  49.1 3.4 %collective-permute-start.5 = (f32[22224]{0:T(1024)S(1)}, f32[22224]{0:T(1024)S(1)}, u32[]{:S(2)}, u32[]{:S(2)}) collective-permute-start(f32[22224]{0:T(1024)S(1)} %concatenate.32), channel_id=1, source_target_pairs={{0,192},{1,193},{2,194},{3,195},{4,196},{5,197},{6,198},{7,199},{8... | collective-permute-start | bytes 266696 | tf_op jit(solution)/shard_map/ppermute | solution.py:158
  50.9 3.6 %collective-permute-start.4 = (f32[22224]{0:T(1024)S(1)}, f32[22224]{0:T(1024)S(1)}, u32[]{:S(2)}, u32[]{:S(2)}) collective-permute-start(f32[22224]{0:T(1024)S(1)} %concatenate.31), channel_id=1, source_target_pairs={{0,384},{1,385},{2,386},{3,387},{4,388},{5,389},{6,390},{7,391},{8... | collective-permute-start | bytes 266696 | tf_op jit(solution)/shard_map/ppermute | solution.py:158
  54.6 8.1 %collective-permute-start.7 = (f32[2,24,128]{2,1,0:T(8,128)S(1)}, f32[2,24,128]{2,1,0:T(8,128)S(1)}, u32[]{:S(2)}, u32[]{:S(2)}) collective-permute-start(f32[2,24,128]{2,1,0:T(8,128)S(1)} %get-tuple-element.163), channel_id=1, source_target_pairs={{192,0},{193,1},{194,2},{195,3},{196,4},{197,5},{198,6},{199,7},{2... | collective-permute-start | bytes 73736 | tf_op jit(solution)/shard_map/ppermute | solution.py:210
  55.9 19.9 %collective-permute-start.8 = (f32[2,24,128]{2,1,0:T(8,128)S(1)}, f32[2,24,128]{2,1,0:T(8,128)S(1)}, u32[]{:S(2)}, u32[]{:S(2)}) collective-permute-start(f32[2,24,128]{2,1,0:T(8,128)S(1)} %get-tuple-element.163), channel_id=1, source_target_pairs={{384,0},{385,1},{386,2},{387,3},{388,4},{389,5},{390,6},{391,7},{3... | collective-permute-start | bytes 73736 | tf_op jit(solution)/shard_map/ppermute | solution.py:210
  57.2 18.6 %collective-permute-start.9 = (f32[2,24,128]{2,1,0:T(8,128)S(1)}, f32[2,24,128]{2,1,0:T(8,128)S(1)}, u32[]{:S(2)}, u32[]{:S(2)}) collective-permute-start(f32[2,24,128]{2,1,0:T(8,128)S(1)} %get-tuple-element.163), channel_id=1, source_target_pairs={{576,0},{577,1},{578,2},{579,3},{580,4},{581,5},{582,6},{583,7},{5... | collective-permute-start | bytes 73736 | tf_op jit(solution)/shard_map/ppermute | solution.py:210
  76.3 0.8 %copy-start.1 = (f32[1,40,24,128]{3,2,1,0:T(8,128)}, f32[1,40,24,128]{3,2,1,0:T(8,128)S(1)}, u32[]{:S(2)}) copy-start(f32[1,40,24,128]{3,2,1,0:T(8,128)S(1)} %get-tuple-element.297) | copy-start | bytes 1474564

commit v14 on v10

--- a/solution.py
+++ b/solution.py
@@ -156,7 +156,7 @@
             [zonal_r[levels].reshape(-1), merid_r[levels].reshape(-1), temper[levels].reshape(-1)]
         )
         arrived = lax.ppermute(payload, "grp", [(0, shift)])
-        own = arrived if own is None else jnp.where(member == shift, arrived, own)
+        own = arrived if own is None else own + arrived
     vel_size = LZ * vcols * vrows
     own_zonal = own[:vel_size].reshape(LZ, vcols, vrows)
     own_merid = own[vel_size : 2 * vel_size].reshape(LZ, vcols, vrows)

time: 77.4 us -> 76.3 us (0.986)
  waiting for transfers between devices: 28 us -> 26.2 us
    ppermute x3, waiting for transfers between devices: 2.01 us -> 0.82 us  [body(): arrived = lax.ppermute(payload, 'grp', [(0, shift)])]
  transfers between devices with their start and end apart: 10 -> 10, of which waited for: 7 -> 8; matrix products, arithmetic and copies ran while one was open for 3% -> 3% of each run, Pallas kernels for 0% -> 0%
where the time goes in v14:
time: 76.3 us; the launch traced here: 75.8 us
  starting transfers between devices  34 us (45%)
  waiting for transfers between devices  26.2 us (34%)
  other arithmetic  10.1 us (13%)
  local copies, waits for them, and re-layouts  5.11 us (7%)
    ppermute x3, waiting for transfers between devices, body(): returned.append(lax.ppermute(heating, 'grp', pairs))  16.7 us
    ppermute x2, starting transfers between devices, exchange(): lax.ppermute(lax.slice_in_dim(block, 0, width, axis=dim), axis, backward)  16 us
    ppermute x2, starting transfers between devices, exchange(): lax.ppermute(lax.slice_in_dim(block, block.shape[dim] - width, None, axis...  9.4 us
    ppermute x2, waiting for transfers between devices, exchange(): lax.ppermute(lax.slice_in_dim(block, 0, width, axis=dim), axis, backward)  6.75 us
    ppermute x3, starting transfers between devices, body(): arrived = lax.ppermute(payload, 'grp', [(0, shift)])  4.73 us
    ppermute x3, starting transfers between devices, body(): returned.append(lax.ppermute(heating, 'grp', pairs))  3.88 us
    select_n x1, other arithmetic, exchange(): return jnp.where(lower | upper, 0.0, block)  2.05 us
    mul x4, other arithmetic, advance_dynamics(): wet_mask * (zonal + coriolis_rows * merid - 0.5 * grad_x(surf_pad))  1.9 us
  transfers between devices with their start and end apart: 10, of which 8 were waited for; matrix products, arithmetic and copies ran while one was open for 3% of the time, Pallas kernels for 0%

profile of v14, /device:TPU:6, one launch (start us, length us, event | category | flops | bytes accessed | tf_op | source)
XLA Modules:
  0.0 75.8 jit_solution(5685482997308709796)
XLA Ops:
  0.0 0.7 convert_bitcast_fusion
  0.7 1.0 %pad_maximum_fusion.3 = (f32[41,7,128]{2,1,0:T(8,128)S(1)}, f32[41,7,128]{2,1,0:T(8,128)S(1)}) fusion(f32[1,24,128]{2,1,0:T(8,128)S(1)} %convert_bitcast_fusion, f32[40,24,128]{2,1,0:T(8,128)} %bitcast.116), kind=kLoop, calls=%fused_computation.112 | loop fusion | flops 73472 | bytes 797696 | tf_op jit(solution)/shard_map/slice | solution.py:18
  1.7 3.5 %collective-permute-start = (f32[41,7,128]{2,1,0:T(8,128)S(1)}, f32[41,7,128]{2,1,0:T(8,128)S(1)}, u32[]{:S(2)}, u32[]{:S(2)}) collective-permute-start(f32[41,7,128]{2,1,0:T(8,128)S(1)} %get-tuple-element.269), channel_id=1, source_target_pairs={{0,4},{4,8},{8,12},{12,16},{16,20},{20,24},{24,28},{28,32},{32,36}... | collective-permute-start | bytes 440840 | tf_op jit(solution)/shard_map/ppermute | solution.py:17
  5.2 14.1 %collective-permute-start.1 = (f32[41,7,128]{2,1,0:T(8,128)S(1)}, f32[41,7,128]{2,1,0:T(8,128)S(1)}, u32[]{:S(2)}, u32[]{:S(2)}) collective-permute-start(f32[41,7,128]{2,1,0:T(8,128)S(1)} %get-tuple-element.270), channel_id=1, source_target_pairs={{4,0},{8,4},{12,8},{16,12},{20,16},{24,20},{28,24},{32,28},{36,32}... | collective-permute-start | bytes 440840 | tf_op jit(solution)/shard_map/ppermute | solution.py:20
  19.3 0.5 add_convert_fusion.1
  19.9 1.8 %collective-permute-done = f32[41,7,128]{2,1,0:T(8,128)S(1)} collective-permute-done((f32[41,7,128]{2,1,0:T(8,128)S(1)}, f32[41,7,128]{2,1,0:T(8,128)S(1)}, u32[]{:S(2)}, u32[]{:S(2)}) %collective-permute-start) | collective-permute-done | bytes 146976 | tf_op jit(solution)/shard_map/ppermute | solution.py:17
  21.6 1.2 %collective-permute-done.1 = f32[41,7,128]{2,1,0:T(8,128)S(1)} collective-permute-done((f32[41,7,128]{2,1,0:T(8,128)S(1)}, f32[41,7,128]{2,1,0:T(8,128)S(1)}, u32[]{:S(2)}, u32[]{:S(2)}) %collective-permute-start.1) | collective-permute-done | bytes 146976 | tf_op jit(solution)/shard_map/ppermute | solution.py:20
  22.8 1.1 %pad_maximum_fusion.1 = f32[41,38,128]{2,1,0:T(8,128)S(1)} fusion(f32[41,7,128]{2,1,0:T(8,128)S(1)} %collective-permute-done.1, f32[1,24,128]{2,1,0:T(8,128)S(1)} %convert_bitcast_fusion, f32[40,24,128]{2,1,0:T(8,128)} %bitcast.117, f32[41,7,128]{2,1,0:T(8,128)S(1)} %collective-permute-done), kind=kLoop, calls=%fused_computation.108 | loop fusion | flops 598272 | bytes 1595392 | tf_op jit(solution)/shard_map/concatenate | solution.py:21
  24.0 0.3 fusion.25
  24.2 0.4 copy.17
  24.7 5.9 %collective-permute-start.2 = (f32[41,38,7]{0,1,2:T(8,128)S(1)}, f32[41,38,7]{0,1,2:T(8,128)S(1)}, u32[]{:S(2)}, u32[]{:S(2)}) collective-permute-start(f32[41,38,7]{0,1,2:T(8,128)S(1)} %copy.17), channel_id=1, source_target_pairs={{0,1},{1,2},{2,3},{3,0},{4,5},{5,6},{6,7},{7,4},{8,9},{9,10},{10,1... | collective-permute-start | bytes 130880 | tf_op jit(solution)/shard_map/ppermute | solution.py:17
  30.6 0.0 copy-start
  30.6 0.4 copy.18
  31.0 1.9 %collective-permute-start.3 = (f32[41,38,7]{0,1,2:T(8,128)S(1)}, f32[41,38,7]{0,1,2:T(8,128)S(1)}, u32[]{:S(2)}, u32[]{:S(2)}) collective-permute-start(f32[41,38,7]{0,1,2:T(8,128)S(1)} %copy.18), channel_id=1, source_target_pairs={{1,0},{2,1},{3,2},{0,3},{5,4},{6,5},{7,6},{4,7},{9,8},{10,9},{11,1... | collective-permute-start | bytes 130880 | tf_op jit(solution)/shard_map/ppermute | solution.py:20
  33.0 0.1 pad.7.clone
  33.1 0.1 collective-permute-done.2
  33.2 0.5 copy.19
  33.7 5.6 %collective-permute-done.3 = f32[41,38,7]{0,1,2:T(8,128)S(1)} collective-permute-done((f32[41,38,7]{0,1,2:T(8,128)S(1)}, f32[41,38,7]{0,1,2:T(8,128)S(1)}, u32[]{:S(2)}, u32[]{:S(2)}) %collective-permute-start.3) | collective-permute-done | bytes 43656 | tf_op jit(solution)/shard_map/ppermute | solution.py:20
  39.3 1.4 %copy.20 = f32[41,38,7]{2,1,0:T(8,128)} copy(f32[41,38,7]{0,1,2:T(8,128)S(1)} %collective-permute-done.3) | data formatting | bytes 87248 | tf_op jit(solution)/shard_map/ppermute | solution.py:20
  40.6 2.1 %maximum_select_fusion = f32[41,38,142]{2,1,0:T(8,128)S(1)} fusion(f32[41,38,7]{2,1,0:T(8,128)} %copy.20, f32[41,7,128]{2,1,0:T(8,128)S(1)} %collective-permute-done.1, f32[1,24,128]{2,1,0:T(8,128)S(1)} %convert_bitcast_fusion, f32[40,24,128]{2,1,0:T(8,128)S(1)} %bitcast.118, f32[41,7,128]{2,1,0:T(8,128)S(1)} %collective-permute-done, ...), kind=kLoop, calls=%fused_computation.107 | loop fusion | flops 1327416 | bytes 1770030 | tf_op jit(solution)/shard_map/jit(_where)/select_n | solution.py:26
  42.7 0.1 compare_convert_fusion
  42.8 3.8 %conditional.2 = (f32[19,30,134]{2,1,0:T(8,128)S(1)}) conditional(s32[]{:T(128)} %convert_element_type.40, () %tuple.46, (f32[6,38,142]{2,1,0:T(8,128)S(1)}, f32[41,38,142]{2,1,0:T(8,128)S(1)}, f32[142]{0:T(256)S(1)}, f32[38,142]{1,0:T(8,128)S(1)}) %tuple.47), branch_computations={%region_0.1_spmd, %region_1.6_spmd} | conditional | flops 3271180 | bytes 8120776 | solution.py:138
  42.8 0.3 add_reduce_fusion
  43.1 0.1 fusion.11
  43.3 0.1 slice.752
  43.3 0.5 subtract_multiply_fusion.3
  43.9 0.3 fusion.1
  44.1 0.1 fusion.8
  44.3 0.1 slice.758
  44.3 0.5 subtract_multiply_fusion.1
  44.9 0.2 fusion.5
  45.1 0.1 fusion.18
  45.2 0.1 slice.771
  45.3 0.4 subtract_multiply_fusion.7
  45.7 0.2 fusion.3
  46.0 0.1 fusion.15
  46.1 0.1 slice.784
  46.1 0.4 subtract_multiply_fusion.5
  46.6 0.1 pad_maximum_fusion
  46.7 0.1 fusion.26
  46.8 0.1 slice_bitcast_fusion.42
  46.9 0.2 reshape.140
  47.1 0.2 reshape.141
  47.3 0.1 concatenate.42
  47.4 1.3 %collective-permute-start.6 = (f32[22224]{0:T(1024)S(1)}, f32[22224]{0:T(1024)S(1)}, u32[]{:S(2)}, u32[]{:S(2)}) collective-permute-start(f32[22224]{0:T(1024)S(1)} %concatenate.42), channel_id=1, source_target_pairs={{0,576},{1,577},{2,578},{3,579},{4,580},{5,581},{6,582},{7,583},{8... | collective-permute-start | bytes 266696 | tf_op jit(solution)/shard_map/ppermute | solution.py:158
  48.7 0.2 reshape.137
  48.9 0.2 reshape.138
  49.1 0.1 concatenate.41
  49.2 2.1 %collective-permute-start.5 = (f32[22224]{0:T(1024)S(1)}, f32[22224]{0:T(1024)S(1)}, u32[]{:S(2)}, u32[]{:S(2)}) collective-permute-start(f32[22224]{0:T(1024)S(1)} %concatenate.41), channel_id=1, source_target_pairs={{0,384},{1,385},{2,386},{3,387},{4,388},{5,389},{6,390},{7,391},{8... | collective-permute-start | bytes 266696 | tf_op jit(solution)/shard_map/ppermute | solution.py:158
  51.3 0.2 reshape.134
  51.5 0.2 reshape.135
  51.7 0.1 concatenate.40
  51.8 1.3 %collective-permute-start.4 = (f32[22224]{0:T(1024)S(1)}, f32[22224]{0:T(1024)S(1)}, u32[]{:S(2)}, u32[]{:S(2)}) collective-permute-start(f32[22224]{0:T(1024)S(1)} %concatenate.40), channel_id=1, source_target_pairs={{0,192},{1,193},{2,194},{3,195},{4,196},{5,197},{6,198},{7,199},{8... | collective-permute-start | bytes 266696 | tf_op jit(solution)/shard_map/ppermute | solution.py:158
  53.1 0.1 compare_convert_fusion.1
  53.2 0.2 collective-permute-done.5
  53.5 0.6 collective-permute-done.4
  54.1 1.3 %collective-permute-start.7 = (f32[2,24,128]{2,1,0:T(8,128)S(1)}, f32[2,24,128]{2,1,0:T(8,128)S(1)}, u32[]{:S(2)}, u32[]{:S(2)}) collective-permute-start(f32[2,24,128]{2,1,0:T(8,128)S(1)} %get-tuple-element.150), channel_id=1, source_target_pairs={{192,0},{193,1},{194,2},{195,3},{196,4},{197,5},{198,6},{199,7},{2... | collective-permute-start | bytes 73736 | tf_op jit(solution)/shard_map/ppermute | solution.py:210
  55.4 1.3 %collective-permute-start.8 = (f32[2,24,128]{2,1,0:T(8,128)S(1)}, f32[2,24,128]{2,1,0:T(8,128)S(1)}, u32[]{:S(2)}, u32[]{:S(2)}) collective-permute-start(f32[2,24,128]{2,1,0:T(8,128)S(1)} %get-tuple-element.150), channel_id=1, source_target_pairs={{384,0},{385,1},{386,2},{387,3},{388,4},{389,5},{390,6},{391,7},{3... | collective-permute-start | bytes 73736 | tf_op jit(solution)/shard_map/ppermute | solution.py:210
  56.7 1.3 %collective-permute-start.9 = (f32[2,24,128]{2,1,0:T(8,128)S(1)}, f32[2,24,128]{2,1,0:T(8,128)S(1)}, u32[]{:S(2)}, u32[]{:S(2)}) collective-permute-start(f32[2,24,128]{2,1,0:T(8,128)S(1)} %get-tuple-element.150), channel_id=1, source_target_pairs={{576,0},{577,1},{578,2},{579,3},{580,4},{581,5},{582,6},{583,7},{5... | collective-permute-start | bytes 73736 | tf_op jit(solution)/shard_map/ppermute | solution.py:210
  58.0 0.1 slice_bitcast_fusion.45
  58.1 7.2 %collective-permute-done.7 = f32[2,24,128]{2,1,0:T(8,128)S(1)} collective-permute-done((f32[2,24,128]{2,1,0:T(8,128)S(1)}, f32[2,24,128]{2,1,0:T(8,128)S(1)}, u32[]{:S(2)}, u32[]{:S(2)}) %collective-permute-start.7) | collective-permute-done | bytes 24608 | tf_op jit(solution)/shard_map/ppermute | solution.py:210
  65.3 9.5 %collective-permute-done.8 = f32[2,24,128]{2,1,0:T(8,128)S(1)} collective-permute-done((f32[2,24,128]{2,1,0:T(8,128)S(1)}, f32[2,24,128]{2,1,0:T(8,128)S(1)}, u32[]{:S(2)}, u32[]{:S(2)}) %collective-permute-start.8) | collective-permute-done | bytes 24608 | tf_op jit(solution)/shard_map/ppermute | solution.py:210
  74.8 0.1 fusion.23
  74.9 0.9 %maximum_select_fusion.1 = f32[1,40,24,128]{3,2,1,0:T(8,128)} fusion(f32[1,40,24,128]{3,2,1,0:T(8,128)S(1)} %get-tuple-element.151, f32[1,1,24,128]{3,2,1,0:T(8,128)S(1)} %slice_bitcast_fusion.45, f32[1,6,24,128]{3,2,1,0:T(8,128)S(1)} %fusion.23, f32[1,12,24,128]{3,2,1,0:T(8,128)S(1)} %slice_bitcast_fusion.42, f32[40]{0:T(128)S(1)} %pad.7.clone, pred[]{:T(512)S(6)} %eq.11), kind=kLoop, calls=%fused_computation.109 | loop fusion | flops 491520 | bytes 1216673 | tf_op jit(solution)/shard_map/jit(_where)/select_n | solution.py:215
  (19 shorter events, 0.2 us)
Async XLA Ops:
  1.7 19.9 %collective-permute-start = (f32[41,7,128]{2,1,0:T(8,128)S(1)}, f32[41,7,128]{2,1,0:T(8,128)S(1)}, u32[]{:S(2)}, u32[]{:S(2)}) collective-permute-start(f32[41,7,128]{2,1,0:T(8,128)S(1)} %get-tuple-element.269), channel_id=1, source_target_pairs={{0,4},{4,8},{8,12},{12,16},{16,20},{20,24},{24,28},{28,32},{32,36}... | collective-permute-start | bytes 440840 | tf_op jit(solution)/shard_map/ppermute | solution.py:17
  5.2 17.6 %collective-permute-start.1 = (f32[41,7,128]{2,1,0:T(8,128)S(1)}, f32[41,7,128]{2,1,0:T(8,128)S(1)}, u32[]{:S(2)}, u32[]{:S(2)}) collective-permute-start(f32[41,7,128]{2,1,0:T(8,128)S(1)} %get-tuple-element.270), channel_id=1, source_target_pairs={{4,0},{8,4},{12,8},{16,12},{20,16},{24,20},{28,24},{32,28},{36,32}... | collective-permute-start | bytes 440840 | tf_op jit(solution)/shard_map/ppermute | solution.py:20
  24.7 8.5 %collective-permute-start.2 = (f32[41,38,7]{0,1,2:T(8,128)S(1)}, f32[41,38,7]{0,1,2:T(8,128)S(1)}, u32[]{:S(2)}, u32[]{:S(2)}) collective-permute-start(f32[41,38,7]{0,1,2:T(8,128)S(1)} %copy.17), channel_id=1, source_target_pairs={{0,1},{1,2},{2,3},{3,0},{4,5},{5,6},{6,7},{7,4},{8,9},{9,10},{10,1... | collective-permute-start | bytes 130880 | tf_op jit(solution)/shard_map/ppermute | solution.py:17
  30.6 10.0 %copy-start = (f32[1,40,24,128]{3,2,1,0:T(8,128)S(1)}, f32[1,40,24,128]{3,2,1,0:T(8,128)}, u32[]{:S(2)}) copy-start(f32[1,40,24,128]{3,2,1,0:T(8,128)} %param.8) | copy-start | bytes 1474564
  31.0 8.2 %collective-permute-start.3 = (f32[41,38,7]{0,1,2:T(8,128)S(1)}, f32[41,38,7]{0,1,2:T(8,128)S(1)}, u32[]{:S(2)}, u32[]{:S(2)}) collective-permute-start(f32[41,38,7]{0,1,2:T(8,128)S(1)} %copy.18), channel_id=1, source_target_pairs={{1,0},{2,1},{3,2},{0,3},{5,4},{6,5},{7,6},{4,7},{9,8},{10,9},{11,1... | collective-permute-start | bytes 130880 | tf_op jit(solution)/shard_map/ppermute | solution.py:20
  46.6 7.4 %copy-start.2 = (f32[20]{0:T(128)S(1)}, f32[20]{0:T(128)}, u32[]{:S(2)}) copy-start(f32[20]{0:T(128)} %param.11) | copy-start | bytes 244
  47.4 5.8 %collective-permute-start.6 = (f32[22224]{0:T(1024)S(1)}, f32[22224]{0:T(1024)S(1)}, u32[]{:S(2)}, u32[]{:S(2)}) collective-permute-start(f32[22224]{0:T(1024)S(1)} %concatenate.42), channel_id=1, source_target_pairs={{0,576},{1,577},{2,578},{3,579},{4,580},{5,581},{6,582},{7,583},{8... | collective-permute-start | bytes 266696 | tf_op jit(solution)/shard_map/ppermute | solution.py:158
  49.2 4.3 %collective-permute-start.5 = (f32[22224]{0:T(1024)S(1)}, f32[22224]{0:T(1024)S(1)}, u32[]{:S(2)}, u32[]{:S(2)}) collective-permute-start(f32[22224]{0:T(1024)S(1)} %concatenate.41), channel_id=1, source_target_pairs={{0,384},{1,385},{2,386},{3,387},{4,388},{5,389},{6,390},{7,391},{8... | collective-permute-start | bytes 266696 | tf_op jit(solution)/shard_map/ppermute | solution.py:158
  51.8 2.2 %collective-permute-start.4 = (f32[22224]{0:T(1024)S(1)}, f32[22224]{0:T(1024)S(1)}, u32[]{:S(2)}, u32[]{:S(2)}) collective-permute-start(f32[22224]{0:T(1024)S(1)} %concatenate.40), channel_id=1, source_target_pairs={{0,192},{1,193},{2,194},{3,195},{4,196},{5,197},{6,198},{7,199},{8... | collective-permute-start | bytes 266696 | tf_op jit(solution)/shard_map/ppermute | solution.py:158
  54.1 11.2 %collective-permute-start.7 = (f32[2,24,128]{2,1,0:T(8,128)S(1)}, f32[2,24,128]{2,1,0:T(8,128)S(1)}, u32[]{:S(2)}, u32[]{:S(2)}) collective-permute-start(f32[2,24,128]{2,1,0:T(8,128)S(1)} %get-tuple-element.150), channel_id=1, source_target_pairs={{192,0},{193,1},{194,2},{195,3},{196,4},{197,5},{198,6},{199,7},{2... | collective-permute-start | bytes 73736 | tf_op jit(solution)/shard_map/ppermute | solution.py:210
  55.4 19.4 %collective-permute-start.8 = (f32[2,24,128]{2,1,0:T(8,128)S(1)}, f32[2,24,128]{2,1,0:T(8,128)S(1)}, u32[]{:S(2)}, u32[]{:S(2)}) collective-permute-start(f32[2,24,128]{2,1,0:T(8,128)S(1)} %get-tuple-element.150), channel_id=1, source_target_pairs={{384,0},{385,1},{386,2},{387,3},{388,4},{389,5},{390,6},{391,7},{3... | collective-permute-start | bytes 73736 | tf_op jit(solution)/shard_map/ppermute | solution.py:210
  56.7 18.1 %collective-permute-start.9 = (f32[2,24,128]{2,1,0:T(8,128)S(1)}, f32[2,24,128]{2,1,0:T(8,128)S(1)}, u32[]{:S(2)}, u32[]{:S(2)}) collective-permute-start(f32[2,24,128]{2,1,0:T(8,128)S(1)} %get-tuple-element.150), channel_id=1, source_target_pairs={{576,0},{577,1},{578,2},{579,3},{580,4},{581,5},{582,6},{583,7},{5... | collective-permute-start | bytes 73736 | tf_op jit(solution)/shard_map/ppermute | solution.py:210
